TPU v7x, 32 devices: a whole 2x2x4 slice. The times are simulated.
32 devices in a mesh: grp: 2 (over y), resp: 16 (over z, x, core).
Axes of the slice: x: 2, y: 2, z: 4, core: 2. Of those that a mesh axis runs over, the one named last changes fastest.
Arguments:
- queries: bfloat16 [4096, 2560], P(('grp', 'resp')), parts along dimension 0, may hold values from -120 to 120
- response_keys: bfloat16 [4096, 512], P(('grp', 'resp')), parts along dimension 0, may hold values from -6 to 6
- response_values: bfloat16 [4096, 512], P(('grp', 'resp')), parts along dimension 0, may hold values from -6 to 6
- document_keys: bfloat16 [256, 512], P(('grp', 'resp')), parts along dimension 0, may hold values from -6 to 6
- document_values: bfloat16 [256, 512], P(('grp', 'resp')), parts along dimension 0, may hold values from -6 to 6
- grad_out: bfloat16 [4096, 2560], P(('grp', 'resp')), parts along dimension 0, may hold values from -6 to 6
- lengths: int32 [64], P(('grp', 'resp')), parts along dimension 0, may hold values from 1 to 64, 1280 in all
- doc_mask: int32 [64, 16], P(('grp', 'resp')), parts along dimension 0, may hold values 0 or 1
Outputs:
- query_gradient: bfloat16 [4096, 2560], P(('grp', 'resp')), parts along dimension 0
- grad_doc_keys: bfloat16 [256, 512], P(('grp', 'resp')), parts along dimension 0
- grad_doc_values: bfloat16 [256, 512], P(('grp', 'resp')), parts along dimension 0
- grad_resp_keys: bfloat16 [4096, 512], P(('grp', 'resp')), parts along dimension 0
- grad_resp_values: bfloat16 [4096, 512], P(('grp', 'resp')), parts along dimension 0
There are 2 independent parts, one for each index of `grp`. A program takes and returns all parts, laid end to end along the dimension named above; each array names one. Nothing has to cross between parts.
All inputs are finite; a program needn't handle non-finite values. No bound on the sum of `lengths` or of `doc_mask` on one device may be relied on, other than what follows from the above.
Results may differ from a plain program's by a relative error of at most 0.0051.
Values may be sent and summed in bfloat16 or wider, within the bound.
No kernel may reach another device: no remote copies, remote signals or barrier semaphores. Data moves between devices by JAX's collectives and lax.ppermute only.
A program may use at most 64 MiB of HBM per device.

v0:
```python
import jax
import jax.numpy as jnp
from jax import lax
from jax.sharding import PartitionSpec as P

KEY_HEADS = 4
GROUP_HEADS = 5
HEAD_SIZE = 128


masked_score = -1e30


def per_device(
    queries,
    response_keys,
    response_values,
    document_keys,
    document_values,
    grad_out,
    lengths,
    doc_mask,
):
    token_rows = queries.shape[0]
    responses_here = lengths.shape[0]
    resp_len = token_rows // responses_here
    slab_rows = document_keys.shape[0]
    mask_blocks = doc_mask.shape[1]
    key_value_width = KEY_HEADS * HEAD_SIZE
    score_scale = HEAD_SIZE ** (-0.5)
    positions = jnp.arange(token_rows, dtype=jnp.int32)
    owners = positions // resp_len
    within = positions % resp_len
    active_rows = within < jnp.repeat(lengths, resp_len)
    query_head_rows = queries.reshape(token_rows, KEY_HEADS, GROUP_HEADS, HEAD_SIZE)
    grad_heads = jnp.where(active_rows[:, None], grad_out, jnp.zeros_like(grad_out)).reshape(
        token_rows, KEY_HEADS, GROUP_HEADS, HEAD_SIZE
    )
    response_own_keys = response_keys.reshape(token_rows, KEY_HEADS, HEAD_SIZE)
    response_own_values = response_values.reshape(token_rows, KEY_HEADS, HEAD_SIZE)
    self_visible = (owners[:, None] == owners[None, :]) & (positions[None, :] <= positions[:, None])
    row_masks = jnp.repeat(doc_mask, resp_len, axis=0).astype(jnp.float32)
    collected_keys, collected_values = (
        lax.all_gather(document_keys, "resp", axis=0, tiled=True),
        lax.all_gather(document_values, "resp", axis=0, tiled=True),
    )
    doc_rows = collected_keys.shape[0]
    block_span = 128
    block_count = doc_rows // block_span
    key_block_list = collected_keys.reshape(block_count, block_span, KEY_HEADS, HEAD_SIZE)
    value_block_list = collected_values.reshape(block_count, block_span, KEY_HEADS, HEAD_SIZE)
    block_index = jnp.arange(block_count, dtype=jnp.int32)

    def visible(first_row, row_count):
        labels = (first_row + jnp.arange(row_count, dtype=jnp.int32)) // slab_rows
        one_hot = (jnp.arange(mask_blocks, dtype=jnp.int32)[:, None] == labels[None, :]).astype(
            jnp.float32
        )
        return jnp.dot(row_masks, one_hot) > 0.5

    def logits(keys_block, is_seen):
        raw_scores = (
            jnp.einsum(
                "tcgd,kcd->tcgk", query_head_rows, keys_block, preferred_element_type=jnp.float32
            )
            * score_scale
        )
        return jnp.where(is_seen[:, None, None, :], raw_scores, masked_score)

    def slopes(values_block):
        return jnp.einsum(
            "tcgd,kcd->tcgk", grad_heads, values_block, preferred_element_type=jnp.float32
        )

    def update_stats(stats_now, keys_block, values_block, is_seen):
        running, denominator, weighted = stats_now
        raw_scores = logits(keys_block, is_seen)
        newest = jnp.maximum(running, jnp.max(raw_scores, axis=-1))
        exp_terms = jnp.where(
            is_seen[:, None, None, :], jnp.exp(raw_scores - newest[..., None]), 0.0
        )
        factor = jnp.exp(running - newest)
        return (
            newest,
            denominator * factor + jnp.sum(exp_terms, axis=-1),
            weighted * factor + jnp.sum(exp_terms * slopes(values_block), axis=-1),
        )

    statistics_shape = (token_rows, KEY_HEADS, GROUP_HEADS)
    first_stats = (
        jnp.full(statistics_shape, masked_score, jnp.float32),
        jnp.zeros(statistics_shape, jnp.float32),
        jnp.zeros(statistics_shape, jnp.float32),
    )
    first_stats = update_stats(first_stats, response_own_keys, response_own_values, self_visible)

    def stats_turn(stats_now, inputs):
        keys_block, values_block, number = inputs
        return (
            update_stats(
                stats_now, keys_block, values_block, visible(number * block_span, block_span)
            ),
            None,
        )

    final_stats, unused = lax.scan(
        stats_turn, first_stats, (key_block_list, value_block_list, block_index)
    )
    running, denominator, weighted = final_stats
    row_drift = weighted / denominator

    def block_grads(keys_block, values_block, is_seen, with_keys):
        raw_scores = logits(keys_block, is_seen)
        probabilities = jnp.where(
            is_seen[:, None, None, :],
            jnp.exp(raw_scores - running[..., None]) / denominator[..., None],
            0.0,
        )
        mixed_grad = (probabilities * (slopes(values_block) - row_drift[..., None])).astype(
            jnp.bfloat16
        )
        query_grad = score_scale * jnp.einsum(
            "tcgk,kcd->tcgd", mixed_grad, keys_block, preferred_element_type=jnp.float32
        )
        if not with_keys:
            return query_grad
        key_grad = score_scale * jnp.einsum(
            "tcgk,tcgd->kcd", mixed_grad, query_head_rows, preferred_element_type=jnp.float32
        )
        value_grad = jnp.einsum(
            "tcgk,tcgd->kcd",
            probabilities.astype(jnp.bfloat16),
            grad_heads,
            preferred_element_type=jnp.float32,
        )
        return (query_grad, key_grad, value_grad)

    response_query, self_key, self_value = block_grads(
        response_own_keys, response_own_values, self_visible, True
    )
    query_initial = jnp.zeros((token_rows, KEY_HEADS, GROUP_HEADS, HEAD_SIZE), jnp.float32)

    def query_turn(query_total, inputs):
        keys_block, values_block, number = inputs
        return (
            query_total
            + block_grads(
                keys_block, values_block, visible(number * block_span, block_span), False
            ),
            None,
        )

    document_query, unused = lax.scan(
        query_turn, query_initial, (key_block_list, value_block_list, block_index)
    )

    def piece_grads(offset, length):
        keys_block = lax.dynamic_slice_in_dim(collected_keys, offset, length, 0).reshape(
            length, KEY_HEADS, HEAD_SIZE
        )
        values_block = lax.dynamic_slice_in_dim(collected_values, offset, length, 0).reshape(
            length, KEY_HEADS, HEAD_SIZE
        )
        unused_query, key_grad, value_grad = block_grads(
            keys_block, values_block, visible(offset, length), True
        )
        return jnp.concatenate(
            [
                key_grad.reshape(length, key_value_width),
                value_grad.reshape(length, key_value_width),
            ],
            axis=1,
        )

    def terms(first_row, row_count):
        if row_count > block_span and row_count % block_span == 0:

            def term_turn(counter, number):
                return (counter, piece_grads(first_row + number * block_span, block_span))

            unused_counter, stacked = lax.scan(
                term_turn,
                jnp.zeros((), jnp.int32),
                jnp.arange(row_count // block_span, dtype=jnp.int32),
            )
            return stacked.reshape(row_count, 2 * key_value_width)
        return piece_grads(first_row, row_count)

    summed = lax.psum_scatter(
        terms(jnp.int32(0), slab_rows * lax.axis_size("resp")),
        "resp",
        scatter_dimension=0,
        tiled=True,
    )
    doc_key_grad = summed[:, :key_value_width]
    doc_value_grad = summed[:, key_value_width:]
    query_gradient = (
        (document_query + response_query)
        .reshape(token_rows, KEY_HEADS * GROUP_HEADS * HEAD_SIZE)
        .astype(jnp.bfloat16)
    )
    return (
        query_gradient,
        doc_key_grad.astype(jnp.bfloat16),
        doc_value_grad.astype(jnp.bfloat16),
        self_key.reshape(token_rows, key_value_width).astype(jnp.bfloat16),
        self_value.reshape(token_rows, key_value_width).astype(jnp.bfloat16),
    )


def solution(mesh):
    return jax.shard_map(
        per_device,
        mesh=mesh,
        in_specs=(
            P(("grp", "resp"), None),
            P(("grp", "resp"), None),
            P(("grp", "resp"), None),
            P(("grp", "resp"), None),
            P(("grp", "resp"), None),
            P(("grp", "resp"), None),
            P(("grp", "resp")),
            P(("grp", "resp"), None),
        ),
        out_specs=(
            P(("grp", "resp"), None),
            P(("grp", "resp"), None),
            P(("grp", "resp"), None),
            P(("grp", "resp"), None),
            P(("grp", "resp"), None),
        ),
        check_vma=False,
    )
```

profile of v0, /device:TPU:0, one launch (start us, length us, event | category | flops | bytes accessed | tf_op | source)
XLA Modules:
  0.0 131.9 jit_solution(2446103246415774838)
XLA Ops:
  7.3 1.5 %copy.61 = bf16[128,2560]{0,1:T(8,128)(2,1)S(1)} copy(bf16[128,2560]{1,0:T(8,128)(2,1)} %param.8) | data formatting | bytes 1310720 | tf_op args[0]
  8.8 23.5 %all_gather.6 = bf16[128,512]{1,0:T(8,128)(2,1)S(1)} all-gather(bf16[8,512]{1,0:T(8,128)(2,1)S(1)} %copy-done.15), channel_id=1, replica_groups=mesh['grp'=2,'resp'=16] {'resp'}, dimensions={0}, use_global_device_ids=true | all-gather | bytes 139264 | tf_op jit(solution)/shard_map/all_gather | solution.py:44
  32.7 0.1 copy.95
  32.8 1.1 copy.66
  34.0 0.5 fusion.20
  34.6 17.8 %all_gather.7 = bf16[128,512]{1,0:T(8,128)(2,1)S(1)} all-gather(bf16[8,512]{1,0:T(8,128)(2,1)S(1)} %copy-done.16), channel_id=1, replica_groups=mesh['grp'=2,'resp'=16] {'resp'}, dimensions={0}, use_global_device_ids=true | all-gather | bytes 139264 | tf_op jit(solution)/shard_map/all_gather | solution.py:45
  52.3 0.8 copy.67
  53.1 0.7 reshape.191
  53.8 0.2 fusion.10
  54.0 0.4 fusion.26
  54.4 0.4 fusion.25
  54.8 0.6 copy-done.5
  55.6 1.5 %select_reduce_fusion = (f32[128,4,5]{0,2,1:T(8,128)S(1)}, f32[128,4,5]{0,2,1:T(8,128)S(1)}, f32[128,4,5,128]{0,3,2,1:T(8,128)}) fusion(f32[128,4,5,128]{0,3,2,1:T(8,128)S(1)} %get-tuple-element.92, f32[128,4,5]{0,2,1:T(8,128)S(1)} %get-tuple-element.88, pred[128,128]{0,1:T(8,128)(4,1)S(1)} %fusion.10, bf16[128,4,5,128]{0,3,2,1:T(8,128)(2,1)S(1)} %bitcast.90, ...), kind=kOutput, calls=%fused_computation.19 | convolution fusion | flops 85519360 | bytes 3454976 | tf_op jit(solution)/shard_map/while/body/eval_jaxpr/tcgd,kcd->tcgk/dot_general | solution.py:71
  57.1 1.5 %fusion.11 = (f32[128,4,5]{0,2,1:T(8,128)S(1)}, f32[128,4,5]{0,2,1:T(8,128)S(1)}, f32[128,4,5,128]{0,3,2,1:T(8,128)}) fusion(f32[128,4,5,128]{0,3,2,1:T(8,128)S(1)} %get-tuple-element.90, f32[128,4,5]{0,2,1:T(8,128)S(1)} %get-tuple-element.87, pred[128,128]{0,1:T(8,128)(4,1)S(1)} %fusion.16, bf16[128,4,5,128]{0,3,2,1:T(8,128)(2,1)S(1)} %bitcast.91, ...), kind=kOutput, calls=%fused_computation.29 | convolution fusion | flops 85519360 | bytes 3454976 | tf_op jit(solution)/shard_map/tcgd,kcd->tcgk/dot_general | solution.py:71
  58.5 0.6 multiply_add_fusion
  59.2 1.1 fusion.13
  60.3 1.8 %copy.78 = f32[128,512]{1,0:T(8,128)} copy(f32[128,512]{0,1:T(8,128)} %bitcast.102) | data formatting | bytes 524288 | tf_op jit(solution)/shard_map/reshape | solution.py:170
  62.1 3.3 %multiply_convert_fusion = (bf16[128,4,5,128]{0,3,2,1:T(8,128)(2,1)}, bf16[128,4,5,128]{0,3,2,1:T(8,128)(2,1)S(1)}) fusion(f32[128,4,5,128]{0,3,2,1:T(8,128)} %get-tuple-element.94, f32[128,4,5]{0,2,1:T(8,128)} %get-tuple-element.82, f32[128,4,5]{0,2,1:T(8,128)} %copy-done.14, f32[128,4,5,128]{0,3,2,1:T(8,128)S(1)} %get-tuple-element.90, ...), kind=kLoop, calls=%fused_computation.11 | loop fusion | flops 3932160 | bytes 6617088 | tf_op jit(solution)/shard_map/convert_element_type | solution.py:119
  65.4 0.8 copy-done
  66.3 1.1 fusion.6
  67.4 1.1 copy.77
  68.5 0.8 pad_maximum_fusion
  69.4 1.9 %fusion.8 = bf16[4,128,128]{2,1,0:T(8,128)(2,1)} fusion(bf16[128,4,5,128]{0,3,2,1:T(8,128)(2,1)S(1)} %bitcast.93, f32[128,4,5,128]{0,3,2,1:T(8,128)S(1)} %get-tuple-element.90, f32[128,4,5]{0,2,1:T(8,128)} %copy-done.14, f32[128,4,5]{0,2,1:T(8,128)} %copy-done.11, pred[128,128]{0,1:T(8,128)(4,1)S(1)} %fusion.16), kind=kOutput, calls=%fused_computation.25 | convolution fusion | flops 85262336 | bytes 2134016 | tf_op jit(solution)/shard_map/tcgk,tcgd->kcd/dot_general | solution.py:130
  71.2 1.7 %copy.83 = bf16[128,512]{1,0:T(8,128)(2,1)} copy(bf16[128,512]{0,1:T(8,128)(2,1)} %bitcast.103) | data formatting | bytes 262144
  73.0 0.3 fusion.27
  73.3 0.3 fusion.5
  73.6 1.1 copy.81
  74.7 0.4 fusion.9
  75.1 0.8 copy.82
  75.9 47.8 %reduce-scatter.2.cloned.1.call-done = f32[8,1024]{1,0:T(8,128)} async-done(((f32[128,1024]{1,0:T(8,128)}), f32[8,1024]{1,0:T(8,128)}) %reduce-scatter.2.cloned.1.call-update) | async-done | bytes 32784 | tf_op jit(solution)/shard_map/reduce_scatter | solution.py:189
  123.7 0.8 convert.4
  124.5 0.6 fusion.24
  (51 shorter events, 0.6 us)
Async XLA Ops:
  7.2 1.6 %copy-start.18 = (s32[2,16]{1,0:T(2,128)S(1)}, s32[2,16]{1,0:T(2,128)}, u32[]{:S(2)}) copy-start(s32[2,16]{1,0:T(2,128)} %param.15) | copy-start | bytes 388
  7.2 1.6 %copy-start.15 = (bf16[8,512]{1,0:T(8,128)(2,1)S(1)}, bf16[8,512]{1,0:T(8,128)(2,1)}, u32[]{:S(2)}) copy-start(bf16[8,512]{1,0:T(8,128)(2,1)} %param.11) | copy-start | bytes 24580
  7.2 25.4 %copy-start.12 = (bf16[128,512]{1,0:T(8,128)(2,1)S(1)}, bf16[128,512]{1,0:T(8,128)(2,1)}, u32[]{:S(2)}) copy-start(bf16[128,512]{1,0:T(8,128)(2,1)} %param.9) | copy-start | bytes 393220
  7.2 25.6 %copy-start.7 = (bf16[128,2560]{1,0:T(8,128)(2,1)S(1)}, bf16[128,2560]{1,0:T(8,128)(2,1)}, u32[]{:S(2)}) copy-start(bf16[128,2560]{1,0:T(8,128)(2,1)} %param.13) | copy-start | bytes 1966084
  7.2 116.5 %reduce-scatter.2.cloned.1.call-start = ((), (), s32[]{:S(2)}) async-start(), calls=%async_computation.1 | async-start | bytes 557056 | tf_op jit(solution)/shard_map/reduce_scatter | solution.py:189
  8.8 25.1 %copy-start.19 = (s32[2]{0:T(128)S(1)}, s32[2]{0:T(128)}, u32[]{:S(2)}) copy-start(s32[2]{0:T(128)} %param.14) | copy-start | bytes 28
  8.8 25.8 %copy-start.16 = (bf16[8,512]{1,0:T(8,128)(2,1)S(1)}, bf16[8,512]{1,0:T(8,128)(2,1)}, u32[]{:S(2)}) copy-start(bf16[8,512]{1,0:T(8,128)(2,1)} %param.12) | copy-start | bytes 24580
  8.8 44.3 %copy-start.13 = (bf16[128,512]{1,0:T(8,128)(2,1)S(1)}, bf16[128,512]{1,0:T(8,128)(2,1)}, u32[]{:S(2)}) copy-start(bf16[128,512]{1,0:T(8,128)(2,1)} %param.10) | copy-start | bytes 393220
  54.0 5.2 %copy-start.10 = (pred[128,128]{0,1:T(8,128)(4,1)}, pred[128,128]{0,1:T(8,128)(4,1)S(1)}, u32[]{:S(2)}) copy-start(pred[128,128]{0,1:T(8,128)(4,1)S(1)} %fusion.10) | copy-start | bytes 49156
  54.4 1.1 copy-start.5
  54.4 1.1 copy-start.17
  54.4 1.1 copy-start.9
  55.5 3.7 %copy-start.11 = (f32[128,4,5]{0,2,1:T(8,128)}, f32[128,4,5]{0,2,1:T(8,128)S(1)}, u32[]{:S(2)}) copy-start(f32[128,4,5]{0,2,1:T(8,128)S(1)} %get-tuple-element.88) | copy-start | bytes 30724
  55.5 3.6 %copy-start.3 = (bf16[128,2560]{0,1:T(8,128)(2,1)}, bf16[128,2560]{0,1:T(8,128)(2,1)S(1)}, u32[]{:S(2)}) copy-start(bf16[128,2560]{0,1:T(8,128)(2,1)S(1)} %broadcast_select_fusion) | copy-start | bytes 1966084
  55.6 1.5 %copy-start.8 = (bf16[128,4,128]{2,1,0:T(4,128)(2,1)S(1)}, bf16[128,4,128]{2,1,0:T(4,128)(2,1)}, u32[]{:S(2)}) copy-start(bf16[128,4,128]{2,1,0:T(4,128)(2,1)} %reshape.191) | copy-start | bytes 393220
  59.2 1.1 copy-start.14
  65.4 0.8 copy-start
  65.4 3.1 %copy-start.6 = (f32[128,512]{1,0:T(8,128)S(1)}, f32[128,512]{1,0:T(8,128)}, u32[]{:S(2)}) copy-start(f32[128,512]{1,0:T(8,128)} %copy.78) | copy-start | bytes 786436
  67.3 2.0 %copy-start.4 = (bf16[128,2560]{0,1:T(8,128)(2,1)S(1)}, bf16[128,2560]{0,1:T(8,128)(2,1)}, u32[]{:S(2)}) copy-start(bf16[128,2560]{0,1:T(8,128)(2,1)} %copy-done.3) | copy-start | bytes 1966084
  69.4 3.6 %copy-start.1 = (bf16[128,4,5,128]{0,3,2,1:T(8,128)(2,1)S(1)}, bf16[128,4,5,128]{0,3,2,1:T(8,128)(2,1)}, u32[]{:S(2)}) copy-start(bf16[128,4,5,128]{0,3,2,1:T(8,128)(2,1)} %copy-done) | copy-start | bytes 1966084
  71.2 2.1 %copy-start.2 = (bf16[128,4,5,128]{0,3,2,1:T(8,128)(2,1)S(1)}, bf16[128,4,5,128]{0,3,2,1:T(8,128)(2,1)}, u32[]{:S(2)}) copy-start(bf16[128,4,5,128]{0,3,2,1:T(8,128)(2,1)} %get-tuple-element.83) | copy-start | bytes 1966084
Sparse Core Ops, SparseCore 0:
  69.5 54.1 reduce-scatter.1
where the time goes:
time: 132 us
  waiting for transfers between devices  47.8 us (36%)
  blocking collectives  41.3 us (31%)
  between operations  14.3 us (11%)
  local copies, waits for them, and re-layouts  13.2 us (10%)
  matrix products  8.96 us (7%)
  other arithmetic  6.25 us (5%)
    reduce_scatter x1, waiting for transfers between devices, per_device(): lax.psum_scatter(terms(jnp.int32(0), slab_rows * lax.axis_size('resp')),...  47.8 us
    all_gather x1, blocking collectives, per_device(): lax.all_gather(document_keys, 'resp', axis=0, tiled=True)  23.5 us
    all_gather x1, blocking collectives, per_device(): lax.all_gather(document_values, 'resp', axis=0, tiled=True)  17.8 us
    unnamed x45, local copies, waits for them, and re-layouts  7.73 us
    convert_element_type x1, other arithmetic, block_grads(): (probabilities * (slopes(values_block) - row_drift[..., None])).astype(jn...  3.35 us
    dot_general x2, matrix products, slopes(): jnp.einsum('tcgd,kcd->tcgk', grad_heads, values_block, preferred_element_...  2.95 us
    dot_general x2, matrix products, block_grads(): jnp.einsum('tcgk,tcgd->kcd', probabilities.astype(jnp.bfloat16), grad_hea...  2.95 us
  transfers between devices with their start and end apart: 1, of which 1 were waited for; matrix products, arithmetic and copies ran while one was open for 5% of the time, Pallas kernels for 0%

commit v1 on v0

--- a/solution.py
+++ b/solution.py
@@ -9,6 +9,51 @@
 
 
 masked_score = -1e30
+
+
+def exchange_bits(size):
+    bits = size.bit_length() - 1
+    if (1 << bits) != size:
+        return None
+    return bits
+
+
+def swap_with(block, axis_name, size, bit):
+    pairs = [(index, index ^ (1 << bit)) for index in range(size)]
+    return lax.ppermute(block, axis_name, pairs)
+
+
+def gather_rows(block, axis_name):
+    size = lax.axis_size(axis_name)
+    bits = exchange_bits(size)
+    if bits is None:
+        return lax.all_gather(block, axis_name, axis=0, tiled=True)
+    me = lax.axis_index(axis_name)
+    stacked = block
+    for bit in reversed(range(bits)):
+        other = swap_with(stacked, axis_name, size, bit)
+        mine_low = ((me >> bit) & 1) == 0
+        stacked = jnp.where(mine_low, jnp.stack([stacked, other]), jnp.stack([other, stacked]))
+    stacked = stacked.reshape((2,) * bits + block.shape)
+    stacked = jnp.transpose(stacked, tuple(reversed(range(bits))) + (bits, bits + 1))
+    return stacked.reshape((size * block.shape[0],) + block.shape[1:])
+
+
+def scatter_sum_rows(block, axis_name):
+    size = lax.axis_size(axis_name)
+    bits = exchange_bits(size)
+    if bits is None:
+        return lax.psum_scatter(block, axis_name, scatter_dimension=0, tiled=True)
+    me = lax.axis_index(axis_name)
+    rows = block.shape[0] // size
+    parts = block.reshape((2,) * bits + (rows,) + block.shape[1:])
+    for bit in range(bits):
+        axis = bits - 1 - bit
+        mine = (me >> bit) & 1
+        keep = lax.dynamic_index_in_dim(parts, mine, axis, keepdims=False)
+        send = lax.dynamic_index_in_dim(parts, 1 - mine, axis, keepdims=False)
+        parts = keep + swap_with(send, axis_name, size, bit)
+    return parts.reshape((rows,) + block.shape[1:])
 
 
 def per_device(
@@ -40,10 +85,9 @@
     response_own_values = response_values.reshape(token_rows, KEY_HEADS, HEAD_SIZE)
     self_visible = (owners[:, None] == owners[None, :]) & (positions[None, :] <= positions[:, None])
     row_masks = jnp.repeat(doc_mask, resp_len, axis=0).astype(jnp.float32)
-    collected_keys, collected_values = (
-        lax.all_gather(document_keys, "resp", axis=0, tiled=True),
-        lax.all_gather(document_values, "resp", axis=0, tiled=True),
-    )
+    collected = gather_rows(jnp.concatenate([document_keys, document_values], axis=1), "resp")
+    collected_keys = collected[:, :key_value_width]
+    collected_values = collected[:, key_value_width:]
     doc_rows = collected_keys.shape[0]
     block_span = 128
     block_count = doc_rows // block_span
@@ -186,12 +230,7 @@
             return stacked.reshape(row_count, 2 * key_value_width)
         return piece_grads(first_row, row_count)
 
-    summed = lax.psum_scatter(
-        terms(jnp.int32(0), slab_rows * lax.axis_size("resp")),
-        "resp",
-        scatter_dimension=0,
-        tiled=True,
-    )
+    summed = scatter_sum_rows(terms(jnp.int32(0), slab_rows * lax.axis_size("resp")), "resp")
     doc_key_grad = summed[:, :key_value_width]
     doc_value_grad = summed[:, key_value_width:]
     query_gradient = (

time: 132 us -> 59.4 us (0.45)
  blocking collectives: 41.3 us -> 0 us
  waiting for transfers between devices: 47.8 us -> 14.3 us
  between operations: 14.3 us -> 0.98 us
  starting transfers between devices: 0.04 us -> 10.9 us
  local copies, waits for them, and re-layouts: 13.2 us -> 15.6 us
  matrix products: 8.96 us -> 10.6 us
    reduce_scatter x1 -> x0, waiting for transfers between devices: 47.8 us -> none  [per_device(): lax.psum_scatter(terms(jnp.int32(0), slab_rows * lax.axis_size('resp')),...]
    all_gather x2 -> x0, blocking collectives: 41.3 us -> none  [the longest x1 23.5 us: per_device(): lax.all_gather(document_keys, 'resp', axis=0, tiled=True)]
    ppermute x0 -> x8, waiting for transfers between devices: none -> 14.3 us  [swap_with(): return lax.ppermute(block, axis_name, pairs)]
    ppermute x0 -> x8, starting transfers between devices: none -> 10.9 us  [swap_with(): return lax.ppermute(block, axis_name, pairs)]
    concatenate x0 -> x4, local copies, waits for them, and re-layouts: none -> 3.3 us  [the longest x3 2.6 us: piece_grads(): jnp.concatenate([key_grad.reshape(length, key_value_width), value_grad.re...]
    reshape x2 -> x0, local copies, waits for them, and re-layouts: 2.95 us -> none  [the longest x1 1.8 us: piece_grads(): value_grad.reshape(length, key_value_width)]
    transpose x0 -> x1, local copies, waits for them, and re-layouts: none -> 1.81 us  [block_grads(): jnp.einsum('tcgk,tcgd->kcd', probabilities.astype(jnp.bfloat16), grad_hea...]
    unnamed x45 -> x43, local copies, waits for them, and re-layouts: 7.73 us -> 7.63 us
  transfers between devices with their start and end apart: 1 -> 8, of which waited for: 1 -> 7; matrix products, arithmetic and copies ran while one was open for 5% -> 19% of each run, Pallas kernels for 0% -> 0%
where the time goes in v1:
time: 59.4 us; the launch traced here: 59 us
  local copies, waits for them, and re-layouts  15.6 us (26%)
  waiting for transfers between devices  14.3 us (24%)
  starting transfers between devices  10.9 us (18%)
  matrix products  10.6 us (18%)
  other arithmetic  6.58 us (11%)
  between operations  0.98 us (2%)
    ppermute x8, waiting for transfers between devices, swap_with(): return lax.ppermute(block, axis_name, pairs)  14.3 us
    ppermute x8, starting transfers between devices, swap_with(): return lax.ppermute(block, axis_name, pairs)  10.9 us
    unnamed x43, local copies, waits for them, and re-layouts  7.63 us
    dot_general x2, matrix products, slopes(): jnp.einsum('tcgd,kcd->tcgk', grad_heads, values_block, preferred_element_...  4.15 us
    convert_element_type x1, other arithmetic, block_grads(): (probabilities * (slopes(values_block) - row_drift[..., None])).astype(jn...  3.37 us
    concatenate x3, local copies, waits for them, and re-layouts, piece_grads(): jnp.concatenate([key_grad.reshape(length, key_value_width), value_grad.re...  2.6 us
    dot_general x2, matrix products, block_grads(): jnp.einsum('tcgk,tcgd->kcd', probabilities.astype(jnp.bfloat16), grad_hea...  2.15 us
    dot_general x2, matrix products, logits(): jnp.einsum('tcgd,kcd->tcgk', query_head_rows, keys_block, preferred_eleme...  2.1 us
  transfers between devices with their start and end apart: 8, of which 7 were waited for; matrix products, arithmetic and copies ran while one was open for 19% of the time, Pallas kernels for 0%

profile of v1, /device:TPU:0, one launch (start us, length us, event | category | flops | bytes accessed | tf_op | source)
XLA Modules:
  0.0 59.0 jit_solution(13557496350218599521)
XLA Ops:
  0.7 0.8 %constant_dynamic-update-slice_fusion.1 = bf16[8,1024]{1,0:T(8,128)(2,1)S(1)} fusion(bf16[8,512]{1,0:T(8,128)(2,1)} %param.11), kind=kLoop, calls=%fused_computation.69 | loop fusion | bytes 16384
  2.1 4.0 %collective-permute-start = (bf16[8,1024]{1,0:T(8,128)(2,1)S(1)}, bf16[8,1024]{1,0:T(8,128)(2,1)S(1)}, u32[]{:S(2)}, u32[]{:S(2)}) collective-permute-start(bf16[8,1024]{1,0:T(8,128)(2,1)S(1)} %constant_dynamic-update-slice_fusion), channel_id=1, source_target_pairs={{0,8},{1,9},{2,10},{3,11},{4,12},{5,13},{6,14},{7,15},{8,0},{9,1},... | collective-permute-start | bytes 49160 | tf_op jit(solution)/shard_map/ppermute | solution.py:23
  6.8 1.4 %copy.72 = bf16[128,2560]{0,1:T(8,128)(2,1)S(1)} copy(bf16[128,2560]{1,0:T(8,128)(2,1)} %param.8) | data formatting | bytes 1310720 | tf_op args[0]
  9.1 0.9 %broadcast_select_fusion = bf16[128,2560]{0,1:T(8,128)(2,1)} fusion(bf16[128,2560]{0,1:T(8,128)(2,1)S(1)} %copy.78, pred[128]{0:T(512)(128)(4,1)S(1)} %fusion.25), kind=kLoop, calls=%fused_computation.38 | loop fusion | flops 327680 | bytes 1310848 | tf_op jit(solution)/shard_map/jit(_where)/select_n | solution.py:81
  10.0 1.0 %fusion.31 = (f32[128,4,5]{0,2,1:T(8,128)}, f32[128,4,5,128]{0,3,2,1:T(8,128)S(1)}) fusion(bf16[128,4,128,1]{0,2,3,1:T(8,128)(2,1)S(1)} %copy.108, bf16[128,4,5,128]{0,3,2,1:T(8,128)(2,1)S(1)} %bitcast.138, pred[128,128]{0,1:T(8,128)(4,1)S(1)} %fusion.19), kind=kOutput, calls=%fused_computation.90 | convolution fusion | flops 84866560 | bytes 2123776 | tf_op jit(solution)/shard_map/tcgd,kcd->tcgk/dot_general | solution.py:107
  11.0 0.8 %fusion.14 = pred[128,128]{0,1:T(8,128)(4,1)} fusion(bf16[128,16]{1,0:T(8,128)(2,1)S(1)} %bitcast.167, s32[128]{0:T(128)S(1)} %get-tuple-element.102), kind=kOutput, calls=%fused_computation.34 | convolution fusion | flops 544768 | bytes 20992 | tf_op jit(solution)/shard_map/while/body/eval_jaxpr/dot_general | solution.py:103
  12.5 1.6 %collective-permute-start.1 = (bf16[2,8,1024]{2,1,0:T(8,128)(2,1)S(1)}, bf16[2,8,1024]{2,1,0:T(8,128)(2,1)S(1)}, u32[]{:S(2)}, u32[]{:S(2)}) collective-permute-start(bf16[2,8,1024]{2,1,0:T(8,128)(2,1)S(1)} %maximum_select_fusion.3), channel_id=1, source_target_pairs={{0,4},{1,5},{2,6},{3,7},{4,0},{5,1},{6,2},{7,3},{8,12},{9,13},{10,... | collective-permute-start | bytes 98312 | tf_op jit(solution)/shard_map/ppermute | solution.py:23
  14.1 2.3 %collective-permute-done.1 = bf16[2,8,1024]{2,1,0:T(8,128)(2,1)S(1)} collective-permute-done((bf16[2,8,1024]{2,1,0:T(8,128)(2,1)S(1)}, bf16[2,8,1024]{2,1,0:T(8,128)(2,1)S(1)}, u32[]{:S(2)}, u32[]{:S(2)}) %collective-permute-start.1) | collective-permute-done | bytes 32800 | tf_op jit(solution)/shard_map/ppermute | solution.py:23
  16.5 1.6 %collective-permute-start.2 = (bf16[2,2,8,1024]{3,2,0,1:T(8,128)(2,1)S(1)}, bf16[2,2,8,1024]{3,2,0,1:T(8,128)(2,1)S(1)}, u32[]{:S(2)}, u32[]{:S(2)}) collective-permute-start(bf16[2,2,8,1024]{3,2,0,1:T(8,128)(2,1)S(1)} %maximum_select_fusion.2), channel_id=1, source_target_pairs={{0,2},{1,3},{2,0},{3,1},{4,6},{5,7},{6,4},{7,5},{8,10},{9,11},{10,... | collective-permute-start | bytes 196616 | tf_op jit(solution)/shard_map/ppermute | solution.py:23
  18.0 2.7 %collective-permute-done.2 = bf16[2,2,8,1024]{3,2,0,1:T(8,128)(2,1)S(1)} collective-permute-done((bf16[2,2,8,1024]{3,2,0,1:T(8,128)(2,1)S(1)}, bf16[2,2,8,1024]{3,2,0,1:T(8,128)(2,1)S(1)}, u32[]{:S(2)}, u32[]{:S(2)}) %collective-permute-start.2) | collective-permute-done | bytes 65568 | tf_op jit(solution)/shard_map/ppermute | solution.py:23
  20.9 1.3 %collective-permute-done.3 = bf16[2,2,2,8,1024]{4,3,0,1,2:T(8,128)(2,1)S(1)} collective-permute-done((bf16[2,2,2,8,1024]{4,3,0,1,2:T(8,128)(2,1)S(1)}, bf16[2,2,2,8,1024]{4,3,0,1,2:T(8,128)(2,1)S(1)}, u32[]{:S(2)}, u32[]{:S(2)}) %collective-permute-start.3) | collective-permute-done | bytes 131104 | tf_op jit(solution)/shard_map/ppermute | solution.py:23
  22.4 0.8 %copy.77 = bf16[128,512]{0,1:T(8,128)(2,1)} copy(bf16[128,512]{1,0:T(8,128)(2,1)S(1)} %get-tuple-element.81) | data formatting | bytes 262144 | tf_op jit(solution)/shard_map/slice | solution.py:90
  23.2 1.1 %fusion.32 = (f32[128,4,5]{0,2,1:T(8,128)S(1)}, f32[128,4,5,128]{0,3,2,1:T(8,128)S(1)}) fusion(bf16[128,4,128,1]{0,2,3,1:T(8,128)(2,1)S(1)} %bitcast.147, bf16[128,4,5,128]{0,3,2,1:T(8,128)(2,1)S(1)} %bitcast.139, pred[128,128]{0,1:T(8,128)(4,1)} %fusion.14), kind=kOutput, calls=%fused_computation.91 | convolution fusion | flops 84866560 | bytes 2123776 | tf_op jit(solution)/shard_map/while/body/eval_jaxpr/tcgd,kcd->tcgk/dot_general | solution.py:107
  24.3 0.7 %broadcast_maximum_fusion = (f32[128,4,5]{0,2,1:T(8,128)S(1)}, f32[128,4,5]{0,2,1:T(8,128)S(1)}) fusion(f32[128,4,5]{0,2,1:T(8,128)} %get-tuple-element.95, f32[128,4,5]{0,2,1:T(8,128)S(1)} %get-tuple-element.97), kind=kLoop, calls=%fused_computation.72 | loop fusion | flops 5120 | bytes 40960 | tf_op jit(solution)/shard_map/max;broadcast_in_dim | solution.py:122
  25.0 2.7 %fusion.15 = (f32[128,4,5]{0,2,1:T(8,128)S(1)}, f32[128,4,5]{0,2,1:T(8,128)S(1)}, f32[128,4,5,128]{0,3,2,1:T(8,128)}) fusion(f32[128,4,5,128]{0,3,2,1:T(8,128)S(1)} %get-tuple-element.96, f32[128,4,5]{0,2,1:T(8,128)S(1)} %get-tuple-element.93, pred[128,128]{0,1:T(8,128)(4,1)S(1)} %fusion.19, bf16[128,4,5,128]{0,3,2,1:T(8,128)(2,1)} %bitcast.142, ...), kind=kOutput, calls=%fused_computation.35 | convolution fusion | flops 85519360 | bytes 3454976 | tf_op jit(solution)/shard_map/tcgd,kcd->tcgk/dot_general | solution.py:115
  27.7 1.5 %select_reduce_fusion = (f32[128,4,5]{0,2,1:T(8,128)S(1)}, f32[128,4,5]{0,2,1:T(8,128)S(1)}, f32[128,4,5,128]{0,3,2,1:T(8,128)}) fusion(f32[128,4,5,128]{0,3,2,1:T(8,128)S(1)} %get-tuple-element.98, f32[128,4,5]{0,2,1:T(8,128)S(1)} %get-tuple-element.94, pred[128,128]{0,1:T(8,128)(4,1)S(1)} %copy-done.8, bf16[128,4,128,1]{0,2,3,1:T(8,128)(2,1)S(1)} %bitcast.154, ...), kind=kOutput, calls=%fused_computation.22 | convolution fusion | flops 85519360 | bytes 3454976 | tf_op jit(solution)/shard_map/while/body/eval_jaxpr/tcgd,kcd->tcgk/dot_general | solution.py:115
  30.4 1.1 %convolution_bitcast_fusion.4 = f32[128,4,128]{0,2,1:T(8,128)} fusion(bf16[128,4,5,128]{0,3,2,1:T(8,128)(2,1)S(1)} %bitcast.144, f32[128,4,5,128]{0,3,2,1:T(8,128)S(1)} %get-tuple-element.98, f32[128,4,5]{0,2,1:T(8,128)S(1)} %get-tuple-element.85, f32[128,4,5]{0,2,1:T(8,128)S(1)} %get-tuple-element.94, pred[128,128]{0,1:T(8,128)(4,1)S(1)} %copy-done.8), kind=kOutput, calls=%fused_computation.25 | convolution fusion | flops 85196800 | bytes 2265088 | tf_op jit(solution)/shard_map/tcgk,tcgd->kcd/dot_general | solution.py:174
  31.5 1.8 %copy.89 = f32[128,4,128]{2,1,0:T(4,128)} copy(f32[128,4,128]{0,2,1:T(8,128)} %convolution_bitcast_fusion.4) | data formatting | bytes 524288 | tf_op jit(solution)/shard_map/tcgk,tcgd->kcd/transpose | solution.py:174
  33.3 1.8 %concatenate.91 = f32[2,2,2,2,8,512]{5,4,3,2,1,0:T(8,128)} reshape(f32[128,4,128]{2,1,0:T(4,128)} %copy.89) | data formatting | bytes 524288 | tf_op jit(solution)/shard_map/concatenate | solution.py:211
  35.1 3.4 %multiply_convert_fusion.1 = (bf16[128,4,5,128]{0,3,2,1:T(8,128)(2,1)S(1)}, bf16[128,4,5,128]{0,3,2,1:T(8,128)(2,1)}) fusion(f32[128,4,5,128]{0,3,2,1:T(8,128)} %get-tuple-element.99, f32[128,4,5]{0,2,1:T(8,128)} %get-tuple-element.86, f32[128,4,5]{0,2,1:T(8,128)} %copy-done.15, f32[128,4,5,128]{0,3,2,1:T(8,128)S(1)} %get-tuple-element.98, ...), kind=kLoop, calls=%fused_computation.16 | loop fusion | flops 3932160 | bytes 6617088 | tf_op jit(solution)/shard_map/while/body/eval_jaxpr/convert_element_type | solution.py:163
  38.5 0.8 %copy-done.1 = bf16[128,4,5,128]{0,3,2,1:T(8,128)(2,1)} copy-done((bf16[128,4,5,128]{0,3,2,1:T(8,128)(2,1)}, bf16[128,4,5,128]{0,3,2,1:T(8,128)(2,1)S(1)}, u32[]{:S(2)}) %copy-start.1) | copy-done | bytes 655384
  39.9 0.8 %concatenate.90 = f32[2,2,2,2,8,512]{5,4,3,2,1,0:T(8,128)} reshape(f32[128,4,128]{2,1,0:T(4,128)S(1)} %copy.87) | data formatting | bytes 524288 | tf_op jit(solution)/shard_map/concatenate | solution.py:211
  40.7 1.0 %constant_dynamic-update-slice_fusion.3 = f32[2,2,2,2,8,1024]{5,4,3,2,1,0:T(8,128)S(1)} fusion(f32[2,2,2,2,8,512]{5,4,3,2,1,0:T(8,128)} %concatenate.90), kind=kLoop, calls=%fused_computation.71 | loop fusion | bytes 524288
  42.0 1.1 %fusion.11 = bf16[4,128,128]{2,1,0:T(8,128)(2,1)} fusion(bf16[128,4,5,128]{0,3,2,1:T(8,128)(2,1)S(1)} %bitcast.145, f32[128,4,5,128]{0,3,2,1:T(8,128)S(1)} %get-tuple-element.96, f32[128,4,5]{0,2,1:T(8,128)S(1)} %copy-done.16, f32[128,4,5]{0,2,1:T(8,128)S(1)} %copy-done.10, pred[128,128]{0,1:T(8,128)(4,1)S(1)} %fusion.19), kind=kOutput, calls=%fused_computation.30 | convolution fusion | flops 85262336 | bytes 2134016 | tf_op jit(solution)/shard_map/tcgk,tcgd->kcd/dot_general | solution.py:174
  43.4 1.6 %collective-permute-start.5 = (f32[2,2,8,1024]{3,2,1,0:T(8,128)S(1)}, f32[2,2,8,1024]{3,2,1,0:T(8,128)S(1)}, u32[]{:S(2)}, u32[]{:S(2)}) collective-permute-start(f32[2,2,8,1024]{3,2,1,0:T(8,128)S(1)} %dynamic-slice_bitcast_fusion.1), channel_id=1, source_target_pairs={{0,2},{1,3},{2,0},{3,1},{4,6},{5,7},{6,4},{7,5},{8,10},{9,11},{10,... | collective-permute-start | bytes 393224 | tf_op jit(solution)/shard_map/ppermute | solution.py:23
  45.3 3.7 %collective-permute-done.5 = f32[2,2,8,1024]{3,2,1,0:T(8,128)S(1)} collective-permute-done((f32[2,2,8,1024]{3,2,1,0:T(8,128)S(1)}, f32[2,2,8,1024]{3,2,1,0:T(8,128)S(1)}, u32[]{:S(2)}, u32[]{:S(2)}) %collective-permute-start.5) | collective-permute-done | bytes 131104 | tf_op jit(solution)/shard_map/ppermute | solution.py:23
  49.1 1.6 %collective-permute-start.6 = (f32[2,8,1024]{2,1,0:T(8,128)S(1)}, f32[2,8,1024]{2,1,0:T(8,128)S(1)}, u32[]{:S(2)}, u32[]{:S(2)}) collective-permute-start(f32[2,8,1024]{2,1,0:T(8,128)S(1)} %dynamic-slice_bitcast_fusion.2), channel_id=1, source_target_pairs={{0,4},{1,5},{2,6},{3,7},{4,0},{5,1},{6,2},{7,3},{8,12},{9,13},{10,... | collective-permute-start | bytes 196616 | tf_op jit(solution)/shard_map/ppermute | solution.py:23
  51.1 2.3 %collective-permute-done.6 = f32[2,8,1024]{2,1,0:T(8,128)S(1)} collective-permute-done((f32[2,8,1024]{2,1,0:T(8,128)S(1)}, f32[2,8,1024]{2,1,0:T(8,128)S(1)}, u32[]{:S(2)}, u32[]{:S(2)}) %collective-permute-start.6) | collective-permute-done | bytes 65568 | tf_op jit(solution)/shard_map/ppermute | solution.py:23
  54.0 0.8 %copy.96 = bf16[128,512]{1,0:T(8,128)(2,1)} copy(bf16[128,512]{0,1:T(8,128)(2,1)S(1)} %bitcast.164) | data formatting | bytes 262144
  54.8 1.1 %copy.94 = bf16[128,2560]{1,0:T(8,128)(2,1)} copy(bf16[128,2560]{0,1:T(8,128)(2,1)S(1)} %bitcast.146) | data formatting | bytes 1310720
  56.0 0.8 %copy.95 = bf16[128,512]{1,0:T(8,128)(2,1)} copy(bf16[128,512]{0,1:T(8,128)(2,1)S(1)} %bitcast.151) | data formatting | bytes 262144
  56.8 1.6 %collective-permute-done.7 = f32[8,1024]{1,0:T(8,128)S(1)} collective-permute-done((f32[8,1024]{1,0:T(8,128)S(1)}, f32[8,1024]{1,0:T(8,128)S(1)}, u32[]{:S(2)}, u32[]{:S(2)}) %collective-permute-start.7) | collective-permute-done | bytes 32800 | tf_op jit(solution)/shard_map/ppermute | solution.py:23
  (81 shorter events, 7.6 us)
Async XLA Ops:
  0.6 7.7 %copy-start.12 = (bf16[128,512]{1,0:T(8,128)(2,1)S(1)}, bf16[128,512]{1,0:T(8,128)(2,1)}, u32[]{:S(2)}) copy-start(bf16[128,512]{1,0:T(8,128)(2,1)} %param.9) | copy-start | bytes 393220
  0.6 7.9 %copy-start.6 = (bf16[128,2560]{1,0:T(8,128)(2,1)S(1)}, bf16[128,2560]{1,0:T(8,128)(2,1)}, u32[]{:S(2)}) copy-start(bf16[128,2560]{1,0:T(8,128)(2,1)} %param.13) | copy-start | bytes 1966084
  2.1 10.3 %collective-permute-start = (bf16[8,1024]{1,0:T(8,128)(2,1)S(1)}, bf16[8,1024]{1,0:T(8,128)(2,1)S(1)}, u32[]{:S(2)}, u32[]{:S(2)}) collective-permute-start(bf16[8,1024]{1,0:T(8,128)(2,1)S(1)} %constant_dynamic-update-slice_fusion), channel_id=1, source_target_pairs={{0,8},{1,9},{2,10},{3,11},{4,12},{5,13},{6,14},{7,15},{8,0},{9,1},... | collective-permute-start | bytes 49160 | tf_op jit(solution)/shard_map/ppermute | solution.py:23
  6.8 2.1 %copy-start.17 = (s32[2]{0:T(128)S(1)}, s32[2]{0:T(128)}, u32[]{:S(2)}) copy-start(s32[2]{0:T(128)} %param.14) | copy-start | bytes 28
  10.0 1.8 %copy-start.13 = (bf16[128,512]{1,0:T(8,128)(2,1)S(1)}, bf16[128,512]{1,0:T(8,128)(2,1)}, u32[]{:S(2)}) copy-start(bf16[128,512]{1,0:T(8,128)(2,1)} %param.10) | copy-start | bytes 393220
  12.5 4.0 %collective-permute-start.1 = (bf16[2,8,1024]{2,1,0:T(8,128)(2,1)S(1)}, bf16[2,8,1024]{2,1,0:T(8,128)(2,1)S(1)}, u32[]{:S(2)}, u32[]{:S(2)}) collective-permute-start(bf16[2,8,1024]{2,1,0:T(8,128)(2,1)S(1)} %maximum_select_fusion.3), channel_id=1, source_target_pairs={{0,4},{1,5},{2,6},{3,7},{4,0},{5,1},{6,2},{7,3},{8,12},{9,13},{10,... | collective-permute-start | bytes 98312 | tf_op jit(solution)/shard_map/ppermute | solution.py:23
  16.5 4.3 %collective-permute-start.2 = (bf16[2,2,8,1024]{3,2,0,1:T(8,128)(2,1)S(1)}, bf16[2,2,8,1024]{3,2,0,1:T(8,128)(2,1)S(1)}, u32[]{:S(2)}, u32[]{:S(2)}) collective-permute-start(bf16[2,2,8,1024]{3,2,0,1:T(8,128)(2,1)S(1)} %maximum_select_fusion.2), channel_id=1, source_target_pairs={{0,2},{1,3},{2,0},{3,1},{4,6},{5,7},{6,4},{7,5},{8,10},{9,11},{10,... | collective-permute-start | bytes 196616 | tf_op jit(solution)/shard_map/ppermute | solution.py:23
  20.8 1.4 %collective-permute-start.3 = (bf16[2,2,2,8,1024]{4,3,0,1,2:T(8,128)(2,1)S(1)}, bf16[2,2,2,8,1024]{4,3,0,1,2:T(8,128)(2,1)S(1)}, u32[]{:S(2)}, u32[]{:S(2)}) collective-permute-start(bf16[2,2,2,8,1024]{4,3,0,1,2:T(8,128)(2,1)S(1)} %maximum_select_fusion.1), channel_id=1, source_target_pairs={{0,1},{1,0},{2,3},{3,2},{4,5},{5,4},{6,7},{7,6},{8,9},{9,8},{10,11... | collective-permute-start | bytes 393224 | tf_op jit(solution)/shard_map/ppermute | solution.py:23
  25.0 4.8 %copy-start.9 = (f32[128,4,5]{0,2,1:T(8,128)}, f32[128,4,5]{0,2,1:T(8,128)S(1)}, u32[]{:S(2)}) copy-start(f32[128,4,5]{0,2,1:T(8,128)S(1)} %get-tuple-element.94) | copy-start | bytes 30724
  25.0 2.7 %copy-start.3 = (bf16[128,2560]{0,1:T(8,128)(2,1)S(1)}, bf16[128,2560]{0,1:T(8,128)(2,1)}, u32[]{:S(2)}) copy-start(bf16[128,2560]{0,1:T(8,128)(2,1)} %broadcast_select_fusion) | copy-start | bytes 1966084
  25.0 2.7 %copy-start.7 = (bf16[128,512]{0,1:T(8,128)(2,1)S(1)}, bf16[128,512]{0,1:T(8,128)(2,1)}, u32[]{:S(2)}) copy-start(bf16[128,512]{0,1:T(8,128)(2,1)} %copy.77) | copy-start | bytes 393220
  25.0 2.7 %copy-start.8 = (pred[128,128]{0,1:T(8,128)(4,1)S(1)}, pred[128,128]{0,1:T(8,128)(4,1)}, u32[]{:S(2)}) copy-start(pred[128,128]{0,1:T(8,128)(4,1)} %fusion.14) | copy-start | bytes 49156
  27.7 1.5 %copy-start.11 = (f32[128,4,5]{0,2,1:T(8,128)S(1)}, f32[128,4,5]{0,2,1:T(8,128)}, u32[]{:S(2)}) copy-start(f32[128,4,5]{0,2,1:T(8,128)} %get-tuple-element.95) | copy-start | bytes 30724
  29.8 0.6 %copy-start.15 = (f32[128,4,5]{0,2,1:T(8,128)}, f32[128,4,5]{0,2,1:T(8,128)S(1)}, u32[]{:S(2)}) copy-start(f32[128,4,5]{0,2,1:T(8,128)S(1)} %get-tuple-element.85) | copy-start | bytes 30724
  38.5 0.8 %copy-start.1 = (bf16[128,4,5,128]{0,3,2,1:T(8,128)(2,1)}, bf16[128,4,5,128]{0,3,2,1:T(8,128)(2,1)S(1)}, u32[]{:S(2)}) copy-start(bf16[128,4,5,128]{0,3,2,1:T(8,128)(2,1)S(1)} %get-tuple-element.89) | copy-start | bytes 1966084
  39.3 2.4 %copy-start.5 = (f32[2,2,2,2,8,512]{5,4,3,2,1,0:T(8,128)S(1)}, f32[2,2,2,2,8,512]{5,4,3,2,1,0:T(8,128)}, u32[]{:S(2)}) copy-start(f32[2,2,2,2,8,512]{5,4,3,2,1,0:T(8,128)} %concatenate.91) | copy-start | bytes 786436
  39.7 2.3 %copy-start.4 = (bf16[128,2560]{0,1:T(8,128)(2,1)S(1)}, bf16[128,2560]{0,1:T(8,128)(2,1)}, u32[]{:S(2)}) copy-start(bf16[128,2560]{0,1:T(8,128)(2,1)} %broadcast_select_fusion) | copy-start | bytes 1966084
  39.7 2.3 %copy-start.10 = (f32[128,4,5]{0,2,1:T(8,128)S(1)}, f32[128,4,5]{0,2,1:T(8,128)}, u32[]{:S(2)}) copy-start(f32[128,4,5]{0,2,1:T(8,128)} %copy-done.9) | copy-start | bytes 30724
  39.7 2.3 %copy-start.16 = (f32[128,4,5]{0,2,1:T(8,128)S(1)}, f32[128,4,5]{0,2,1:T(8,128)}, u32[]{:S(2)}) copy-start(f32[128,4,5]{0,2,1:T(8,128)} %copy-done.15) | copy-start | bytes 30724
  41.8 1.6 %collective-permute-start.4 = (f32[2,2,2,8,1024]{4,3,2,1,0:T(8,128)S(1)}, f32[2,2,2,8,1024]{4,3,2,1,0:T(8,128)S(1)}, u32[]{:S(2)}, u32[]{:S(2)}) collective-permute-start(f32[2,2,2,8,1024]{4,3,2,1,0:T(8,128)S(1)} %dynamic-slice_bitcast_fusion), channel_id=1, source_target_pairs={{0,1},{1,0},{2,3},{3,2},{4,5},{5,4},{6,7},{7,6},{8,9},{9,8},{10,11... | collective-permute-start | bytes 786440 | tf_op jit(solution)/shard_map/ppermute | solution.py:23
  43.1 1.9 %copy-start = (bf16[128,4,5,128]{0,3,2,1:T(8,128)(2,1)S(1)}, bf16[128,4,5,128]{0,3,2,1:T(8,128)(2,1)}, u32[]{:S(2)}) copy-start(bf16[128,4,5,128]{0,3,2,1:T(8,128)(2,1)} %get-tuple-element.90) | copy-start | bytes 1966084
  43.4 5.6 %collective-permute-start.5 = (f32[2,2,8,1024]{3,2,1,0:T(8,128)S(1)}, f32[2,2,8,1024]{3,2,1,0:T(8,128)S(1)}, u32[]{:S(2)}, u32[]{:S(2)}) collective-permute-start(f32[2,2,8,1024]{3,2,1,0:T(8,128)S(1)} %dynamic-slice_bitcast_fusion.1), channel_id=1, source_target_pairs={{0,2},{1,3},{2,0},{3,1},{4,6},{5,7},{6,4},{7,5},{8,10},{9,11},{10,... | collective-permute-start | bytes 393224 | tf_op jit(solution)/shard_map/ppermute | solution.py:23
  45.0 5.7 %copy-start.2 = (bf16[128,4,5,128]{0,3,2,1:T(8,128)(2,1)S(1)}, bf16[128,4,5,128]{0,3,2,1:T(8,128)(2,1)}, u32[]{:S(2)}) copy-start(bf16[128,4,5,128]{0,3,2,1:T(8,128)(2,1)} %copy-done.1) | copy-start | bytes 1966084
  49.1 4.3 %collective-permute-start.6 = (f32[2,8,1024]{2,1,0:T(8,128)S(1)}, f32[2,8,1024]{2,1,0:T(8,128)S(1)}, u32[]{:S(2)}, u32[]{:S(2)}) collective-permute-start(f32[2,8,1024]{2,1,0:T(8,128)S(1)} %dynamic-slice_bitcast_fusion.2), channel_id=1, source_target_pairs={{0,4},{1,5},{2,6},{3,7},{4,0},{5,1},{6,2},{7,3},{8,12},{9,13},{10,... | collective-permute-start | bytes 196616 | tf_op jit(solution)/shard_map/ppermute | solution.py:23
  51.1 2.9 %copy-start.14 = (bf16[4,128,128]{2,1,0:T(8,128)(2,1)S(1)}, bf16[4,128,128]{2,1,0:T(8,128)(2,1)}, u32[]{:S(2)}) copy-start(bf16[4,128,128]{2,1,0:T(8,128)(2,1)} %fusion.11) | copy-start | bytes 393220
  53.5 4.9 %collective-permute-start.7 = (f32[8,1024]{1,0:T(8,128)S(1)}, f32[8,1024]{1,0:T(8,128)S(1)}, u32[]{:S(2)}, u32[]{:S(2)}) collective-permute-start(f32[8,1024]{1,0:T(8,128)S(1)} %dynamic-slice_bitcast_fusion.3), channel_id=1, source_target_pairs={{0,8},{1,9},{2,10},{3,11},{4,12},{5,13},{6,14},{7,15},{8,0},{9,1},... | collective-permute-start | bytes 98312 | tf_op jit(solution)/shard_map/ppermute | solution.py:23

commit v2 on v1

v2 whole, which is shorter than its diff:
```python
import jax
import jax.numpy as jnp
from jax import lax
from jax.experimental import pallas as pl
from jax.sharding import PartitionSpec as P

KEY_HEADS = 4
GROUP_HEADS = 5
HEAD_SIZE = 128


masked_score = -1e30


def exchange_bits(size):
    bits = size.bit_length() - 1
    if (1 << bits) != size:
        return None
    return bits


def swap_with(block, axis_name, size, bit):
    pairs = [(index, index ^ (1 << bit)) for index in range(size)]
    return lax.ppermute(block, axis_name, pairs)


def gather_rows(block, axis_name):
    size = lax.axis_size(axis_name)
    bits = exchange_bits(size)
    if bits is None:
        return lax.all_gather(block, axis_name, axis=0, tiled=True)
    me = lax.axis_index(axis_name)
    stacked = block
    for bit in reversed(range(bits)):
        other = swap_with(stacked, axis_name, size, bit)
        mine_low = ((me >> bit) & 1) == 0
        stacked = jnp.where(mine_low, jnp.stack([stacked, other]), jnp.stack([other, stacked]))
    stacked = stacked.reshape((2,) * bits + block.shape)
    stacked = jnp.transpose(stacked, tuple(reversed(range(bits))) + (bits, bits + 1))
    return stacked.reshape((size * block.shape[0],) + block.shape[1:])


def scatter_sum_rows(block, axis_name):
    size = lax.axis_size(axis_name)
    bits = exchange_bits(size)
    if bits is None:
        return lax.psum_scatter(block, axis_name, scatter_dimension=0, tiled=True)
    me = lax.axis_index(axis_name)
    rows = block.shape[0] // size
    parts = block.reshape((2,) * bits + (rows,) + block.shape[1:])
    for bit in range(bits):
        axis = bits - 1 - bit
        mine = (me >> bit) & 1
        keep = lax.dynamic_index_in_dim(parts, mine, axis, keepdims=False)
        send = lax.dynamic_index_in_dim(parts, 1 - mine, axis, keepdims=False)
        parts = keep + swap_with(send, axis_name, size, bit)
    return parts.reshape((rows,) + block.shape[1:])


def contract_rows(left, right):
    return lax.dot_general(
        left, right, (((0,), (0,)), ((), ())), preferred_element_type=jnp.float32
    )


def contract_cols(left, right):
    return lax.dot_general(
        left, right, (((1,), (1,)), ((), ())), preferred_element_type=jnp.float32
    )


def attention_kernel(
    q_ref, do_ref, kv_ref, ks_ref, vs_ref, vis_ref, self_ref, live_ref,
    dq_ref, doc_ref, sk_ref, sv_ref,
):
    token_rows = q_ref.shape[0]
    width = KEY_HEADS * HEAD_SIZE
    score_scale = HEAD_SIZE ** (-0.5)
    doc_seen = jnp.concatenate([vis_ref[...]] * GROUP_HEADS, axis=0) > 0.5
    self_seen = jnp.concatenate([self_ref[...]] * GROUP_HEADS, axis=0) > 0.5
    live = jnp.concatenate([live_ref[...]] * GROUP_HEADS, axis=0) > 0.5
    for c in range(KEY_HEADS):
        kd = kv_ref[:, c * HEAD_SIZE:(c + 1) * HEAD_SIZE]
        vd = kv_ref[:, width + c * HEAD_SIZE:width + (c + 1) * HEAD_SIZE]
        ks = ks_ref[:, c * HEAD_SIZE:(c + 1) * HEAD_SIZE]
        vs = vs_ref[:, c * HEAD_SIZE:(c + 1) * HEAD_SIZE]
        heads = [c * GROUP_HEADS + g for g in range(GROUP_HEADS)]
        q = jnp.concatenate([q_ref[:, h * HEAD_SIZE:(h + 1) * HEAD_SIZE] for h in heads], axis=0)
        do = jnp.concatenate([do_ref[:, h * HEAD_SIZE:(h + 1) * HEAD_SIZE] for h in heads], axis=0)
        do = jnp.where(live, do, jnp.zeros_like(do))
        sd = jnp.where(doc_seen, contract_cols(q, kd) * score_scale, masked_score)
        ss = jnp.where(self_seen, contract_cols(q, ks) * score_scale, masked_score)
        top = jnp.maximum(jnp.max(sd, axis=1, keepdims=True), jnp.max(ss, axis=1, keepdims=True))
        ed = jnp.where(doc_seen, jnp.exp(sd - top), 0.0)
        es = jnp.where(self_seen, jnp.exp(ss - top), 0.0)
        total = jnp.sum(ed, axis=1, keepdims=True) + jnp.sum(es, axis=1, keepdims=True)
        pd = ed / total
        ps = es / total
        gd = contract_cols(do, vd)
        gs = contract_cols(do, vs)
        drift = jnp.sum(pd * gd, axis=1, keepdims=True) + jnp.sum(ps * gs, axis=1, keepdims=True)
        dsd = (pd * (gd - drift)).astype(jnp.bfloat16)
        dss = (ps * (gs - drift)).astype(jnp.bfloat16)
        dq = (
            jnp.dot(dsd, kd, preferred_element_type=jnp.float32)
            + jnp.dot(dss, ks, preferred_element_type=jnp.float32)
        ) * score_scale
        for g, h in enumerate(heads):
            dq_ref[:, h * HEAD_SIZE:(h + 1) * HEAD_SIZE] = dq[
                g * token_rows:(g + 1) * token_rows
            ].astype(dq_ref.dtype)
        doc_ref[:, c * HEAD_SIZE:(c + 1) * HEAD_SIZE] = contract_rows(dsd, q) * score_scale
        doc_ref[:, width + c * HEAD_SIZE:width + (c + 1) * HEAD_SIZE] = contract_rows(
            pd.astype(jnp.bfloat16), do
        )
        sk_ref[:, c * HEAD_SIZE:(c + 1) * HEAD_SIZE] = (
            contract_rows(dss, q) * score_scale
        ).astype(sk_ref.dtype)
        sv_ref[:, c * HEAD_SIZE:(c + 1) * HEAD_SIZE] = contract_rows(
            ps.astype(jnp.bfloat16), do
        ).astype(sv_ref.dtype)


def per_device(
    queries,
    response_keys,
    response_values,
    document_keys,
    document_values,
    grad_out,
    lengths,
    doc_mask,
):
    token_rows = queries.shape[0]
    responses_here = lengths.shape[0]
    resp_len = token_rows // responses_here
    mask_blocks = doc_mask.shape[1]
    key_value_width = KEY_HEADS * HEAD_SIZE
    positions = jnp.arange(token_rows, dtype=jnp.int32)
    owners = positions // resp_len
    within = positions % resp_len
    live = (within < jnp.repeat(lengths, resp_len)).astype(jnp.float32)[:, None]
    self_visible = (
        (owners[:, None] == owners[None, :]) & (positions[None, :] <= positions[:, None])
    ).astype(jnp.float32)
    collected = gather_rows(jnp.concatenate([document_keys, document_values], axis=1), "resp")
    doc_rows = collected.shape[0]
    block_rows = doc_rows // mask_blocks
    row_masks = jnp.repeat(doc_mask, resp_len, axis=0)
    doc_visible = (jnp.repeat(row_masks, block_rows, axis=1) == 1).astype(jnp.float32)
    query_gradient, doc_terms, self_key, self_value = pl.pallas_call(
        attention_kernel,
        out_shape=(
            jax.ShapeDtypeStruct(queries.shape, jnp.bfloat16),
            jax.ShapeDtypeStruct((doc_rows, 2 * key_value_width), jnp.float32),
            jax.ShapeDtypeStruct(response_keys.shape, jnp.bfloat16),
            jax.ShapeDtypeStruct(response_values.shape, jnp.bfloat16),
        ),
    )(
        queries,
        grad_out,
        collected,
        response_keys,
        response_values,
        doc_visible,
        self_visible,
        live,
    )
    summed = scatter_sum_rows(doc_terms, "resp")
    return (
        query_gradient,
        summed[:, :key_value_width].astype(jnp.bfloat16),
        summed[:, key_value_width:].astype(jnp.bfloat16),
        self_key,
        self_value,
    )


def solution(mesh):
    return jax.shard_map(
        per_device,
        mesh=mesh,
        in_specs=(
            P(("grp", "resp"), None),
            P(("grp", "resp"), None),
            P(("grp", "resp"), None),
            P(("grp", "resp"), None),
            P(("grp", "resp"), None),
            P(("grp", "resp"), None),
            P(("grp", "resp")),
            P(("grp", "resp"), None),
        ),
        out_specs=(
            P(("grp", "resp"), None),
            P(("grp", "resp"), None),
            P(("grp", "resp"), None),
            P(("grp", "resp"), None),
            P(("grp", "resp"), None),
        ),
        check_vma=False,
    )
```

time: 59.4 us -> 44.2 us (0.74)
  matrix products: 10.6 us -> 0 us
  local copies, waits for them, and re-layouts: 15.6 us -> 5.07 us
  Pallas kernels: 0 us -> 6.47 us
  other arithmetic: 6.58 us -> 1.52 us
  waiting for transfers between devices: 14.3 us -> 18 us
  starting transfers between devices: 10.9 us -> 12.1 us
    dot_general x11 -> x0, matrix products: 10.6 us -> none  [the longest x2 4.15 us: slopes(): jnp.einsum('tcgd,kcd->tcgk', grad_heads, values_block, preferred_element_...]
    pallas_call x0 -> x1, Pallas kernels: none -> 6.47 us  [per_device(): pl.pallas_call(attention_kernel, out_shape=(jax.ShapeDtypeStruct(queries....]
    unnamed x43 -> x7, local copies, waits for them, and re-layouts: 7.63 us -> 1.36 us
    ppermute x8, waiting for transfers between devices: 14.3 us -> 18 us  [swap_with(): return lax.ppermute(block, axis_name, pairs)]
    convert_element_type x2 -> x3, other arithmetic: 4.05 us -> 1.35 us  [the longest x1 0.71 us: per_device(): self_visible = ((owners[:, None] == owners[None, :]) & (positions[None, :...]
    concatenate x3 -> x0, local copies, waits for them, and re-layouts: 2.6 us -> none  [piece_grads(): jnp.concatenate([key_grad.reshape(length, key_value_width), value_grad.re...]
    ppermute x8, starting transfers between devices: 10.9 us -> 12.1 us  [swap_with(): return lax.ppermute(block, axis_name, pairs)]
    transpose x1, local copies, waits for them, and re-layouts: 1.81 us -> 0.72 us  [gather_rows(): jnp.transpose(stacked, tuple(reversed(range(bits))) + (bits, bits + 1))]
  transfers between devices with their start and end apart: 8 -> 8, of which waited for: 7 -> 7; matrix products, arithmetic and copies ran while one was open for 19% -> 6% of each run, Pallas kernels for 0% -> 0%
where the time goes in v2:
time: 44.2 us; the launch traced here: 43.9 us
  waiting for transfers between devices  18 us (41%)
  starting transfers between devices  12.1 us (27%)
  Pallas kernels  6.47 us (15%)
  local copies, waits for them, and re-layouts  5.07 us (11%)
  other arithmetic  1.52 us (3%)
  between operations  0.76 us (2%)
    ppermute x8, waiting for transfers between devices, swap_with(): return lax.ppermute(block, axis_name, pairs)  18 us
    ppermute x8, starting transfers between devices, swap_with(): return lax.ppermute(block, axis_name, pairs)  12.1 us
    pallas_call x1, Pallas kernels, per_device(): pl.pallas_call(attention_kernel, out_shape=(jax.ShapeDtypeStruct(queries....  6.47 us
    unnamed x7, local copies, waits for them, and re-layouts  1.36 us
    dynamic_slice x1, local copies, waits for them, and re-layouts, scatter_sum_rows(): keep = lax.dynamic_index_in_dim(parts, mine, axis, keepdims=False)  1.06 us
    convert_element_type x4, local copies, waits for them, and re-layouts, per_device(): (jnp.repeat(row_masks, block_rows, axis=1) == 1).astype(jnp.float32)  0.89 us
  transfers between devices with their start and end apart: 8, of which 7 were waited for; matrix products, arithmetic and copies ran while one was open for 6% of the time, Pallas kernels for 0%

profile of v2, /device:TPU:0, one launch (start us, length us, event | category | flops | bytes accessed | tf_op | source)
XLA Modules:
  0.0 43.9 jit_solution(4782549060560623624)
XLA Ops:
  0.6 0.0 copy-start
  0.6 0.7 %constant_dynamic-update-slice_fusion.1 = bf16[8,1024]{1,0:T(8,128)(2,1)S(1)} fusion(bf16[8,512]{1,0:T(8,128)(2,1)} %param.11), kind=kLoop, calls=%fused_computation.22 | loop fusion | bytes 16384
  1.4 4.0 %collective-permute-start = (bf16[8,1024]{1,0:T(8,128)(2,1)S(1)}, bf16[8,1024]{1,0:T(8,128)(2,1)S(1)}, u32[]{:S(2)}, u32[]{:S(2)}) collective-permute-start(bf16[8,1024]{1,0:T(8,128)(2,1)S(1)} %constant_dynamic-update-slice_fusion), channel_id=1, source_target_pairs={{0,8},{1,9},{2,10},{3,11},{4,12},{5,13},{6,14},{7,15},{8,0},{9,1},... | collective-permute-start | bytes 49160 | tf_op jit(solution)/shard_map/ppermute | solution.py:24
  5.4 0.1 copy.22
  5.5 0.1 broadcast_in_dim.6
  5.6 0.1 convert_element_type.23
  5.7 0.6 %copy-done.2 = s32[2]{0:T(128)S(1)} copy-done((s32[2]{0:T(128)S(1)}, s32[2]{0:T(128)}, u32[]{:S(2)}) %copy-start.2) | copy-done | bytes 32
  6.3 0.1 broadcast_in_dim.16
  6.4 0.1 reshape.382
  6.5 0.7 %fusion.2.self_ref = f32[128,128]{1,0:T(8,128)} fusion(s32[128]{0:T(128)S(1)} %and_select_fusion.1), kind=kLoop, calls=%fused_computation.14 | loop fusion | flops 65536 | bytes 66048 | tf_op jit(solution)/shard_map/convert_element_type | solution.py:145
  7.2 0.7 %copy.24.vis_ref = f32[128,128]{1,0:T(8,128)} copy(f32[128,128]{0,1:T(8,128)S(1)} %broadcast_bitcast_fusion) | data formatting | bytes 131072 | tf_op jit(solution)/shard_map/convert_element_type | solution.py:150
  7.9 0.1 copy.23
  8.0 0.6 %convert_element_type.26.live_ref = f32[128,1]{1,0:T(8,128)} convert(pred[128,1]{1,0:T(8,128)(4,1)S(1)} %copy.23) | non-fusion elementwise | flops 128 | bytes 640 | tf_op jit(solution)/shard_map/convert_element_type | solution.py:142
  8.7 0.0 collective-permute-done
  8.7 1.6 %collective-permute-start.1 = (bf16[2,8,1024]{2,1,0:T(8,128)(2,1)S(1)}, bf16[2,8,1024]{2,1,0:T(8,128)(2,1)S(1)}, u32[]{:S(2)}, u32[]{:S(2)}) collective-permute-start(bf16[2,8,1024]{2,1,0:T(8,128)(2,1)S(1)} %maximum_select_fusion.6), channel_id=1, source_target_pairs={{0,4},{1,5},{2,6},{3,7},{4,0},{5,1},{6,2},{7,3},{8,12},{9,13},{10,... | collective-permute-start | bytes 98312 | tf_op jit(solution)/shard_map/ppermute | solution.py:24
  10.3 2.3 %collective-permute-done.1 = bf16[2,8,1024]{2,1,0:T(8,128)(2,1)S(1)} collective-permute-done((bf16[2,8,1024]{2,1,0:T(8,128)(2,1)S(1)}, bf16[2,8,1024]{2,1,0:T(8,128)(2,1)S(1)}, u32[]{:S(2)}, u32[]{:S(2)}) %collective-permute-start.1) | collective-permute-done | bytes 32800 | tf_op jit(solution)/shard_map/ppermute | solution.py:24
  12.7 1.6 %collective-permute-start.2 = (bf16[2,2,8,1024]{3,2,1,0:T(8,128)(2,1)S(1)}, bf16[2,2,8,1024]{3,2,1,0:T(8,128)(2,1)S(1)}, u32[]{:S(2)}, u32[]{:S(2)}) collective-permute-start(bf16[2,2,8,1024]{3,2,1,0:T(8,128)(2,1)S(1)} %maximum_select_fusion.4), channel_id=1, source_target_pairs={{0,2},{1,3},{2,0},{3,1},{4,6},{5,7},{6,4},{7,5},{8,10},{9,11},{10,... | collective-permute-start | bytes 196616 | tf_op jit(solution)/shard_map/ppermute | solution.py:24
  14.2 2.8 %collective-permute-done.2 = bf16[2,2,8,1024]{3,2,1,0:T(8,128)(2,1)S(1)} collective-permute-done((bf16[2,2,8,1024]{3,2,1,0:T(8,128)(2,1)S(1)}, bf16[2,2,8,1024]{3,2,1,0:T(8,128)(2,1)S(1)}, u32[]{:S(2)}, u32[]{:S(2)}) %collective-permute-start.2) | collective-permute-done | bytes 65568 | tf_op jit(solution)/shard_map/ppermute | solution.py:24
  17.0 0.1 collective-permute-start.3
  17.1 1.3 %collective-permute-done.3 = bf16[2,2,2,8,1024]{4,3,2,1,0:T(8,128)(2,1)S(1)} collective-permute-done((bf16[2,2,2,8,1024]{4,3,2,1,0:T(8,128)(2,1)S(1)}, bf16[2,2,2,8,1024]{4,3,2,1,0:T(8,128)(2,1)S(1)}, u32[]{:S(2)}, u32[]{:S(2)}) %collective-permute-start.3) | collective-permute-done | bytes 131104 | tf_op jit(solution)/shard_map/ppermute | solution.py:24
  18.5 0.7 %copy.21 = bf16[2,2,2,2,8,1024]{5,4,3,2,1,0:T(8,128)(2,1)} copy(bf16[2,2,2,2,8,1024]{5,4,0,1,2,3:T(8,128)(2,1)S(1)} %fusion) | data formatting | bytes 524288 | tf_op jit(solution)/shard_map/transpose | solution.py:39
  19.2 6.5 %shard_map.119 = (bf16[128,2560]{1,0:T(8,128)(2,1)}, f32[128,1024]{1,0:T(8,128)}, bf16[128,512]{1,0:T(8,128)(2,1)}, bf16[128,512]{1,0:T(8,128)(2,1)}) custom-call(bf16[128,2560]{1,0:T(8,128)(2,1)} %q_ref.1, bf16[128,2560]{1,0:T(8,128)(2,1)} %do_ref.1, bf16[128,1024]{1,0:T(8,128)(2,1)} %bitcast.40, bf16[128,512]{1,0:T(8,128)(2,1)} %ks_ref.1, ...), custom_call_target="tpu_custom_call" | custom-call | tf_op jit(solution)/shard_map/pallas_call | solution.py:151
  25.7 1.1 %constant_dynamic-slice_fusion.1 = (f32[2,2,2,1,8,1024]{5,4,3,2,1,0:T(8,128)S(1)}, f32[2,2,2,1,8,1024]{5,4,3,2,1,0:T(8,128)S(1)}) fusion(f32[2,2,2,2,8,1024]{5,4,3,2,1,0:T(8,128)} %bitcast.41, s32[]{:T(128)S(6)} %select_n.154, s32[]{:T(128)S(6)} %select_n.155), kind=kLoop, calls=%fused_computation.24 | loop fusion | bytes 1048584 | tf_op jit(solution)/shard_map/jit(dynamic_index_in_dim)/dynamic_slice | solution.py:54
  26.8 0.2 collective-permute-start.4
  27.0 1.4 %collective-permute-done.4 = f32[2,2,2,8,1024]{4,3,1,0,2:T(8,128)S(1)} collective-permute-done((f32[2,2,2,8,1024]{4,3,1,0,2:T(8,128)S(1)}, f32[2,2,2,8,1024]{4,3,1,0,2:T(8,128)S(1)}, u32[]{:S(2)}, u32[]{:S(2)}) %collective-permute-start.4) | collective-permute-done | bytes 262176 | tf_op jit(solution)/shard_map/ppermute | solution.py:24
  28.4 1.6 %collective-permute-start.5 = (f32[2,2,8,1024]{3,2,1,0:T(8,128)S(1)}, f32[2,2,8,1024]{3,2,1,0:T(8,128)S(1)}, u32[]{:S(2)}, u32[]{:S(2)}) collective-permute-start(f32[2,2,8,1024]{3,2,1,0:T(8,128)S(1)} %dynamic-slice_bitcast_fusion), channel_id=1, source_target_pairs={{0,2},{1,3},{2,0},{3,1},{4,6},{5,7},{6,4},{7,5},{8,10},{9,11},{10,... | collective-permute-start | bytes 393224 | tf_op jit(solution)/shard_map/ppermute | solution.py:24
  30.0 4.1 %collective-permute-done.5 = f32[2,2,8,1024]{3,2,1,0:T(8,128)S(1)} collective-permute-done((f32[2,2,8,1024]{3,2,1,0:T(8,128)S(1)}, f32[2,2,8,1024]{3,2,1,0:T(8,128)S(1)}, u32[]{:S(2)}, u32[]{:S(2)}) %collective-permute-start.5) | collective-permute-done | bytes 131104 | tf_op jit(solution)/shard_map/ppermute | solution.py:24
  34.1 1.6 %collective-permute-start.6 = (f32[2,8,1024]{2,1,0:T(8,128)S(1)}, f32[2,8,1024]{2,1,0:T(8,128)S(1)}, u32[]{:S(2)}, u32[]{:S(2)}) collective-permute-start(f32[2,8,1024]{2,1,0:T(8,128)S(1)} %dynamic-slice_bitcast_fusion.1), channel_id=1, source_target_pairs={{0,4},{1,5},{2,6},{3,7},{4,0},{5,1},{6,2},{7,3},{8,12},{9,13},{10,... | collective-permute-start | bytes 196616 | tf_op jit(solution)/shard_map/ppermute | solution.py:24
  35.7 2.7 %collective-permute-done.6 = f32[2,8,1024]{2,1,0:T(8,128)S(1)} collective-permute-done((f32[2,8,1024]{2,1,0:T(8,128)S(1)}, f32[2,8,1024]{2,1,0:T(8,128)S(1)}, u32[]{:S(2)}, u32[]{:S(2)}) %collective-permute-start.6) | collective-permute-done | bytes 65568 | tf_op jit(solution)/shard_map/ppermute | solution.py:24
  38.4 1.4 %collective-permute-start.7 = (f32[8,1024]{1,0:T(8,128)S(1)}, f32[8,1024]{1,0:T(8,128)S(1)}, u32[]{:S(2)}, u32[]{:S(2)}) collective-permute-start(f32[8,1024]{1,0:T(8,128)S(1)} %dynamic-slice_bitcast_fusion.2), channel_id=1, source_target_pairs={{0,8},{1,9},{2,10},{3,11},{4,12},{5,13},{6,14},{7,15},{8,0},{9,1},... | collective-permute-start | bytes 98312 | tf_op jit(solution)/shard_map/ppermute | solution.py:24
  39.9 3.5 %collective-permute-done.7 = f32[8,1024]{1,0:T(8,128)S(1)} collective-permute-done((f32[8,1024]{1,0:T(8,128)S(1)}, f32[8,1024]{1,0:T(8,128)S(1)}, u32[]{:S(2)}, u32[]{:S(2)}) %collective-permute-start.7) | collective-permute-done | bytes 32800 | tf_op jit(solution)/shard_map/ppermute | solution.py:24
  43.3 0.6 %fusion.5 = (bf16[8,512]{1,0:T(8,128)(2,1)}, bf16[8,512]{1,0:T(8,128)(2,1)}) fusion(bf16[8,1024]{1,0:T(8,128)(2,1)S(1)} %fusion.3), kind=kLoop, calls=%fused_computation.32 | loop fusion | bytes 32768 | tf_op jit(solution)/shard_map/slice | solution.py:173
  (26 shorter events, 0.3 us)
Async XLA Ops:
  0.6 0.7 %copy-start = (bf16[8,512]{1,0:T(8,128)(2,1)S(1)}, bf16[8,512]{1,0:T(8,128)(2,1)}, u32[]{:S(2)}) copy-start(bf16[8,512]{1,0:T(8,128)(2,1)} %param.12) | copy-start | bytes 24580
  1.4 4.0 %copy-start.1 = (s32[2,16]{1,0:T(2,128)S(1)}, s32[2,16]{1,0:T(2,128)}, u32[]{:S(2)}) copy-start(s32[2,16]{1,0:T(2,128)} %param.15) | copy-start | bytes 388
  1.4 7.3 %collective-permute-start = (bf16[8,1024]{1,0:T(8,128)(2,1)S(1)}, bf16[8,1024]{1,0:T(8,128)(2,1)S(1)}, u32[]{:S(2)}, u32[]{:S(2)}) collective-permute-start(bf16[8,1024]{1,0:T(8,128)(2,1)S(1)} %constant_dynamic-update-slice_fusion), channel_id=1, source_target_pairs={{0,8},{1,9},{2,10},{3,11},{4,12},{5,13},{6,14},{7,15},{8,0},{9,1},... | collective-permute-start | bytes 49160 | tf_op jit(solution)/shard_map/ppermute | solution.py:24
  5.6 0.7 %copy-start.2 = (s32[2]{0:T(128)S(1)}, s32[2]{0:T(128)}, u32[]{:S(2)}) copy-start(s32[2]{0:T(128)} %param.14) | copy-start | bytes 28
  8.7 4.0 %collective-permute-start.1 = (bf16[2,8,1024]{2,1,0:T(8,128)(2,1)S(1)}, bf16[2,8,1024]{2,1,0:T(8,128)(2,1)S(1)}, u32[]{:S(2)}, u32[]{:S(2)}) collective-permute-start(bf16[2,8,1024]{2,1,0:T(8,128)(2,1)S(1)} %maximum_select_fusion.6), channel_id=1, source_target_pairs={{0,4},{1,5},{2,6},{3,7},{4,0},{5,1},{6,2},{7,3},{8,12},{9,13},{10,... | collective-permute-start | bytes 98312 | tf_op jit(solution)/shard_map/ppermute | solution.py:24
  12.7 4.3 %collective-permute-start.2 = (bf16[2,2,8,1024]{3,2,1,0:T(8,128)(2,1)S(1)}, bf16[2,2,8,1024]{3,2,1,0:T(8,128)(2,1)S(1)}, u32[]{:S(2)}, u32[]{:S(2)}) collective-permute-start(bf16[2,2,8,1024]{3,2,1,0:T(8,128)(2,1)S(1)} %maximum_select_fusion.4), channel_id=1, source_target_pairs={{0,2},{1,3},{2,0},{3,1},{4,6},{5,7},{6,4},{7,5},{8,10},{9,11},{10,... | collective-permute-start | bytes 196616 | tf_op jit(solution)/shard_map/ppermute | solution.py:24
  17.0 1.4 %collective-permute-start.3 = (bf16[2,2,2,8,1024]{4,3,2,1,0:T(8,128)(2,1)S(1)}, bf16[2,2,2,8,1024]{4,3,2,1,0:T(8,128)(2,1)S(1)}, u32[]{:S(2)}, u32[]{:S(2)}) collective-permute-start(bf16[2,2,2,8,1024]{4,3,2,1,0:T(8,128)(2,1)S(1)} %maximum_select_fusion.2), channel_id=1, source_target_pairs={{0,1},{1,0},{2,3},{3,2},{4,5},{5,4},{6,7},{7,6},{8,9},{9,8},{10,11... | collective-permute-start | bytes 393224 | tf_op jit(solution)/shard_map/ppermute | solution.py:24
  26.8 1.6 %collective-permute-start.4 = (f32[2,2,2,8,1024]{4,3,1,0,2:T(8,128)S(1)}, f32[2,2,2,8,1024]{4,3,1,0,2:T(8,128)S(1)}, u32[]{:S(2)}, u32[]{:S(2)}) collective-permute-start(f32[2,2,2,8,1024]{4,3,1,0,2:T(8,128)S(1)} %bitcast.45), channel_id=1, source_target_pairs={{0,1},{1,0},{2,3},{3,2},{4,5},{5,4},{6,7},{7,6},{8,9},{9,8},{10,11... | collective-permute-start | bytes 786440 | tf_op jit(solution)/shard_map/ppermute | solution.py:24
  28.4 5.6 %collective-permute-start.5 = (f32[2,2,8,1024]{3,2,1,0:T(8,128)S(1)}, f32[2,2,8,1024]{3,2,1,0:T(8,128)S(1)}, u32[]{:S(2)}, u32[]{:S(2)}) collective-permute-start(f32[2,2,8,1024]{3,2,1,0:T(8,128)S(1)} %dynamic-slice_bitcast_fusion), channel_id=1, source_target_pairs={{0,2},{1,3},{2,0},{3,1},{4,6},{5,7},{6,4},{7,5},{8,10},{9,11},{10,... | collective-permute-start | bytes 393224 | tf_op jit(solution)/shard_map/ppermute | solution.py:24
  34.1 4.3 %collective-permute-start.6 = (f32[2,8,1024]{2,1,0:T(8,128)S(1)}, f32[2,8,1024]{2,1,0:T(8,128)S(1)}, u32[]{:S(2)}, u32[]{:S(2)}) collective-permute-start(f32[2,8,1024]{2,1,0:T(8,128)S(1)} %dynamic-slice_bitcast_fusion.1), channel_id=1, source_target_pairs={{0,4},{1,5},{2,6},{3,7},{4,0},{5,1},{6,2},{7,3},{8,12},{9,13},{10,... | collective-permute-start | bytes 196616 | tf_op jit(solution)/shard_map/ppermute | solution.py:24
  38.4 4.9 %collective-permute-start.7 = (f32[8,1024]{1,0:T(8,128)S(1)}, f32[8,1024]{1,0:T(8,128)S(1)}, u32[]{:S(2)}, u32[]{:S(2)}) collective-permute-start(f32[8,1024]{1,0:T(8,128)S(1)} %dynamic-slice_bitcast_fusion.2), channel_id=1, source_target_pairs={{0,8},{1,9},{2,10},{3,11},{4,12},{5,13},{6,14},{7,15},{8,0},{9,1},... | collective-permute-start | bytes 98312 | tf_op jit(solution)/shard_map/ppermute | solution.py:24

commit v3 on v2

--- a/solution.py
+++ b/solution.py
@@ -1,4 +1,5 @@
 import jax
+import numpy as np
 import jax.numpy as jnp
 from jax import lax
 from jax.experimental import pallas as pl
@@ -22,6 +23,13 @@
 def swap_with(block, axis_name, size, bit):
     pairs = [(index, index ^ (1 << bit)) for index in range(size)]
     return lax.ppermute(block, axis_name, pairs)
+
+
+def reversed_order(size):
+    bits = exchange_bits(size)
+    if not bits:
+        return list(range(size))
+    return [int(format(spot, "0%db" % bits)[::-1], 2) for spot in range(size)]
 
 
 def gather_rows(block, axis_name):
@@ -35,26 +43,24 @@
         other = swap_with(stacked, axis_name, size, bit)
         mine_low = ((me >> bit) & 1) == 0
         stacked = jnp.where(mine_low, jnp.stack([stacked, other]), jnp.stack([other, stacked]))
-    stacked = stacked.reshape((2,) * bits + block.shape)
-    stacked = jnp.transpose(stacked, tuple(reversed(range(bits))) + (bits, bits + 1))
     return stacked.reshape((size * block.shape[0],) + block.shape[1:])
 
 
 def scatter_sum_rows(block, axis_name):
     size = lax.axis_size(axis_name)
     bits = exchange_bits(size)
-    if bits is None:
+    if not bits:
         return lax.psum_scatter(block, axis_name, scatter_dimension=0, tiled=True)
     me = lax.axis_index(axis_name)
-    rows = block.shape[0] // size
-    parts = block.reshape((2,) * bits + (rows,) + block.shape[1:])
+    parts = block.reshape((2, block.shape[0] // 2) + block.shape[1:])
     for bit in range(bits):
-        axis = bits - 1 - bit
         mine = (me >> bit) & 1
-        keep = lax.dynamic_index_in_dim(parts, mine, axis, keepdims=False)
-        send = lax.dynamic_index_in_dim(parts, 1 - mine, axis, keepdims=False)
+        keep = lax.dynamic_index_in_dim(parts, mine, 0, keepdims=False)
+        send = lax.dynamic_index_in_dim(parts, 1 - mine, 0, keepdims=False)
         parts = keep + swap_with(send, axis_name, size, bit)
-    return parts.reshape((rows,) + block.shape[1:])
+        if bit + 1 < bits:
+            parts = parts.reshape((2, parts.shape[0] // 2) + parts.shape[1:])
+    return parts
 
 
 def contract_rows(left, right):
@@ -146,8 +152,11 @@
     collected = gather_rows(jnp.concatenate([document_keys, document_values], axis=1), "resp")
     doc_rows = collected.shape[0]
     block_rows = doc_rows // mask_blocks
+    slab_rows = document_keys.shape[0]
+    holders = np.repeat(np.array(reversed_order(lax.axis_size("resp"))), slab_rows)
+    global_rows = holders * slab_rows + np.tile(np.arange(slab_rows), lax.axis_size("resp"))
     row_masks = jnp.repeat(doc_mask, resp_len, axis=0)
-    doc_visible = (jnp.repeat(row_masks, block_rows, axis=1) == 1).astype(jnp.float32)
+    doc_visible = (row_masks[:, global_rows // block_rows] == 1).astype(jnp.float32)
     query_gradient, doc_terms, self_key, self_value = pl.pallas_call(
         attention_kernel,
         out_shape=(

time: 44.2 us -> 44.8 us (1.014)
  other arithmetic: 1.52 us -> 2.86 us
  local copies, waits for them, and re-layouts: 5.07 us -> 4.28 us
  waiting for transfers between devices: 18 us -> 18.6 us
  starting transfers between devices: 12.1 us -> 11.5 us
    dynamic_slice x2 -> x0, local copies, waits for them, and re-layouts: 1.08 us -> none  [the longest x1 1.06 us: scatter_sum_rows(): keep = lax.dynamic_index_in_dim(parts, mine, axis, keepdims=False)]
    squeeze x3 -> x4, local copies, waits for them, and re-layouts: 0.05 us -> 1.09 us  [scatter_sum_rows(): send = lax.dynamic_index_in_dim(parts, 1 - mine, 0, keepdims=False)]
    convert_element_type x4 -> x0, local copies, waits for them, and re-layouts: 0.89 us -> none  [per_device(): (jnp.repeat(row_masks, block_rows, axis=1) == 1).astype(jnp.float32)]
    select_n x6 -> x7, other arithmetic: 0.06 us -> 0.81 us  [gather_rows(): jnp.where(mine_low, jnp.stack([stacked, other]), jnp.stack([other, stacke...]
    gather x0 -> x2, local copies, waits for them, and re-layouts: none -> 0.73 us  [per_device(): row_masks[:, global_rows // block_rows] == 1]
    transpose x1 -> x0, local copies, waits for them, and re-layouts: 0.72 us -> none  [gather_rows(): jnp.transpose(stacked, tuple(reversed(range(bits))) + (bits, bits + 1))]
    convert_element_type x1, other arithmetic: 0.01 us -> 0.63 us  [per_device(): (row_masks[:, global_rows // block_rows] == 1).astype(jnp.float32)]
    ppermute x8, starting transfers between devices: 12.1 us -> 11.5 us  [swap_with(): return lax.ppermute(block, axis_name, pairs)]
  transfers between devices with their start and end apart: 8 -> 8, of which waited for: 7 -> 7; matrix products, arithmetic and copies ran while one was open for 6% -> 7% of each run, Pallas kernels for 0% -> 0%
where the time goes in v3:
time: 44.8 us; the launch traced here: 44.5 us
  waiting for transfers between devices  18.6 us (42%)
  starting transfers between devices  11.5 us (26%)
  Pallas kernels  6.47 us (14%)
  local copies, waits for them, and re-layouts  4.28 us (10%)
  other arithmetic  2.86 us (6%)
  between operations  0.76 us (2%)
    ppermute x8, waiting for transfers between devices, swap_with(): return lax.ppermute(block, axis_name, pairs)  18.6 us
    ppermute x8, starting transfers between devices, swap_with(): return lax.ppermute(block, axis_name, pairs)  11.5 us
    pallas_call x1, Pallas kernels, per_device(): pl.pallas_call(attention_kernel, out_shape=(jax.ShapeDtypeStruct(queries....  6.47 us
    unnamed x12, local copies, waits for them, and re-layouts  1.4 us
    squeeze x4, local copies, waits for them, and re-layouts, scatter_sum_rows(): send = lax.dynamic_index_in_dim(parts, 1 - mine, 0, keepdims=False)  1.09 us
  transfers between devices with their start and end apart: 8, of which 7 were waited for; matrix products, arithmetic and copies ran while one was open for 7% of the time, Pallas kernels for 0%

profile of v3, /device:TPU:0, one launch (start us, length us, event | category | flops | bytes accessed | tf_op | source)
XLA Modules:
  0.0 44.5 jit_solution(4445588240405275157)
XLA Ops:
  0.6 0.7 %constant_dynamic-update-slice_fusion.1 = bf16[8,1024]{1,0:T(8,128)(2,1)S(1)} fusion(bf16[8,512]{1,0:T(8,128)(2,1)} %param.13), kind=kLoop, calls=%fused_computation.24 | loop fusion | bytes 16384
  1.4 4.0 %collective-permute-start = (bf16[8,1024]{1,0:T(8,128)(2,1)S(1)}, bf16[8,1024]{1,0:T(8,128)(2,1)S(1)}, u32[]{:S(2)}, u32[]{:S(2)}) collective-permute-start(bf16[8,1024]{1,0:T(8,128)(2,1)S(1)} %constant_dynamic-update-slice_fusion), channel_id=1, source_target_pairs={{0,8},{1,9},{2,10},{3,11},{4,12},{5,13},{6,14},{7,15},{8,0},{9,1},... | collective-permute-start | bytes 49160 | tf_op jit(solution)/shard_map/ppermute | solution.py:25
  5.4 0.1 copy.18
  5.5 0.1 broadcast_in_dim.6
  5.6 0.1 reshape.387
  5.6 0.6 %copy-done.3 = s32[128]{0:T(128)S(1)} copy-done((s32[128]{0:T(128)S(1)}, s32[128]{0:T(128)}, u32[]{:S(2)}) %copy-start.3) | copy-done | bytes 536
  6.2 0.6 %gather_fusion = s32[128,128]{1,0:T(8,128)S(1)} fusion(s32[128,16]{0,1:T(8,128)S(1)} %reshape.387, s32[1024]{0:T(1024)S(1)} %pad_clamp_fusion), kind=kCustom, calls=%fused_computation | custom fusion | bytes 131584 | tf_op jit(solution)/shard_map/gather | solution.py:159
  6.9 0.1 copy.19
  7.0 0.6 %convert_bitcast_fusion.vis_ref = f32[128,128]{1,0:T(8,128)} fusion(s32[128,128]{0,1:T(8,128)S(1)} %copy.19), kind=kLoop, calls=%fused_computation.12 | loop fusion | flops 32768 | bytes 131072 | tf_op jit(solution)/shard_map/convert_element_type | solution.py:159
  7.6 0.1 broadcast_in_dim.16
  7.7 0.1 reshape.388
  7.8 0.7 %fusion.2.self_ref = f32[128,128]{1,0:T(8,128)} fusion(s32[128]{0:T(128)S(1)} %and_select_fusion.1), kind=kLoop, calls=%fused_computation.16 | loop fusion | flops 65536 | bytes 66048 | tf_op jit(solution)/shard_map/convert_element_type | solution.py:151
  8.5 0.1 copy.20
  8.6 0.6 %convert_element_type.20.live_ref = f32[128,1]{1,0:T(8,128)} convert(pred[128,1]{1,0:T(8,128)(4,1)S(1)} %copy.20) | non-fusion elementwise | flops 128 | bytes 640 | tf_op jit(solution)/shard_map/convert_element_type | solution.py:148
  9.3 1.6 %collective-permute-start.1 = (bf16[2,8,1024]{2,1,0:T(8,128)(2,1)S(1)}, bf16[2,8,1024]{2,1,0:T(8,128)(2,1)S(1)}, u32[]{:S(2)}, u32[]{:S(2)}) collective-permute-start(bf16[2,8,1024]{2,1,0:T(8,128)(2,1)S(1)} %maximum_select_fusion.6), channel_id=1, source_target_pairs={{0,4},{1,5},{2,6},{3,7},{4,0},{5,1},{6,2},{7,3},{8,12},{9,13},{10,... | collective-permute-start | bytes 98312 | tf_op jit(solution)/shard_map/ppermute | solution.py:25
  10.9 2.3 %collective-permute-done.1 = bf16[2,8,1024]{2,1,0:T(8,128)(2,1)S(1)} collective-permute-done((bf16[2,8,1024]{2,1,0:T(8,128)(2,1)S(1)}, bf16[2,8,1024]{2,1,0:T(8,128)(2,1)S(1)}, u32[]{:S(2)}, u32[]{:S(2)}) %collective-permute-start.1) | collective-permute-done | bytes 32800 | tf_op jit(solution)/shard_map/ppermute | solution.py:25
  13.3 1.6 %collective-permute-start.2 = (bf16[2,2,8,1024]{3,2,1,0:T(8,128)(2,1)S(1)}, bf16[2,2,8,1024]{3,2,1,0:T(8,128)(2,1)S(1)}, u32[]{:S(2)}, u32[]{:S(2)}) collective-permute-start(bf16[2,2,8,1024]{3,2,1,0:T(8,128)(2,1)S(1)} %maximum_select_fusion.4), channel_id=1, source_target_pairs={{0,2},{1,3},{2,0},{3,1},{4,6},{5,7},{6,4},{7,5},{8,10},{9,11},{10,... | collective-permute-start | bytes 196616 | tf_op jit(solution)/shard_map/ppermute | solution.py:25
  14.8 2.8 %collective-permute-done.2 = bf16[2,2,8,1024]{3,2,1,0:T(8,128)(2,1)S(1)} collective-permute-done((bf16[2,2,8,1024]{3,2,1,0:T(8,128)(2,1)S(1)}, bf16[2,2,8,1024]{3,2,1,0:T(8,128)(2,1)S(1)}, u32[]{:S(2)}, u32[]{:S(2)}) %collective-permute-start.2) | collective-permute-done | bytes 65568 | tf_op jit(solution)/shard_map/ppermute | solution.py:25
  17.6 0.1 collective-permute-start.3
  17.7 1.3 %collective-permute-done.3 = bf16[2,2,2,8,1024]{4,3,2,1,0:T(8,128)(2,1)S(1)} collective-permute-done((bf16[2,2,2,8,1024]{4,3,2,1,0:T(8,128)(2,1)S(1)}, bf16[2,2,2,8,1024]{4,3,2,1,0:T(8,128)(2,1)S(1)}, u32[]{:S(2)}, u32[]{:S(2)}) %collective-permute-start.3) | collective-permute-done | bytes 131104 | tf_op jit(solution)/shard_map/ppermute | solution.py:25
  19.0 0.7 %maximum_select_fusion = bf16[2,2,2,2,8,1024]{5,4,3,2,1,0:T(8,128)(2,1)} fusion(bf16[1,2,2,2,8,1024]{5,4,3,2,1,0:T(8,128)(2,1)S(1)} %bitcast.61, bf16[1,2,2,2,8,1024]{5,4,3,2,1,0:T(8,128)(2,1)S(1)} %maximum_select_fusion.1, pred[]{:T(512)S(6)} %eq.33), kind=kLoop, calls=%fused_computation.1 | loop fusion | flops 393216 | bytes 524289 | tf_op jit(solution)/shard_map/jit(_where)/select_n | solution.py:45
  19.8 6.5 %shard_map.137 = (bf16[128,2560]{1,0:T(8,128)(2,1)}, f32[128,1024]{1,0:T(8,128)}, bf16[128,512]{1,0:T(8,128)(2,1)}, bf16[128,512]{1,0:T(8,128)(2,1)}) custom-call(bf16[128,2560]{1,0:T(8,128)(2,1)} %q_ref.1, bf16[128,2560]{1,0:T(8,128)(2,1)} %do_ref.1, bf16[128,1024]{1,0:T(8,128)(2,1)} %bitcast.45, bf16[128,512]{1,0:T(8,128)(2,1)} %ks_ref.1, ...), custom_call_target="tpu_custom_call" | custom-call | tf_op jit(solution)/shard_map/pallas_call | solution.py:160
  26.3 1.0 %dynamic-slice_bitcast_fusion = f32[64,1024]{1,0:T(8,128)S(1)} fusion(f32[2,64,1024]{2,1,0:T(8,128)} %bitcast.48, s32[]{:T(128)S(6)} %select_n.164), kind=kLoop, calls=%fused_computation.3 | loop fusion | bytes 524292 | tf_op jit(solution)/shard_map/jit(dynamic_index_in_dim)/squeeze | solution.py:59
  27.3 0.2 collective-permute-start.4
  27.5 1.4 %collective-permute-done.4 = f32[64,1024]{1,0:T(8,128)S(1)} collective-permute-done((f32[64,1024]{1,0:T(8,128)S(1)}, f32[64,1024]{1,0:T(8,128)S(1)}, u32[]{:S(2)}, u32[]{:S(2)}) %collective-permute-start.4) | collective-permute-done | bytes 262176 | tf_op jit(solution)/shard_map/ppermute | solution.py:25
  29.0 1.6 %collective-permute-start.5 = (f32[32,1024]{1,0:T(8,128)S(1)}, f32[32,1024]{1,0:T(8,128)S(1)}, u32[]{:S(2)}, u32[]{:S(2)}) collective-permute-start(f32[32,1024]{1,0:T(8,128)S(1)} %dynamic-slice_bitcast_fusion.1), channel_id=1, source_target_pairs={{0,2},{1,3},{2,0},{3,1},{4,6},{5,7},{6,4},{7,5},{8,10},{9,11},{10,... | collective-permute-start | bytes 393224 | tf_op jit(solution)/shard_map/ppermute | solution.py:25
  30.5 4.1 %collective-permute-done.5 = f32[32,1024]{1,0:T(8,128)S(1)} collective-permute-done((f32[32,1024]{1,0:T(8,128)S(1)}, f32[32,1024]{1,0:T(8,128)S(1)}, u32[]{:S(2)}, u32[]{:S(2)}) %collective-permute-start.5) | collective-permute-done | bytes 131104 | tf_op jit(solution)/shard_map/ppermute | solution.py:25
  34.6 1.6 %collective-permute-start.6 = (f32[16,1024]{1,0:T(8,128)S(1)}, f32[16,1024]{1,0:T(8,128)S(1)}, u32[]{:S(2)}, u32[]{:S(2)}) collective-permute-start(f32[16,1024]{1,0:T(8,128)S(1)} %dynamic-slice_bitcast_fusion.2), channel_id=1, source_target_pairs={{0,4},{1,5},{2,6},{3,7},{4,0},{5,1},{6,2},{7,3},{8,12},{9,13},{10,... | collective-permute-start | bytes 196616 | tf_op jit(solution)/shard_map/ppermute | solution.py:25
  36.3 2.7 %collective-permute-done.6 = f32[16,1024]{1,0:T(8,128)S(1)} collective-permute-done((f32[16,1024]{1,0:T(8,128)S(1)}, f32[16,1024]{1,0:T(8,128)S(1)}, u32[]{:S(2)}, u32[]{:S(2)}) %collective-permute-start.6) | collective-permute-done | bytes 65568 | tf_op jit(solution)/shard_map/ppermute | solution.py:25
  39.0 0.8 %collective-permute-start.7 = (f32[8,1024]{1,0:T(8,128)S(1)}, f32[8,1024]{1,0:T(8,128)S(1)}, u32[]{:S(2)}, u32[]{:S(2)}) collective-permute-start(f32[8,1024]{1,0:T(8,128)S(1)} %dynamic-slice_bitcast_fusion.3), channel_id=1, source_target_pairs={{0,8},{1,9},{2,10},{3,11},{4,12},{5,13},{6,14},{7,15},{8,0},{9,1},... | collective-permute-start | bytes 98312 | tf_op jit(solution)/shard_map/ppermute | solution.py:25
  39.8 4.1 %collective-permute-done.7 = f32[8,1024]{1,0:T(8,128)S(1)} collective-permute-done((f32[8,1024]{1,0:T(8,128)S(1)}, f32[8,1024]{1,0:T(8,128)S(1)}, u32[]{:S(2)}, u32[]{:S(2)}) %collective-permute-start.7) | collective-permute-done | bytes 32800 | tf_op jit(solution)/shard_map/ppermute | solution.py:25
  43.9 0.6 %fusion.5 = (bf16[8,512]{1,0:T(8,128)(2,1)}, bf16[8,512]{1,0:T(8,128)(2,1)}) fusion(bf16[8,1024]{1,0:T(8,128)(2,1)S(1)} %fusion.3), kind=kLoop, calls=%fused_computation.31 | loop fusion | bytes 32768 | tf_op jit(solution)/shard_map/slice | solution.py:182
  (29 shorter events, 0.2 us)
Async XLA Ops:
  0.6 0.7 %copy-start.1 = (bf16[8,512]{1,0:T(8,128)(2,1)S(1)}, bf16[8,512]{1,0:T(8,128)(2,1)}, u32[]{:S(2)}) copy-start(bf16[8,512]{1,0:T(8,128)(2,1)} %param.14) | copy-start | bytes 24580
  1.4 4.0 %copy-start.2 = (s32[2,16]{1,0:T(2,128)S(1)}, s32[2,16]{1,0:T(2,128)}, u32[]{:S(2)}) copy-start(s32[2,16]{1,0:T(2,128)} %param.17) | copy-start | bytes 388
  1.4 7.9 %collective-permute-start = (bf16[8,1024]{1,0:T(8,128)(2,1)S(1)}, bf16[8,1024]{1,0:T(8,128)(2,1)S(1)}, u32[]{:S(2)}, u32[]{:S(2)}) collective-permute-start(bf16[8,1024]{1,0:T(8,128)(2,1)S(1)} %constant_dynamic-update-slice_fusion), channel_id=1, source_target_pairs={{0,8},{1,9},{2,10},{3,11},{4,12},{5,13},{6,14},{7,15},{8,0},{9,1},... | collective-permute-start | bytes 49160 | tf_op jit(solution)/shard_map/ppermute | solution.py:25
  5.6 0.7 %copy-start.3 = (s32[128]{0:T(128)S(1)}, s32[128]{0:T(128)}, u32[]{:S(2)}) copy-start(s32[128]{0:T(128)} %constant.85) | copy-start | bytes 1540
  7.0 0.7 %copy-start.4 = (s32[2]{0:T(128)S(1)}, s32[2]{0:T(128)}, u32[]{:S(2)}) copy-start(s32[2]{0:T(128)} %param.16) | copy-start | bytes 28
  9.3 4.0 %collective-permute-start.1 = (bf16[2,8,1024]{2,1,0:T(8,128)(2,1)S(1)}, bf16[2,8,1024]{2,1,0:T(8,128)(2,1)S(1)}, u32[]{:S(2)}, u32[]{:S(2)}) collective-permute-start(bf16[2,8,1024]{2,1,0:T(8,128)(2,1)S(1)} %maximum_select_fusion.6), channel_id=1, source_target_pairs={{0,4},{1,5},{2,6},{3,7},{4,0},{5,1},{6,2},{7,3},{8,12},{9,13},{10,... | collective-permute-start | bytes 98312 | tf_op jit(solution)/shard_map/ppermute | solution.py:25
  13.3 4.3 %collective-permute-start.2 = (bf16[2,2,8,1024]{3,2,1,0:T(8,128)(2,1)S(1)}, bf16[2,2,8,1024]{3,2,1,0:T(8,128)(2,1)S(1)}, u32[]{:S(2)}, u32[]{:S(2)}) collective-permute-start(bf16[2,2,8,1024]{3,2,1,0:T(8,128)(2,1)S(1)} %maximum_select_fusion.4), channel_id=1, source_target_pairs={{0,2},{1,3},{2,0},{3,1},{4,6},{5,7},{6,4},{7,5},{8,10},{9,11},{10,... | collective-permute-start | bytes 196616 | tf_op jit(solution)/shard_map/ppermute | solution.py:25
  17.6 1.4 %collective-permute-start.3 = (bf16[2,2,2,8,1024]{4,3,2,1,0:T(8,128)(2,1)S(1)}, bf16[2,2,2,8,1024]{4,3,2,1,0:T(8,128)(2,1)S(1)}, u32[]{:S(2)}, u32[]{:S(2)}) collective-permute-start(bf16[2,2,2,8,1024]{4,3,2,1,0:T(8,128)(2,1)S(1)} %maximum_select_fusion.2), channel_id=1, source_target_pairs={{0,1},{1,0},{2,3},{3,2},{4,5},{5,4},{6,7},{7,6},{8,9},{9,8},{10,11... | collective-permute-start | bytes 393224 | tf_op jit(solution)/shard_map/ppermute | solution.py:25
  26.3 2.6 %copy-start = (f32[128,1024]{1,0:T(8,128)S(1)}, f32[128,1024]{1,0:T(8,128)}, u32[]{:S(2)}) copy-start(f32[128,1024]{1,0:T(8,128)} %get-tuple-element.10) | copy-start | bytes 1572868
  27.3 1.6 %collective-permute-start.4 = (f32[64,1024]{1,0:T(8,128)S(1)}, f32[64,1024]{1,0:T(8,128)S(1)}, u32[]{:S(2)}, u32[]{:S(2)}) collective-permute-start(f32[64,1024]{1,0:T(8,128)S(1)} %dynamic-slice_bitcast_fusion), channel_id=1, source_target_pairs={{0,1},{1,0},{2,3},{3,2},{4,5},{5,4},{6,7},{7,6},{8,9},{9,8},{10,11... | collective-permute-start | bytes 786440 | tf_op jit(solution)/shard_map/ppermute | solution.py:25
  29.0 5.6 %collective-permute-start.5 = (f32[32,1024]{1,0:T(8,128)S(1)}, f32[32,1024]{1,0:T(8,128)S(1)}, u32[]{:S(2)}, u32[]{:S(2)}) collective-permute-start(f32[32,1024]{1,0:T(8,128)S(1)} %dynamic-slice_bitcast_fusion.1), channel_id=1, source_target_pairs={{0,2},{1,3},{2,0},{3,1},{4,6},{5,7},{6,4},{7,5},{8,10},{9,11},{10,... | collective-permute-start | bytes 393224 | tf_op jit(solution)/shard_map/ppermute | solution.py:25
  34.6 4.3 %collective-permute-start.6 = (f32[16,1024]{1,0:T(8,128)S(1)}, f32[16,1024]{1,0:T(8,128)S(1)}, u32[]{:S(2)}, u32[]{:S(2)}) collective-permute-start(f32[16,1024]{1,0:T(8,128)S(1)} %dynamic-slice_bitcast_fusion.2), channel_id=1, source_target_pairs={{0,4},{1,5},{2,6},{3,7},{4,0},{5,1},{6,2},{7,3},{8,12},{9,13},{10,... | collective-permute-start | bytes 196616 | tf_op jit(solution)/shard_map/ppermute | solution.py:25
  39.0 4.9 %collective-permute-start.7 = (f32[8,1024]{1,0:T(8,128)S(1)}, f32[8,1024]{1,0:T(8,128)S(1)}, u32[]{:S(2)}, u32[]{:S(2)}) collective-permute-start(f32[8,1024]{1,0:T(8,128)S(1)} %dynamic-slice_bitcast_fusion.3), channel_id=1, source_target_pairs={{0,8},{1,9},{2,10},{3,11},{4,12},{5,13},{6,14},{7,15},{8,0},{9,1},... | collective-permute-start | bytes 98312 | tf_op jit(solution)/shard_map/ppermute | solution.py:25

commit v4 on v2

--- a/solution.py
+++ b/solution.py
@@ -1,4 +1,5 @@
 import jax
+import numpy as np
 import jax.numpy as jnp
 from jax import lax
 from jax.experimental import pallas as pl
@@ -24,37 +25,31 @@
     return lax.ppermute(block, axis_name, pairs)
 
 
-def gather_rows(block, axis_name):
+def exchange_pattern(size):
+    bits = exchange_bits(size)
+    return [int(format(spot, "0%db" % bits)[::-1], 2) for spot in range(size)]
+
+
+def gather_rows(blocks, axis_name):
     size = lax.axis_size(axis_name)
     bits = exchange_bits(size)
-    if bits is None:
-        return lax.all_gather(block, axis_name, axis=0, tiled=True)
-    me = lax.axis_index(axis_name)
-    stacked = block
+    halves = None
     for bit in reversed(range(bits)):
-        other = swap_with(stacked, axis_name, size, bit)
-        mine_low = ((me >> bit) & 1) == 0
-        stacked = jnp.where(mine_low, jnp.stack([stacked, other]), jnp.stack([other, stacked]))
-    stacked = stacked.reshape((2,) * bits + block.shape)
-    stacked = jnp.transpose(stacked, tuple(reversed(range(bits))) + (bits, bits + 1))
-    return stacked.reshape((size * block.shape[0],) + block.shape[1:])
-
-
-def scatter_sum_rows(block, axis_name):
+        if halves is not None:
+            blocks = jnp.concatenate(halves)
+        halves = (blocks, swap_with(blocks, axis_name, size, bit))
+    return halves
+
+
+def scatter_sum_rows(keep, send, axis_name):
     size = lax.axis_size(axis_name)
     bits = exchange_bits(size)
-    if bits is None:
-        return lax.psum_scatter(block, axis_name, scatter_dimension=0, tiled=True)
-    me = lax.axis_index(axis_name)
-    rows = block.shape[0] // size
-    parts = block.reshape((2,) * bits + (rows,) + block.shape[1:])
     for bit in range(bits):
-        axis = bits - 1 - bit
-        mine = (me >> bit) & 1
-        keep = lax.dynamic_index_in_dim(parts, mine, axis, keepdims=False)
-        send = lax.dynamic_index_in_dim(parts, 1 - mine, axis, keepdims=False)
-        parts = keep + swap_with(send, axis_name, size, bit)
-    return parts.reshape((rows,) + block.shape[1:])
+        if bit > 0:
+            split = keep.shape[0] // 2
+            keep, send = keep[:split], keep[split:]
+        keep = keep + swap_with(send, axis_name, size, bit)
+    return keep
 
 
 def contract_rows(left, right):
@@ -70,18 +65,21 @@
 
 
 def attention_kernel(
-    q_ref, do_ref, kv_ref, ks_ref, vs_ref, vis_ref, self_ref, live_ref,
-    dq_ref, doc_ref, sk_ref, sv_ref,
+    q_ref, do_ref, kva_ref, kvb_ref, ks_ref, vs_ref, vis_ref, self_ref, live_ref,
+    dq_ref, keep_ref, send_ref, sk_ref, sv_ref,
 ):
     token_rows = q_ref.shape[0]
     width = KEY_HEADS * HEAD_SIZE
+    half = kva_ref.shape[0]
     score_scale = HEAD_SIZE ** (-0.5)
     doc_seen = jnp.concatenate([vis_ref[...]] * GROUP_HEADS, axis=0) > 0.5
     self_seen = jnp.concatenate([self_ref[...]] * GROUP_HEADS, axis=0) > 0.5
     live = jnp.concatenate([live_ref[...]] * GROUP_HEADS, axis=0) > 0.5
     for c in range(KEY_HEADS):
-        kd = kv_ref[:, c * HEAD_SIZE:(c + 1) * HEAD_SIZE]
-        vd = kv_ref[:, width + c * HEAD_SIZE:width + (c + 1) * HEAD_SIZE]
+        columns = slice(c * HEAD_SIZE, (c + 1) * HEAD_SIZE)
+        value_columns = slice(width + c * HEAD_SIZE, width + (c + 1) * HEAD_SIZE)
+        kd = jnp.concatenate([kva_ref[:, columns], kvb_ref[:, columns]], axis=0)
+        vd = jnp.concatenate([kva_ref[:, value_columns], kvb_ref[:, value_columns]], axis=0)
         ks = ks_ref[:, c * HEAD_SIZE:(c + 1) * HEAD_SIZE]
         vs = vs_ref[:, c * HEAD_SIZE:(c + 1) * HEAD_SIZE]
         heads = [c * GROUP_HEADS + g for g in range(GROUP_HEADS)]
@@ -109,10 +107,12 @@
             dq_ref[:, h * HEAD_SIZE:(h + 1) * HEAD_SIZE] = dq[
                 g * token_rows:(g + 1) * token_rows
             ].astype(dq_ref.dtype)
-        doc_ref[:, c * HEAD_SIZE:(c + 1) * HEAD_SIZE] = contract_rows(dsd, q) * score_scale
-        doc_ref[:, width + c * HEAD_SIZE:width + (c + 1) * HEAD_SIZE] = contract_rows(
-            pd.astype(jnp.bfloat16), do
-        )
+        doc_key = contract_rows(dsd, q) * score_scale
+        doc_value = contract_rows(pd.astype(jnp.bfloat16), do)
+        keep_ref[:, columns] = doc_key[:half]
+        send_ref[:, columns] = doc_key[half:]
+        keep_ref[:, value_columns] = doc_value[:half]
+        send_ref[:, value_columns] = doc_value[half:]
         sk_ref[:, c * HEAD_SIZE:(c + 1) * HEAD_SIZE] = (
             contract_rows(dss, q) * score_scale
         ).astype(sk_ref.dtype)
@@ -143,30 +143,41 @@
     self_visible = (
         (owners[:, None] == owners[None, :]) & (positions[None, :] <= positions[:, None])
     ).astype(jnp.float32)
-    collected = gather_rows(jnp.concatenate([document_keys, document_values], axis=1), "resp")
-    doc_rows = collected.shape[0]
+    size = lax.axis_size("resp")
+    doc_mine, doc_other = gather_rows(
+        jnp.concatenate([document_keys, document_values], axis=1), "resp"
+    )
+    slab_rows = document_keys.shape[0]
+    doc_rows = size * slab_rows
+    half_rows = doc_rows // 2
     block_rows = doc_rows // mask_blocks
+    holders = jnp.bitwise_xor(
+        lax.axis_index("resp"), jnp.asarray(np.repeat(exchange_pattern(size), slab_rows), jnp.int32)
+    )
+    global_rows = holders * slab_rows + jnp.asarray(np.tile(np.arange(slab_rows), size), jnp.int32)
     row_masks = jnp.repeat(doc_mask, resp_len, axis=0)
-    doc_visible = (jnp.repeat(row_masks, block_rows, axis=1) == 1).astype(jnp.float32)
-    query_gradient, doc_terms, self_key, self_value = pl.pallas_call(
+    doc_visible = (jnp.take(row_masks, global_rows // block_rows, axis=1) == 1).astype(jnp.float32)
+    query_gradient, doc_keep, doc_send, self_key, self_value = pl.pallas_call(
         attention_kernel,
         out_shape=(
             jax.ShapeDtypeStruct(queries.shape, jnp.bfloat16),
-            jax.ShapeDtypeStruct((doc_rows, 2 * key_value_width), jnp.float32),
+            jax.ShapeDtypeStruct((half_rows, 2 * key_value_width), jnp.float32),
+            jax.ShapeDtypeStruct((half_rows, 2 * key_value_width), jnp.float32),
             jax.ShapeDtypeStruct(response_keys.shape, jnp.bfloat16),
             jax.ShapeDtypeStruct(response_values.shape, jnp.bfloat16),
         ),
     )(
         queries,
         grad_out,
-        collected,
+        doc_mine,
+        doc_other,
         response_keys,
         response_values,
         doc_visible,
         self_visible,
         live,
     )
-    summed = scatter_sum_rows(doc_terms, "resp")
+    summed = scatter_sum_rows(doc_keep, doc_send, "resp")
     return (
         query_gradient,
         summed[:, :key_value_width].astype(jnp.bfloat16),

time: 44.2 us -> 43.9 us (level)
  other arithmetic: 1.52 us -> 3.05 us
  waiting for transfers between devices: 18 us -> 16.7 us
  local copies, waits for them, and re-layouts: 5.07 us -> 4.61 us
    unnamed x7 -> x16, local copies, waits for them, and re-layouts: 1.36 us -> 2.79 us
    ppermute x8, waiting for transfers between devices: 18 us -> 16.7 us  [swap_with(): return lax.ppermute(block, axis_name, pairs)]
    dynamic_slice x2 -> x0, local copies, waits for them, and re-layouts: 1.08 us -> none  [the longest x1 1.06 us: scatter_sum_rows(): keep = lax.dynamic_index_in_dim(parts, mine, axis, keepdims=False)]
    add x3, other arithmetic: 0.06 us -> 1.02 us  [scatter_sum_rows(): keep = keep + swap_with(send, axis_name, size, bit)]
    convert_element_type x4 -> x0, local copies, waits for them, and re-layouts: 0.89 us -> none  [per_device(): (jnp.repeat(row_masks, block_rows, axis=1) == 1).astype(jnp.float32)]
    gather x0 -> x2, local copies, waits for them, and re-layouts: none -> 0.74 us  [per_device(): jnp.take(row_masks, global_rows // block_rows, axis=1) == 1]
    transpose x1 -> x0, local copies, waits for them, and re-layouts: 0.72 us -> none  [gather_rows(): jnp.transpose(stacked, tuple(reversed(range(bits))) + (bits, bits + 1))]
    convert_element_type x1, other arithmetic: 0.01 us -> 0.64 us  [per_device(): (jnp.take(row_masks, global_rows // block_rows, axis=1) == 1).astype(jnp....]
  transfers between devices with their start and end apart: 8 -> 8, of which waited for: 7 -> 7; matrix products, arithmetic and copies ran while one was open for 6% -> 8% of each run, Pallas kernels for 0% -> 0%
where the time goes in v4:
time: 43.9 us; the launch traced here: 43.6 us
  waiting for transfers between devices  16.7 us (38%)
  starting transfers between devices  12.1 us (28%)
  Pallas kernels  6.47 us (15%)
  local copies, waits for them, and re-layouts  4.61 us (11%)
  other arithmetic  3.05 us (7%)
  between operations  0.74 us (2%)
    ppermute x8, waiting for transfers between devices, swap_with(): return lax.ppermute(block, axis_name, pairs)  16.7 us
    ppermute x8, starting transfers between devices, swap_with(): return lax.ppermute(block, axis_name, pairs)  12.1 us
    pallas_call x1, Pallas kernels, per_device(): pl.pallas_call(attention_kernel, out_shape=(jax.ShapeDtypeStruct(queries....  6.47 us
    unnamed x16, local copies, waits for them, and re-layouts  2.79 us
    add x3, other arithmetic, scatter_sum_rows(): keep = keep + swap_with(send, axis_name, size, bit)  1.02 us
  transfers between devices with their start and end apart: 8, of which 7 were waited for; matrix products, arithmetic and copies ran while one was open for 8% of the time, Pallas kernels for 0%

profile of v4, /device:TPU:0, one launch (start us, length us, event | category | flops | bytes accessed | tf_op | source)
XLA Modules:
  0.0 43.6 jit_solution(5686855155419431107)
XLA Ops:
  0.6 0.7 %constant_dynamic-update-slice_fusion.1 = bf16[8,1024]{1,0:T(8,128)(2,1)S(1)} fusion(bf16[8,512]{1,0:T(8,128)(2,1)} %param.13), kind=kLoop, calls=%fused_computation.15 | loop fusion | bytes 16384
  1.4 4.0 %collective-permute-start = (bf16[8,1024]{1,0:T(8,128)(2,1)S(1)}, bf16[8,1024]{1,0:T(8,128)(2,1)S(1)}, u32[]{:S(2)}, u32[]{:S(2)}) collective-permute-start(bf16[8,1024]{1,0:T(8,128)(2,1)S(1)} %constant_dynamic-update-slice_fusion), channel_id=1, source_target_pairs={{0,8},{1,9},{2,10},{3,11},{4,12},{5,13},{6,14},{7,15},{8,0},{9,1},... | collective-permute-start | bytes 49160 | tf_op jit(solution)/shard_map/ppermute | solution.py:25
  5.4 0.7 %copy-done.4 = s32[128]{0:T(128)S(1)} copy-done((s32[128]{0:T(128)S(1)}, s32[128]{0:T(128)}, u32[]{:S(2)}) %copy-start.4) | copy-done | bytes 536
  6.1 0.7 %copy-done.3 = s32[2,16]{1,0:T(2,128)S(1)} copy-done((s32[2,16]{1,0:T(2,128)S(1)}, s32[2,16]{1,0:T(2,128)}, u32[]{:S(2)}) %copy-start.3) | copy-done | bytes 152
  6.8 0.1 copy.18
  6.8 0.1 broadcast_in_dim.24
  6.9 0.1 reshape.82
  7.0 0.6 %gather_fusion = s32[128,128]{1,0:T(8,128)S(1)} fusion(s32[128,16]{0,1:T(8,128)S(1)} %reshape.82, s32[1024]{0:T(1024)S(1)} %pad_clamp_fusion), kind=kCustom, calls=%fused_computation | custom fusion | bytes 131584 | tf_op jit(solution)/shard_map/jit(_take)/gather | solution.py:159
  7.7 0.1 copy.19
  7.8 0.6 %convert_bitcast_fusion.vis_ref = f32[128,128]{1,0:T(8,128)} fusion(s32[128,128]{0,1:T(8,128)S(1)} %copy.19, pred[128]{0:T(512)(128)(4,1)S(1)} %get-tuple-element.15), kind=kLoop, calls=%fused_computation.5 | loop fusion | flops 49152 | bytes 131200 | tf_op jit(solution)/shard_map/convert_element_type | solution.py:159
  8.5 0.1 reshape.83
  8.6 1.6 %collective-permute-start.1 = (bf16[16,1024]{1,0:T(8,128)(2,1)S(1)}, bf16[16,1024]{1,0:T(8,128)(2,1)S(1)}, u32[]{:S(2)}, u32[]{:S(2)}) collective-permute-start(bf16[16,1024]{1,0:T(8,128)(2,1)S(1)} %pad_maximum_fusion.2), channel_id=1, source_target_pairs={{0,4},{1,5},{2,6},{3,7},{4,0},{5,1},{6,2},{7,3},{8,12},{9,13},{10,... | collective-permute-start | bytes 98312 | tf_op jit(solution)/shard_map/ppermute | solution.py:25
  10.2 0.1 copy.20
  10.3 0.6 %convert_element_type.20.live_ref = f32[128,1]{1,0:T(8,128)} convert(pred[128,1]{1,0:T(8,128)(4,1)S(1)} %copy.20) | non-fusion elementwise | flops 128 | bytes 640 | tf_op jit(solution)/shard_map/convert_element_type | solution.py:142
  11.0 1.6 %collective-permute-done.1 = bf16[16,1024]{1,0:T(8,128)(2,1)S(1)} collective-permute-done((bf16[16,1024]{1,0:T(8,128)(2,1)S(1)}, bf16[16,1024]{1,0:T(8,128)(2,1)S(1)}, u32[]{:S(2)}, u32[]{:S(2)}) %collective-permute-start.1) | collective-permute-done | bytes 32800 | tf_op jit(solution)/shard_map/ppermute | solution.py:25
  12.5 1.5 %collective-permute-start.2 = (bf16[32,1024]{1,0:T(8,128)(2,1)S(1)}, bf16[32,1024]{1,0:T(8,128)(2,1)S(1)}, u32[]{:S(2)}, u32[]{:S(2)}) collective-permute-start(bf16[32,1024]{1,0:T(8,128)(2,1)S(1)} %pad_maximum_fusion.1), channel_id=1, source_target_pairs={{0,2},{1,3},{2,0},{3,1},{4,6},{5,7},{6,4},{7,5},{8,10},{9,11},{10,... | collective-permute-start | bytes 196616 | tf_op jit(solution)/shard_map/ppermute | solution.py:25
  14.0 2.8 %collective-permute-done.2 = bf16[32,1024]{1,0:T(8,128)(2,1)S(1)} collective-permute-done((bf16[32,1024]{1,0:T(8,128)(2,1)S(1)}, bf16[32,1024]{1,0:T(8,128)(2,1)S(1)}, u32[]{:S(2)}, u32[]{:S(2)}) %collective-permute-start.2) | collective-permute-done | bytes 65568 | tf_op jit(solution)/shard_map/ppermute | solution.py:25
  16.8 0.1 collective-permute-start.3
  16.9 0.7 %fusion.1.self_ref = f32[128,128]{1,0:T(8,128)} fusion(s32[128]{0:T(128)S(1)} %and_select_fusion.1), kind=kLoop, calls=%fused_computation.9 | loop fusion | flops 65536 | bytes 66048 | tf_op jit(solution)/shard_map/convert_element_type | solution.py:145
  17.6 0.6 %collective-permute-done.3.kvb_ref = bf16[64,1024]{1,0:T(8,128)(2,1)S(1)} collective-permute-done((bf16[64,1024]{1,0:T(8,128)(2,1)S(1)}, bf16[64,1024]{1,0:T(8,128)(2,1)S(1)}, u32[]{:S(2)}, u32[]{:S(2)}) %collective-permute-start.3) | collective-permute-done | bytes 131104 | tf_op jit(solution)/shard_map/ppermute | solution.py:25
  18.2 0.7 %copy-done.1 = bf16[64,1024]{1,0:T(8,128)(2,1)} copy-done((bf16[64,1024]{1,0:T(8,128)(2,1)}, bf16[64,1024]{1,0:T(8,128)(2,1)S(1)}, u32[]{:S(2)}) %copy-start.1) | copy-done | bytes 131096
  18.9 6.5 %shard_map.137 = (bf16[128,2560]{1,0:T(8,128)(2,1)}, f32[64,1024]{1,0:T(8,128)}, f32[64,1024]{1,0:T(8,128)}, bf16[128,512]{1,0:T(8,128)(2,1)}, bf16[128,512]{1,0:T(8,128)(2,1)}) custom-call(bf16[128,2560]{1,0:T(8,128)(2,1)} %q_ref.1, bf16[128,2560]{1,0:T(8,128)(2,1)} %do_ref.1, bf16[64,1024]{1,0:T(8,128)(2,1)} %copy-done, bf16[64,1024]{1,0:T(8,128)(2,1)} %copy-done.1, ...), custom_call_target="tpu_custom_call" | custom-call | tf_op jit(solution)/shard_map/pallas_call | solution.py:160
  25.4 0.1 collective-permute-start.4
  25.5 1.6 %collective-permute-done.4 = f32[64,1024]{1,0:T(8,128)S(1)} collective-permute-done((f32[64,1024]{1,0:T(8,128)}, f32[64,1024]{1,0:T(8,128)S(1)}, u32[]{:S(2)}, u32[]{:S(2)}) %collective-permute-start.4) | collective-permute-done | bytes 262176 | tf_op jit(solution)/shard_map/ppermute | solution.py:25
  27.1 1.0 %add.50 = f32[64,1024]{1,0:T(8,128)S(1)} add(f32[64,1024]{1,0:T(8,128)} %get-tuple-element.11, f32[64,1024]{1,0:T(8,128)S(1)} %collective-permute-done.4) | non-fusion elementwise | flops 65536 | bytes 786432 | tf_op jit(solution)/shard_map/add | solution.py:51
  28.1 1.6 %collective-permute-start.5 = (f32[32,1024]{1,0:T(8,128)S(1)}, f32[32,1024]{1,0:T(8,128)S(1)}, u32[]{:S(2)}, u32[]{:S(2)}) collective-permute-start(f32[32,1024]{1,0:T(8,128)S(1)} %slice.37), channel_id=1, source_target_pairs={{0,2},{1,3},{2,0},{3,1},{4,6},{5,7},{6,4},{7,5},{8,10},{9,11},{10,... | collective-permute-start | bytes 393224 | tf_op jit(solution)/shard_map/ppermute | solution.py:25
  29.7 4.1 %collective-permute-done.5 = f32[32,1024]{1,0:T(8,128)S(1)} collective-permute-done((f32[32,1024]{1,0:T(8,128)S(1)}, f32[32,1024]{1,0:T(8,128)S(1)}, u32[]{:S(2)}, u32[]{:S(2)}) %collective-permute-start.5) | collective-permute-done | bytes 131104 | tf_op jit(solution)/shard_map/ppermute | solution.py:25
  33.8 1.6 %collective-permute-start.6 = (f32[16,1024]{1,0:T(8,128)S(1)}, f32[16,1024]{1,0:T(8,128)S(1)}, u32[]{:S(2)}, u32[]{:S(2)}) collective-permute-start(f32[16,1024]{1,0:T(8,128)S(1)} %slice.39), channel_id=1, source_target_pairs={{0,4},{1,5},{2,6},{3,7},{4,0},{5,1},{6,2},{7,3},{8,12},{9,13},{10,... | collective-permute-start | bytes 196616 | tf_op jit(solution)/shard_map/ppermute | solution.py:25
  35.4 2.7 %collective-permute-done.6 = f32[16,1024]{1,0:T(8,128)S(1)} collective-permute-done((f32[16,1024]{1,0:T(8,128)S(1)}, f32[16,1024]{1,0:T(8,128)S(1)}, u32[]{:S(2)}, u32[]{:S(2)}) %collective-permute-start.6) | collective-permute-done | bytes 65568 | tf_op jit(solution)/shard_map/ppermute | solution.py:25
  38.1 1.5 %collective-permute-start.7 = (f32[8,1024]{1,0:T(8,128)S(1)}, f32[8,1024]{1,0:T(8,128)S(1)}, u32[]{:S(2)}, u32[]{:S(2)}) collective-permute-start(f32[8,1024]{1,0:T(8,128)S(1)} %slice.41), channel_id=1, source_target_pairs={{0,8},{1,9},{2,10},{3,11},{4,12},{5,13},{6,14},{7,15},{8,0},{9,1},... | collective-permute-start | bytes 98312 | tf_op jit(solution)/shard_map/ppermute | solution.py:25
  39.6 3.4 %collective-permute-done.7 = f32[8,1024]{1,0:T(8,128)S(1)} collective-permute-done((f32[8,1024]{1,0:T(8,128)S(1)}, f32[8,1024]{1,0:T(8,128)S(1)}, u32[]{:S(2)}, u32[]{:S(2)}) %collective-permute-start.7) | collective-permute-done | bytes 32800 | tf_op jit(solution)/shard_map/ppermute | solution.py:25
  43.0 0.6 %fusion.4 = (bf16[8,512]{1,0:T(8,128)(2,1)}, bf16[8,512]{1,0:T(8,128)(2,1)}) fusion(bf16[8,1024]{1,0:T(8,128)(2,1)S(1)} %fusion.2), kind=kLoop, calls=%fused_computation.28 | loop fusion | bytes 32768 | tf_op jit(solution)/shard_map/slice | solution.py:184
  (27 shorter events, 0.2 us)
Async XLA Ops:
  0.6 0.7 %copy-start.2 = (bf16[8,512]{1,0:T(8,128)(2,1)S(1)}, bf16[8,512]{1,0:T(8,128)(2,1)}, u32[]{:S(2)}) copy-start(bf16[8,512]{1,0:T(8,128)(2,1)} %param.14) | copy-start | bytes 24580
  1.4 7.2 %collective-permute-start = (bf16[8,1024]{1,0:T(8,128)(2,1)S(1)}, bf16[8,1024]{1,0:T(8,128)(2,1)S(1)}, u32[]{:S(2)}, u32[]{:S(2)}) collective-permute-start(bf16[8,1024]{1,0:T(8,128)(2,1)S(1)} %constant_dynamic-update-slice_fusion), channel_id=1, source_target_pairs={{0,8},{1,9},{2,10},{3,11},{4,12},{5,13},{6,14},{7,15},{8,0},{9,1},... | collective-permute-start | bytes 49160 | tf_op jit(solution)/shard_map/ppermute | solution.py:25
  5.4 0.7 %copy-start.4 = (s32[128]{0:T(128)S(1)}, s32[128]{0:T(128)}, u32[]{:S(2)}) copy-start(s32[128]{0:T(128)} %constant.71.clone) | copy-start | bytes 1540
  5.4 0.7 %copy-start.5 = (s32[128]{0:T(128)S(1)}, s32[128]{0:T(128)}, u32[]{:S(2)}) copy-start(s32[128]{0:T(128)} %constant.70.clone) | copy-start | bytes 1540
  6.1 0.7 %copy-start.3 = (s32[2,16]{1,0:T(2,128)S(1)}, s32[2,16]{1,0:T(2,128)}, u32[]{:S(2)}) copy-start(s32[2,16]{1,0:T(2,128)} %param.17) | copy-start | bytes 388
  7.7 0.7 %copy-start.6 = (s32[2]{0:T(128)S(1)}, s32[2]{0:T(128)}, u32[]{:S(2)}) copy-start(s32[2]{0:T(128)} %param.16) | copy-start | bytes 28
  8.6 4.0 %collective-permute-start.1 = (bf16[16,1024]{1,0:T(8,128)(2,1)S(1)}, bf16[16,1024]{1,0:T(8,128)(2,1)S(1)}, u32[]{:S(2)}, u32[]{:S(2)}) collective-permute-start(bf16[16,1024]{1,0:T(8,128)(2,1)S(1)} %pad_maximum_fusion.2), channel_id=1, source_target_pairs={{0,4},{1,5},{2,6},{3,7},{4,0},{5,1},{6,2},{7,3},{8,12},{9,13},{10,... | collective-permute-start | bytes 98312 | tf_op jit(solution)/shard_map/ppermute | solution.py:25
  12.5 4.3 %collective-permute-start.2 = (bf16[32,1024]{1,0:T(8,128)(2,1)S(1)}, bf16[32,1024]{1,0:T(8,128)(2,1)S(1)}, u32[]{:S(2)}, u32[]{:S(2)}) collective-permute-start(bf16[32,1024]{1,0:T(8,128)(2,1)S(1)} %pad_maximum_fusion.1), channel_id=1, source_target_pairs={{0,2},{1,3},{2,0},{3,1},{4,6},{5,7},{6,4},{7,5},{8,10},{9,11},{10,... | collective-permute-start | bytes 196616 | tf_op jit(solution)/shard_map/ppermute | solution.py:25
  16.8 1.4 %copy-start = (bf16[64,1024]{1,0:T(8,128)(2,1)}, bf16[64,1024]{1,0:T(8,128)(2,1)S(1)}, u32[]{:S(2)}) copy-start(bf16[64,1024]{1,0:T(8,128)(2,1)S(1)} %pad_maximum_fusion.kva_ref) | copy-start | bytes 393220
  16.8 1.4 %collective-permute-start.3 = (bf16[64,1024]{1,0:T(8,128)(2,1)S(1)}, bf16[64,1024]{1,0:T(8,128)(2,1)S(1)}, u32[]{:S(2)}, u32[]{:S(2)}) collective-permute-start(bf16[64,1024]{1,0:T(8,128)(2,1)S(1)} %pad_maximum_fusion.kva_ref), channel_id=1, source_target_pairs={{0,1},{1,0},{2,3},{3,2},{4,5},{5,4},{6,7},{7,6},{8,9},{9,8},{10,11... | collective-permute-start | bytes 393224 | tf_op jit(solution)/shard_map/ppermute | solution.py:25
  18.2 0.7 %copy-start.1 = (bf16[64,1024]{1,0:T(8,128)(2,1)}, bf16[64,1024]{1,0:T(8,128)(2,1)S(1)}, u32[]{:S(2)}) copy-start(bf16[64,1024]{1,0:T(8,128)(2,1)S(1)} %collective-permute-done.3.kvb_ref) | copy-start | bytes 393220
  25.4 1.7 %collective-permute-start.4 = (f32[64,1024]{1,0:T(8,128)}, f32[64,1024]{1,0:T(8,128)S(1)}, u32[]{:S(2)}, u32[]{:S(2)}) collective-permute-start(f32[64,1024]{1,0:T(8,128)} %get-tuple-element.12), channel_id=1, source_target_pairs={{0,1},{1,0},{2,3},{3,2},{4,5},{5,4},{6,7},{7,6},{8,9},{9,8},{10,11... | collective-permute-start | bytes 786440 | tf_op jit(solution)/shard_map/ppermute | solution.py:25
  28.1 5.6 %collective-permute-start.5 = (f32[32,1024]{1,0:T(8,128)S(1)}, f32[32,1024]{1,0:T(8,128)S(1)}, u32[]{:S(2)}, u32[]{:S(2)}) collective-permute-start(f32[32,1024]{1,0:T(8,128)S(1)} %slice.37), channel_id=1, source_target_pairs={{0,2},{1,3},{2,0},{3,1},{4,6},{5,7},{6,4},{7,5},{8,10},{9,11},{10,... | collective-permute-start | bytes 393224 | tf_op jit(solution)/shard_map/ppermute | solution.py:25
  33.8 4.3 %collective-permute-start.6 = (f32[16,1024]{1,0:T(8,128)S(1)}, f32[16,1024]{1,0:T(8,128)S(1)}, u32[]{:S(2)}, u32[]{:S(2)}) collective-permute-start(f32[16,1024]{1,0:T(8,128)S(1)} %slice.39), channel_id=1, source_target_pairs={{0,4},{1,5},{2,6},{3,7},{4,0},{5,1},{6,2},{7,3},{8,12},{9,13},{10,... | collective-permute-start | bytes 196616 | tf_op jit(solution)/shard_map/ppermute | solution.py:25
  38.1 4.9 %collective-permute-start.7 = (f32[8,1024]{1,0:T(8,128)S(1)}, f32[8,1024]{1,0:T(8,128)S(1)}, u32[]{:S(2)}, u32[]{:S(2)}) collective-permute-start(f32[8,1024]{1,0:T(8,128)S(1)} %slice.41), channel_id=1, source_target_pairs={{0,8},{1,9},{2,10},{3,11},{4,12},{5,13},{6,14},{7,15},{8,0},{9,1},... | collective-permute-start | bytes 98312 | tf_op jit(solution)/shard_map/ppermute | solution.py:25

commit v5 on v4

v5 whole, which is shorter than its diff:
```python
import jax
import numpy as np
import jax.numpy as jnp
from jax import lax
from jax.experimental import pallas as pl
from jax.sharding import PartitionSpec as P

KEY_HEADS = 4
GROUP_HEADS = 5
HEAD_SIZE = 128


masked_score = -1e30


def exchange_bits(size):
    bits = size.bit_length() - 1
    if (1 << bits) != size:
        return None
    return bits


def swap_with(block, axis_name, size, bit):
    pairs = [(index, index ^ (1 << bit)) for index in range(size)]
    return lax.ppermute(block, axis_name, pairs)


def exchange_pattern(size):
    bits = exchange_bits(size)
    return [int(format(spot, "0%db" % bits)[::-1], 2) for spot in range(size)]


def gather_rows(blocks, axis_name):
    size = lax.axis_size(axis_name)
    bits = exchange_bits(size)
    halves = None
    for bit in reversed(range(bits)):
        if halves is not None:
            blocks = jnp.concatenate(halves)
        halves = (blocks, swap_with(blocks, axis_name, size, bit))
    return halves


def scatter_sum_rows(keep, send, axis_name):
    size = lax.axis_size(axis_name)
    bits = exchange_bits(size)
    for bit in range(bits):
        if bit > 0:
            split = keep.shape[0] // 2
            keep, send = keep[:split], keep[split:]
        keep = keep + swap_with(send, axis_name, size, bit)
    return keep


def contract_rows(left, right):
    return lax.dot_general(
        left, right, (((0,), (0,)), ((), ())), preferred_element_type=jnp.float32
    )


def contract_cols(left, right):
    return lax.dot_general(
        left, right, (((1,), (1,)), ((), ())), preferred_element_type=jnp.float32
    )


def stacked_heads(ref, c):
    return jnp.concatenate(
        [
            ref[:, h * HEAD_SIZE:(h + 1) * HEAD_SIZE]
            for h in range(c * GROUP_HEADS, (c + 1) * GROUP_HEADS)
        ],
        axis=0,
    )


def live_rows(owner_ref, within_ref, lengths_ref):
    owner = owner_ref[...]
    limit = jnp.zeros_like(owner)
    for response in range(lengths_ref.shape[1]):
        limit = jnp.where(owner == response, lengths_ref[:, response:response + 1], limit)
    return jnp.concatenate([within_ref[...] < limit] * GROUP_HEADS, axis=0)


def head_columns(c, offset=0):
    return slice(offset + c * HEAD_SIZE, offset + (c + 1) * HEAD_SIZE)


def self_stats_kernel(
    q_ref, do_ref, ks_ref, vs_ref, self_ref, owner_ref, within_ref, lengths_ref, stats_ref
):
    score_scale = HEAD_SIZE ** (-0.5)
    self_seen = jnp.concatenate([self_ref[...]] * GROUP_HEADS, axis=0) > 0.5
    live = live_rows(owner_ref, within_ref, lengths_ref)
    stats_ref[...] = jnp.zeros_like(stats_ref)
    for c in range(KEY_HEADS):
        q = stacked_heads(q_ref, c)
        do = stacked_heads(do_ref, c)
        do = jnp.where(live, do, jnp.zeros_like(do))
        ss = jnp.where(self_seen, contract_cols(q, ks_ref[:, head_columns(c)]) * score_scale, masked_score)
        top = jnp.max(ss, axis=1, keepdims=True)
        es = jnp.where(self_seen, jnp.exp(ss - top), 0.0)
        gs = contract_cols(do, vs_ref[:, head_columns(c)])
        stats_ref[:, c:c + 1] = top
        stats_ref[:, KEY_HEADS + c:KEY_HEADS + c + 1] = jnp.sum(es, axis=1, keepdims=True)
        stats_ref[:, 2 * KEY_HEADS + c:2 * KEY_HEADS + c + 1] = jnp.sum(es * gs, axis=1, keepdims=True)


def document_kernel(
    q_ref, do_ref, kva_ref, kvb_ref, vis_ref, self_stats_ref, owner_ref, within_ref, lengths_ref,
    keep_ref, send_ref, stats_ref, dsd_ref,
):
    width = KEY_HEADS * HEAD_SIZE
    half = kva_ref.shape[0]
    score_scale = HEAD_SIZE ** (-0.5)
    doc_seen = jnp.concatenate([vis_ref[...]] * GROUP_HEADS, axis=0) > 0.5
    live = live_rows(owner_ref, within_ref, lengths_ref)
    stats_ref[...] = jnp.zeros_like(stats_ref)
    for c in range(KEY_HEADS):
        kd = jnp.concatenate([kva_ref[:, head_columns(c)], kvb_ref[:, head_columns(c)]], axis=0)
        vd = jnp.concatenate(
            [kva_ref[:, head_columns(c, width)], kvb_ref[:, head_columns(c, width)]], axis=0
        )
        q = stacked_heads(q_ref, c)
        do = stacked_heads(do_ref, c)
        do = jnp.where(live, do, jnp.zeros_like(do))
        self_top = self_stats_ref[:, c:c + 1]
        self_total = self_stats_ref[:, KEY_HEADS + c:KEY_HEADS + c + 1]
        self_weighted = self_stats_ref[:, 2 * KEY_HEADS + c:2 * KEY_HEADS + c + 1]
        sd = jnp.where(doc_seen, contract_cols(q, kd) * score_scale, masked_score)
        top = jnp.maximum(jnp.max(sd, axis=1, keepdims=True), self_top)
        ed = jnp.where(doc_seen, jnp.exp(sd - top), 0.0)
        factor = jnp.exp(self_top - top)
        gd = contract_cols(do, vd)
        total = jnp.sum(ed, axis=1, keepdims=True) + self_total * factor
        drift = (jnp.sum(ed * gd, axis=1, keepdims=True) + self_weighted * factor) / total
        pd = ed / total
        dsd = (pd * (gd - drift)).astype(jnp.bfloat16)
        dsd_ref[c] = dsd
        stats_ref[:, c:c + 1] = top
        stats_ref[:, KEY_HEADS + c:KEY_HEADS + c + 1] = total
        stats_ref[:, 2 * KEY_HEADS + c:2 * KEY_HEADS + c + 1] = drift
        doc_key = contract_rows(dsd, q) * score_scale
        doc_value = contract_rows(pd.astype(jnp.bfloat16), do)
        keep_ref[:, head_columns(c)] = doc_key[:half]
        send_ref[:, head_columns(c)] = doc_key[half:]
        keep_ref[:, head_columns(c, width)] = doc_value[:half]
        send_ref[:, head_columns(c, width)] = doc_value[half:]


def response_kernel(
    q_ref, do_ref, kva_ref, kvb_ref, ks_ref, vs_ref, stats_ref, dsd_ref, self_ref,
    owner_ref, within_ref, lengths_ref,
    dq_ref, sk_ref, sv_ref,
):
    token_rows = q_ref.shape[0]
    score_scale = HEAD_SIZE ** (-0.5)
    self_seen = jnp.concatenate([self_ref[...]] * GROUP_HEADS, axis=0) > 0.5
    live = live_rows(owner_ref, within_ref, lengths_ref)
    for c in range(KEY_HEADS):
        kd = jnp.concatenate([kva_ref[:, head_columns(c)], kvb_ref[:, head_columns(c)]], axis=0)
        ks = ks_ref[:, head_columns(c)]
        q = stacked_heads(q_ref, c)
        do = stacked_heads(do_ref, c)
        do = jnp.where(live, do, jnp.zeros_like(do))
        top = stats_ref[:, c:c + 1]
        total = stats_ref[:, KEY_HEADS + c:KEY_HEADS + c + 1]
        drift = stats_ref[:, 2 * KEY_HEADS + c:2 * KEY_HEADS + c + 1]
        ss = jnp.where(self_seen, contract_cols(q, ks) * score_scale, masked_score)
        ps = jnp.where(self_seen, jnp.exp(ss - top), 0.0) / total
        gs = contract_cols(do, vs_ref[:, head_columns(c)])
        dss = (ps * (gs - drift)).astype(jnp.bfloat16)
        dq = (
            jnp.dot(dsd_ref[c], kd, preferred_element_type=jnp.float32)
            + jnp.dot(dss, ks, preferred_element_type=jnp.float32)
        ) * score_scale
        for g in range(GROUP_HEADS):
            h = c * GROUP_HEADS + g
            dq_ref[:, h * HEAD_SIZE:(h + 1) * HEAD_SIZE] = dq[
                g * token_rows:(g + 1) * token_rows
            ].astype(dq_ref.dtype)
        sk_ref[:, head_columns(c)] = (contract_rows(dss, q) * score_scale).astype(sk_ref.dtype)
        sv_ref[:, head_columns(c)] = contract_rows(ps.astype(jnp.bfloat16), do).astype(
            sv_ref.dtype
        )


def per_device(
    queries,
    response_keys,
    response_values,
    document_keys,
    document_values,
    grad_out,
    lengths,
    doc_mask,
):
    token_rows = queries.shape[0]
    responses_here = lengths.shape[0]
    resp_len = token_rows // responses_here
    mask_blocks = doc_mask.shape[1]
    key_value_width = KEY_HEADS * HEAD_SIZE
    stacked_rows = GROUP_HEADS * token_rows
    positions = np.arange(token_rows)
    owners = positions // resp_len
    owner_column = jnp.asarray(owners[:, None], jnp.int32)
    within_column = jnp.asarray((positions % resp_len)[:, None], jnp.int32)
    self_visible = jnp.asarray(
        (owners[:, None] == owners[None, :]) & (positions[None, :] <= positions[:, None]),
        jnp.float32,
    )
    lengths_row = lengths.reshape(1, responses_here)
    self_stats = pl.pallas_call(
        self_stats_kernel,
        out_shape=jax.ShapeDtypeStruct((stacked_rows, 128), jnp.float32),
    )(
        queries, grad_out, response_keys, response_values, self_visible,
        owner_column, within_column, lengths_row,
    )
    size = lax.axis_size("resp")
    doc_mine, doc_other = gather_rows(
        jnp.concatenate([document_keys, document_values], axis=1), "resp"
    )
    slab_rows = document_keys.shape[0]
    doc_rows = size * slab_rows
    half_rows = doc_rows // 2
    block_rows = doc_rows // mask_blocks
    holders = jnp.bitwise_xor(
        lax.axis_index("resp"), jnp.asarray(np.repeat(exchange_pattern(size), slab_rows), jnp.int32)
    )
    global_rows = holders * slab_rows + jnp.asarray(np.tile(np.arange(slab_rows), size), jnp.int32)
    row_masks = jnp.repeat(doc_mask, resp_len, axis=0)
    doc_visible = (jnp.take(row_masks, global_rows // block_rows, axis=1) == 1).astype(jnp.float32)
    doc_keep, doc_send, row_stats, doc_dscore = pl.pallas_call(
        document_kernel,
        out_shape=(
            jax.ShapeDtypeStruct((half_rows, 2 * key_value_width), jnp.float32),
            jax.ShapeDtypeStruct((half_rows, 2 * key_value_width), jnp.float32),
            jax.ShapeDtypeStruct((stacked_rows, 128), jnp.float32),
            jax.ShapeDtypeStruct((KEY_HEADS, stacked_rows, doc_rows), jnp.bfloat16),
        ),
    )(
        queries, grad_out, doc_mine, doc_other, doc_visible, self_stats,
        owner_column, within_column, lengths_row,
    )
    summed = scatter_sum_rows(doc_keep, doc_send, "resp")
    query_gradient, self_key, self_value = pl.pallas_call(
        response_kernel,
        out_shape=(
            jax.ShapeDtypeStruct(queries.shape, jnp.bfloat16),
            jax.ShapeDtypeStruct(response_keys.shape, jnp.bfloat16),
            jax.ShapeDtypeStruct(response_values.shape, jnp.bfloat16),
        ),
    )(
        queries, grad_out, doc_mine, doc_other, response_keys, response_values,
        row_stats, doc_dscore, self_visible, owner_column, within_column, lengths_row,
    )
    return (
        query_gradient,
        summed[:, :key_value_width].astype(jnp.bfloat16),
        summed[:, key_value_width:].astype(jnp.bfloat16),
        self_key,
        self_value,
    )


def solution(mesh):
    return jax.shard_map(
        per_device,
        mesh=mesh,
        in_specs=(
            P(("grp", "resp"), None),
            P(("grp", "resp"), None),
            P(("grp", "resp"), None),
            P(("grp", "resp"), None),
            P(("grp", "resp"), None),
            P(("grp", "resp"), None),
            P(("grp", "resp")),
            P(("grp", "resp"), None),
        ),
        out_specs=(
            P(("grp", "resp"), None),
            P(("grp", "resp"), None),
            P(("grp", "resp"), None),
            P(("grp", "resp"), None),
            P(("grp", "resp"), None),
        ),
        check_vma=False,
    )
```

time: 43.9 us -> 47 us (1.071)
  Pallas kernels: 6.47 us -> 15 us
  waiting for transfers between devices: 16.7 us -> 13.9 us
  local copies, waits for them, and re-layouts: 4.61 us -> 2.98 us
  other arithmetic: 3.05 us -> 1.7 us
    pallas_call x1 -> x3, Pallas kernels: 6.47 us -> 15 us  [the longest x1 7.16 us: per_device(): pl.pallas_call(document_kernel, out_shape=(jax.ShapeDtypeStruct((half_row...]
    ppermute x8, waiting for transfers between devices: 16.7 us -> 13.9 us  [swap_with(): return lax.ppermute(block, axis_name, pairs)]
    convert_element_type x2 -> x0, other arithmetic: 1.33 us -> none  [the longest x1 0.71 us: per_device(): self_visible = ((owners[:, None] == owners[None, :]) & (positions[None, :...]
    unnamed x16 -> x14, local copies, waits for them, and re-layouts: 2.79 us -> 1.46 us
  transfers between devices with their start and end apart: 8 -> 8, of which waited for: 7 -> 6; matrix products, arithmetic and copies ran while one was open for 8% -> 3% of each run, Pallas kernels for 0% -> 17%
where the time goes in v5:
time: 47 us; the launch traced here: 46.8 us
  Pallas kernels  15 us (32%)
  waiting for transfers between devices  13.9 us (30%)
  starting transfers between devices  12.5 us (27%)
  local copies, waits for them, and re-layouts  2.98 us (6%)
  other arithmetic  1.7 us (4%)
  between operations  0.73 us (2%)
    ppermute x8, waiting for transfers between devices, swap_with(): return lax.ppermute(block, axis_name, pairs)  13.9 us
    ppermute x8, starting transfers between devices, swap_with(): return lax.ppermute(block, axis_name, pairs)  12.5 us
    pallas_call x1, Pallas kernels, per_device(): pl.pallas_call(document_kernel, out_shape=(jax.ShapeDtypeStruct((half_row...  7.16 us
    pallas_call x1, Pallas kernels, per_device(): pl.pallas_call(response_kernel, out_shape=(jax.ShapeDtypeStruct(queries.s...  4.51 us
    pallas_call x1, Pallas kernels, per_device(): pl.pallas_call(self_stats_kernel, out_shape=jax.ShapeDtypeStruct((stacked...  3.36 us
    unnamed x14, local copies, waits for them, and re-layouts  1.46 us
    add x3, other arithmetic, scatter_sum_rows(): keep = keep + swap_with(send, axis_name, size, bit)  1.02 us
  transfers between devices with their start and end apart: 8, of which 6 were waited for; matrix products, arithmetic and copies ran while one was open for 3% of the time, Pallas kernels for 17%

profile of v5, /device:TPU:0, one launch (start us, length us, event | category | flops | bytes accessed | tf_op | source)
XLA Modules:
  0.0 46.8 jit_solution(3317108498184938023)
XLA Ops:
  0.6 0.0 copy-start.2
  0.6 0.7 %constant_dynamic-update-slice_fusion.1 = bf16[8,1024]{1,0:T(8,128)(2,1)S(1)} fusion(bf16[8,512]{1,0:T(8,128)(2,1)} %param.16), kind=kLoop, calls=%fused_computation.12 | loop fusion | bytes 16384
  1.3 0.0 copy-done.2
  1.4 4.0 %collective-permute-start = (bf16[8,1024]{1,0:T(8,128)(2,1)S(1)}, bf16[8,1024]{1,0:T(8,128)(2,1)S(1)}, u32[]{:S(2)}, u32[]{:S(2)}) collective-permute-start(bf16[8,1024]{1,0:T(8,128)(2,1)S(1)} %constant_dynamic-update-slice_fusion), channel_id=1, source_target_pairs={{0,8},{1,9},{2,10},{3,11},{4,12},{5,13},{6,14},{7,15},{8,0},{9,1},... | collective-permute-start | bytes 49160 | tf_op jit(solution)/shard_map/ppermute | solution.py:25
  5.4 1.7 %collective-permute-done = bf16[8,1024]{1,0:T(8,128)(2,1)S(1)} collective-permute-done((bf16[8,1024]{1,0:T(8,128)(2,1)S(1)}, bf16[8,1024]{1,0:T(8,128)(2,1)S(1)}, u32[]{:S(2)}, u32[]{:S(2)}) %collective-permute-start) | collective-permute-done | bytes 16416 | tf_op jit(solution)/shard_map/ppermute | solution.py:25
  7.1 1.9 %collective-permute-start.1 = (bf16[16,1024]{1,0:T(8,128)(2,1)S(1)}, bf16[16,1024]{1,0:T(8,128)(2,1)S(1)}, u32[]{:S(2)}, u32[]{:S(2)}) collective-permute-start(bf16[16,1024]{1,0:T(8,128)(2,1)S(1)} %pad_maximum_fusion.2), channel_id=1, source_target_pairs={{0,4},{1,5},{2,6},{3,7},{4,0},{5,1},{6,2},{7,3},{8,12},{9,13},{10,... | collective-permute-start | bytes 98312 | tf_op jit(solution)/shard_map/ppermute | solution.py:25
  9.0 0.0 copy-done.4
  9.1 0.1 copy.18
  9.1 0.1 broadcast_in_dim.16
  9.2 0.1 reshape.21
  9.3 1.7 %collective-permute-done.1 = bf16[16,1024]{1,0:T(8,128)(2,1)S(1)} collective-permute-done((bf16[16,1024]{1,0:T(8,128)(2,1)S(1)}, bf16[16,1024]{1,0:T(8,128)(2,1)S(1)}, u32[]{:S(2)}, u32[]{:S(2)}) %collective-permute-start.1) | collective-permute-done | bytes 32800 | tf_op jit(solution)/shard_map/ppermute | solution.py:25
  11.0 1.9 %collective-permute-start.2 = (bf16[32,1024]{1,0:T(8,128)(2,1)S(1)}, bf16[32,1024]{1,0:T(8,128)(2,1)S(1)}, u32[]{:S(2)}, u32[]{:S(2)}) collective-permute-start(bf16[32,1024]{1,0:T(8,128)(2,1)S(1)} %pad_maximum_fusion.1), channel_id=1, source_target_pairs={{0,2},{1,3},{2,0},{3,1},{4,6},{5,7},{6,4},{7,5},{8,10},{9,11},{10,... | collective-permute-start | bytes 196616 | tf_op jit(solution)/shard_map/ppermute | solution.py:25
  12.9 0.6 %gather_fusion = s32[128,128]{1,0:T(8,128)S(1)} fusion(s32[128,16]{0,1:T(8,128)S(1)} %reshape.21, s32[1024]{0:T(1024)S(1)} %pad_clamp_fusion), kind=kCustom, calls=%fused_computation | custom fusion | bytes 131584 | tf_op jit(solution)/shard_map/jit(_take)/gather | solution.py:233
  13.6 0.1 copy.19
  13.7 3.4 %shard_map.164.self_stats_ref = f32[640,128]{1,0:T(8,128)} custom-call(bf16[128,2560]{1,0:T(8,128)(2,1)} %q_ref.5, bf16[128,2560]{1,0:T(8,128)(2,1)} %do_ref.5, bf16[128,512]{1,0:T(8,128)(2,1)} %ks_ref.3, bf16[128,512]{1,0:T(8,128)(2,1)} %vs_ref.3, f32[128,128]{1,0:T(8,128)} %constant.50.clone.self_ref, s32[128,1]{1,0:T(8,128)} %constant.48.clone.owner_ref, ...), custom_call_target="tpu_custom_call" | custom-call | tf_op jit(solution)/shard_map/pallas_call | solution.py:213
  17.0 0.0 collective-permute-done.2
  17.0 0.1 collective-permute-start.3
  17.1 0.6 %convert_bitcast_fusion.vis_ref = f32[128,128]{1,0:T(8,128)} fusion(s32[128,128]{0,1:T(8,128)S(1)} %copy.19, pred[128]{0:T(512)(128)(4,1)S(1)} %get-tuple-element.19), kind=kLoop, calls=%fused_computation.5 | loop fusion | flops 49152 | bytes 131200 | tf_op jit(solution)/shard_map/convert_element_type | solution.py:233
  17.8 0.7 %collective-permute-done.3.kvb_ref = bf16[64,1024]{1,0:T(8,128)(2,1)S(1)} collective-permute-done((bf16[64,1024]{1,0:T(8,128)(2,1)S(1)}, bf16[64,1024]{1,0:T(8,128)(2,1)S(1)}, u32[]{:S(2)}, u32[]{:S(2)}) %collective-permute-start.3) | collective-permute-done | bytes 131104 | tf_op jit(solution)/shard_map/ppermute | solution.py:25
  18.5 0.7 %copy-done.1 = bf16[64,1024]{1,0:T(8,128)(2,1)} copy-done((bf16[64,1024]{1,0:T(8,128)(2,1)}, bf16[64,1024]{1,0:T(8,128)(2,1)S(1)}, u32[]{:S(2)}) %copy-start.1) | copy-done | bytes 131096
  19.1 7.2 %shard_map.165 = (f32[64,1024]{1,0:T(8,128)}, f32[64,1024]{1,0:T(8,128)}, f32[640,128]{1,0:T(8,128)}, bf16[4,640,128]{2,1,0:T(8,128)(2,1)}) custom-call(bf16[128,2560]{1,0:T(8,128)(2,1)} %q_ref.5, bf16[128,2560]{1,0:T(8,128)(2,1)} %do_ref.5, bf16[64,1024]{1,0:T(8,128)(2,1)} %copy-done, bf16[64,1024]{1,0:T(8,128)(2,1)} %copy-done.1, ...), custom_call_target="tpu_custom_call" | custom-call | tf_op jit(solution)/shard_map/pallas_call | solution.py:234
  26.3 0.1 collective-permute-start.4
  26.4 1.6 %collective-permute-done.4 = f32[64,1024]{1,0:T(8,128)S(1)} collective-permute-done((f32[64,1024]{1,0:T(8,128)}, f32[64,1024]{1,0:T(8,128)S(1)}, u32[]{:S(2)}, u32[]{:S(2)}) %collective-permute-start.4) | collective-permute-done | bytes 262176 | tf_op jit(solution)/shard_map/ppermute | solution.py:25
  28.0 1.0 %add.27 = f32[64,1024]{1,0:T(8,128)S(1)} add(f32[64,1024]{1,0:T(8,128)} %get-tuple-element.15, f32[64,1024]{1,0:T(8,128)S(1)} %collective-permute-done.4) | non-fusion elementwise | flops 65536 | bytes 786432 | tf_op jit(solution)/shard_map/add | solution.py:51
  29.0 0.2 collective-permute-start.5
  29.3 5.4 %collective-permute-done.5 = f32[32,1024]{1,0:T(8,128)S(1)} collective-permute-done((f32[32,1024]{1,0:T(8,128)S(1)}, f32[32,1024]{1,0:T(8,128)S(1)}, u32[]{:S(2)}, u32[]{:S(2)}) %collective-permute-start.5) | collective-permute-done | bytes 131104 | tf_op jit(solution)/shard_map/ppermute | solution.py:25
  34.7 1.6 %collective-permute-start.6 = (f32[16,1024]{1,0:T(8,128)S(1)}, f32[16,1024]{1,0:T(8,128)S(1)}, u32[]{:S(2)}, u32[]{:S(2)}) collective-permute-start(f32[16,1024]{1,0:T(8,128)S(1)} %slice.39), channel_id=1, source_target_pairs={{0,4},{1,5},{2,6},{3,7},{4,0},{5,1},{6,2},{7,3},{8,12},{9,13},{10,... | collective-permute-start | bytes 196616 | tf_op jit(solution)/shard_map/ppermute | solution.py:25
  36.3 2.7 %collective-permute-done.6 = f32[16,1024]{1,0:T(8,128)S(1)} collective-permute-done((f32[16,1024]{1,0:T(8,128)S(1)}, f32[16,1024]{1,0:T(8,128)S(1)}, u32[]{:S(2)}, u32[]{:S(2)}) %collective-permute-start.6) | collective-permute-done | bytes 65568 | tf_op jit(solution)/shard_map/ppermute | solution.py:25
  39.0 2.6 %collective-permute-start.7 = (f32[8,1024]{1,0:T(8,128)S(1)}, f32[8,1024]{1,0:T(8,128)S(1)}, u32[]{:S(2)}, u32[]{:S(2)}) collective-permute-start(f32[8,1024]{1,0:T(8,128)S(1)} %slice.41), channel_id=1, source_target_pairs={{0,8},{1,9},{2,10},{3,11},{4,12},{5,13},{6,14},{7,15},{8,0},{9,1},... | collective-permute-start | bytes 98312 | tf_op jit(solution)/shard_map/ppermute | solution.py:25
  41.6 4.5 %shard_map.166 = (bf16[128,2560]{1,0:T(8,128)(2,1)}, bf16[128,512]{1,0:T(8,128)(2,1)}, bf16[128,512]{1,0:T(8,128)(2,1)}) custom-call(bf16[128,2560]{1,0:T(8,128)(2,1)} %q_ref.5, bf16[128,2560]{1,0:T(8,128)(2,1)} %do_ref.5, bf16[64,1024]{1,0:T(8,128)(2,1)} %copy-done, bf16[64,1024]{1,0:T(8,128)(2,1)} %copy-done.1, bf16[128,512]{1,0:T(8,128)(2,1)} %ks_ref.3, ...), custom_call_target="tpu_custom_call" | custom-call | tf_op jit(solution)/shard_map/pallas_call | solution.py:247
  46.2 0.0 collective-permute-done.7
  46.2 0.6 %fusion.1 = (bf16[8,512]{1,0:T(8,128)(2,1)}, bf16[8,512]{1,0:T(8,128)(2,1)}) fusion(bf16[8,1024]{1,0:T(8,128)(2,1)S(1)} %fusion), kind=kLoop, calls=%fused_computation.19 | loop fusion | bytes 32768 | tf_op jit(solution)/shard_map/slice | solution.py:261
  (20 shorter events, 0.1 us)
Async XLA Ops:
  0.6 0.7 %copy-start.2 = (bf16[8,512]{1,0:T(8,128)(2,1)S(1)}, bf16[8,512]{1,0:T(8,128)(2,1)}, u32[]{:S(2)}) copy-start(bf16[8,512]{1,0:T(8,128)(2,1)} %param.17) | copy-start | bytes 24580
  1.4 5.8 %collective-permute-start = (bf16[8,1024]{1,0:T(8,128)(2,1)S(1)}, bf16[8,1024]{1,0:T(8,128)(2,1)S(1)}, u32[]{:S(2)}, u32[]{:S(2)}) collective-permute-start(bf16[8,1024]{1,0:T(8,128)(2,1)S(1)} %constant_dynamic-update-slice_fusion), channel_id=1, source_target_pairs={{0,8},{1,9},{2,10},{3,11},{4,12},{5,13},{6,14},{7,15},{8,0},{9,1},... | collective-permute-start | bytes 49160 | tf_op jit(solution)/shard_map/ppermute | solution.py:25
  5.4 3.6 %copy-start.4 = (s32[128]{0:T(128)S(1)}, s32[128]{0:T(128)}, u32[]{:S(2)}) copy-start(s32[128]{0:T(128)} %constant.51.clone) | copy-start | bytes 1540
  5.4 3.6 %copy-start.5 = (s32[128]{0:T(128)S(1)}, s32[128]{0:T(128)}, u32[]{:S(2)}) copy-start(s32[128]{0:T(128)} %constant.52.clone) | copy-start | bytes 1540
  7.1 1.9 %copy-start.3 = (s32[2,16]{1,0:T(2,128)S(1)}, s32[2,16]{1,0:T(2,128)}, u32[]{:S(2)}) copy-start(s32[2,16]{1,0:T(2,128)} %param.20) | copy-start | bytes 388
  7.1 3.9 %collective-permute-start.1 = (bf16[16,1024]{1,0:T(8,128)(2,1)S(1)}, bf16[16,1024]{1,0:T(8,128)(2,1)S(1)}, u32[]{:S(2)}, u32[]{:S(2)}) collective-permute-start(bf16[16,1024]{1,0:T(8,128)(2,1)S(1)} %pad_maximum_fusion.2), channel_id=1, source_target_pairs={{0,4},{1,5},{2,6},{3,7},{4,0},{5,1},{6,2},{7,3},{8,12},{9,13},{10,... | collective-permute-start | bytes 98312 | tf_op jit(solution)/shard_map/ppermute | solution.py:25
  11.0 6.0 %collective-permute-start.2 = (bf16[32,1024]{1,0:T(8,128)(2,1)S(1)}, bf16[32,1024]{1,0:T(8,128)(2,1)S(1)}, u32[]{:S(2)}, u32[]{:S(2)}) collective-permute-start(bf16[32,1024]{1,0:T(8,128)(2,1)S(1)} %pad_maximum_fusion.1), channel_id=1, source_target_pairs={{0,2},{1,3},{2,0},{3,1},{4,6},{5,7},{6,4},{7,5},{8,10},{9,11},{10,... | collective-permute-start | bytes 196616 | tf_op jit(solution)/shard_map/ppermute | solution.py:25
  17.0 1.4 %copy-start = (bf16[64,1024]{1,0:T(8,128)(2,1)}, bf16[64,1024]{1,0:T(8,128)(2,1)S(1)}, u32[]{:S(2)}) copy-start(bf16[64,1024]{1,0:T(8,128)(2,1)S(1)} %pad_maximum_fusion.kva_ref) | copy-start | bytes 393220
  17.0 1.4 %collective-permute-start.3 = (bf16[64,1024]{1,0:T(8,128)(2,1)S(1)}, bf16[64,1024]{1,0:T(8,128)(2,1)S(1)}, u32[]{:S(2)}, u32[]{:S(2)}) collective-permute-start(bf16[64,1024]{1,0:T(8,128)(2,1)S(1)} %pad_maximum_fusion.kva_ref), channel_id=1, source_target_pairs={{0,1},{1,0},{2,3},{3,2},{4,5},{5,4},{6,7},{7,6},{8,9},{9,8},{10,11... | collective-permute-start | bytes 393224 | tf_op jit(solution)/shard_map/ppermute | solution.py:25
  18.5 0.7 %copy-start.1 = (bf16[64,1024]{1,0:T(8,128)(2,1)}, bf16[64,1024]{1,0:T(8,128)(2,1)S(1)}, u32[]{:S(2)}) copy-start(bf16[64,1024]{1,0:T(8,128)(2,1)S(1)} %collective-permute-done.3.kvb_ref) | copy-start | bytes 393220
  26.3 1.7 %collective-permute-start.4 = (f32[64,1024]{1,0:T(8,128)}, f32[64,1024]{1,0:T(8,128)S(1)}, u32[]{:S(2)}, u32[]{:S(2)}) collective-permute-start(f32[64,1024]{1,0:T(8,128)} %get-tuple-element.16), channel_id=1, source_target_pairs={{0,1},{1,0},{2,3},{3,2},{4,5},{5,4},{6,7},{7,6},{8,9},{9,8},{10,11... | collective-permute-start | bytes 786440 | tf_op jit(solution)/shard_map/ppermute | solution.py:25
  29.0 5.6 %collective-permute-start.5 = (f32[32,1024]{1,0:T(8,128)S(1)}, f32[32,1024]{1,0:T(8,128)S(1)}, u32[]{:S(2)}, u32[]{:S(2)}) collective-permute-start(f32[32,1024]{1,0:T(8,128)S(1)} %slice.37), channel_id=1, source_target_pairs={{0,2},{1,3},{2,0},{3,1},{4,6},{5,7},{6,4},{7,5},{8,10},{9,11},{10,... | collective-permute-start | bytes 393224 | tf_op jit(solution)/shard_map/ppermute | solution.py:25
  34.7 4.3 %collective-permute-start.6 = (f32[16,1024]{1,0:T(8,128)S(1)}, f32[16,1024]{1,0:T(8,128)S(1)}, u32[]{:S(2)}, u32[]{:S(2)}) collective-permute-start(f32[16,1024]{1,0:T(8,128)S(1)} %slice.39), channel_id=1, source_target_pairs={{0,4},{1,5},{2,6},{3,7},{4,0},{5,1},{6,2},{7,3},{8,12},{9,13},{10,... | collective-permute-start | bytes 196616 | tf_op jit(solution)/shard_map/ppermute | solution.py:25
  39.0 7.1 %collective-permute-start.7 = (f32[8,1024]{1,0:T(8,128)S(1)}, f32[8,1024]{1,0:T(8,128)S(1)}, u32[]{:S(2)}, u32[]{:S(2)}) collective-permute-start(f32[8,1024]{1,0:T(8,128)S(1)} %slice.41), channel_id=1, source_target_pairs={{0,8},{1,9},{2,10},{3,11},{4,12},{5,13},{6,14},{7,15},{8,0},{9,1},... | collective-permute-start | bytes 98312 | tf_op jit(solution)/shard_map/ppermute | solution.py:25

commit v6 on v4

--- a/solution.py
+++ b/solution.py
@@ -64,6 +64,16 @@
     )
 
 
+def stacked_heads(ref, c):
+    return jnp.concatenate(
+        [
+            ref[:, h * HEAD_SIZE:(h + 1) * HEAD_SIZE]
+            for h in range(c * GROUP_HEADS, (c + 1) * GROUP_HEADS)
+        ],
+        axis=0,
+    )
+
+
 def attention_kernel(
     q_ref, do_ref, kva_ref, kvb_ref, ks_ref, vs_ref, vis_ref, self_ref, live_ref,
     dq_ref, keep_ref, send_ref, sk_ref, sv_ref,
@@ -72,52 +82,48 @@
     width = KEY_HEADS * HEAD_SIZE
     half = kva_ref.shape[0]
     score_scale = HEAD_SIZE ** (-0.5)
-    doc_seen = jnp.concatenate([vis_ref[...]] * GROUP_HEADS, axis=0) > 0.5
-    self_seen = jnp.concatenate([self_ref[...]] * GROUP_HEADS, axis=0) > 0.5
-    live = jnp.concatenate([live_ref[...]] * GROUP_HEADS, axis=0) > 0.5
+    doc_seen = jnp.concatenate([vis_ref[...]] * GROUP_HEADS, axis=1) > 0.5
+    self_seen = jnp.concatenate([self_ref[...]] * GROUP_HEADS, axis=1) > 0.5
+    live = jnp.concatenate([live_ref[...]] * GROUP_HEADS, axis=1)
     for c in range(KEY_HEADS):
         columns = slice(c * HEAD_SIZE, (c + 1) * HEAD_SIZE)
         value_columns = slice(width + c * HEAD_SIZE, width + (c + 1) * HEAD_SIZE)
         kd = jnp.concatenate([kva_ref[:, columns], kvb_ref[:, columns]], axis=0)
         vd = jnp.concatenate([kva_ref[:, value_columns], kvb_ref[:, value_columns]], axis=0)
-        ks = ks_ref[:, c * HEAD_SIZE:(c + 1) * HEAD_SIZE]
-        vs = vs_ref[:, c * HEAD_SIZE:(c + 1) * HEAD_SIZE]
-        heads = [c * GROUP_HEADS + g for g in range(GROUP_HEADS)]
-        q = jnp.concatenate([q_ref[:, h * HEAD_SIZE:(h + 1) * HEAD_SIZE] for h in heads], axis=0)
-        do = jnp.concatenate([do_ref[:, h * HEAD_SIZE:(h + 1) * HEAD_SIZE] for h in heads], axis=0)
-        do = jnp.where(live, do, jnp.zeros_like(do))
-        sd = jnp.where(doc_seen, contract_cols(q, kd) * score_scale, masked_score)
-        ss = jnp.where(self_seen, contract_cols(q, ks) * score_scale, masked_score)
-        top = jnp.maximum(jnp.max(sd, axis=1, keepdims=True), jnp.max(ss, axis=1, keepdims=True))
+        ks = ks_ref[:, columns]
+        vs = vs_ref[:, columns]
+        q = stacked_heads(q_ref, c)
+        do = stacked_heads(do_ref, c)
+        sd = jnp.where(doc_seen, contract_cols(kd, q) * score_scale, masked_score)
+        ss = jnp.where(self_seen, contract_cols(ks, q) * score_scale, masked_score)
+        top = jnp.maximum(jnp.max(sd, axis=0, keepdims=True), jnp.max(ss, axis=0, keepdims=True))
         ed = jnp.where(doc_seen, jnp.exp(sd - top), 0.0)
         es = jnp.where(self_seen, jnp.exp(ss - top), 0.0)
-        total = jnp.sum(ed, axis=1, keepdims=True) + jnp.sum(es, axis=1, keepdims=True)
+        total = jnp.sum(ed, axis=0, keepdims=True) + jnp.sum(es, axis=0, keepdims=True)
         pd = ed / total
         ps = es / total
-        gd = contract_cols(do, vd)
-        gs = contract_cols(do, vs)
-        drift = jnp.sum(pd * gd, axis=1, keepdims=True) + jnp.sum(ps * gs, axis=1, keepdims=True)
+        gd = contract_cols(vd, do) * live
+        gs = contract_cols(vs, do) * live
+        drift = jnp.sum(pd * gd, axis=0, keepdims=True) + jnp.sum(ps * gs, axis=0, keepdims=True)
         dsd = (pd * (gd - drift)).astype(jnp.bfloat16)
         dss = (ps * (gs - drift)).astype(jnp.bfloat16)
-        dq = (
-            jnp.dot(dsd, kd, preferred_element_type=jnp.float32)
-            + jnp.dot(dss, ks, preferred_element_type=jnp.float32)
-        ) * score_scale
-        for g, h in enumerate(heads):
+        dq = (contract_rows(dsd, kd) + contract_rows(dss, ks)) * score_scale
+        for g in range(GROUP_HEADS):
+            h = c * GROUP_HEADS + g
             dq_ref[:, h * HEAD_SIZE:(h + 1) * HEAD_SIZE] = dq[
                 g * token_rows:(g + 1) * token_rows
             ].astype(dq_ref.dtype)
-        doc_key = contract_rows(dsd, q) * score_scale
-        doc_value = contract_rows(pd.astype(jnp.bfloat16), do)
+        doc_key = jnp.dot(dsd, q, preferred_element_type=jnp.float32) * score_scale
+        doc_value = jnp.dot((pd * live).astype(jnp.bfloat16), do, preferred_element_type=jnp.float32)
         keep_ref[:, columns] = doc_key[:half]
         send_ref[:, columns] = doc_key[half:]
         keep_ref[:, value_columns] = doc_value[:half]
         send_ref[:, value_columns] = doc_value[half:]
-        sk_ref[:, c * HEAD_SIZE:(c + 1) * HEAD_SIZE] = (
-            contract_rows(dss, q) * score_scale
+        sk_ref[:, columns] = (
+            jnp.dot(dss, q, preferred_element_type=jnp.float32) * score_scale
         ).astype(sk_ref.dtype)
-        sv_ref[:, c * HEAD_SIZE:(c + 1) * HEAD_SIZE] = contract_rows(
-            ps.astype(jnp.bfloat16), do
+        sv_ref[:, columns] = jnp.dot(
+            (ps * live).astype(jnp.bfloat16), do, preferred_element_type=jnp.float32
         ).astype(sv_ref.dtype)
 
 
@@ -139,10 +145,13 @@
     positions = jnp.arange(token_rows, dtype=jnp.int32)
     owners = positions // resp_len
     within = positions % resp_len
-    live = (within < jnp.repeat(lengths, resp_len)).astype(jnp.float32)[:, None]
-    self_visible = (
-        (owners[:, None] == owners[None, :]) & (positions[None, :] <= positions[:, None])
-    ).astype(jnp.float32)
+    live = (within < jnp.repeat(lengths, resp_len)).astype(jnp.float32)[None, :]
+    spots = np.arange(token_rows)
+    holders_here = spots // resp_len
+    self_visible = jnp.asarray(
+        (holders_here[:, None] == holders_here[None, :]) & (spots[:, None] <= spots[None, :]),
+        jnp.float32,
+    )
     size = lax.axis_size("resp")
     doc_mine, doc_other = gather_rows(
         jnp.concatenate([document_keys, document_values], axis=1), "resp"
@@ -156,7 +165,9 @@
     )
     global_rows = holders * slab_rows + jnp.asarray(np.tile(np.arange(slab_rows), size), jnp.int32)
     row_masks = jnp.repeat(doc_mask, resp_len, axis=0)
-    doc_visible = (jnp.take(row_masks, global_rows // block_rows, axis=1) == 1).astype(jnp.float32)
+    doc_visible = (jnp.take(row_masks.T, global_rows // block_rows, axis=0) == 1).astype(
+        jnp.float32
+    )
     query_gradient, doc_keep, doc_send, self_key, self_value = pl.pallas_call(
         attention_kernel,
         out_shape=(

time: 43.9 us -> 42 us (0.957)
  waiting for transfers between devices: 16.7 us -> 13.7 us
  starting transfers between devices: 12.1 us -> 14.7 us
  other arithmetic: 3.05 us -> 2.29 us
  Pallas kernels: 6.47 us -> 5.88 us
    ppermute x8, waiting for transfers between devices: 16.7 us -> 13.7 us  [swap_with(): return lax.ppermute(block, axis_name, pairs)]
    ppermute x8, starting transfers between devices: 12.1 us -> 14.7 us  [swap_with(): return lax.ppermute(block, axis_name, pairs)]
    convert_element_type x3 -> x2, other arithmetic: 1.97 us -> 1.23 us  [the longest x1 0.71 us: per_device(): (jnp.take(row_masks.T, global_rows // block_rows, axis=0) == 1).astype(jn...]
    pallas_call x1, Pallas kernels: 6.47 us -> 5.88 us  [per_device(): pl.pallas_call(attention_kernel, out_shape=(jax.ShapeDtypeStruct(queries....]
  transfers between devices with their start and end apart: 8 -> 8, of which waited for: 7 -> 8; matrix products, arithmetic and copies ran while one was open for 8% -> 6% of each run, Pallas kernels for 0% -> 0%
where the time goes in v6:
time: 42 us; the launch traced here: 41.7 us
  starting transfers between devices  14.7 us (35%)
  waiting for transfers between devices  13.7 us (33%)
  Pallas kernels  5.88 us (14%)
  local copies, waits for them, and re-layouts  4.38 us (10%)
  other arithmetic  2.29 us (5%)
  between operations  0.71 us (2%)
    ppermute x8, starting transfers between devices, swap_with(): return lax.ppermute(block, axis_name, pairs)  14.7 us
    ppermute x8, waiting for transfers between devices, swap_with(): return lax.ppermute(block, axis_name, pairs)  13.7 us
    pallas_call x1, Pallas kernels, per_device(): pl.pallas_call(attention_kernel, out_shape=(jax.ShapeDtypeStruct(queries....  5.88 us
    unnamed x16, local copies, waits for them, and re-layouts  2.79 us
    add x3, other arithmetic, scatter_sum_rows(): keep = keep + swap_with(send, axis_name, size, bit)  1.02 us
  transfers between devices with their start and end apart: 8, of which 8 were waited for; matrix products, arithmetic and copies ran while one was open for 6% of the time, Pallas kernels for 0%

profile of v6, /device:TPU:0, one launch (start us, length us, event | category | flops | bytes accessed | tf_op | source)
XLA Modules:
  0.0 41.7 jit_solution(4903429597125333441)
XLA Ops:
  0.6 0.7 %constant_dynamic-update-slice_fusion.1 = bf16[8,1024]{1,0:T(8,128)(2,1)S(1)} fusion(bf16[8,512]{1,0:T(8,128)(2,1)} %param.14), kind=kLoop, calls=%fused_computation.12 | loop fusion | bytes 16384
  1.4 4.0 %collective-permute-start = (bf16[8,1024]{1,0:T(8,128)(2,1)S(1)}, bf16[8,1024]{1,0:T(8,128)(2,1)S(1)}, u32[]{:S(2)}, u32[]{:S(2)}) collective-permute-start(bf16[8,1024]{1,0:T(8,128)(2,1)S(1)} %constant_dynamic-update-slice_fusion), channel_id=1, source_target_pairs={{0,8},{1,9},{2,10},{3,11},{4,12},{5,13},{6,14},{7,15},{8,0},{9,1},... | collective-permute-start | bytes 49160 | tf_op jit(solution)/shard_map/ppermute | solution.py:25
  5.4 0.7 %copy-done.4 = s32[128]{0:T(128)S(1)} copy-done((s32[128]{0:T(128)S(1)}, s32[128]{0:T(128)}, u32[]{:S(2)}) %copy-start.4) | copy-done | bytes 536
  6.0 0.0 copy-done.5
  6.1 1.0 %collective-permute-done = bf16[8,1024]{1,0:T(8,128)(2,1)S(1)} collective-permute-done((bf16[8,1024]{1,0:T(8,128)(2,1)S(1)}, bf16[8,1024]{1,0:T(8,128)(2,1)S(1)}, u32[]{:S(2)}, u32[]{:S(2)}) %collective-permute-start) | collective-permute-done | bytes 16416 | tf_op jit(solution)/shard_map/ppermute | solution.py:25
  7.1 1.9 %collective-permute-start.1 = (bf16[16,1024]{1,0:T(8,128)(2,1)S(1)}, bf16[16,1024]{1,0:T(8,128)(2,1)S(1)}, u32[]{:S(2)}, u32[]{:S(2)}) collective-permute-start(bf16[16,1024]{1,0:T(8,128)(2,1)S(1)} %pad_maximum_fusion.2), channel_id=1, source_target_pairs={{0,4},{1,5},{2,6},{3,7},{4,0},{5,1},{6,2},{7,3},{8,12},{9,13},{10,... | collective-permute-start | bytes 98312 | tf_op jit(solution)/shard_map/ppermute | solution.py:25
  9.0 0.7 %copy-done.3 = s32[2,16]{1,0:T(2,128)S(1)} copy-done((s32[2,16]{1,0:T(2,128)S(1)}, s32[2,16]{1,0:T(2,128)}, u32[]{:S(2)}) %copy-start.3) | copy-done | bytes 152
  9.7 0.1 copy.16
  9.8 0.1 broadcast_in_dim.20
  9.9 0.1 reshape.56
  9.9 0.6 %gather_fusion = s32[128,128]{1,0:T(8,128)S(1)} fusion(s32[16,128]{1,0:T(8,128)S(1)} %bitcast.3, s32[1024]{0:T(1024)S(1)} %pad_clamp_fusion), kind=kCustom, calls=%fused_computation | custom fusion | bytes 131584 | tf_op jit(solution)/shard_map/jit(_take)/gather | solution.py:168
  10.6 0.4 %collective-permute-done.1 = bf16[16,1024]{1,0:T(8,128)(2,1)S(1)} collective-permute-done((bf16[16,1024]{1,0:T(8,128)(2,1)S(1)}, bf16[16,1024]{1,0:T(8,128)(2,1)S(1)}, u32[]{:S(2)}, u32[]{:S(2)}) %collective-permute-start.1) | collective-permute-done | bytes 32800 | tf_op jit(solution)/shard_map/ppermute | solution.py:25
  11.0 1.9 %collective-permute-start.2 = (bf16[32,1024]{1,0:T(8,128)(2,1)S(1)}, bf16[32,1024]{1,0:T(8,128)(2,1)S(1)}, u32[]{:S(2)}, u32[]{:S(2)}) collective-permute-start(bf16[32,1024]{1,0:T(8,128)(2,1)S(1)} %pad_maximum_fusion.1), channel_id=1, source_target_pairs={{0,2},{1,3},{2,0},{3,1},{4,6},{5,7},{6,4},{7,5},{8,10},{9,11},{10,... | collective-permute-start | bytes 196616 | tf_op jit(solution)/shard_map/ppermute | solution.py:25
  12.9 0.7 %fusion.vis_ref = f32[128,128]{1,0:T(8,128)} fusion(s32[128,128]{1,0:T(8,128)S(1)} %gather_fusion, pred[128]{0:T(512)(128)(4,1)S(1)} %get-tuple-element.15), kind=kLoop, calls=%fused_computation.6 | loop fusion | flops 49152 | bytes 131200 | tf_op jit(solution)/shard_map/convert_element_type | solution.py:168
  13.6 0.1 broadcast_in_dim.23
  13.7 0.1 reshape.57
  13.8 1.5 %collective-permute-done.2 = bf16[32,1024]{1,0:T(8,128)(2,1)S(1)} collective-permute-done((bf16[32,1024]{1,0:T(8,128)(2,1)S(1)}, bf16[32,1024]{1,0:T(8,128)(2,1)S(1)}, u32[]{:S(2)}, u32[]{:S(2)}) %collective-permute-start.2) | collective-permute-done | bytes 65568 | tf_op jit(solution)/shard_map/ppermute | solution.py:25
  15.3 0.1 collective-permute-start.3
  15.4 0.5 %compare_convert_fusion.live_ref = f32[1,128]{1,0:T(1,128)} fusion(s32[1,128]{1,0:T(1,128)S(1)} %reshape.57), kind=kLoop, calls=%fused_computation.14 | loop fusion | flops 1024 | bytes 1024 | tf_op jit(solution)/shard_map/convert_element_type | solution.py:148
  15.9 0.8 %collective-permute-done.3.kvb_ref = bf16[64,1024]{1,0:T(8,128)(2,1)S(1)} collective-permute-done((bf16[64,1024]{1,0:T(8,128)(2,1)S(1)}, bf16[64,1024]{1,0:T(8,128)(2,1)S(1)}, u32[]{:S(2)}, u32[]{:S(2)}) %collective-permute-start.3) | collective-permute-done | bytes 131104 | tf_op jit(solution)/shard_map/ppermute | solution.py:25
  16.7 0.7 %copy-done.1 = bf16[64,1024]{1,0:T(8,128)(2,1)} copy-done((bf16[64,1024]{1,0:T(8,128)(2,1)}, bf16[64,1024]{1,0:T(8,128)(2,1)S(1)}, u32[]{:S(2)}) %copy-start.1) | copy-done | bytes 131096
  17.4 5.9 %shard_map.146 = (bf16[128,2560]{1,0:T(8,128)(2,1)}, f32[64,1024]{1,0:T(8,128)}, f32[64,1024]{1,0:T(8,128)}, bf16[128,512]{1,0:T(8,128)(2,1)}, bf16[128,512]{1,0:T(8,128)(2,1)}) custom-call(bf16[128,2560]{1,0:T(8,128)(2,1)} %q_ref.1, bf16[128,2560]{1,0:T(8,128)(2,1)} %do_ref.1, bf16[64,1024]{1,0:T(8,128)(2,1)} %copy-done, bf16[64,1024]{1,0:T(8,128)(2,1)} %copy-done.1, ...), custom_call_target="tpu_custom_call" | custom-call | tf_op jit(solution)/shard_map/pallas_call | solution.py:171
  23.3 0.1 collective-permute-start.4
  23.4 1.6 %collective-permute-done.4 = f32[64,1024]{1,0:T(8,128)S(1)} collective-permute-done((f32[64,1024]{1,0:T(8,128)}, f32[64,1024]{1,0:T(8,128)S(1)}, u32[]{:S(2)}, u32[]{:S(2)}) %collective-permute-start.4) | collective-permute-done | bytes 262176 | tf_op jit(solution)/shard_map/ppermute | solution.py:25
  25.0 1.0 %add.41 = f32[64,1024]{1,0:T(8,128)S(1)} add(f32[64,1024]{1,0:T(8,128)} %get-tuple-element.11, f32[64,1024]{1,0:T(8,128)S(1)} %collective-permute-done.4) | non-fusion elementwise | flops 65536 | bytes 786432 | tf_op jit(solution)/shard_map/add | solution.py:51
  26.0 1.9 %collective-permute-start.5 = (f32[32,1024]{1,0:T(8,128)S(1)}, f32[32,1024]{1,0:T(8,128)S(1)}, u32[]{:S(2)}, u32[]{:S(2)}) collective-permute-start(f32[32,1024]{1,0:T(8,128)S(1)} %slice.37), channel_id=1, source_target_pairs={{0,2},{1,3},{2,0},{3,1},{4,6},{5,7},{6,4},{7,5},{8,10},{9,11},{10,... | collective-permute-start | bytes 393224 | tf_op jit(solution)/shard_map/ppermute | solution.py:25
  28.0 3.8 %collective-permute-done.5 = f32[32,1024]{1,0:T(8,128)S(1)} collective-permute-done((f32[32,1024]{1,0:T(8,128)S(1)}, f32[32,1024]{1,0:T(8,128)S(1)}, u32[]{:S(2)}, u32[]{:S(2)}) %collective-permute-start.5) | collective-permute-done | bytes 131104 | tf_op jit(solution)/shard_map/ppermute | solution.py:25
  31.8 1.8 %collective-permute-start.6 = (f32[16,1024]{1,0:T(8,128)S(1)}, f32[16,1024]{1,0:T(8,128)S(1)}, u32[]{:S(2)}, u32[]{:S(2)}) collective-permute-start(f32[16,1024]{1,0:T(8,128)S(1)} %slice.39), channel_id=1, source_target_pairs={{0,4},{1,5},{2,6},{3,7},{4,0},{5,1},{6,2},{7,3},{8,12},{9,13},{10,... | collective-permute-start | bytes 196616 | tf_op jit(solution)/shard_map/ppermute | solution.py:25
  33.6 2.5 %collective-permute-done.6 = f32[16,1024]{1,0:T(8,128)S(1)} collective-permute-done((f32[16,1024]{1,0:T(8,128)S(1)}, f32[16,1024]{1,0:T(8,128)S(1)}, u32[]{:S(2)}, u32[]{:S(2)}) %collective-permute-start.6) | collective-permute-done | bytes 65568 | tf_op jit(solution)/shard_map/ppermute | solution.py:25
  36.2 2.9 %collective-permute-start.7 = (f32[8,1024]{1,0:T(8,128)S(1)}, f32[8,1024]{1,0:T(8,128)S(1)}, u32[]{:S(2)}, u32[]{:S(2)}) collective-permute-start(f32[8,1024]{1,0:T(8,128)S(1)} %slice.41), channel_id=1, source_target_pairs={{0,8},{1,9},{2,10},{3,11},{4,12},{5,13},{6,14},{7,15},{8,0},{9,1},... | collective-permute-start | bytes 98312 | tf_op jit(solution)/shard_map/ppermute | solution.py:25
  39.0 2.0 %collective-permute-done.7 = f32[8,1024]{1,0:T(8,128)S(1)} collective-permute-done((f32[8,1024]{1,0:T(8,128)S(1)}, f32[8,1024]{1,0:T(8,128)S(1)}, u32[]{:S(2)}, u32[]{:S(2)}) %collective-permute-start.7) | collective-permute-done | bytes 32800 | tf_op jit(solution)/shard_map/ppermute | solution.py:25
  41.0 0.6 %fusion.2 = (bf16[8,512]{1,0:T(8,128)(2,1)}, bf16[8,512]{1,0:T(8,128)(2,1)}) fusion(bf16[8,1024]{1,0:T(8,128)(2,1)S(1)} %fusion.1), kind=kLoop, calls=%fused_computation.21 | loop fusion | bytes 32768 | tf_op jit(solution)/shard_map/slice | solution.py:195
  (22 shorter events, 0.1 us)
Async XLA Ops:
  0.6 0.7 %copy-start.2 = (bf16[8,512]{1,0:T(8,128)(2,1)S(1)}, bf16[8,512]{1,0:T(8,128)(2,1)}, u32[]{:S(2)}) copy-start(bf16[8,512]{1,0:T(8,128)(2,1)} %param.15) | copy-start | bytes 24580
  1.4 5.8 %collective-permute-start = (bf16[8,1024]{1,0:T(8,128)(2,1)S(1)}, bf16[8,1024]{1,0:T(8,128)(2,1)S(1)}, u32[]{:S(2)}, u32[]{:S(2)}) collective-permute-start(bf16[8,1024]{1,0:T(8,128)(2,1)S(1)} %constant_dynamic-update-slice_fusion), channel_id=1, source_target_pairs={{0,8},{1,9},{2,10},{3,11},{4,12},{5,13},{6,14},{7,15},{8,0},{9,1},... | collective-permute-start | bytes 49160 | tf_op jit(solution)/shard_map/ppermute | solution.py:25
  5.4 0.7 %copy-start.4 = (s32[128]{0:T(128)S(1)}, s32[128]{0:T(128)}, u32[]{:S(2)}) copy-start(s32[128]{0:T(128)} %constant.61.clone) | copy-start | bytes 1540
  5.4 0.7 %copy-start.5 = (s32[128]{0:T(128)S(1)}, s32[128]{0:T(128)}, u32[]{:S(2)}) copy-start(s32[128]{0:T(128)} %constant.60.clone) | copy-start | bytes 1540
  7.1 3.9 %collective-permute-start.1 = (bf16[16,1024]{1,0:T(8,128)(2,1)S(1)}, bf16[16,1024]{1,0:T(8,128)(2,1)S(1)}, u32[]{:S(2)}, u32[]{:S(2)}) collective-permute-start(bf16[16,1024]{1,0:T(8,128)(2,1)S(1)} %pad_maximum_fusion.2), channel_id=1, source_target_pairs={{0,4},{1,5},{2,6},{3,7},{4,0},{5,1},{6,2},{7,3},{8,12},{9,13},{10,... | collective-permute-start | bytes 98312 | tf_op jit(solution)/shard_map/ppermute | solution.py:25
  9.0 0.7 %copy-start.3 = (s32[2,16]{1,0:T(2,128)S(1)}, s32[2,16]{1,0:T(2,128)}, u32[]{:S(2)}) copy-start(s32[2,16]{1,0:T(2,128)} %param.18) | copy-start | bytes 388
  11.0 4.3 %collective-permute-start.2 = (bf16[32,1024]{1,0:T(8,128)(2,1)S(1)}, bf16[32,1024]{1,0:T(8,128)(2,1)S(1)}, u32[]{:S(2)}, u32[]{:S(2)}) collective-permute-start(bf16[32,1024]{1,0:T(8,128)(2,1)S(1)} %pad_maximum_fusion.1), channel_id=1, source_target_pairs={{0,2},{1,3},{2,0},{3,1},{4,6},{5,7},{6,4},{7,5},{8,10},{9,11},{10,... | collective-permute-start | bytes 196616 | tf_op jit(solution)/shard_map/ppermute | solution.py:25
  12.9 0.7 %copy-start.6 = (s32[2]{0:T(128)S(1)}, s32[2]{0:T(128)}, u32[]{:S(2)}) copy-start(s32[2]{0:T(128)} %param.17) | copy-start | bytes 28
  15.3 1.4 %copy-start = (bf16[64,1024]{1,0:T(8,128)(2,1)}, bf16[64,1024]{1,0:T(8,128)(2,1)S(1)}, u32[]{:S(2)}) copy-start(bf16[64,1024]{1,0:T(8,128)(2,1)S(1)} %pad_maximum_fusion.kva_ref) | copy-start | bytes 393220
  15.3 1.4 %collective-permute-start.3 = (bf16[64,1024]{1,0:T(8,128)(2,1)S(1)}, bf16[64,1024]{1,0:T(8,128)(2,1)S(1)}, u32[]{:S(2)}, u32[]{:S(2)}) collective-permute-start(bf16[64,1024]{1,0:T(8,128)(2,1)S(1)} %pad_maximum_fusion.kva_ref), channel_id=1, source_target_pairs={{0,1},{1,0},{2,3},{3,2},{4,5},{5,4},{6,7},{7,6},{8,9},{9,8},{10,11... | collective-permute-start | bytes 393224 | tf_op jit(solution)/shard_map/ppermute | solution.py:25
  16.7 0.7 %copy-start.1 = (bf16[64,1024]{1,0:T(8,128)(2,1)}, bf16[64,1024]{1,0:T(8,128)(2,1)S(1)}, u32[]{:S(2)}) copy-start(bf16[64,1024]{1,0:T(8,128)(2,1)S(1)} %collective-permute-done.3.kvb_ref) | copy-start | bytes 393220
  23.3 1.7 %collective-permute-start.4 = (f32[64,1024]{1,0:T(8,128)}, f32[64,1024]{1,0:T(8,128)S(1)}, u32[]{:S(2)}, u32[]{:S(2)}) collective-permute-start(f32[64,1024]{1,0:T(8,128)} %get-tuple-element.12), channel_id=1, source_target_pairs={{0,1},{1,0},{2,3},{3,2},{4,5},{5,4},{6,7},{7,6},{8,9},{9,8},{10,11... | collective-permute-start | bytes 786440 | tf_op jit(solution)/shard_map/ppermute | solution.py:25
  26.0 5.8 %collective-permute-start.5 = (f32[32,1024]{1,0:T(8,128)S(1)}, f32[32,1024]{1,0:T(8,128)S(1)}, u32[]{:S(2)}, u32[]{:S(2)}) collective-permute-start(f32[32,1024]{1,0:T(8,128)S(1)} %slice.37), channel_id=1, source_target_pairs={{0,2},{1,3},{2,0},{3,1},{4,6},{5,7},{6,4},{7,5},{8,10},{9,11},{10,... | collective-permute-start | bytes 393224 | tf_op jit(solution)/shard_map/ppermute | solution.py:25
  31.8 4.3 %collective-permute-start.6 = (f32[16,1024]{1,0:T(8,128)S(1)}, f32[16,1024]{1,0:T(8,128)S(1)}, u32[]{:S(2)}, u32[]{:S(2)}) collective-permute-start(f32[16,1024]{1,0:T(8,128)S(1)} %slice.39), channel_id=1, source_target_pairs={{0,4},{1,5},{2,6},{3,7},{4,0},{5,1},{6,2},{7,3},{8,12},{9,13},{10,... | collective-permute-start | bytes 196616 | tf_op jit(solution)/shard_map/ppermute | solution.py:25
  36.2 4.9 %collective-permute-start.7 = (f32[8,1024]{1,0:T(8,128)S(1)}, f32[8,1024]{1,0:T(8,128)S(1)}, u32[]{:S(2)}, u32[]{:S(2)}) collective-permute-start(f32[8,1024]{1,0:T(8,128)S(1)} %slice.41), channel_id=1, source_target_pairs={{0,8},{1,9},{2,10},{3,11},{4,12},{5,13},{6,14},{7,15},{8,0},{9,1},... | collective-permute-start | bytes 98312 | tf_op jit(solution)/shard_map/ppermute | solution.py:25

commit v7 on v6

--- a/solution.py
+++ b/solution.py
@@ -44,12 +44,15 @@
 def scatter_sum_rows(keep, send, axis_name):
     size = lax.axis_size(axis_name)
     bits = exchange_bits(size)
+    pending = [keep]
     for bit in range(bits):
         if bit > 0:
-            split = keep.shape[0] // 2
-            keep, send = keep[:split], keep[split:]
-        keep = keep + swap_with(send, axis_name, size, bit)
-    return keep
+            split = pending[0].shape[0] // 2
+            send = sum(part[split:] for part in pending[1:])
+            send = pending[0][split:] + send
+            pending = [part[:split] for part in pending]
+        pending.append(swap_with(send, axis_name, size, bit))
+    return sum(pending[1:], pending[0])
 
 
 def contract_rows(left, right):
@@ -97,13 +100,14 @@
         sd = jnp.where(doc_seen, contract_cols(kd, q) * score_scale, masked_score)
         ss = jnp.where(self_seen, contract_cols(ks, q) * score_scale, masked_score)
         top = jnp.maximum(jnp.max(sd, axis=0, keepdims=True), jnp.max(ss, axis=0, keepdims=True))
-        ed = jnp.where(doc_seen, jnp.exp(sd - top), 0.0)
-        es = jnp.where(self_seen, jnp.exp(ss - top), 0.0)
+        ed = jnp.exp(sd - top)
+        es = jnp.exp(ss - top)
         total = jnp.sum(ed, axis=0, keepdims=True) + jnp.sum(es, axis=0, keepdims=True)
-        pd = ed / total
-        ps = es / total
-        gd = contract_cols(vd, do) * live
-        gs = contract_cols(vs, do) * live
+        weight = live / total
+        pd = ed * weight
+        ps = es * weight
+        gd = contract_cols(vd, do)
+        gs = contract_cols(vs, do)
         drift = jnp.sum(pd * gd, axis=0, keepdims=True) + jnp.sum(ps * gs, axis=0, keepdims=True)
         dsd = (pd * (gd - drift)).astype(jnp.bfloat16)
         dss = (ps * (gs - drift)).astype(jnp.bfloat16)
@@ -114,7 +118,7 @@
                 g * token_rows:(g + 1) * token_rows
             ].astype(dq_ref.dtype)
         doc_key = jnp.dot(dsd, q, preferred_element_type=jnp.float32) * score_scale
-        doc_value = jnp.dot((pd * live).astype(jnp.bfloat16), do, preferred_element_type=jnp.float32)
+        doc_value = jnp.dot(pd.astype(jnp.bfloat16), do, preferred_element_type=jnp.float32)
         keep_ref[:, columns] = doc_key[:half]
         send_ref[:, columns] = doc_key[half:]
         keep_ref[:, value_columns] = doc_value[:half]
@@ -123,7 +127,7 @@
             jnp.dot(dss, q, preferred_element_type=jnp.float32) * score_scale
         ).astype(sk_ref.dtype)
         sv_ref[:, columns] = jnp.dot(
-            (ps * live).astype(jnp.bfloat16), do, preferred_element_type=jnp.float32
+            ps.astype(jnp.bfloat16), do, preferred_element_type=jnp.float32
         ).astype(sv_ref.dtype)
 
 

time: 42 us -> 41.6 us (level)
    unnamed x16 -> x18, local copies, waits for them, and re-layouts: 2.79 us -> 2.81 us
where the time goes in v7:
time: 41.6 us; the launch traced here: 41.3 us
  starting transfers between devices  14.7 us (35%)
  waiting for transfers between devices  13.7 us (33%)
  Pallas kernels  5.61 us (13%)
  local copies, waits for them, and re-layouts  4.38 us (11%)
  other arithmetic  2.22 us (5%)
  between operations  0.69 us (2%)
    ppermute x8, starting transfers between devices, swap_with(): return lax.ppermute(block, axis_name, pairs)  14.7 us
    ppermute x8, waiting for transfers between devices, swap_with(): return lax.ppermute(block, axis_name, pairs)  13.7 us
    pallas_call x1, Pallas kernels, per_device(): pl.pallas_call(attention_kernel, out_shape=(jax.ShapeDtypeStruct(queries....  5.61 us
    unnamed x18, local copies, waits for them, and re-layouts  2.81 us
    add x3, other arithmetic, scatter_sum_rows(): send = pending[0][split:] + send  0.95 us
  transfers between devices with their start and end apart: 8, of which 8 were waited for; matrix products, arithmetic and copies ran while one was open for 6% of the time, Pallas kernels for 0%

profile of v7, /device:TPU:0, one launch (start us, length us, event | category | flops | bytes accessed | tf_op | source)
XLA Modules:
  0.0 41.3 jit_solution(8203861594375852405)
XLA Ops:
  0.6 0.7 %constant_dynamic-update-slice_fusion.1 = bf16[8,1024]{1,0:T(8,128)(2,1)S(1)} fusion(bf16[8,512]{1,0:T(8,128)(2,1)} %param.14), kind=kLoop, calls=%fused_computation.19 | loop fusion | bytes 16384
  1.4 4.0 %collective-permute-start = (bf16[8,1024]{1,0:T(8,128)(2,1)S(1)}, bf16[8,1024]{1,0:T(8,128)(2,1)S(1)}, u32[]{:S(2)}, u32[]{:S(2)}) collective-permute-start(bf16[8,1024]{1,0:T(8,128)(2,1)S(1)} %constant_dynamic-update-slice_fusion), channel_id=1, source_target_pairs={{0,8},{1,9},{2,10},{3,11},{4,12},{5,13},{6,14},{7,15},{8,0},{9,1},... | collective-permute-start | bytes 49160 | tf_op jit(solution)/shard_map/ppermute | solution.py:25
  5.4 0.7 %copy-done.5 = s32[128]{0:T(128)S(1)} copy-done((s32[128]{0:T(128)S(1)}, s32[128]{0:T(128)}, u32[]{:S(2)}) %copy-start.5) | copy-done | bytes 536
  6.0 0.0 copy-done.6
  6.1 1.0 %collective-permute-done = bf16[8,1024]{1,0:T(8,128)(2,1)S(1)} collective-permute-done((bf16[8,1024]{1,0:T(8,128)(2,1)S(1)}, bf16[8,1024]{1,0:T(8,128)(2,1)S(1)}, u32[]{:S(2)}, u32[]{:S(2)}) %collective-permute-start) | collective-permute-done | bytes 16416 | tf_op jit(solution)/shard_map/ppermute | solution.py:25
  7.1 1.9 %collective-permute-start.1 = (bf16[16,1024]{1,0:T(8,128)(2,1)S(1)}, bf16[16,1024]{1,0:T(8,128)(2,1)S(1)}, u32[]{:S(2)}, u32[]{:S(2)}) collective-permute-start(bf16[16,1024]{1,0:T(8,128)(2,1)S(1)} %pad_maximum_fusion.2), channel_id=1, source_target_pairs={{0,4},{1,5},{2,6},{3,7},{4,0},{5,1},{6,2},{7,3},{8,12},{9,13},{10,... | collective-permute-start | bytes 98312 | tf_op jit(solution)/shard_map/ppermute | solution.py:25
  9.0 0.7 %copy-done.4 = s32[2,16]{1,0:T(2,128)S(1)} copy-done((s32[2,16]{1,0:T(2,128)S(1)}, s32[2,16]{1,0:T(2,128)}, u32[]{:S(2)}) %copy-start.4) | copy-done | bytes 152
  9.7 0.1 copy.16
  9.8 0.1 broadcast_in_dim.20
  9.9 0.1 reshape.56
  9.9 0.6 %gather_fusion = s32[128,128]{1,0:T(8,128)S(1)} fusion(s32[16,128]{1,0:T(8,128)S(1)} %bitcast.3, s32[1024]{0:T(1024)S(1)} %pad_clamp_fusion), kind=kCustom, calls=%fused_computation | custom fusion | bytes 131584 | tf_op jit(solution)/shard_map/jit(_take)/gather | solution.py:172
  10.6 0.4 %collective-permute-done.1 = bf16[16,1024]{1,0:T(8,128)(2,1)S(1)} collective-permute-done((bf16[16,1024]{1,0:T(8,128)(2,1)S(1)}, bf16[16,1024]{1,0:T(8,128)(2,1)S(1)}, u32[]{:S(2)}, u32[]{:S(2)}) %collective-permute-start.1) | collective-permute-done | bytes 32800 | tf_op jit(solution)/shard_map/ppermute | solution.py:25
  11.0 1.9 %collective-permute-start.2 = (bf16[32,1024]{1,0:T(8,128)(2,1)S(1)}, bf16[32,1024]{1,0:T(8,128)(2,1)S(1)}, u32[]{:S(2)}, u32[]{:S(2)}) collective-permute-start(bf16[32,1024]{1,0:T(8,128)(2,1)S(1)} %pad_maximum_fusion.1), channel_id=1, source_target_pairs={{0,2},{1,3},{2,0},{3,1},{4,6},{5,7},{6,4},{7,5},{8,10},{9,11},{10,... | collective-permute-start | bytes 196616 | tf_op jit(solution)/shard_map/ppermute | solution.py:25
  12.9 0.7 %fusion.1.vis_ref = f32[128,128]{1,0:T(8,128)} fusion(s32[128,128]{1,0:T(8,128)S(1)} %gather_fusion, pred[128]{0:T(512)(128)(4,1)S(1)} %get-tuple-element.15), kind=kLoop, calls=%fused_computation.7 | loop fusion | flops 49152 | bytes 131200 | tf_op jit(solution)/shard_map/convert_element_type | solution.py:172
  13.6 0.1 broadcast_in_dim.23
  13.7 0.1 reshape.57
  13.8 1.5 %collective-permute-done.2 = bf16[32,1024]{1,0:T(8,128)(2,1)S(1)} collective-permute-done((bf16[32,1024]{1,0:T(8,128)(2,1)S(1)}, bf16[32,1024]{1,0:T(8,128)(2,1)S(1)}, u32[]{:S(2)}, u32[]{:S(2)}) %collective-permute-start.2) | collective-permute-done | bytes 65568 | tf_op jit(solution)/shard_map/ppermute | solution.py:25
  15.3 0.1 collective-permute-start.3
  15.4 0.5 %compare_convert_fusion.live_ref = f32[1,128]{1,0:T(1,128)} fusion(s32[1,128]{1,0:T(1,128)S(1)} %reshape.57), kind=kLoop, calls=%fused_computation.21 | loop fusion | flops 1024 | bytes 1024 | tf_op jit(solution)/shard_map/convert_element_type | solution.py:152
  15.9 0.8 %collective-permute-done.3.kvb_ref = bf16[64,1024]{1,0:T(8,128)(2,1)S(1)} collective-permute-done((bf16[64,1024]{1,0:T(8,128)(2,1)S(1)}, bf16[64,1024]{1,0:T(8,128)(2,1)S(1)}, u32[]{:S(2)}, u32[]{:S(2)}) %collective-permute-start.3) | collective-permute-done | bytes 131104 | tf_op jit(solution)/shard_map/ppermute | solution.py:25
  16.7 0.7 %copy-done.2 = bf16[64,1024]{1,0:T(8,128)(2,1)} copy-done((bf16[64,1024]{1,0:T(8,128)(2,1)}, bf16[64,1024]{1,0:T(8,128)(2,1)S(1)}, u32[]{:S(2)}) %copy-start.2) | copy-done | bytes 131096
  17.4 5.6 %shard_map.146 = (bf16[128,2560]{1,0:T(8,128)(2,1)}, f32[64,1024]{1,0:T(8,128)}, f32[64,1024]{1,0:T(8,128)}, bf16[128,512]{1,0:T(8,128)(2,1)}, bf16[128,512]{1,0:T(8,128)(2,1)}) custom-call(bf16[128,2560]{1,0:T(8,128)(2,1)} %q_ref.1, bf16[128,2560]{1,0:T(8,128)(2,1)} %do_ref.1, bf16[64,1024]{1,0:T(8,128)(2,1)} %copy-done, bf16[64,1024]{1,0:T(8,128)(2,1)} %copy-done.2, ...), custom_call_target="tpu_custom_call" | custom-call | tf_op jit(solution)/shard_map/pallas_call | solution.py:175
  23.0 0.1 collective-permute-start.4
  23.2 1.6 %collective-permute-done.4 = f32[64,1024]{1,0:T(8,128)S(1)} collective-permute-done((f32[64,1024]{1,0:T(8,128)}, f32[64,1024]{1,0:T(8,128)S(1)}, u32[]{:S(2)}, u32[]{:S(2)}) %collective-permute-start.4) | collective-permute-done | bytes 262176 | tf_op jit(solution)/shard_map/ppermute | solution.py:25
  24.8 0.9 %slice_add_fusion = f32[32,1024]{1,0:T(8,128)S(1)} fusion(f32[64,1024]{1,0:T(8,128)S(1)} %collective-permute-done.4, f32[64,1024]{1,0:T(8,128)} %get-tuple-element.11), kind=kLoop, calls=%fused_computation.1 | loop fusion | flops 32768 | bytes 393216 | tf_op jit(solution)/shard_map/add | solution.py:52
  25.7 1.9 %collective-permute-start.5 = (f32[32,1024]{1,0:T(8,128)S(1)}, f32[32,1024]{1,0:T(8,128)S(1)}, u32[]{:S(2)}, u32[]{:S(2)}) collective-permute-start(f32[32,1024]{1,0:T(8,128)S(1)} %slice_add_fusion), channel_id=1, source_target_pairs={{0,2},{1,3},{2,0},{3,1},{4,6},{5,7},{6,4},{7,5},{8,10},{9,11},{10,... | collective-permute-start | bytes 393224 | tf_op jit(solution)/shard_map/ppermute | solution.py:25
  27.6 3.8 %collective-permute-done.5 = f32[32,1024]{1,0:T(8,128)S(1)} collective-permute-done((f32[32,1024]{1,0:T(8,128)S(1)}, f32[32,1024]{1,0:T(8,128)S(1)}, u32[]{:S(2)}, u32[]{:S(2)}) %collective-permute-start.5) | collective-permute-done | bytes 131104 | tf_op jit(solution)/shard_map/ppermute | solution.py:25
  31.5 1.9 %collective-permute-start.6 = (f32[16,1024]{1,0:T(8,128)S(1)}, f32[16,1024]{1,0:T(8,128)S(1)}, u32[]{:S(2)}, u32[]{:S(2)}) collective-permute-start(f32[16,1024]{1,0:T(8,128)S(1)} %fusion), channel_id=1, source_target_pairs={{0,4},{1,5},{2,6},{3,7},{4,0},{5,1},{6,2},{7,3},{8,12},{9,13},{10,... | collective-permute-start | bytes 196616 | tf_op jit(solution)/shard_map/ppermute | solution.py:25
  33.3 2.5 %collective-permute-done.6 = f32[16,1024]{1,0:T(8,128)S(1)} collective-permute-done((f32[16,1024]{1,0:T(8,128)S(1)}, f32[16,1024]{1,0:T(8,128)S(1)}, u32[]{:S(2)}, u32[]{:S(2)}) %collective-permute-start.6) | collective-permute-done | bytes 65568 | tf_op jit(solution)/shard_map/ppermute | solution.py:25
  35.8 2.9 %collective-permute-start.7 = (f32[8,1024]{1,0:T(8,128)S(1)}, f32[8,1024]{1,0:T(8,128)S(1)}, u32[]{:S(2)}, u32[]{:S(2)}) collective-permute-start(f32[8,1024]{1,0:T(8,128)S(1)} %fusion.2), channel_id=1, source_target_pairs={{0,8},{1,9},{2,10},{3,11},{4,12},{5,13},{6,14},{7,15},{8,0},{9,1},... | collective-permute-start | bytes 98312 | tf_op jit(solution)/shard_map/ppermute | solution.py:25
  38.7 2.0 %collective-permute-done.7 = f32[8,1024]{1,0:T(8,128)S(1)} collective-permute-done((f32[8,1024]{1,0:T(8,128)S(1)}, f32[8,1024]{1,0:T(8,128)S(1)}, u32[]{:S(2)}, u32[]{:S(2)}) %collective-permute-start.7) | collective-permute-done | bytes 32800 | tf_op jit(solution)/shard_map/ppermute | solution.py:25
  40.7 0.6 %fusion.5 = (bf16[8,512]{1,0:T(8,128)(2,1)}, bf16[8,512]{1,0:T(8,128)(2,1)}) fusion(bf16[8,1024]{1,0:T(8,128)(2,1)S(1)} %fusion.4), kind=kLoop, calls=%fused_computation.28 | loop fusion | bytes 32768 | tf_op jit(solution)/shard_map/slice | solution.py:199
  (21 shorter events, 0.1 us)
Async XLA Ops:
  0.6 0.7 %copy-start.3 = (bf16[8,512]{1,0:T(8,128)(2,1)S(1)}, bf16[8,512]{1,0:T(8,128)(2,1)}, u32[]{:S(2)}) copy-start(bf16[8,512]{1,0:T(8,128)(2,1)} %param.15) | copy-start | bytes 24580
  1.4 5.8 %collective-permute-start = (bf16[8,1024]{1,0:T(8,128)(2,1)S(1)}, bf16[8,1024]{1,0:T(8,128)(2,1)S(1)}, u32[]{:S(2)}, u32[]{:S(2)}) collective-permute-start(bf16[8,1024]{1,0:T(8,128)(2,1)S(1)} %constant_dynamic-update-slice_fusion), channel_id=1, source_target_pairs={{0,8},{1,9},{2,10},{3,11},{4,12},{5,13},{6,14},{7,15},{8,0},{9,1},... | collective-permute-start | bytes 49160 | tf_op jit(solution)/shard_map/ppermute | solution.py:25
  5.4 0.7 %copy-start.5 = (s32[128]{0:T(128)S(1)}, s32[128]{0:T(128)}, u32[]{:S(2)}) copy-start(s32[128]{0:T(128)} %constant.61.clone) | copy-start | bytes 1540
  5.4 0.7 %copy-start.6 = (s32[128]{0:T(128)S(1)}, s32[128]{0:T(128)}, u32[]{:S(2)}) copy-start(s32[128]{0:T(128)} %constant.60.clone) | copy-start | bytes 1540
  7.1 3.9 %collective-permute-start.1 = (bf16[16,1024]{1,0:T(8,128)(2,1)S(1)}, bf16[16,1024]{1,0:T(8,128)(2,1)S(1)}, u32[]{:S(2)}, u32[]{:S(2)}) collective-permute-start(bf16[16,1024]{1,0:T(8,128)(2,1)S(1)} %pad_maximum_fusion.2), channel_id=1, source_target_pairs={{0,4},{1,5},{2,6},{3,7},{4,0},{5,1},{6,2},{7,3},{8,12},{9,13},{10,... | collective-permute-start | bytes 98312 | tf_op jit(solution)/shard_map/ppermute | solution.py:25
  9.0 0.7 %copy-start.4 = (s32[2,16]{1,0:T(2,128)S(1)}, s32[2,16]{1,0:T(2,128)}, u32[]{:S(2)}) copy-start(s32[2,16]{1,0:T(2,128)} %param.18) | copy-start | bytes 388
  11.0 4.3 %collective-permute-start.2 = (bf16[32,1024]{1,0:T(8,128)(2,1)S(1)}, bf16[32,1024]{1,0:T(8,128)(2,1)S(1)}, u32[]{:S(2)}, u32[]{:S(2)}) collective-permute-start(bf16[32,1024]{1,0:T(8,128)(2,1)S(1)} %pad_maximum_fusion.1), channel_id=1, source_target_pairs={{0,2},{1,3},{2,0},{3,1},{4,6},{5,7},{6,4},{7,5},{8,10},{9,11},{10,... | collective-permute-start | bytes 196616 | tf_op jit(solution)/shard_map/ppermute | solution.py:25
  12.9 0.7 %copy-start.7 = (s32[2]{0:T(128)S(1)}, s32[2]{0:T(128)}, u32[]{:S(2)}) copy-start(s32[2]{0:T(128)} %param.17) | copy-start | bytes 28
  15.3 1.4 %copy-start = (bf16[64,1024]{1,0:T(8,128)(2,1)}, bf16[64,1024]{1,0:T(8,128)(2,1)S(1)}, u32[]{:S(2)}) copy-start(bf16[64,1024]{1,0:T(8,128)(2,1)S(1)} %pad_maximum_fusion.kva_ref) | copy-start | bytes 393220
  15.3 1.4 %collective-permute-start.3 = (bf16[64,1024]{1,0:T(8,128)(2,1)S(1)}, bf16[64,1024]{1,0:T(8,128)(2,1)S(1)}, u32[]{:S(2)}, u32[]{:S(2)}) collective-permute-start(bf16[64,1024]{1,0:T(8,128)(2,1)S(1)} %pad_maximum_fusion.kva_ref), channel_id=1, source_target_pairs={{0,1},{1,0},{2,3},{3,2},{4,5},{5,4},{6,7},{7,6},{8,9},{9,8},{10,11... | collective-permute-start | bytes 393224 | tf_op jit(solution)/shard_map/ppermute | solution.py:25
  16.7 0.7 %copy-start.2 = (bf16[64,1024]{1,0:T(8,128)(2,1)}, bf16[64,1024]{1,0:T(8,128)(2,1)S(1)}, u32[]{:S(2)}) copy-start(bf16[64,1024]{1,0:T(8,128)(2,1)S(1)} %collective-permute-done.3.kvb_ref) | copy-start | bytes 393220
  23.0 8.4 %copy-start.1 = (f32[64,1024]{1,0:T(8,128)S(1)}, f32[64,1024]{1,0:T(8,128)}, u32[]{:S(2)}) copy-start(f32[64,1024]{1,0:T(8,128)} %get-tuple-element.11) | copy-start | bytes 786436
  23.0 1.7 %collective-permute-start.4 = (f32[64,1024]{1,0:T(8,128)}, f32[64,1024]{1,0:T(8,128)S(1)}, u32[]{:S(2)}, u32[]{:S(2)}) collective-permute-start(f32[64,1024]{1,0:T(8,128)} %get-tuple-element.12), channel_id=1, source_target_pairs={{0,1},{1,0},{2,3},{3,2},{4,5},{5,4},{6,7},{7,6},{8,9},{9,8},{10,11... | collective-permute-start | bytes 786440 | tf_op jit(solution)/shard_map/ppermute | solution.py:25
  25.7 5.7 %collective-permute-start.5 = (f32[32,1024]{1,0:T(8,128)S(1)}, f32[32,1024]{1,0:T(8,128)S(1)}, u32[]{:S(2)}, u32[]{:S(2)}) collective-permute-start(f32[32,1024]{1,0:T(8,128)S(1)} %slice_add_fusion), channel_id=1, source_target_pairs={{0,2},{1,3},{2,0},{3,1},{4,6},{5,7},{6,4},{7,5},{8,10},{9,11},{10,... | collective-permute-start | bytes 393224 | tf_op jit(solution)/shard_map/ppermute | solution.py:25
  31.5 4.3 %collective-permute-start.6 = (f32[16,1024]{1,0:T(8,128)S(1)}, f32[16,1024]{1,0:T(8,128)S(1)}, u32[]{:S(2)}, u32[]{:S(2)}) collective-permute-start(f32[16,1024]{1,0:T(8,128)S(1)} %fusion), channel_id=1, source_target_pairs={{0,4},{1,5},{2,6},{3,7},{4,0},{5,1},{6,2},{7,3},{8,12},{9,13},{10,... | collective-permute-start | bytes 196616 | tf_op jit(solution)/shard_map/ppermute | solution.py:25
  35.8 4.9 %collective-permute-start.7 = (f32[8,1024]{1,0:T(8,128)S(1)}, f32[8,1024]{1,0:T(8,128)S(1)}, u32[]{:S(2)}, u32[]{:S(2)}) collective-permute-start(f32[8,1024]{1,0:T(8,128)S(1)} %fusion.2), channel_id=1, source_target_pairs={{0,8},{1,9},{2,10},{3,11},{4,12},{5,13},{6,14},{7,15},{8,0},{9,1},... | collective-permute-start | bytes 98312 | tf_op jit(solution)/shard_map/ppermute | solution.py:25

commit v8 on v7

--- a/solution.py
+++ b/solution.py
@@ -49,9 +49,9 @@
         if bit > 0:
             split = pending[0].shape[0] // 2
             send = sum(part[split:] for part in pending[1:])
-            send = pending[0][split:] + send
+            send = (pending[0][split:] + send).astype(jnp.bfloat16)
             pending = [part[:split] for part in pending]
-        pending.append(swap_with(send, axis_name, size, bit))
+        pending.append(swap_with(send, axis_name, size, bit).astype(jnp.float32))
     return sum(pending[1:], pending[0])
 
 
@@ -120,9 +120,9 @@
         doc_key = jnp.dot(dsd, q, preferred_element_type=jnp.float32) * score_scale
         doc_value = jnp.dot(pd.astype(jnp.bfloat16), do, preferred_element_type=jnp.float32)
         keep_ref[:, columns] = doc_key[:half]
-        send_ref[:, columns] = doc_key[half:]
+        send_ref[:, columns] = doc_key[half:].astype(send_ref.dtype)
         keep_ref[:, value_columns] = doc_value[:half]
-        send_ref[:, value_columns] = doc_value[half:]
+        send_ref[:, value_columns] = doc_value[half:].astype(send_ref.dtype)
         sk_ref[:, columns] = (
             jnp.dot(dss, q, preferred_element_type=jnp.float32) * score_scale
         ).astype(sk_ref.dtype)
@@ -177,7 +177,7 @@
         out_shape=(
             jax.ShapeDtypeStruct(queries.shape, jnp.bfloat16),
             jax.ShapeDtypeStruct((half_rows, 2 * key_value_width), jnp.float32),
-            jax.ShapeDtypeStruct((half_rows, 2 * key_value_width), jnp.float32),
+            jax.ShapeDtypeStruct((half_rows, 2 * key_value_width), jnp.bfloat16),
             jax.ShapeDtypeStruct(response_keys.shape, jnp.bfloat16),
             jax.ShapeDtypeStruct(response_values.shape, jnp.bfloat16),
         ),

time: 41.6 us -> 38.6 us (0.928)
  waiting for transfers between devices: 13.7 us -> 11.3 us
  other arithmetic: 2.22 us -> 1.37 us
    ppermute x8, waiting for transfers between devices: 13.7 us -> 11.3 us  [swap_with(): return lax.ppermute(block, axis_name, pairs)]
    add x3 -> x0, other arithmetic: 0.95 us -> none  [scatter_sum_rows(): send = pending[0][split:] + send]
where the time goes in v8:
time: 38.6 us; the launch traced here: 38.3 us
  starting transfers between devices  14.9 us (39%)
  waiting for transfers between devices  11.3 us (29%)
  Pallas kernels  5.57 us (14%)
  local copies, waits for them, and re-layouts  4.36 us (11%)
  other arithmetic  1.37 us (4%)
  between operations  0.72 us (2%)
    ppermute x8, starting transfers between devices, swap_with(): return lax.ppermute(block, axis_name, pairs)  14.9 us
    ppermute x8, waiting for transfers between devices, swap_with(): return lax.ppermute(block, axis_name, pairs)  11.3 us
    pallas_call x1, Pallas kernels, per_device(): pl.pallas_call(attention_kernel, out_shape=(jax.ShapeDtypeStruct(queries....  5.57 us
    unnamed x18, local copies, waits for them, and re-layouts  2.79 us
  transfers between devices with their start and end apart: 8, of which 8 were waited for; matrix products, arithmetic and copies ran while one was open for 6% of the time, Pallas kernels for 0%

profile of v8, /device:TPU:0, one launch (start us, length us, event | category | flops | bytes accessed | tf_op | source)
XLA Modules:
  0.0 38.3 jit_solution(1330979136493167858)
XLA Ops:
  0.6 0.7 %constant_dynamic-update-slice_fusion.1 = bf16[8,1024]{1,0:T(8,128)(2,1)S(1)} fusion(bf16[8,512]{1,0:T(8,128)(2,1)} %param.14), kind=kLoop, calls=%fused_computation.22 | loop fusion | bytes 16384
  1.4 4.0 %collective-permute-start = (bf16[8,1024]{1,0:T(8,128)(2,1)S(1)}, bf16[8,1024]{1,0:T(8,128)(2,1)S(1)}, u32[]{:S(2)}, u32[]{:S(2)}) collective-permute-start(bf16[8,1024]{1,0:T(8,128)(2,1)S(1)} %constant_dynamic-update-slice_fusion), channel_id=1, source_target_pairs={{0,8},{1,9},{2,10},{3,11},{4,12},{5,13},{6,14},{7,15},{8,0},{9,1},... | collective-permute-start | bytes 49160 | tf_op jit(solution)/shard_map/ppermute | solution.py:25
  5.4 0.7 %copy-done.5 = s32[128]{0:T(128)S(1)} copy-done((s32[128]{0:T(128)S(1)}, s32[128]{0:T(128)}, u32[]{:S(2)}) %copy-start.5) | copy-done | bytes 536
  6.0 0.0 copy-done.6
  6.1 1.0 %collective-permute-done = bf16[8,1024]{1,0:T(8,128)(2,1)S(1)} collective-permute-done((bf16[8,1024]{1,0:T(8,128)(2,1)S(1)}, bf16[8,1024]{1,0:T(8,128)(2,1)S(1)}, u32[]{:S(2)}, u32[]{:S(2)}) %collective-permute-start) | collective-permute-done | bytes 16416 | tf_op jit(solution)/shard_map/ppermute | solution.py:25
  7.1 1.9 %collective-permute-start.1 = (bf16[16,1024]{1,0:T(8,128)(2,1)S(1)}, bf16[16,1024]{1,0:T(8,128)(2,1)S(1)}, u32[]{:S(2)}, u32[]{:S(2)}) collective-permute-start(bf16[16,1024]{1,0:T(8,128)(2,1)S(1)} %pad_maximum_fusion.2), channel_id=1, source_target_pairs={{0,4},{1,5},{2,6},{3,7},{4,0},{5,1},{6,2},{7,3},{8,12},{9,13},{10,... | collective-permute-start | bytes 98312 | tf_op jit(solution)/shard_map/ppermute | solution.py:25
  9.0 0.7 %copy-done.4 = s32[2,16]{1,0:T(2,128)S(1)} copy-done((s32[2,16]{1,0:T(2,128)S(1)}, s32[2,16]{1,0:T(2,128)}, u32[]{:S(2)}) %copy-start.4) | copy-done | bytes 152
  9.7 0.1 copy.16
  9.8 0.1 broadcast_in_dim.20
  9.9 0.1 reshape.56
  9.9 0.6 %gather_fusion = s32[128,128]{1,0:T(8,128)S(1)} fusion(s32[16,128]{1,0:T(8,128)S(1)} %bitcast.3, s32[1024]{0:T(1024)S(1)} %pad_clamp_fusion), kind=kCustom, calls=%fused_computation | custom fusion | bytes 131584 | tf_op jit(solution)/shard_map/jit(_take)/gather | solution.py:172
  10.6 0.4 %collective-permute-done.1 = bf16[16,1024]{1,0:T(8,128)(2,1)S(1)} collective-permute-done((bf16[16,1024]{1,0:T(8,128)(2,1)S(1)}, bf16[16,1024]{1,0:T(8,128)(2,1)S(1)}, u32[]{:S(2)}, u32[]{:S(2)}) %collective-permute-start.1) | collective-permute-done | bytes 32800 | tf_op jit(solution)/shard_map/ppermute | solution.py:25
  11.0 1.9 %collective-permute-start.2 = (bf16[32,1024]{1,0:T(8,128)(2,1)S(1)}, bf16[32,1024]{1,0:T(8,128)(2,1)S(1)}, u32[]{:S(2)}, u32[]{:S(2)}) collective-permute-start(bf16[32,1024]{1,0:T(8,128)(2,1)S(1)} %pad_maximum_fusion.1), channel_id=1, source_target_pairs={{0,2},{1,3},{2,0},{3,1},{4,6},{5,7},{6,4},{7,5},{8,10},{9,11},{10,... | collective-permute-start | bytes 196616 | tf_op jit(solution)/shard_map/ppermute | solution.py:25
  12.9 0.7 %fusion.3.vis_ref = f32[128,128]{1,0:T(8,128)} fusion(s32[128,128]{1,0:T(8,128)S(1)} %gather_fusion, pred[128]{0:T(512)(128)(4,1)S(1)} %get-tuple-element.15), kind=kLoop, calls=%fused_computation.9 | loop fusion | flops 49152 | bytes 131200 | tf_op jit(solution)/shard_map/convert_element_type | solution.py:172
  13.6 0.1 broadcast_in_dim.23
  13.7 0.1 reshape.57
  13.8 1.5 %collective-permute-done.2 = bf16[32,1024]{1,0:T(8,128)(2,1)S(1)} collective-permute-done((bf16[32,1024]{1,0:T(8,128)(2,1)S(1)}, bf16[32,1024]{1,0:T(8,128)(2,1)S(1)}, u32[]{:S(2)}, u32[]{:S(2)}) %collective-permute-start.2) | collective-permute-done | bytes 65568 | tf_op jit(solution)/shard_map/ppermute | solution.py:25
  15.3 0.0 copy-start
  15.3 0.1 collective-permute-start.3
  15.4 0.5 %compare_convert_fusion.live_ref = f32[1,128]{1,0:T(1,128)} fusion(s32[1,128]{1,0:T(1,128)S(1)} %reshape.57), kind=kLoop, calls=%fused_computation.24 | loop fusion | flops 1024 | bytes 1024 | tf_op jit(solution)/shard_map/convert_element_type | solution.py:152
  15.9 0.8 %collective-permute-done.3.kvb_ref = bf16[64,1024]{1,0:T(8,128)(2,1)S(1)} collective-permute-done((bf16[64,1024]{1,0:T(8,128)(2,1)S(1)}, bf16[64,1024]{1,0:T(8,128)(2,1)S(1)}, u32[]{:S(2)}, u32[]{:S(2)}) %collective-permute-start.3) | collective-permute-done | bytes 131104 | tf_op jit(solution)/shard_map/ppermute | solution.py:25
  16.7 0.6 %copy-done.2 = bf16[64,1024]{1,0:T(8,128)(2,1)} copy-done((bf16[64,1024]{1,0:T(8,128)(2,1)}, bf16[64,1024]{1,0:T(8,128)(2,1)S(1)}, u32[]{:S(2)}) %copy-start.2) | copy-done | bytes 131096
  17.4 5.6 %shard_map.146 = (bf16[128,2560]{1,0:T(8,128)(2,1)}, f32[64,1024]{1,0:T(8,128)}, bf16[64,1024]{1,0:T(8,128)(2,1)}, bf16[128,512]{1,0:T(8,128)(2,1)}, bf16[128,512]{1,0:T(8,128)(2,1)}) custom-call(bf16[128,2560]{1,0:T(8,128)(2,1)} %q_ref.1, bf16[128,2560]{1,0:T(8,128)(2,1)} %do_ref.1, bf16[64,1024]{1,0:T(8,128)(2,1)} %copy-done, bf16[64,1024]{1,0:T(8,128)(2,1)} %copy-done.2, ...), custom_call_target="tpu_custom_call" | custom-call | tf_op jit(solution)/shard_map/pallas_call | solution.py:175
  23.0 0.1 collective-permute-start.4
  23.1 1.4 %collective-permute-done.4 = bf16[64,1024]{1,0:T(8,128)(2,1)S(1)} collective-permute-done((bf16[64,1024]{1,0:T(8,128)(2,1)}, bf16[64,1024]{1,0:T(8,128)(2,1)S(1)}, u32[]{:S(2)}, u32[]{:S(2)}) %collective-permute-start.4) | collective-permute-done | bytes 131104 | tf_op jit(solution)/shard_map/ppermute | solution.py:25
  24.6 1.9 %collective-permute-start.5 = (bf16[32,1024]{1,0:T(8,128)(2,1)S(1)}, bf16[32,1024]{1,0:T(8,128)(2,1)S(1)}, u32[]{:S(2)}, u32[]{:S(2)}) collective-permute-start(bf16[32,1024]{1,0:T(8,128)(2,1)S(1)} %fusion), channel_id=1, source_target_pairs={{0,2},{1,3},{2,0},{3,1},{4,6},{5,7},{6,4},{7,5},{8,10},{9,11},{10,... | collective-permute-start | bytes 196616 | tf_op jit(solution)/shard_map/ppermute | solution.py:25
  26.5 2.4 %collective-permute-done.5 = bf16[32,1024]{1,0:T(8,128)(2,1)S(1)} collective-permute-done((bf16[32,1024]{1,0:T(8,128)(2,1)S(1)}, bf16[32,1024]{1,0:T(8,128)(2,1)S(1)}, u32[]{:S(2)}, u32[]{:S(2)}) %collective-permute-start.5) | collective-permute-done | bytes 65568 | tf_op jit(solution)/shard_map/ppermute | solution.py:25
  28.9 2.0 %collective-permute-start.6 = (bf16[16,1024]{1,0:T(8,128)(2,1)S(1)}, bf16[16,1024]{1,0:T(8,128)(2,1)S(1)}, u32[]{:S(2)}, u32[]{:S(2)}) collective-permute-start(bf16[16,1024]{1,0:T(8,128)(2,1)S(1)} %fusion.2), channel_id=1, source_target_pairs={{0,4},{1,5},{2,6},{3,7},{4,0},{5,1},{6,2},{7,3},{8,12},{9,13},{10,... | collective-permute-start | bytes 98312 | tf_op jit(solution)/shard_map/ppermute | solution.py:25
  30.9 2.0 %collective-permute-done.6 = bf16[16,1024]{1,0:T(8,128)(2,1)S(1)} collective-permute-done((bf16[16,1024]{1,0:T(8,128)(2,1)S(1)}, bf16[16,1024]{1,0:T(8,128)(2,1)S(1)}, u32[]{:S(2)}, u32[]{:S(2)}) %collective-permute-start.6) | collective-permute-done | bytes 32800 | tf_op jit(solution)/shard_map/ppermute | solution.py:25
  32.9 3.0 %collective-permute-start.7 = (bf16[8,1024]{1,0:T(8,128)(2,1)S(1)}, bf16[8,1024]{1,0:T(8,128)(2,1)S(1)}, u32[]{:S(2)}, u32[]{:S(2)}) collective-permute-start(bf16[8,1024]{1,0:T(8,128)(2,1)S(1)} %fusion.5), channel_id=1, source_target_pairs={{0,8},{1,9},{2,10},{3,11},{4,12},{5,13},{6,14},{7,15},{8,0},{9,1},... | collective-permute-start | bytes 49160 | tf_op jit(solution)/shard_map/ppermute | solution.py:25
  35.9 1.7 %collective-permute-done.7 = bf16[8,1024]{1,0:T(8,128)(2,1)S(1)} collective-permute-done((bf16[8,1024]{1,0:T(8,128)(2,1)S(1)}, bf16[8,1024]{1,0:T(8,128)(2,1)S(1)}, u32[]{:S(2)}, u32[]{:S(2)}) %collective-permute-start.7) | collective-permute-done | bytes 16416 | tf_op jit(solution)/shard_map/ppermute | solution.py:25
  37.7 0.6 %fusion.8 = (bf16[8,512]{1,0:T(8,128)(2,1)}, bf16[8,512]{1,0:T(8,128)(2,1)}) fusion(bf16[8,1024]{1,0:T(8,128)(2,1)S(1)} %fusion.7), kind=kLoop, calls=%fused_computation.31 | loop fusion | bytes 32768 | tf_op jit(solution)/shard_map/slice | solution.py:199
  (24 shorter events, 0.2 us)
Async XLA Ops:
  0.6 0.7 %copy-start.3 = (bf16[8,512]{1,0:T(8,128)(2,1)S(1)}, bf16[8,512]{1,0:T(8,128)(2,1)}, u32[]{:S(2)}) copy-start(bf16[8,512]{1,0:T(8,128)(2,1)} %param.15) | copy-start | bytes 24580
  1.4 5.8 %collective-permute-start = (bf16[8,1024]{1,0:T(8,128)(2,1)S(1)}, bf16[8,1024]{1,0:T(8,128)(2,1)S(1)}, u32[]{:S(2)}, u32[]{:S(2)}) collective-permute-start(bf16[8,1024]{1,0:T(8,128)(2,1)S(1)} %constant_dynamic-update-slice_fusion), channel_id=1, source_target_pairs={{0,8},{1,9},{2,10},{3,11},{4,12},{5,13},{6,14},{7,15},{8,0},{9,1},... | collective-permute-start | bytes 49160 | tf_op jit(solution)/shard_map/ppermute | solution.py:25
  5.4 0.7 %copy-start.5 = (s32[128]{0:T(128)S(1)}, s32[128]{0:T(128)}, u32[]{:S(2)}) copy-start(s32[128]{0:T(128)} %constant.61.clone) | copy-start | bytes 1540
  5.4 0.7 %copy-start.6 = (s32[128]{0:T(128)S(1)}, s32[128]{0:T(128)}, u32[]{:S(2)}) copy-start(s32[128]{0:T(128)} %constant.60.clone) | copy-start | bytes 1540
  7.1 3.9 %collective-permute-start.1 = (bf16[16,1024]{1,0:T(8,128)(2,1)S(1)}, bf16[16,1024]{1,0:T(8,128)(2,1)S(1)}, u32[]{:S(2)}, u32[]{:S(2)}) collective-permute-start(bf16[16,1024]{1,0:T(8,128)(2,1)S(1)} %pad_maximum_fusion.2), channel_id=1, source_target_pairs={{0,4},{1,5},{2,6},{3,7},{4,0},{5,1},{6,2},{7,3},{8,12},{9,13},{10,... | collective-permute-start | bytes 98312 | tf_op jit(solution)/shard_map/ppermute | solution.py:25
  9.0 0.7 %copy-start.4 = (s32[2,16]{1,0:T(2,128)S(1)}, s32[2,16]{1,0:T(2,128)}, u32[]{:S(2)}) copy-start(s32[2,16]{1,0:T(2,128)} %param.18) | copy-start | bytes 388
  11.0 4.3 %collective-permute-start.2 = (bf16[32,1024]{1,0:T(8,128)(2,1)S(1)}, bf16[32,1024]{1,0:T(8,128)(2,1)S(1)}, u32[]{:S(2)}, u32[]{:S(2)}) collective-permute-start(bf16[32,1024]{1,0:T(8,128)(2,1)S(1)} %pad_maximum_fusion.1), channel_id=1, source_target_pairs={{0,2},{1,3},{2,0},{3,1},{4,6},{5,7},{6,4},{7,5},{8,10},{9,11},{10,... | collective-permute-start | bytes 196616 | tf_op jit(solution)/shard_map/ppermute | solution.py:25
  12.9 0.7 %copy-start.7 = (s32[2]{0:T(128)S(1)}, s32[2]{0:T(128)}, u32[]{:S(2)}) copy-start(s32[2]{0:T(128)} %param.17) | copy-start | bytes 28
  15.3 1.4 %copy-start = (bf16[64,1024]{1,0:T(8,128)(2,1)}, bf16[64,1024]{1,0:T(8,128)(2,1)S(1)}, u32[]{:S(2)}) copy-start(bf16[64,1024]{1,0:T(8,128)(2,1)S(1)} %pad_maximum_fusion.kva_ref) | copy-start | bytes 393220
  15.3 1.4 %collective-permute-start.3 = (bf16[64,1024]{1,0:T(8,128)(2,1)S(1)}, bf16[64,1024]{1,0:T(8,128)(2,1)S(1)}, u32[]{:S(2)}, u32[]{:S(2)}) collective-permute-start(bf16[64,1024]{1,0:T(8,128)(2,1)S(1)} %pad_maximum_fusion.kva_ref), channel_id=1, source_target_pairs={{0,1},{1,0},{2,3},{3,2},{4,5},{5,4},{6,7},{7,6},{8,9},{9,8},{10,11... | collective-permute-start | bytes 393224 | tf_op jit(solution)/shard_map/ppermute | solution.py:25
  16.7 0.6 %copy-start.2 = (bf16[64,1024]{1,0:T(8,128)(2,1)}, bf16[64,1024]{1,0:T(8,128)(2,1)S(1)}, u32[]{:S(2)}) copy-start(bf16[64,1024]{1,0:T(8,128)(2,1)S(1)} %collective-permute-done.3.kvb_ref) | copy-start | bytes 393220
  23.0 1.6 %copy-start.1 = (f32[64,1024]{1,0:T(8,128)S(1)}, f32[64,1024]{1,0:T(8,128)}, u32[]{:S(2)}) copy-start(f32[64,1024]{1,0:T(8,128)} %get-tuple-element.11) | copy-start | bytes 786436
  23.0 1.6 %collective-permute-start.4 = (bf16[64,1024]{1,0:T(8,128)(2,1)}, bf16[64,1024]{1,0:T(8,128)(2,1)S(1)}, u32[]{:S(2)}, u32[]{:S(2)}) collective-permute-start(bf16[64,1024]{1,0:T(8,128)(2,1)} %get-tuple-element.12), channel_id=1, source_target_pairs={{0,1},{1,0},{2,3},{3,2},{4,5},{5,4},{6,7},{7,6},{8,9},{9,8},{10,11... | collective-permute-start | bytes 393224 | tf_op jit(solution)/shard_map/ppermute | solution.py:25
  24.6 4.3 %collective-permute-start.5 = (bf16[32,1024]{1,0:T(8,128)(2,1)S(1)}, bf16[32,1024]{1,0:T(8,128)(2,1)S(1)}, u32[]{:S(2)}, u32[]{:S(2)}) collective-permute-start(bf16[32,1024]{1,0:T(8,128)(2,1)S(1)} %fusion), channel_id=1, source_target_pairs={{0,2},{1,3},{2,0},{3,1},{4,6},{5,7},{6,4},{7,5},{8,10},{9,11},{10,... | collective-permute-start | bytes 196616 | tf_op jit(solution)/shard_map/ppermute | solution.py:25
  28.9 4.0 %collective-permute-start.6 = (bf16[16,1024]{1,0:T(8,128)(2,1)S(1)}, bf16[16,1024]{1,0:T(8,128)(2,1)S(1)}, u32[]{:S(2)}, u32[]{:S(2)}) collective-permute-start(bf16[16,1024]{1,0:T(8,128)(2,1)S(1)} %fusion.2), channel_id=1, source_target_pairs={{0,4},{1,5},{2,6},{3,7},{4,0},{5,1},{6,2},{7,3},{8,12},{9,13},{10,... | collective-permute-start | bytes 98312 | tf_op jit(solution)/shard_map/ppermute | solution.py:25
  32.9 4.7 %collective-permute-start.7 = (bf16[8,1024]{1,0:T(8,128)(2,1)S(1)}, bf16[8,1024]{1,0:T(8,128)(2,1)S(1)}, u32[]{:S(2)}, u32[]{:S(2)}) collective-permute-start(bf16[8,1024]{1,0:T(8,128)(2,1)S(1)} %fusion.5), channel_id=1, source_target_pairs={{0,8},{1,9},{2,10},{3,11},{4,12},{5,13},{6,14},{7,15},{8,0},{9,1},... | collective-permute-start | bytes 49160 | tf_op jit(solution)/shard_map/ppermute | solution.py:25

commit v9 on v7

--- a/solution.py
+++ b/solution.py
@@ -47,10 +47,10 @@
     pending = [keep]
     for bit in range(bits):
         if bit > 0:
-            split = pending[0].shape[0] // 2
-            send = sum(part[split:] for part in pending[1:])
-            send = pending[0][split:] + send
-            pending = [part[:split] for part in pending]
+            split = pending[0].shape[2] // 2
+            send = sum(part[:, :, split:] for part in pending[1:])
+            send = pending[0][:, :, split:] + send
+            pending = [part[:, :, :split] for part in pending]
         pending.append(swap_with(send, axis_name, size, bit))
     return sum(pending[1:], pending[0])
 
@@ -78,57 +78,56 @@
 
 
 def attention_kernel(
-    q_ref, do_ref, kva_ref, kvb_ref, ks_ref, vs_ref, vis_ref, self_ref, live_ref,
+    q_ref, do_ref, ka_ref, va_ref, kb_ref, vb_ref, ks_ref, vs_ref, vis_ref, self_ref, live_ref,
     dq_ref, keep_ref, send_ref, sk_ref, sv_ref,
 ):
     token_rows = q_ref.shape[0]
-    width = KEY_HEADS * HEAD_SIZE
-    half = kva_ref.shape[0]
+    half = ka_ref.shape[0]
     score_scale = HEAD_SIZE ** (-0.5)
     doc_seen = jnp.concatenate([vis_ref[...]] * GROUP_HEADS, axis=1) > 0.5
     self_seen = jnp.concatenate([self_ref[...]] * GROUP_HEADS, axis=1) > 0.5
     live = jnp.concatenate([live_ref[...]] * GROUP_HEADS, axis=1)
-    for c in range(KEY_HEADS):
-        columns = slice(c * HEAD_SIZE, (c + 1) * HEAD_SIZE)
-        value_columns = slice(width + c * HEAD_SIZE, width + (c + 1) * HEAD_SIZE)
-        kd = jnp.concatenate([kva_ref[:, columns], kvb_ref[:, columns]], axis=0)
-        vd = jnp.concatenate([kva_ref[:, value_columns], kvb_ref[:, value_columns]], axis=0)
-        ks = ks_ref[:, columns]
-        vs = vs_ref[:, columns]
-        q = stacked_heads(q_ref, c)
-        do = stacked_heads(do_ref, c)
-        sd = jnp.where(doc_seen, contract_cols(kd, q) * score_scale, masked_score)
-        ss = jnp.where(self_seen, contract_cols(ks, q) * score_scale, masked_score)
-        top = jnp.maximum(jnp.max(sd, axis=0, keepdims=True), jnp.max(ss, axis=0, keepdims=True))
-        ed = jnp.exp(sd - top)
-        es = jnp.exp(ss - top)
-        total = jnp.sum(ed, axis=0, keepdims=True) + jnp.sum(es, axis=0, keepdims=True)
-        weight = live / total
-        pd = ed * weight
-        ps = es * weight
-        gd = contract_cols(vd, do)
-        gs = contract_cols(vs, do)
-        drift = jnp.sum(pd * gd, axis=0, keepdims=True) + jnp.sum(ps * gs, axis=0, keepdims=True)
-        dsd = (pd * (gd - drift)).astype(jnp.bfloat16)
-        dss = (ps * (gs - drift)).astype(jnp.bfloat16)
-        dq = (contract_rows(dsd, kd) + contract_rows(dss, ks)) * score_scale
-        for g in range(GROUP_HEADS):
-            h = c * GROUP_HEADS + g
-            dq_ref[:, h * HEAD_SIZE:(h + 1) * HEAD_SIZE] = dq[
-                g * token_rows:(g + 1) * token_rows
-            ].astype(dq_ref.dtype)
-        doc_key = jnp.dot(dsd, q, preferred_element_type=jnp.float32) * score_scale
-        doc_value = jnp.dot(pd.astype(jnp.bfloat16), do, preferred_element_type=jnp.float32)
-        keep_ref[:, columns] = doc_key[:half]
-        send_ref[:, columns] = doc_key[half:]
-        keep_ref[:, value_columns] = doc_value[:half]
-        send_ref[:, value_columns] = doc_value[half:]
-        sk_ref[:, columns] = (
-            jnp.dot(dss, q, preferred_element_type=jnp.float32) * score_scale
-        ).astype(sk_ref.dtype)
-        sv_ref[:, columns] = jnp.dot(
-            ps.astype(jnp.bfloat16), do, preferred_element_type=jnp.float32
-        ).astype(sv_ref.dtype)
+    kd = jnp.concatenate([ka_ref[...], kb_ref[...]], axis=0)
+    vd = jnp.concatenate([va_ref[...], vb_ref[...]], axis=0)
+    ks = ks_ref[...]
+    vs = vs_ref[...]
+    q = jnp.concatenate(
+        [q_ref[:, g * HEAD_SIZE:(g + 1) * HEAD_SIZE] for g in range(GROUP_HEADS)], axis=0
+    )
+    do = jnp.concatenate(
+        [do_ref[:, g * HEAD_SIZE:(g + 1) * HEAD_SIZE] for g in range(GROUP_HEADS)], axis=0
+    )
+    sd = jnp.where(doc_seen, contract_cols(kd, q) * score_scale, masked_score)
+    ss = jnp.where(self_seen, contract_cols(ks, q) * score_scale, masked_score)
+    top = jnp.maximum(jnp.max(sd, axis=0, keepdims=True), jnp.max(ss, axis=0, keepdims=True))
+    ed = jnp.exp(sd - top)
+    es = jnp.exp(ss - top)
+    total = jnp.sum(ed, axis=0, keepdims=True) + jnp.sum(es, axis=0, keepdims=True)
+    weight = live / total
+    pd = ed * weight
+    ps = es * weight
+    gd = contract_cols(vd, do)
+    gs = contract_cols(vs, do)
+    drift = jnp.sum(pd * gd, axis=0, keepdims=True) + jnp.sum(ps * gs, axis=0, keepdims=True)
+    dsd = (pd * (gd - drift)).astype(jnp.bfloat16)
+    dss = (ps * (gs - drift)).astype(jnp.bfloat16)
+    dq = (contract_rows(dsd, kd) + contract_rows(dss, ks)) * score_scale
+    for g in range(GROUP_HEADS):
+        dq_ref[:, g * HEAD_SIZE:(g + 1) * HEAD_SIZE] = dq[
+            g * token_rows:(g + 1) * token_rows
+        ].astype(dq_ref.dtype)
+    doc_key = jnp.dot(dsd, q, preferred_element_type=jnp.float32) * score_scale
+    doc_value = jnp.dot(pd.astype(jnp.bfloat16), do, preferred_element_type=jnp.float32)
+    keep_ref[0, 0] = doc_key[:half]
+    send_ref[0, 0] = doc_key[half:]
+    keep_ref[0, 1] = doc_value[:half]
+    send_ref[0, 1] = doc_value[half:]
+    sk_ref[...] = (jnp.dot(dss, q, preferred_element_type=jnp.float32) * score_scale).astype(
+        sk_ref.dtype
+    )
+    sv_ref[...] = jnp.dot(
+        ps.astype(jnp.bfloat16), do, preferred_element_type=jnp.float32
+    ).astype(sv_ref.dtype)
 
 
 def per_device(
@@ -172,12 +171,36 @@
     doc_visible = (jnp.take(row_masks.T, global_rows // block_rows, axis=0) == 1).astype(
         jnp.float32
     )
+    head_block = GROUP_HEADS * HEAD_SIZE
+    part_shape = (KEY_HEADS, 2, half_rows, HEAD_SIZE)
+    part_spec = pl.BlockSpec((1, 2, half_rows, HEAD_SIZE), lambda c: (c, 0, 0, 0))
     query_gradient, doc_keep, doc_send, self_key, self_value = pl.pallas_call(
         attention_kernel,
+        grid=(KEY_HEADS,),
+        in_specs=[
+            pl.BlockSpec((token_rows, head_block), lambda c: (0, c)),
+            pl.BlockSpec((token_rows, head_block), lambda c: (0, c)),
+            pl.BlockSpec((half_rows, HEAD_SIZE), lambda c: (0, c)),
+            pl.BlockSpec((half_rows, HEAD_SIZE), lambda c: (0, c + KEY_HEADS)),
+            pl.BlockSpec((half_rows, HEAD_SIZE), lambda c: (0, c)),
+            pl.BlockSpec((half_rows, HEAD_SIZE), lambda c: (0, c + KEY_HEADS)),
+            pl.BlockSpec((token_rows, HEAD_SIZE), lambda c: (0, c)),
+            pl.BlockSpec((token_rows, HEAD_SIZE), lambda c: (0, c)),
+            pl.BlockSpec((doc_rows, token_rows), lambda c: (0, 0)),
+            pl.BlockSpec((token_rows, token_rows), lambda c: (0, 0)),
+            pl.BlockSpec((1, token_rows), lambda c: (0, 0)),
+        ],
+        out_specs=[
+            pl.BlockSpec((token_rows, head_block), lambda c: (0, c)),
+            part_spec,
+            part_spec,
+            pl.BlockSpec((token_rows, HEAD_SIZE), lambda c: (0, c)),
+            pl.BlockSpec((token_rows, HEAD_SIZE), lambda c: (0, c)),
+        ],
         out_shape=(
             jax.ShapeDtypeStruct(queries.shape, jnp.bfloat16),
-            jax.ShapeDtypeStruct((half_rows, 2 * key_value_width), jnp.float32),
-            jax.ShapeDtypeStruct((half_rows, 2 * key_value_width), jnp.float32),
+            jax.ShapeDtypeStruct(part_shape, jnp.float32),
+            jax.ShapeDtypeStruct(part_shape, jnp.float32),
             jax.ShapeDtypeStruct(response_keys.shape, jnp.bfloat16),
             jax.ShapeDtypeStruct(response_values.shape, jnp.bfloat16),
         ),
@@ -185,6 +208,8 @@
         queries,
         grad_out,
         doc_mine,
+        doc_mine,
+        doc_other,
         doc_other,
         response_keys,
         response_values,
@@ -193,10 +218,11 @@
         live,
     )
     summed = scatter_sum_rows(doc_keep, doc_send, "resp")
+    doc_grads = jnp.transpose(summed, (1, 2, 0, 3)).reshape(2, slab_rows, key_value_width)
     return (
         query_gradient,
-        summed[:, :key_value_width].astype(jnp.bfloat16),
-        summed[:, key_value_width:].astype(jnp.bfloat16),
+        doc_grads[0].astype(jnp.bfloat16),
+        doc_grads[1].astype(jnp.bfloat16),
         self_key,
         self_value,
     )

time: 41.6 us -> 42 us (level)
    slice x1 -> x0, local copies, waits for them, and re-layouts: 0.61 us -> none  [per_device(): summed[:, key_value_width:].astype(jnp.bfloat16)]
    convert_element_type x0 -> x1, local copies, waits for them, and re-layouts: none -> 0.61 us  [per_device(): doc_grads[1].astype(jnp.bfloat16)]
  transfers between devices with their start and end apart: 8 -> 8, of which waited for: 8 -> 8; matrix products, arithmetic and copies ran while one was open for 6% -> 5% of each run, Pallas kernels for 0% -> 0%
where the time goes in v9:
time: 42 us; the launch traced here: 41.7 us
  starting transfers between devices  14.8 us (35%)
  waiting for transfers between devices  13.7 us (33%)
  Pallas kernels  5.86 us (14%)
  local copies, waits for them, and re-layouts  4.38 us (10%)
  other arithmetic  2.25 us (5%)
  between operations  0.7 us (2%)
    ppermute x8, starting transfers between devices, swap_with(): return lax.ppermute(block, axis_name, pairs)  14.8 us
    ppermute x8, waiting for transfers between devices, swap_with(): return lax.ppermute(block, axis_name, pairs)  13.7 us
    pallas_call x1, Pallas kernels, per_device(): pl.pallas_call(attention_kernel, grid=(KEY_HEADS,), in_specs=[pl.BlockSpe...  5.86 us
    unnamed x18, local copies, waits for them, and re-layouts  2.81 us
    add x3, other arithmetic, scatter_sum_rows(): send = pending[0][:, :, split:] + send  0.96 us
  transfers between devices with their start and end apart: 8, of which 8 were waited for; matrix products, arithmetic and copies ran while one was open for 5% of the time, Pallas kernels for 0%

profile of v9, /device:TPU:0, one launch (start us, length us, event | category | flops | bytes accessed | tf_op | source)
XLA Modules:
  0.0 41.7 jit_solution(1913362190955299840)
XLA Ops:
  0.6 0.7 %constant_dynamic-update-slice_fusion.1 = bf16[8,1024]{1,0:T(8,128)(2,1)S(1)} fusion(bf16[8,512]{1,0:T(8,128)(2,1)} %param.14), kind=kLoop, calls=%fused_computation.22 | loop fusion | bytes 16384
  1.4 4.0 %collective-permute-start = (bf16[8,1024]{1,0:T(8,128)(2,1)S(1)}, bf16[8,1024]{1,0:T(8,128)(2,1)S(1)}, u32[]{:S(2)}, u32[]{:S(2)}) collective-permute-start(bf16[8,1024]{1,0:T(8,128)(2,1)S(1)} %constant_dynamic-update-slice_fusion), channel_id=1, source_target_pairs={{0,8},{1,9},{2,10},{3,11},{4,12},{5,13},{6,14},{7,15},{8,0},{9,1},... | collective-permute-start | bytes 49160 | tf_op jit(solution)/shard_map/ppermute | solution.py:25
  5.4 0.7 %copy-done.5 = s32[128]{0:T(128)S(1)} copy-done((s32[128]{0:T(128)S(1)}, s32[128]{0:T(128)}, u32[]{:S(2)}) %copy-start.5) | copy-done | bytes 536
  6.0 0.0 copy-done.6
  6.1 1.0 %collective-permute-done = bf16[8,1024]{1,0:T(8,128)(2,1)S(1)} collective-permute-done((bf16[8,1024]{1,0:T(8,128)(2,1)S(1)}, bf16[8,1024]{1,0:T(8,128)(2,1)S(1)}, u32[]{:S(2)}, u32[]{:S(2)}) %collective-permute-start) | collective-permute-done | bytes 16416 | tf_op jit(solution)/shard_map/ppermute | solution.py:25
  7.1 1.9 %collective-permute-start.1 = (bf16[16,1024]{1,0:T(8,128)(2,1)S(1)}, bf16[16,1024]{1,0:T(8,128)(2,1)S(1)}, u32[]{:S(2)}, u32[]{:S(2)}) collective-permute-start(bf16[16,1024]{1,0:T(8,128)(2,1)S(1)} %pad_maximum_fusion.2), channel_id=1, source_target_pairs={{0,4},{1,5},{2,6},{3,7},{4,0},{5,1},{6,2},{7,3},{8,12},{9,13},{10,... | collective-permute-start | bytes 98312 | tf_op jit(solution)/shard_map/ppermute | solution.py:25
  9.0 0.7 %copy-done.4 = s32[2,16]{1,0:T(2,128)S(1)} copy-done((s32[2,16]{1,0:T(2,128)S(1)}, s32[2,16]{1,0:T(2,128)}, u32[]{:S(2)}) %copy-start.4) | copy-done | bytes 152
  9.7 0.1 copy.16
  9.8 0.1 broadcast_in_dim.20
  9.9 0.1 reshape.63
  9.9 0.6 %gather_fusion = s32[128,128]{1,0:T(8,128)S(1)} fusion(s32[16,128]{1,0:T(8,128)S(1)} %bitcast.9, s32[1024]{0:T(1024)S(1)} %pad_clamp_fusion), kind=kCustom, calls=%fused_computation | custom fusion | bytes 131584 | tf_op jit(solution)/shard_map/jit(_take)/gather | solution.py:171
  10.6 0.4 %collective-permute-done.1 = bf16[16,1024]{1,0:T(8,128)(2,1)S(1)} collective-permute-done((bf16[16,1024]{1,0:T(8,128)(2,1)S(1)}, bf16[16,1024]{1,0:T(8,128)(2,1)S(1)}, u32[]{:S(2)}, u32[]{:S(2)}) %collective-permute-start.1) | collective-permute-done | bytes 32800 | tf_op jit(solution)/shard_map/ppermute | solution.py:25
  11.0 1.9 %collective-permute-start.2 = (bf16[32,1024]{1,0:T(8,128)(2,1)S(1)}, bf16[32,1024]{1,0:T(8,128)(2,1)S(1)}, u32[]{:S(2)}, u32[]{:S(2)}) collective-permute-start(bf16[32,1024]{1,0:T(8,128)(2,1)S(1)} %pad_maximum_fusion.1), channel_id=1, source_target_pairs={{0,2},{1,3},{2,0},{3,1},{4,6},{5,7},{6,4},{7,5},{8,10},{9,11},{10,... | collective-permute-start | bytes 196616 | tf_op jit(solution)/shard_map/ppermute | solution.py:25
  12.9 0.7 %fusion.1.vis_ref = f32[128,128]{1,0:T(8,128)} fusion(s32[128,128]{1,0:T(8,128)S(1)} %gather_fusion, pred[128]{0:T(512)(128)(4,1)S(1)} %get-tuple-element.15), kind=kLoop, calls=%fused_computation.7 | loop fusion | flops 49152 | bytes 131200 | tf_op jit(solution)/shard_map/convert_element_type | solution.py:171
  13.6 0.1 broadcast_in_dim.23
  13.7 0.1 reshape.64
  13.8 1.5 %collective-permute-done.2 = bf16[32,1024]{1,0:T(8,128)(2,1)S(1)} collective-permute-done((bf16[32,1024]{1,0:T(8,128)(2,1)S(1)}, bf16[32,1024]{1,0:T(8,128)(2,1)S(1)}, u32[]{:S(2)}, u32[]{:S(2)}) %collective-permute-start.2) | collective-permute-done | bytes 65568 | tf_op jit(solution)/shard_map/ppermute | solution.py:25
  15.3 0.1 collective-permute-start.3
  15.4 0.5 %compare_convert_fusion.live_ref = f32[1,128]{1,0:T(1,128)} fusion(s32[1,128]{1,0:T(1,128)S(1)} %reshape.64), kind=kLoop, calls=%fused_computation.24 | loop fusion | flops 1024 | bytes 1024 | tf_op jit(solution)/shard_map/convert_element_type | solution.py:151
  15.9 0.8 %collective-permute-done.3.kb_ref.vb_ref = bf16[64,1024]{1,0:T(8,128)(2,1)S(1)} collective-permute-done((bf16[64,1024]{1,0:T(8,128)(2,1)S(1)}, bf16[64,1024]{1,0:T(8,128)(2,1)S(1)}, u32[]{:S(2)}, u32[]{:S(2)}) %collective-permute-start.3) | collective-permute-done | bytes 131104 | tf_op jit(solution)/shard_map/ppermute | solution.py:25
  16.7 0.7 %copy-done.1 = bf16[64,1024]{1,0:T(8,128)(2,1)} copy-done((bf16[64,1024]{1,0:T(8,128)(2,1)}, bf16[64,1024]{1,0:T(8,128)(2,1)S(1)}, u32[]{:S(2)}) %copy-start.1) | copy-done | bytes 131096
  17.4 5.9 %shard_map.146 = (bf16[128,2560]{1,0:T(8,128)(2,1)}, f32[4,2,64,128]{3,2,1,0:T(8,128)}, f32[4,2,64,128]{3,2,1,0:T(8,128)}, bf16[128,512]{1,0:T(8,128)(2,1)}, bf16[128,512]{1,0:T(8,128)(2,1)}) custom-call(bf16[128,2560]{1,0:T(8,128)(2,1)} %q_ref.1, bf16[128,2560]{1,0:T(8,128)(2,1)} %do_ref.1, bf16[64,1024]{1,0:T(8,128)(2,1)} %copy-done, ...), custom_call_target="tpu_custom_call" | custom-call | tf_op jit(solution)/shard_map/pallas_call | solution.py:177
  23.3 0.2 collective-permute-start.4
  23.5 1.6 %collective-permute-done.4 = f32[4,2,64,128]{3,2,1,0:T(8,128)S(1)} collective-permute-done((f32[4,2,64,128]{3,2,1,0:T(8,128)}, f32[4,2,64,128]{3,2,1,0:T(8,128)S(1)}, u32[]{:S(2)}, u32[]{:S(2)}) %collective-permute-start.4) | collective-permute-done | bytes 262176 | tf_op jit(solution)/shard_map/ppermute | solution.py:25
  25.1 0.9 %slice_add_fusion = f32[4,2,32,128]{3,2,1,0:T(8,128)S(1)} fusion(f32[4,2,64,128]{3,2,1,0:T(8,128)S(1)} %collective-permute-done.4, f32[4,2,64,128]{3,2,1,0:T(8,128)} %get-tuple-element.11), kind=kLoop, calls=%fused_computation.1 | loop fusion | flops 32768 | bytes 393216 | tf_op jit(solution)/shard_map/add | solution.py:52
  26.0 2.0 %collective-permute-start.5 = (f32[4,2,32,128]{3,2,1,0:T(8,128)S(1)}, f32[4,2,32,128]{3,2,1,0:T(8,128)S(1)}, u32[]{:S(2)}, u32[]{:S(2)}) collective-permute-start(f32[4,2,32,128]{3,2,1,0:T(8,128)S(1)} %slice_add_fusion), channel_id=1, source_target_pairs={{0,2},{1,3},{2,0},{3,1},{4,6},{5,7},{6,4},{7,5},{8,10},{9,11},{10,... | collective-permute-start | bytes 393224 | tf_op jit(solution)/shard_map/ppermute | solution.py:25
  28.0 3.8 %collective-permute-done.5 = f32[4,2,32,128]{3,2,1,0:T(8,128)S(1)} collective-permute-done((f32[4,2,32,128]{3,2,1,0:T(8,128)S(1)}, f32[4,2,32,128]{3,2,1,0:T(8,128)S(1)}, u32[]{:S(2)}, u32[]{:S(2)}) %collective-permute-start.5) | collective-permute-done | bytes 131104 | tf_op jit(solution)/shard_map/ppermute | solution.py:25
  31.8 1.8 %collective-permute-start.6 = (f32[4,2,16,128]{3,2,1,0:T(8,128)S(1)}, f32[4,2,16,128]{3,2,1,0:T(8,128)S(1)}, u32[]{:S(2)}, u32[]{:S(2)}) collective-permute-start(f32[4,2,16,128]{3,2,1,0:T(8,128)S(1)} %fusion), channel_id=1, source_target_pairs={{0,4},{1,5},{2,6},{3,7},{4,0},{5,1},{6,2},{7,3},{8,12},{9,13},{10,... | collective-permute-start | bytes 196616 | tf_op jit(solution)/shard_map/ppermute | solution.py:25
  33.6 2.5 %collective-permute-done.6 = f32[4,2,16,128]{3,2,1,0:T(8,128)S(1)} collective-permute-done((f32[4,2,16,128]{3,2,1,0:T(8,128)S(1)}, f32[4,2,16,128]{3,2,1,0:T(8,128)S(1)}, u32[]{:S(2)}, u32[]{:S(2)}) %collective-permute-start.6) | collective-permute-done | bytes 65568 | tf_op jit(solution)/shard_map/ppermute | solution.py:25
  36.2 2.9 %collective-permute-start.7 = (f32[4,2,8,128]{3,2,1,0:T(8,128)S(1)}, f32[4,2,8,128]{3,2,1,0:T(8,128)S(1)}, u32[]{:S(2)}, u32[]{:S(2)}) collective-permute-start(f32[4,2,8,128]{3,2,1,0:T(8,128)S(1)} %fusion.2), channel_id=1, source_target_pairs={{0,8},{1,9},{2,10},{3,11},{4,12},{5,13},{6,14},{7,15},{8,0},{9,1},... | collective-permute-start | bytes 98312 | tf_op jit(solution)/shard_map/ppermute | solution.py:25
  39.0 2.0 %collective-permute-done.7 = f32[4,2,8,128]{3,2,1,0:T(8,128)S(1)} collective-permute-done((f32[4,2,8,128]{3,2,1,0:T(8,128)S(1)}, f32[4,2,8,128]{3,2,1,0:T(8,128)S(1)}, u32[]{:S(2)}, u32[]{:S(2)}) %collective-permute-start.7) | collective-permute-done | bytes 32800 | tf_op jit(solution)/shard_map/ppermute | solution.py:25
  41.1 0.6 %slice_bitcast_fusion = (bf16[8,512]{1,0:T(8,128)(2,1)}, bf16[8,512]{1,0:T(8,128)(2,1)}) fusion(bf16[2,8,4,128]{3,1,0,2:T(8,128)(2,1)S(1)} %fusion.5), kind=kLoop, calls=%fused_computation.18 | loop fusion | bytes 32768 | tf_op jit(solution)/shard_map/convert_element_type | solution.py:225
  (21 shorter events, 0.1 us)
Async XLA Ops:
  0.6 0.7 %copy-start.3 = (bf16[8,512]{1,0:T(8,128)(2,1)S(1)}, bf16[8,512]{1,0:T(8,128)(2,1)}, u32[]{:S(2)}) copy-start(bf16[8,512]{1,0:T(8,128)(2,1)} %param.15) | copy-start | bytes 24580
  1.4 5.8 %collective-permute-start = (bf16[8,1024]{1,0:T(8,128)(2,1)S(1)}, bf16[8,1024]{1,0:T(8,128)(2,1)S(1)}, u32[]{:S(2)}, u32[]{:S(2)}) collective-permute-start(bf16[8,1024]{1,0:T(8,128)(2,1)S(1)} %constant_dynamic-update-slice_fusion), channel_id=1, source_target_pairs={{0,8},{1,9},{2,10},{3,11},{4,12},{5,13},{6,14},{7,15},{8,0},{9,1},... | collective-permute-start | bytes 49160 | tf_op jit(solution)/shard_map/ppermute | solution.py:25
  5.4 0.7 %copy-start.5 = (s32[128]{0:T(128)S(1)}, s32[128]{0:T(128)}, u32[]{:S(2)}) copy-start(s32[128]{0:T(128)} %constant.61.clone) | copy-start | bytes 1540
  5.4 0.7 %copy-start.6 = (s32[128]{0:T(128)S(1)}, s32[128]{0:T(128)}, u32[]{:S(2)}) copy-start(s32[128]{0:T(128)} %constant.60.clone) | copy-start | bytes 1540
  7.1 3.9 %collective-permute-start.1 = (bf16[16,1024]{1,0:T(8,128)(2,1)S(1)}, bf16[16,1024]{1,0:T(8,128)(2,1)S(1)}, u32[]{:S(2)}, u32[]{:S(2)}) collective-permute-start(bf16[16,1024]{1,0:T(8,128)(2,1)S(1)} %pad_maximum_fusion.2), channel_id=1, source_target_pairs={{0,4},{1,5},{2,6},{3,7},{4,0},{5,1},{6,2},{7,3},{8,12},{9,13},{10,... | collective-permute-start | bytes 98312 | tf_op jit(solution)/shard_map/ppermute | solution.py:25
  9.0 0.7 %copy-start.4 = (s32[2,16]{1,0:T(2,128)S(1)}, s32[2,16]{1,0:T(2,128)}, u32[]{:S(2)}) copy-start(s32[2,16]{1,0:T(2,128)} %param.18) | copy-start | bytes 388
  11.0 4.3 %collective-permute-start.2 = (bf16[32,1024]{1,0:T(8,128)(2,1)S(1)}, bf16[32,1024]{1,0:T(8,128)(2,1)S(1)}, u32[]{:S(2)}, u32[]{:S(2)}) collective-permute-start(bf16[32,1024]{1,0:T(8,128)(2,1)S(1)} %pad_maximum_fusion.1), channel_id=1, source_target_pairs={{0,2},{1,3},{2,0},{3,1},{4,6},{5,7},{6,4},{7,5},{8,10},{9,11},{10,... | collective-permute-start | bytes 196616 | tf_op jit(solution)/shard_map/ppermute | solution.py:25
  12.9 0.7 %copy-start.7 = (s32[2]{0:T(128)S(1)}, s32[2]{0:T(128)}, u32[]{:S(2)}) copy-start(s32[2]{0:T(128)} %param.17) | copy-start | bytes 28
  15.3 1.4 %copy-start = (bf16[64,1024]{1,0:T(8,128)(2,1)}, bf16[64,1024]{1,0:T(8,128)(2,1)S(1)}, u32[]{:S(2)}) copy-start(bf16[64,1024]{1,0:T(8,128)(2,1)S(1)} %pad_maximum_fusion.ka_ref.va_ref) | copy-start | bytes 393220
  15.3 1.4 %collective-permute-start.3 = (bf16[64,1024]{1,0:T(8,128)(2,1)S(1)}, bf16[64,1024]{1,0:T(8,128)(2,1)S(1)}, u32[]{:S(2)}, u32[]{:S(2)}) collective-permute-start(bf16[64,1024]{1,0:T(8,128)(2,1)S(1)} %pad_maximum_fusion.ka_ref.va_ref), channel_id=1, source_target_pairs={{0,1},{1,0},{2,3},{3,2},{4,5},{5,4},{6,7},{7,6},{8,9},{9,8},{10,11... | collective-permute-start | bytes 393224 | tf_op jit(solution)/shard_map/ppermute | solution.py:25
  16.7 0.7 %copy-start.1 = (bf16[64,1024]{1,0:T(8,128)(2,1)}, bf16[64,1024]{1,0:T(8,128)(2,1)S(1)}, u32[]{:S(2)}) copy-start(bf16[64,1024]{1,0:T(8,128)(2,1)S(1)} %collective-permute-done.3.kb_ref.vb_ref) | copy-start | bytes 393220
  23.3 8.5 %copy-start.2 = (f32[4,2,64,128]{3,2,1,0:T(8,128)S(1)}, f32[4,2,64,128]{3,2,1,0:T(8,128)}, u32[]{:S(2)}) copy-start(f32[4,2,64,128]{3,2,1,0:T(8,128)} %get-tuple-element.11) | copy-start | bytes 786436
  23.3 1.8 %collective-permute-start.4 = (f32[4,2,64,128]{3,2,1,0:T(8,128)}, f32[4,2,64,128]{3,2,1,0:T(8,128)S(1)}, u32[]{:S(2)}, u32[]{:S(2)}) collective-permute-start(f32[4,2,64,128]{3,2,1,0:T(8,128)} %get-tuple-element.12), channel_id=1, source_target_pairs={{0,1},{1,0},{2,3},{3,2},{4,5},{5,4},{6,7},{7,6},{8,9},{9,8},{10,11... | collective-permute-start | bytes 786440 | tf_op jit(solution)/shard_map/ppermute | solution.py:25
  26.0 5.8 %collective-permute-start.5 = (f32[4,2,32,128]{3,2,1,0:T(8,128)S(1)}, f32[4,2,32,128]{3,2,1,0:T(8,128)S(1)}, u32[]{:S(2)}, u32[]{:S(2)}) collective-permute-start(f32[4,2,32,128]{3,2,1,0:T(8,128)S(1)} %slice_add_fusion), channel_id=1, source_target_pairs={{0,2},{1,3},{2,0},{3,1},{4,6},{5,7},{6,4},{7,5},{8,10},{9,11},{10,... | collective-permute-start | bytes 393224 | tf_op jit(solution)/shard_map/ppermute | solution.py:25
  31.8 4.3 %collective-permute-start.6 = (f32[4,2,16,128]{3,2,1,0:T(8,128)S(1)}, f32[4,2,16,128]{3,2,1,0:T(8,128)S(1)}, u32[]{:S(2)}, u32[]{:S(2)}) collective-permute-start(f32[4,2,16,128]{3,2,1,0:T(8,128)S(1)} %fusion), channel_id=1, source_target_pairs={{0,4},{1,5},{2,6},{3,7},{4,0},{5,1},{6,2},{7,3},{8,12},{9,13},{10,... | collective-permute-start | bytes 196616 | tf_op jit(solution)/shard_map/ppermute | solution.py:25
  36.2 4.9 %collective-permute-start.7 = (f32[4,2,8,128]{3,2,1,0:T(8,128)S(1)}, f32[4,2,8,128]{3,2,1,0:T(8,128)S(1)}, u32[]{:S(2)}, u32[]{:S(2)}) collective-permute-start(f32[4,2,8,128]{3,2,1,0:T(8,128)S(1)} %fusion.2), channel_id=1, source_target_pairs={{0,8},{1,9},{2,10},{3,11},{4,12},{5,13},{6,14},{7,15},{8,0},{9,1},... | collective-permute-start | bytes 98312 | tf_op jit(solution)/shard_map/ppermute | solution.py:25

commit v10 on v7

--- a/solution.py
+++ b/solution.py
@@ -81,54 +81,47 @@
     q_ref, do_ref, kva_ref, kvb_ref, ks_ref, vs_ref, vis_ref, self_ref, live_ref,
     dq_ref, keep_ref, send_ref, sk_ref, sv_ref,
 ):
-    token_rows = q_ref.shape[0]
     width = KEY_HEADS * HEAD_SIZE
     half = kva_ref.shape[0]
+    doc_rows = 2 * half
     score_scale = HEAD_SIZE ** (-0.5)
-    doc_seen = jnp.concatenate([vis_ref[...]] * GROUP_HEADS, axis=1) > 0.5
-    self_seen = jnp.concatenate([self_ref[...]] * GROUP_HEADS, axis=1) > 0.5
-    live = jnp.concatenate([live_ref[...]] * GROUP_HEADS, axis=1)
+    seen = jnp.concatenate([vis_ref[...], self_ref[...]], axis=0) > 0.5
+    live = live_ref[...]
     for c in range(KEY_HEADS):
         columns = slice(c * HEAD_SIZE, (c + 1) * HEAD_SIZE)
         value_columns = slice(width + c * HEAD_SIZE, width + (c + 1) * HEAD_SIZE)
-        kd = jnp.concatenate([kva_ref[:, columns], kvb_ref[:, columns]], axis=0)
-        vd = jnp.concatenate([kva_ref[:, value_columns], kvb_ref[:, value_columns]], axis=0)
-        ks = ks_ref[:, columns]
-        vs = vs_ref[:, columns]
-        q = stacked_heads(q_ref, c)
-        do = stacked_heads(do_ref, c)
-        sd = jnp.where(doc_seen, contract_cols(kd, q) * score_scale, masked_score)
-        ss = jnp.where(self_seen, contract_cols(ks, q) * score_scale, masked_score)
-        top = jnp.maximum(jnp.max(sd, axis=0, keepdims=True), jnp.max(ss, axis=0, keepdims=True))
-        ed = jnp.exp(sd - top)
-        es = jnp.exp(ss - top)
-        total = jnp.sum(ed, axis=0, keepdims=True) + jnp.sum(es, axis=0, keepdims=True)
-        weight = live / total
-        pd = ed * weight
-        ps = es * weight
-        gd = contract_cols(vd, do)
-        gs = contract_cols(vs, do)
-        drift = jnp.sum(pd * gd, axis=0, keepdims=True) + jnp.sum(ps * gs, axis=0, keepdims=True)
-        dsd = (pd * (gd - drift)).astype(jnp.bfloat16)
-        dss = (ps * (gs - drift)).astype(jnp.bfloat16)
-        dq = (contract_rows(dsd, kd) + contract_rows(dss, ks)) * score_scale
+        keys = jnp.concatenate(
+            [kva_ref[:, columns], kvb_ref[:, columns], ks_ref[:, columns]], axis=0
+        )
+        values = jnp.concatenate(
+            [kva_ref[:, value_columns], kvb_ref[:, value_columns], vs_ref[:, columns]], axis=0
+        )
+        key_total = jnp.zeros(keys.shape, jnp.float32)
+        value_total = jnp.zeros(keys.shape, jnp.float32)
         for g in range(GROUP_HEADS):
             h = c * GROUP_HEADS + g
-            dq_ref[:, h * HEAD_SIZE:(h + 1) * HEAD_SIZE] = dq[
-                g * token_rows:(g + 1) * token_rows
-            ].astype(dq_ref.dtype)
-        doc_key = jnp.dot(dsd, q, preferred_element_type=jnp.float32) * score_scale
-        doc_value = jnp.dot(pd.astype(jnp.bfloat16), do, preferred_element_type=jnp.float32)
-        keep_ref[:, columns] = doc_key[:half]
-        send_ref[:, columns] = doc_key[half:]
-        keep_ref[:, value_columns] = doc_value[:half]
-        send_ref[:, value_columns] = doc_value[half:]
-        sk_ref[:, columns] = (
-            jnp.dot(dss, q, preferred_element_type=jnp.float32) * score_scale
-        ).astype(sk_ref.dtype)
-        sv_ref[:, columns] = jnp.dot(
-            ps.astype(jnp.bfloat16), do, preferred_element_type=jnp.float32
-        ).astype(sv_ref.dtype)
+            head = slice(h * HEAD_SIZE, (h + 1) * HEAD_SIZE)
+            q = q_ref[:, head]
+            do = do_ref[:, head]
+            score = jnp.where(seen, contract_cols(keys, q) * score_scale, masked_score)
+            top = jnp.max(score, axis=0, keepdims=True)
+            grown = jnp.exp(score - top)
+            prob = grown * (live / jnp.sum(grown, axis=0, keepdims=True))
+            slope = contract_cols(values, do)
+            drift = jnp.sum(prob * slope, axis=0, keepdims=True)
+            dscore = (prob * (slope - drift)).astype(jnp.bfloat16)
+            dq_ref[:, head] = (contract_rows(dscore, keys) * score_scale).astype(dq_ref.dtype)
+            key_total = key_total + jnp.dot(dscore, q, preferred_element_type=jnp.float32)
+            value_total = value_total + jnp.dot(
+                prob.astype(jnp.bfloat16), do, preferred_element_type=jnp.float32
+            )
+        key_total = key_total * score_scale
+        keep_ref[:, columns] = key_total[:half]
+        send_ref[:, columns] = key_total[half:doc_rows]
+        keep_ref[:, value_columns] = value_total[:half]
+        send_ref[:, value_columns] = value_total[half:doc_rows]
+        sk_ref[:, columns] = key_total[doc_rows:].astype(sk_ref.dtype)
+        sv_ref[:, columns] = value_total[doc_rows:].astype(sv_ref.dtype)
 
 
 def per_device(

time: 41.6 us -> 44.6 us (1.072)
  Pallas kernels: 5.61 us -> 8.61 us
    pallas_call x1, Pallas kernels: 5.61 us -> 8.61 us  [per_device(): pl.pallas_call(attention_kernel, out_shape=(jax.ShapeDtypeStruct(queries....]
  transfers between devices with their start and end apart: 8 -> 8, of which waited for: 8 -> 8; matrix products, arithmetic and copies ran while one was open for 6% -> 5% of each run, Pallas kernels for 0% -> 0%
where the time goes in v10:
time: 44.6 us; the launch traced here: 44.3 us
  starting transfers between devices  14.7 us (33%)
  waiting for transfers between devices  13.7 us (31%)
  Pallas kernels  8.61 us (19%)
  local copies, waits for them, and re-layouts  4.38 us (10%)
  other arithmetic  2.22 us (5%)
  between operations  0.69 us (2%)
    ppermute x8, starting transfers between devices, swap_with(): return lax.ppermute(block, axis_name, pairs)  14.7 us
    ppermute x8, waiting for transfers between devices, swap_with(): return lax.ppermute(block, axis_name, pairs)  13.7 us
    pallas_call x1, Pallas kernels, per_device(): pl.pallas_call(attention_kernel, out_shape=(jax.ShapeDtypeStruct(queries....  8.61 us
    unnamed x18, local copies, waits for them, and re-layouts  2.81 us
    add x3, other arithmetic, scatter_sum_rows(): send = pending[0][split:] + send  0.95 us
  transfers between devices with their start and end apart: 8, of which 8 were waited for; matrix products, arithmetic and copies ran while one was open for 5% of the time, Pallas kernels for 0%

profile of v10, /device:TPU:0, one launch (start us, length us, event | category | flops | bytes accessed | tf_op | source)
XLA Modules:
  0.0 44.3 jit_solution(10692512232622324129)
XLA Ops:
  0.6 0.7 %constant_dynamic-update-slice_fusion.1 = bf16[8,1024]{1,0:T(8,128)(2,1)S(1)} fusion(bf16[8,512]{1,0:T(8,128)(2,1)} %param.14), kind=kLoop, calls=%fused_computation.19 | loop fusion | bytes 16384
  1.4 4.0 %collective-permute-start = (bf16[8,1024]{1,0:T(8,128)(2,1)S(1)}, bf16[8,1024]{1,0:T(8,128)(2,1)S(1)}, u32[]{:S(2)}, u32[]{:S(2)}) collective-permute-start(bf16[8,1024]{1,0:T(8,128)(2,1)S(1)} %constant_dynamic-update-slice_fusion), channel_id=1, source_target_pairs={{0,8},{1,9},{2,10},{3,11},{4,12},{5,13},{6,14},{7,15},{8,0},{9,1},... | collective-permute-start | bytes 49160 | tf_op jit(solution)/shard_map/ppermute | solution.py:25
  5.4 0.7 %copy-done.5 = s32[128]{0:T(128)S(1)} copy-done((s32[128]{0:T(128)S(1)}, s32[128]{0:T(128)}, u32[]{:S(2)}) %copy-start.5) | copy-done | bytes 536
  6.0 0.0 copy-done.6
  6.1 1.0 %collective-permute-done = bf16[8,1024]{1,0:T(8,128)(2,1)S(1)} collective-permute-done((bf16[8,1024]{1,0:T(8,128)(2,1)S(1)}, bf16[8,1024]{1,0:T(8,128)(2,1)S(1)}, u32[]{:S(2)}, u32[]{:S(2)}) %collective-permute-start) | collective-permute-done | bytes 16416 | tf_op jit(solution)/shard_map/ppermute | solution.py:25
  7.1 1.9 %collective-permute-start.1 = (bf16[16,1024]{1,0:T(8,128)(2,1)S(1)}, bf16[16,1024]{1,0:T(8,128)(2,1)S(1)}, u32[]{:S(2)}, u32[]{:S(2)}) collective-permute-start(bf16[16,1024]{1,0:T(8,128)(2,1)S(1)} %pad_maximum_fusion.2), channel_id=1, source_target_pairs={{0,4},{1,5},{2,6},{3,7},{4,0},{5,1},{6,2},{7,3},{8,12},{9,13},{10,... | collective-permute-start | bytes 98312 | tf_op jit(solution)/shard_map/ppermute | solution.py:25
  9.0 0.7 %copy-done.4 = s32[2,16]{1,0:T(2,128)S(1)} copy-done((s32[2,16]{1,0:T(2,128)S(1)}, s32[2,16]{1,0:T(2,128)}, u32[]{:S(2)}) %copy-start.4) | copy-done | bytes 152
  9.7 0.1 copy.16
  9.8 0.1 broadcast_in_dim.20
  9.9 0.1 reshape.56
  9.9 0.6 %gather_fusion = s32[128,128]{1,0:T(8,128)S(1)} fusion(s32[16,128]{1,0:T(8,128)S(1)} %bitcast.3, s32[1024]{0:T(1024)S(1)} %pad_clamp_fusion), kind=kCustom, calls=%fused_computation | custom fusion | bytes 131584 | tf_op jit(solution)/shard_map/jit(_take)/gather | solution.py:165
  10.6 0.4 collective-permute-done.1
  11.0 1.9 %collective-permute-start.2 = (bf16[32,1024]{1,0:T(8,128)(2,1)S(1)}, bf16[32,1024]{1,0:T(8,128)(2,1)S(1)}, u32[]{:S(2)}, u32[]{:S(2)}) collective-permute-start(bf16[32,1024]{1,0:T(8,128)(2,1)S(1)} %pad_maximum_fusion.1), channel_id=1, source_target_pairs={{0,2},{1,3},{2,0},{3,1},{4,6},{5,7},{6,4},{7,5},{8,10},{9,11},{10,... | collective-permute-start | bytes 196616 | tf_op jit(solution)/shard_map/ppermute | solution.py:25
  12.9 0.7 %fusion.1.vis_ref = f32[128,128]{1,0:T(8,128)} fusion(s32[128,128]{1,0:T(8,128)S(1)} %gather_fusion, pred[128]{0:T(512)(128)(4,1)S(1)} %get-tuple-element.15), kind=kLoop, calls=%fused_computation.7 | loop fusion | flops 49152 | bytes 131200 | tf_op jit(solution)/shard_map/convert_element_type | solution.py:165
  13.6 0.1 broadcast_in_dim.23
  13.7 0.1 reshape.57
  13.8 1.5 %collective-permute-done.2 = bf16[32,1024]{1,0:T(8,128)(2,1)S(1)} collective-permute-done((bf16[32,1024]{1,0:T(8,128)(2,1)S(1)}, bf16[32,1024]{1,0:T(8,128)(2,1)S(1)}, u32[]{:S(2)}, u32[]{:S(2)}) %collective-permute-start.2) | collective-permute-done | bytes 65568 | tf_op jit(solution)/shard_map/ppermute | solution.py:25
  15.3 0.1 collective-permute-start.3
  15.4 0.5 %compare_convert_fusion.live_ref = f32[1,128]{1,0:T(1,128)} fusion(s32[1,128]{1,0:T(1,128)S(1)} %reshape.57), kind=kLoop, calls=%fused_computation.21 | loop fusion | flops 1024 | bytes 1024 | tf_op jit(solution)/shard_map/convert_element_type | solution.py:145
  15.9 0.8 %collective-permute-done.3.kvb_ref = bf16[64,1024]{1,0:T(8,128)(2,1)S(1)} collective-permute-done((bf16[64,1024]{1,0:T(8,128)(2,1)S(1)}, bf16[64,1024]{1,0:T(8,128)(2,1)S(1)}, u32[]{:S(2)}, u32[]{:S(2)}) %collective-permute-start.3) | collective-permute-done | bytes 131104 | tf_op jit(solution)/shard_map/ppermute | solution.py:25
  16.7 0.7 %copy-done.2 = bf16[64,1024]{1,0:T(8,128)(2,1)} copy-done((bf16[64,1024]{1,0:T(8,128)(2,1)}, bf16[64,1024]{1,0:T(8,128)(2,1)S(1)}, u32[]{:S(2)}) %copy-start.2) | copy-done | bytes 131096
  17.4 8.6 %shard_map.146 = (bf16[128,2560]{1,0:T(8,128)(2,1)}, f32[64,1024]{1,0:T(8,128)}, f32[64,1024]{1,0:T(8,128)}, bf16[128,512]{1,0:T(8,128)(2,1)}, bf16[128,512]{1,0:T(8,128)(2,1)}) custom-call(bf16[128,2560]{1,0:T(8,128)(2,1)} %q_ref.1, bf16[128,2560]{1,0:T(8,128)(2,1)} %do_ref.1, bf16[64,1024]{1,0:T(8,128)(2,1)} %copy-done, bf16[64,1024]{1,0:T(8,128)(2,1)} %copy-done.2, ...), custom_call_target="tpu_custom_call" | custom-call | tf_op jit(solution)/shard_map/pallas_call | solution.py:168
  26.0 0.1 collective-permute-start.4
  26.2 1.6 %collective-permute-done.4 = f32[64,1024]{1,0:T(8,128)S(1)} collective-permute-done((f32[64,1024]{1,0:T(8,128)}, f32[64,1024]{1,0:T(8,128)S(1)}, u32[]{:S(2)}, u32[]{:S(2)}) %collective-permute-start.4) | collective-permute-done | bytes 262176 | tf_op jit(solution)/shard_map/ppermute | solution.py:25
  27.8 0.9 %slice_add_fusion = f32[32,1024]{1,0:T(8,128)S(1)} fusion(f32[64,1024]{1,0:T(8,128)S(1)} %collective-permute-done.4, f32[64,1024]{1,0:T(8,128)} %get-tuple-element.11), kind=kLoop, calls=%fused_computation.1 | loop fusion | flops 32768 | bytes 393216 | tf_op jit(solution)/shard_map/add | solution.py:52
  28.7 1.9 %collective-permute-start.5 = (f32[32,1024]{1,0:T(8,128)S(1)}, f32[32,1024]{1,0:T(8,128)S(1)}, u32[]{:S(2)}, u32[]{:S(2)}) collective-permute-start(f32[32,1024]{1,0:T(8,128)S(1)} %slice_add_fusion), channel_id=1, source_target_pairs={{0,2},{1,3},{2,0},{3,1},{4,6},{5,7},{6,4},{7,5},{8,10},{9,11},{10,... | collective-permute-start | bytes 393224 | tf_op jit(solution)/shard_map/ppermute | solution.py:25
  30.6 3.8 %collective-permute-done.5 = f32[32,1024]{1,0:T(8,128)S(1)} collective-permute-done((f32[32,1024]{1,0:T(8,128)S(1)}, f32[32,1024]{1,0:T(8,128)S(1)}, u32[]{:S(2)}, u32[]{:S(2)}) %collective-permute-start.5) | collective-permute-done | bytes 131104 | tf_op jit(solution)/shard_map/ppermute | solution.py:25
  34.5 1.8 %collective-permute-start.6 = (f32[16,1024]{1,0:T(8,128)S(1)}, f32[16,1024]{1,0:T(8,128)S(1)}, u32[]{:S(2)}, u32[]{:S(2)}) collective-permute-start(f32[16,1024]{1,0:T(8,128)S(1)} %fusion), channel_id=1, source_target_pairs={{0,4},{1,5},{2,6},{3,7},{4,0},{5,1},{6,2},{7,3},{8,12},{9,13},{10,... | collective-permute-start | bytes 196616 | tf_op jit(solution)/shard_map/ppermute | solution.py:25
  36.3 2.5 %collective-permute-done.6 = f32[16,1024]{1,0:T(8,128)S(1)} collective-permute-done((f32[16,1024]{1,0:T(8,128)S(1)}, f32[16,1024]{1,0:T(8,128)S(1)}, u32[]{:S(2)}, u32[]{:S(2)}) %collective-permute-start.6) | collective-permute-done | bytes 65568 | tf_op jit(solution)/shard_map/ppermute | solution.py:25
  38.8 2.9 %collective-permute-start.7 = (f32[8,1024]{1,0:T(8,128)S(1)}, f32[8,1024]{1,0:T(8,128)S(1)}, u32[]{:S(2)}, u32[]{:S(2)}) collective-permute-start(f32[8,1024]{1,0:T(8,128)S(1)} %fusion.2), channel_id=1, source_target_pairs={{0,8},{1,9},{2,10},{3,11},{4,12},{5,13},{6,14},{7,15},{8,0},{9,1},... | collective-permute-start | bytes 98312 | tf_op jit(solution)/shard_map/ppermute | solution.py:25
  41.7 2.0 %collective-permute-done.7 = f32[8,1024]{1,0:T(8,128)S(1)} collective-permute-done((f32[8,1024]{1,0:T(8,128)S(1)}, f32[8,1024]{1,0:T(8,128)S(1)}, u32[]{:S(2)}, u32[]{:S(2)}) %collective-permute-start.7) | collective-permute-done | bytes 32800 | tf_op jit(solution)/shard_map/ppermute | solution.py:25
  43.7 0.6 %fusion.5 = (bf16[8,512]{1,0:T(8,128)(2,1)}, bf16[8,512]{1,0:T(8,128)(2,1)}) fusion(bf16[8,1024]{1,0:T(8,128)(2,1)S(1)} %fusion.4), kind=kLoop, calls=%fused_computation.28 | loop fusion | bytes 32768 | tf_op jit(solution)/shard_map/slice | solution.py:192
  (21 shorter events, 0.1 us)
Async XLA Ops:
  0.6 0.7 %copy-start.3 = (bf16[8,512]{1,0:T(8,128)(2,1)S(1)}, bf16[8,512]{1,0:T(8,128)(2,1)}, u32[]{:S(2)}) copy-start(bf16[8,512]{1,0:T(8,128)(2,1)} %param.15) | copy-start | bytes 24580
  1.4 5.8 %collective-permute-start = (bf16[8,1024]{1,0:T(8,128)(2,1)S(1)}, bf16[8,1024]{1,0:T(8,128)(2,1)S(1)}, u32[]{:S(2)}, u32[]{:S(2)}) collective-permute-start(bf16[8,1024]{1,0:T(8,128)(2,1)S(1)} %constant_dynamic-update-slice_fusion), channel_id=1, source_target_pairs={{0,8},{1,9},{2,10},{3,11},{4,12},{5,13},{6,14},{7,15},{8,0},{9,1},... | collective-permute-start | bytes 49160 | tf_op jit(solution)/shard_map/ppermute | solution.py:25
  5.4 0.7 %copy-start.5 = (s32[128]{0:T(128)S(1)}, s32[128]{0:T(128)}, u32[]{:S(2)}) copy-start(s32[128]{0:T(128)} %constant.61.clone) | copy-start | bytes 1540
  5.4 0.7 %copy-start.6 = (s32[128]{0:T(128)S(1)}, s32[128]{0:T(128)}, u32[]{:S(2)}) copy-start(s32[128]{0:T(128)} %constant.60.clone) | copy-start | bytes 1540
  7.1 3.9 %collective-permute-start.1 = (bf16[16,1024]{1,0:T(8,128)(2,1)S(1)}, bf16[16,1024]{1,0:T(8,128)(2,1)S(1)}, u32[]{:S(2)}, u32[]{:S(2)}) collective-permute-start(bf16[16,1024]{1,0:T(8,128)(2,1)S(1)} %pad_maximum_fusion.2), channel_id=1, source_target_pairs={{0,4},{1,5},{2,6},{3,7},{4,0},{5,1},{6,2},{7,3},{8,12},{9,13},{10,... | collective-permute-start | bytes 98312 | tf_op jit(solution)/shard_map/ppermute | solution.py:25
  9.0 0.7 %copy-start.4 = (s32[2,16]{1,0:T(2,128)S(1)}, s32[2,16]{1,0:T(2,128)}, u32[]{:S(2)}) copy-start(s32[2,16]{1,0:T(2,128)} %param.18) | copy-start | bytes 388
  11.0 4.3 %collective-permute-start.2 = (bf16[32,1024]{1,0:T(8,128)(2,1)S(1)}, bf16[32,1024]{1,0:T(8,128)(2,1)S(1)}, u32[]{:S(2)}, u32[]{:S(2)}) collective-permute-start(bf16[32,1024]{1,0:T(8,128)(2,1)S(1)} %pad_maximum_fusion.1), channel_id=1, source_target_pairs={{0,2},{1,3},{2,0},{3,1},{4,6},{5,7},{6,4},{7,5},{8,10},{9,11},{10,... | collective-permute-start | bytes 196616 | tf_op jit(solution)/shard_map/ppermute | solution.py:25
  12.9 0.7 %copy-start.7 = (s32[2]{0:T(128)S(1)}, s32[2]{0:T(128)}, u32[]{:S(2)}) copy-start(s32[2]{0:T(128)} %param.17) | copy-start | bytes 28
  15.3 1.4 %copy-start = (bf16[64,1024]{1,0:T(8,128)(2,1)}, bf16[64,1024]{1,0:T(8,128)(2,1)S(1)}, u32[]{:S(2)}) copy-start(bf16[64,1024]{1,0:T(8,128)(2,1)S(1)} %pad_maximum_fusion.kva_ref) | copy-start | bytes 393220
  15.3 1.4 %collective-permute-start.3 = (bf16[64,1024]{1,0:T(8,128)(2,1)S(1)}, bf16[64,1024]{1,0:T(8,128)(2,1)S(1)}, u32[]{:S(2)}, u32[]{:S(2)}) collective-permute-start(bf16[64,1024]{1,0:T(8,128)(2,1)S(1)} %pad_maximum_fusion.kva_ref), channel_id=1, source_target_pairs={{0,1},{1,0},{2,3},{3,2},{4,5},{5,4},{6,7},{7,6},{8,9},{9,8},{10,11... | collective-permute-start | bytes 393224 | tf_op jit(solution)/shard_map/ppermute | solution.py:25
  16.7 0.7 %copy-start.2 = (bf16[64,1024]{1,0:T(8,128)(2,1)}, bf16[64,1024]{1,0:T(8,128)(2,1)S(1)}, u32[]{:S(2)}) copy-start(bf16[64,1024]{1,0:T(8,128)(2,1)S(1)} %collective-permute-done.3.kvb_ref) | copy-start | bytes 393220
  26.0 8.4 %copy-start.1 = (f32[64,1024]{1,0:T(8,128)S(1)}, f32[64,1024]{1,0:T(8,128)}, u32[]{:S(2)}) copy-start(f32[64,1024]{1,0:T(8,128)} %get-tuple-element.11) | copy-start | bytes 786436
  26.0 1.7 %collective-permute-start.4 = (f32[64,1024]{1,0:T(8,128)}, f32[64,1024]{1,0:T(8,128)S(1)}, u32[]{:S(2)}, u32[]{:S(2)}) collective-permute-start(f32[64,1024]{1,0:T(8,128)} %get-tuple-element.12), channel_id=1, source_target_pairs={{0,1},{1,0},{2,3},{3,2},{4,5},{5,4},{6,7},{7,6},{8,9},{9,8},{10,11... | collective-permute-start | bytes 786440 | tf_op jit(solution)/shard_map/ppermute | solution.py:25
  28.7 5.8 %collective-permute-start.5 = (f32[32,1024]{1,0:T(8,128)S(1)}, f32[32,1024]{1,0:T(8,128)S(1)}, u32[]{:S(2)}, u32[]{:S(2)}) collective-permute-start(f32[32,1024]{1,0:T(8,128)S(1)} %slice_add_fusion), channel_id=1, source_target_pairs={{0,2},{1,3},{2,0},{3,1},{4,6},{5,7},{6,4},{7,5},{8,10},{9,11},{10,... | collective-permute-start | bytes 393224 | tf_op jit(solution)/shard_map/ppermute | solution.py:25
  34.5 4.3 %collective-permute-start.6 = (f32[16,1024]{1,0:T(8,128)S(1)}, f32[16,1024]{1,0:T(8,128)S(1)}, u32[]{:S(2)}, u32[]{:S(2)}) collective-permute-start(f32[16,1024]{1,0:T(8,128)S(1)} %fusion), channel_id=1, source_target_pairs={{0,4},{1,5},{2,6},{3,7},{4,0},{5,1},{6,2},{7,3},{8,12},{9,13},{10,... | collective-permute-start | bytes 196616 | tf_op jit(solution)/shard_map/ppermute | solution.py:25
  38.8 4.9 %collective-permute-start.7 = (f32[8,1024]{1,0:T(8,128)S(1)}, f32[8,1024]{1,0:T(8,128)S(1)}, u32[]{:S(2)}, u32[]{:S(2)}) collective-permute-start(f32[8,1024]{1,0:T(8,128)S(1)} %fusion.2), channel_id=1, source_target_pairs={{0,8},{1,9},{2,10},{3,11},{4,12},{5,13},{6,14},{7,15},{8,0},{9,1},... | collective-permute-start | bytes 98312 | tf_op jit(solution)/shard_map/ppermute | solution.py:25

commit v11 on v10

--- a/solution.py
+++ b/solution.py
@@ -81,12 +81,15 @@
     q_ref, do_ref, kva_ref, kvb_ref, ks_ref, vs_ref, vis_ref, self_ref, live_ref,
     dq_ref, keep_ref, send_ref, sk_ref, sv_ref,
 ):
+    token_rows = q_ref.shape[0]
     width = KEY_HEADS * HEAD_SIZE
     half = kva_ref.shape[0]
     doc_rows = 2 * half
     score_scale = HEAD_SIZE ** (-0.5)
-    seen = jnp.concatenate([vis_ref[...], self_ref[...]], axis=0) > 0.5
-    live = live_ref[...]
+    seen = jnp.concatenate(
+        [jnp.concatenate([vis_ref[...], self_ref[...]], axis=0)] * GROUP_HEADS, axis=1
+    ) > 0.5
+    live = jnp.concatenate([live_ref[...]] * GROUP_HEADS, axis=1)
     for c in range(KEY_HEADS):
         columns = slice(c * HEAD_SIZE, (c + 1) * HEAD_SIZE)
         value_columns = slice(width + c * HEAD_SIZE, width + (c + 1) * HEAD_SIZE)
@@ -96,26 +99,23 @@
         values = jnp.concatenate(
             [kva_ref[:, value_columns], kvb_ref[:, value_columns], vs_ref[:, columns]], axis=0
         )
-        key_total = jnp.zeros(keys.shape, jnp.float32)
-        value_total = jnp.zeros(keys.shape, jnp.float32)
+        q = stacked_heads(q_ref, c)
+        do = stacked_heads(do_ref, c)
+        score = jnp.where(seen, contract_cols(keys, q) * score_scale, masked_score)
+        top = jnp.max(score, axis=0, keepdims=True)
+        grown = jnp.exp(score - top)
+        prob = grown * (live / jnp.sum(grown, axis=0, keepdims=True))
+        slope = contract_cols(values, do)
+        drift = jnp.sum(prob * slope, axis=0, keepdims=True)
+        dscore = (prob * (slope - drift)).astype(jnp.bfloat16)
+        dq = contract_rows(dscore, keys) * score_scale
         for g in range(GROUP_HEADS):
             h = c * GROUP_HEADS + g
-            head = slice(h * HEAD_SIZE, (h + 1) * HEAD_SIZE)
-            q = q_ref[:, head]
-            do = do_ref[:, head]
-            score = jnp.where(seen, contract_cols(keys, q) * score_scale, masked_score)
-            top = jnp.max(score, axis=0, keepdims=True)
-            grown = jnp.exp(score - top)
-            prob = grown * (live / jnp.sum(grown, axis=0, keepdims=True))
-            slope = contract_cols(values, do)
-            drift = jnp.sum(prob * slope, axis=0, keepdims=True)
-            dscore = (prob * (slope - drift)).astype(jnp.bfloat16)
-            dq_ref[:, head] = (contract_rows(dscore, keys) * score_scale).astype(dq_ref.dtype)
-            key_total = key_total + jnp.dot(dscore, q, preferred_element_type=jnp.float32)
-            value_total = value_total + jnp.dot(
-                prob.astype(jnp.bfloat16), do, preferred_element_type=jnp.float32
-            )
-        key_total = key_total * score_scale
+            dq_ref[:, h * HEAD_SIZE:(h + 1) * HEAD_SIZE] = dq[
+                g * token_rows:(g + 1) * token_rows
+            ].astype(dq_ref.dtype)
+        key_total = jnp.dot(dscore, q, preferred_element_type=jnp.float32) * score_scale
+        value_total = jnp.dot(prob.astype(jnp.bfloat16), do, preferred_element_type=jnp.float32)
         keep_ref[:, columns] = key_total[:half]
         send_ref[:, columns] = key_total[half:doc_rows]
         keep_ref[:, value_columns] = value_total[:half]

time: 44.6 us -> 41.5 us (0.930)
  Pallas kernels: 8.61 us -> 5.48 us
    pallas_call x1, Pallas kernels: 8.61 us -> 5.48 us  [per_device(): pl.pallas_call(attention_kernel, out_shape=(jax.ShapeDtypeStruct(queries....]
  transfers between devices with their start and end apart: 8 -> 8, of which waited for: 8 -> 8; matrix products, arithmetic and copies ran while one was open for 5% -> 6% of each run, Pallas kernels for 0% -> 0%
where the time goes in v11:
time: 41.5 us; the launch traced here: 41.2 us
  starting transfers between devices  14.7 us (35%)
  waiting for transfers between devices  13.7 us (33%)
  Pallas kernels  5.48 us (13%)
  local copies, waits for them, and re-layouts  4.38 us (11%)
  other arithmetic  2.22 us (5%)
  between operations  0.69 us (2%)
    ppermute x8, starting transfers between devices, swap_with(): return lax.ppermute(block, axis_name, pairs)  14.7 us
    ppermute x8, waiting for transfers between devices, swap_with(): return lax.ppermute(block, axis_name, pairs)  13.7 us
    pallas_call x1, Pallas kernels, per_device(): pl.pallas_call(attention_kernel, out_shape=(jax.ShapeDtypeStruct(queries....  5.48 us
    unnamed x18, local copies, waits for them, and re-layouts  2.81 us
    add x3, other arithmetic, scatter_sum_rows(): send = pending[0][split:] + send  0.95 us
  transfers between devices with their start and end apart: 8, of which 8 were waited for; matrix products, arithmetic and copies ran while one was open for 6% of the time, Pallas kernels for 0%

profile of v11, /device:TPU:0, one launch (start us, length us, event | category | flops | bytes accessed | tf_op | source)
XLA Modules:
  0.0 41.2 jit_solution(9852247320858210563)
XLA Ops:
  0.6 0.7 %constant_dynamic-update-slice_fusion.1 = bf16[8,1024]{1,0:T(8,128)(2,1)S(1)} fusion(bf16[8,512]{1,0:T(8,128)(2,1)} %param.14), kind=kLoop, calls=%fused_computation.19 | loop fusion | bytes 16384
  1.4 4.0 %collective-permute-start = (bf16[8,1024]{1,0:T(8,128)(2,1)S(1)}, bf16[8,1024]{1,0:T(8,128)(2,1)S(1)}, u32[]{:S(2)}, u32[]{:S(2)}) collective-permute-start(bf16[8,1024]{1,0:T(8,128)(2,1)S(1)} %constant_dynamic-update-slice_fusion), channel_id=1, source_target_pairs={{0,8},{1,9},{2,10},{3,11},{4,12},{5,13},{6,14},{7,15},{8,0},{9,1},... | collective-permute-start | bytes 49160 | tf_op jit(solution)/shard_map/ppermute | solution.py:25
  5.4 0.7 %copy-done.5 = s32[128]{0:T(128)S(1)} copy-done((s32[128]{0:T(128)S(1)}, s32[128]{0:T(128)}, u32[]{:S(2)}) %copy-start.5) | copy-done | bytes 536
  6.0 0.0 copy-done.6
  6.1 1.0 %collective-permute-done = bf16[8,1024]{1,0:T(8,128)(2,1)S(1)} collective-permute-done((bf16[8,1024]{1,0:T(8,128)(2,1)S(1)}, bf16[8,1024]{1,0:T(8,128)(2,1)S(1)}, u32[]{:S(2)}, u32[]{:S(2)}) %collective-permute-start) | collective-permute-done | bytes 16416 | tf_op jit(solution)/shard_map/ppermute | solution.py:25
  7.1 1.9 %collective-permute-start.1 = (bf16[16,1024]{1,0:T(8,128)(2,1)S(1)}, bf16[16,1024]{1,0:T(8,128)(2,1)S(1)}, u32[]{:S(2)}, u32[]{:S(2)}) collective-permute-start(bf16[16,1024]{1,0:T(8,128)(2,1)S(1)} %pad_maximum_fusion.2), channel_id=1, source_target_pairs={{0,4},{1,5},{2,6},{3,7},{4,0},{5,1},{6,2},{7,3},{8,12},{9,13},{10,... | collective-permute-start | bytes 98312 | tf_op jit(solution)/shard_map/ppermute | solution.py:25
  9.0 0.7 %copy-done.4 = s32[2,16]{1,0:T(2,128)S(1)} copy-done((s32[2,16]{1,0:T(2,128)S(1)}, s32[2,16]{1,0:T(2,128)}, u32[]{:S(2)}) %copy-start.4) | copy-done | bytes 152
  9.7 0.1 copy.16
  9.8 0.1 broadcast_in_dim.20
  9.9 0.1 reshape.56
  9.9 0.6 %gather_fusion = s32[128,128]{1,0:T(8,128)S(1)} fusion(s32[16,128]{1,0:T(8,128)S(1)} %bitcast.3, s32[1024]{0:T(1024)S(1)} %pad_clamp_fusion), kind=kCustom, calls=%fused_computation | custom fusion | bytes 131584 | tf_op jit(solution)/shard_map/jit(_take)/gather | solution.py:165
  10.6 0.4 %collective-permute-done.1 = bf16[16,1024]{1,0:T(8,128)(2,1)S(1)} collective-permute-done((bf16[16,1024]{1,0:T(8,128)(2,1)S(1)}, bf16[16,1024]{1,0:T(8,128)(2,1)S(1)}, u32[]{:S(2)}, u32[]{:S(2)}) %collective-permute-start.1) | collective-permute-done | bytes 32800 | tf_op jit(solution)/shard_map/ppermute | solution.py:25
  11.0 1.9 %collective-permute-start.2 = (bf16[32,1024]{1,0:T(8,128)(2,1)S(1)}, bf16[32,1024]{1,0:T(8,128)(2,1)S(1)}, u32[]{:S(2)}, u32[]{:S(2)}) collective-permute-start(bf16[32,1024]{1,0:T(8,128)(2,1)S(1)} %pad_maximum_fusion.1), channel_id=1, source_target_pairs={{0,2},{1,3},{2,0},{3,1},{4,6},{5,7},{6,4},{7,5},{8,10},{9,11},{10,... | collective-permute-start | bytes 196616 | tf_op jit(solution)/shard_map/ppermute | solution.py:25
  12.9 0.7 %fusion.1.vis_ref = f32[128,128]{1,0:T(8,128)} fusion(s32[128,128]{1,0:T(8,128)S(1)} %gather_fusion, pred[128]{0:T(512)(128)(4,1)S(1)} %get-tuple-element.15), kind=kLoop, calls=%fused_computation.7 | loop fusion | flops 49152 | bytes 131200 | tf_op jit(solution)/shard_map/convert_element_type | solution.py:165
  13.6 0.1 broadcast_in_dim.23
  13.7 0.1 reshape.57
  13.8 1.5 %collective-permute-done.2 = bf16[32,1024]{1,0:T(8,128)(2,1)S(1)} collective-permute-done((bf16[32,1024]{1,0:T(8,128)(2,1)S(1)}, bf16[32,1024]{1,0:T(8,128)(2,1)S(1)}, u32[]{:S(2)}, u32[]{:S(2)}) %collective-permute-start.2) | collective-permute-done | bytes 65568 | tf_op jit(solution)/shard_map/ppermute | solution.py:25
  15.3 0.1 collective-permute-start.3
  15.4 0.5 %compare_convert_fusion.live_ref = f32[1,128]{1,0:T(1,128)} fusion(s32[1,128]{1,0:T(1,128)S(1)} %reshape.57), kind=kLoop, calls=%fused_computation.21 | loop fusion | flops 1024 | bytes 1024 | tf_op jit(solution)/shard_map/convert_element_type | solution.py:145
  15.9 0.8 %collective-permute-done.3.kvb_ref = bf16[64,1024]{1,0:T(8,128)(2,1)S(1)} collective-permute-done((bf16[64,1024]{1,0:T(8,128)(2,1)S(1)}, bf16[64,1024]{1,0:T(8,128)(2,1)S(1)}, u32[]{:S(2)}, u32[]{:S(2)}) %collective-permute-start.3) | collective-permute-done | bytes 131104 | tf_op jit(solution)/shard_map/ppermute | solution.py:25
  16.7 0.7 %copy-done.2 = bf16[64,1024]{1,0:T(8,128)(2,1)} copy-done((bf16[64,1024]{1,0:T(8,128)(2,1)}, bf16[64,1024]{1,0:T(8,128)(2,1)S(1)}, u32[]{:S(2)}) %copy-start.2) | copy-done | bytes 131096
  17.4 5.5 %shard_map.146 = (bf16[128,2560]{1,0:T(8,128)(2,1)}, f32[64,1024]{1,0:T(8,128)}, f32[64,1024]{1,0:T(8,128)}, bf16[128,512]{1,0:T(8,128)(2,1)}, bf16[128,512]{1,0:T(8,128)(2,1)}) custom-call(bf16[128,2560]{1,0:T(8,128)(2,1)} %q_ref.1, bf16[128,2560]{1,0:T(8,128)(2,1)} %do_ref.1, bf16[64,1024]{1,0:T(8,128)(2,1)} %copy-done, bf16[64,1024]{1,0:T(8,128)(2,1)} %copy-done.2, ...), custom_call_target="tpu_custom_call" | custom-call | tf_op jit(solution)/shard_map/pallas_call | solution.py:168
  22.9 0.1 collective-permute-start.4
  23.0 1.6 %collective-permute-done.4 = f32[64,1024]{1,0:T(8,128)S(1)} collective-permute-done((f32[64,1024]{1,0:T(8,128)}, f32[64,1024]{1,0:T(8,128)S(1)}, u32[]{:S(2)}, u32[]{:S(2)}) %collective-permute-start.4) | collective-permute-done | bytes 262176 | tf_op jit(solution)/shard_map/ppermute | solution.py:25
  24.6 0.9 %slice_add_fusion = f32[32,1024]{1,0:T(8,128)S(1)} fusion(f32[64,1024]{1,0:T(8,128)S(1)} %collective-permute-done.4, f32[64,1024]{1,0:T(8,128)} %get-tuple-element.11), kind=kLoop, calls=%fused_computation.1 | loop fusion | flops 32768 | bytes 393216 | tf_op jit(solution)/shard_map/add | solution.py:52
  25.6 1.9 %collective-permute-start.5 = (f32[32,1024]{1,0:T(8,128)S(1)}, f32[32,1024]{1,0:T(8,128)S(1)}, u32[]{:S(2)}, u32[]{:S(2)}) collective-permute-start(f32[32,1024]{1,0:T(8,128)S(1)} %slice_add_fusion), channel_id=1, source_target_pairs={{0,2},{1,3},{2,0},{3,1},{4,6},{5,7},{6,4},{7,5},{8,10},{9,11},{10,... | collective-permute-start | bytes 393224 | tf_op jit(solution)/shard_map/ppermute | solution.py:25
  27.5 3.8 %collective-permute-done.5 = f32[32,1024]{1,0:T(8,128)S(1)} collective-permute-done((f32[32,1024]{1,0:T(8,128)S(1)}, f32[32,1024]{1,0:T(8,128)S(1)}, u32[]{:S(2)}, u32[]{:S(2)}) %collective-permute-start.5) | collective-permute-done | bytes 131104 | tf_op jit(solution)/shard_map/ppermute | solution.py:25
  31.3 1.9 %collective-permute-start.6 = (f32[16,1024]{1,0:T(8,128)S(1)}, f32[16,1024]{1,0:T(8,128)S(1)}, u32[]{:S(2)}, u32[]{:S(2)}) collective-permute-start(f32[16,1024]{1,0:T(8,128)S(1)} %fusion), channel_id=1, source_target_pairs={{0,4},{1,5},{2,6},{3,7},{4,0},{5,1},{6,2},{7,3},{8,12},{9,13},{10,... | collective-permute-start | bytes 196616 | tf_op jit(solution)/shard_map/ppermute | solution.py:25
  33.2 2.5 %collective-permute-done.6 = f32[16,1024]{1,0:T(8,128)S(1)} collective-permute-done((f32[16,1024]{1,0:T(8,128)S(1)}, f32[16,1024]{1,0:T(8,128)S(1)}, u32[]{:S(2)}, u32[]{:S(2)}) %collective-permute-start.6) | collective-permute-done | bytes 65568 | tf_op jit(solution)/shard_map/ppermute | solution.py:25
  35.7 2.9 %collective-permute-start.7 = (f32[8,1024]{1,0:T(8,128)S(1)}, f32[8,1024]{1,0:T(8,128)S(1)}, u32[]{:S(2)}, u32[]{:S(2)}) collective-permute-start(f32[8,1024]{1,0:T(8,128)S(1)} %fusion.2), channel_id=1, source_target_pairs={{0,8},{1,9},{2,10},{3,11},{4,12},{5,13},{6,14},{7,15},{8,0},{9,1},... | collective-permute-start | bytes 98312 | tf_op jit(solution)/shard_map/ppermute | solution.py:25
  38.5 2.0 %collective-permute-done.7 = f32[8,1024]{1,0:T(8,128)S(1)} collective-permute-done((f32[8,1024]{1,0:T(8,128)S(1)}, f32[8,1024]{1,0:T(8,128)S(1)}, u32[]{:S(2)}, u32[]{:S(2)}) %collective-permute-start.7) | collective-permute-done | bytes 32800 | tf_op jit(solution)/shard_map/ppermute | solution.py:25
  40.6 0.6 %fusion.5 = (bf16[8,512]{1,0:T(8,128)(2,1)}, bf16[8,512]{1,0:T(8,128)(2,1)}) fusion(bf16[8,1024]{1,0:T(8,128)(2,1)S(1)} %fusion.4), kind=kLoop, calls=%fused_computation.28 | loop fusion | bytes 32768 | tf_op jit(solution)/shard_map/slice | solution.py:192
  (21 shorter events, 0.1 us)
Async XLA Ops:
  0.6 0.7 %copy-start.3 = (bf16[8,512]{1,0:T(8,128)(2,1)S(1)}, bf16[8,512]{1,0:T(8,128)(2,1)}, u32[]{:S(2)}) copy-start(bf16[8,512]{1,0:T(8,128)(2,1)} %param.15) | copy-start | bytes 24580
  1.4 5.8 %collective-permute-start = (bf16[8,1024]{1,0:T(8,128)(2,1)S(1)}, bf16[8,1024]{1,0:T(8,128)(2,1)S(1)}, u32[]{:S(2)}, u32[]{:S(2)}) collective-permute-start(bf16[8,1024]{1,0:T(8,128)(2,1)S(1)} %constant_dynamic-update-slice_fusion), channel_id=1, source_target_pairs={{0,8},{1,9},{2,10},{3,11},{4,12},{5,13},{6,14},{7,15},{8,0},{9,1},... | collective-permute-start | bytes 49160 | tf_op jit(solution)/shard_map/ppermute | solution.py:25
  5.4 0.7 %copy-start.5 = (s32[128]{0:T(128)S(1)}, s32[128]{0:T(128)}, u32[]{:S(2)}) copy-start(s32[128]{0:T(128)} %constant.61.clone) | copy-start | bytes 1540
  5.4 0.7 %copy-start.6 = (s32[128]{0:T(128)S(1)}, s32[128]{0:T(128)}, u32[]{:S(2)}) copy-start(s32[128]{0:T(128)} %constant.60.clone) | copy-start | bytes 1540
  7.1 3.9 %collective-permute-start.1 = (bf16[16,1024]{1,0:T(8,128)(2,1)S(1)}, bf16[16,1024]{1,0:T(8,128)(2,1)S(1)}, u32[]{:S(2)}, u32[]{:S(2)}) collective-permute-start(bf16[16,1024]{1,0:T(8,128)(2,1)S(1)} %pad_maximum_fusion.2), channel_id=1, source_target_pairs={{0,4},{1,5},{2,6},{3,7},{4,0},{5,1},{6,2},{7,3},{8,12},{9,13},{10,... | collective-permute-start | bytes 98312 | tf_op jit(solution)/shard_map/ppermute | solution.py:25
  9.0 0.7 %copy-start.4 = (s32[2,16]{1,0:T(2,128)S(1)}, s32[2,16]{1,0:T(2,128)}, u32[]{:S(2)}) copy-start(s32[2,16]{1,0:T(2,128)} %param.18) | copy-start | bytes 388
  11.0 4.3 %collective-permute-start.2 = (bf16[32,1024]{1,0:T(8,128)(2,1)S(1)}, bf16[32,1024]{1,0:T(8,128)(2,1)S(1)}, u32[]{:S(2)}, u32[]{:S(2)}) collective-permute-start(bf16[32,1024]{1,0:T(8,128)(2,1)S(1)} %pad_maximum_fusion.1), channel_id=1, source_target_pairs={{0,2},{1,3},{2,0},{3,1},{4,6},{5,7},{6,4},{7,5},{8,10},{9,11},{10,... | collective-permute-start | bytes 196616 | tf_op jit(solution)/shard_map/ppermute | solution.py:25
  12.9 0.7 %copy-start.7 = (s32[2]{0:T(128)S(1)}, s32[2]{0:T(128)}, u32[]{:S(2)}) copy-start(s32[2]{0:T(128)} %param.17) | copy-start | bytes 28
  15.3 1.4 %copy-start = (bf16[64,1024]{1,0:T(8,128)(2,1)}, bf16[64,1024]{1,0:T(8,128)(2,1)S(1)}, u32[]{:S(2)}) copy-start(bf16[64,1024]{1,0:T(8,128)(2,1)S(1)} %pad_maximum_fusion.kva_ref) | copy-start | bytes 393220
  15.3 1.4 %collective-permute-start.3 = (bf16[64,1024]{1,0:T(8,128)(2,1)S(1)}, bf16[64,1024]{1,0:T(8,128)(2,1)S(1)}, u32[]{:S(2)}, u32[]{:S(2)}) collective-permute-start(bf16[64,1024]{1,0:T(8,128)(2,1)S(1)} %pad_maximum_fusion.kva_ref), channel_id=1, source_target_pairs={{0,1},{1,0},{2,3},{3,2},{4,5},{5,4},{6,7},{7,6},{8,9},{9,8},{10,11... | collective-permute-start | bytes 393224 | tf_op jit(solution)/shard_map/ppermute | solution.py:25
  16.7 0.7 %copy-start.2 = (bf16[64,1024]{1,0:T(8,128)(2,1)}, bf16[64,1024]{1,0:T(8,128)(2,1)S(1)}, u32[]{:S(2)}) copy-start(bf16[64,1024]{1,0:T(8,128)(2,1)S(1)} %collective-permute-done.3.kvb_ref) | copy-start | bytes 393220
  22.9 8.4 %copy-start.1 = (f32[64,1024]{1,0:T(8,128)S(1)}, f32[64,1024]{1,0:T(8,128)}, u32[]{:S(2)}) copy-start(f32[64,1024]{1,0:T(8,128)} %get-tuple-element.11) | copy-start | bytes 786436
  22.9 1.7 %collective-permute-start.4 = (f32[64,1024]{1,0:T(8,128)}, f32[64,1024]{1,0:T(8,128)S(1)}, u32[]{:S(2)}, u32[]{:S(2)}) collective-permute-start(f32[64,1024]{1,0:T(8,128)} %get-tuple-element.12), channel_id=1, source_target_pairs={{0,1},{1,0},{2,3},{3,2},{4,5},{5,4},{6,7},{7,6},{8,9},{9,8},{10,11... | collective-permute-start | bytes 786440 | tf_op jit(solution)/shard_map/ppermute | solution.py:25
  25.6 5.7 %collective-permute-start.5 = (f32[32,1024]{1,0:T(8,128)S(1)}, f32[32,1024]{1,0:T(8,128)S(1)}, u32[]{:S(2)}, u32[]{:S(2)}) collective-permute-start(f32[32,1024]{1,0:T(8,128)S(1)} %slice_add_fusion), channel_id=1, source_target_pairs={{0,2},{1,3},{2,0},{3,1},{4,6},{5,7},{6,4},{7,5},{8,10},{9,11},{10,... | collective-permute-start | bytes 393224 | tf_op jit(solution)/shard_map/ppermute | solution.py:25
  31.3 4.3 %collective-permute-start.6 = (f32[16,1024]{1,0:T(8,128)S(1)}, f32[16,1024]{1,0:T(8,128)S(1)}, u32[]{:S(2)}, u32[]{:S(2)}) collective-permute-start(f32[16,1024]{1,0:T(8,128)S(1)} %fusion), channel_id=1, source_target_pairs={{0,4},{1,5},{2,6},{3,7},{4,0},{5,1},{6,2},{7,3},{8,12},{9,13},{10,... | collective-permute-start | bytes 196616 | tf_op jit(solution)/shard_map/ppermute | solution.py:25
  35.7 4.9 %collective-permute-start.7 = (f32[8,1024]{1,0:T(8,128)S(1)}, f32[8,1024]{1,0:T(8,128)S(1)}, u32[]{:S(2)}, u32[]{:S(2)}) collective-permute-start(f32[8,1024]{1,0:T(8,128)S(1)} %fusion.2), channel_id=1, source_target_pairs={{0,8},{1,9},{2,10},{3,11},{4,12},{5,13},{6,14},{7,15},{8,0},{9,1},... | collective-permute-start | bytes 98312 | tf_op jit(solution)/shard_map/ppermute | solution.py:25

commit v12 on v11

--- a/solution.py
+++ b/solution.py
@@ -51,7 +51,11 @@
             send = sum(part[split:] for part in pending[1:])
             send = pending[0][split:] + send
             pending = [part[:split] for part in pending]
-        pending.append(swap_with(send, axis_name, size, bit))
+        if bit in (1, 2):
+            send = swap_with(send.astype(jnp.bfloat16), axis_name, size, bit).astype(jnp.float32)
+        else:
+            send = swap_with(send, axis_name, size, bit)
+        pending.append(send)
     return sum(pending[1:], pending[0])
 
 

time: 41.5 us -> 39.8 us (0.959)
  waiting for transfers between devices: 13.7 us -> 11.7 us
    ppermute x8, waiting for transfers between devices: 13.7 us -> 11.7 us  [swap_with(): return lax.ppermute(block, axis_name, pairs)]
    convert_element_type x0 -> x4, other arithmetic: none -> 1.03 us  [the longest x2 1.01 us: scatter_sum_rows(): send.astype(jnp.bfloat16)]
    add x3 -> x1, other arithmetic: 0.95 us -> 0.01 us  [scatter_sum_rows(): send = pending[0][split:] + send]
where the time goes in v12:
time: 39.8 us; the launch traced here: 39.5 us
  starting transfers between devices  14.9 us (37%)
  waiting for transfers between devices  11.7 us (29%)
  Pallas kernels  5.48 us (14%)
  local copies, waits for them, and re-layouts  4.38 us (11%)
  other arithmetic  2.31 us (6%)
  between operations  0.71 us (2%)
    ppermute x8, starting transfers between devices, swap_with(): return lax.ppermute(block, axis_name, pairs)  14.9 us
    ppermute x8, waiting for transfers between devices, swap_with(): return lax.ppermute(block, axis_name, pairs)  11.7 us
    pallas_call x1, Pallas kernels, per_device(): pl.pallas_call(attention_kernel, out_shape=(jax.ShapeDtypeStruct(queries....  5.48 us
    unnamed x18, local copies, waits for them, and re-layouts  2.81 us
    convert_element_type x2, other arithmetic, scatter_sum_rows(): send.astype(jnp.bfloat16)  1.01 us
  transfers between devices with their start and end apart: 8, of which 8 were waited for; matrix products, arithmetic and copies ran while one was open for 6% of the time, Pallas kernels for 0%

profile of v12, /device:TPU:0, one launch (start us, length us, event | category | flops | bytes accessed | tf_op | source)
XLA Modules:
  0.0 39.5 jit_solution(7134902434660190395)
XLA Ops:
  0.6 0.7 %constant_dynamic-update-slice_fusion.1 = bf16[8,1024]{1,0:T(8,128)(2,1)S(1)} fusion(bf16[8,512]{1,0:T(8,128)(2,1)} %param.14), kind=kLoop, calls=%fused_computation.21 | loop fusion | bytes 16384
  1.4 4.0 %collective-permute-start = (bf16[8,1024]{1,0:T(8,128)(2,1)S(1)}, bf16[8,1024]{1,0:T(8,128)(2,1)S(1)}, u32[]{:S(2)}, u32[]{:S(2)}) collective-permute-start(bf16[8,1024]{1,0:T(8,128)(2,1)S(1)} %constant_dynamic-update-slice_fusion), channel_id=1, source_target_pairs={{0,8},{1,9},{2,10},{3,11},{4,12},{5,13},{6,14},{7,15},{8,0},{9,1},... | collective-permute-start | bytes 49160 | tf_op jit(solution)/shard_map/ppermute | solution.py:25
  5.4 0.7 %copy-done.5 = s32[128]{0:T(128)S(1)} copy-done((s32[128]{0:T(128)S(1)}, s32[128]{0:T(128)}, u32[]{:S(2)}) %copy-start.5) | copy-done | bytes 536
  6.0 0.0 copy-done.6
  6.1 1.0 %collective-permute-done = bf16[8,1024]{1,0:T(8,128)(2,1)S(1)} collective-permute-done((bf16[8,1024]{1,0:T(8,128)(2,1)S(1)}, bf16[8,1024]{1,0:T(8,128)(2,1)S(1)}, u32[]{:S(2)}, u32[]{:S(2)}) %collective-permute-start) | collective-permute-done | bytes 16416 | tf_op jit(solution)/shard_map/ppermute | solution.py:25
  7.1 1.9 %collective-permute-start.1 = (bf16[16,1024]{1,0:T(8,128)(2,1)S(1)}, bf16[16,1024]{1,0:T(8,128)(2,1)S(1)}, u32[]{:S(2)}, u32[]{:S(2)}) collective-permute-start(bf16[16,1024]{1,0:T(8,128)(2,1)S(1)} %pad_maximum_fusion.2), channel_id=1, source_target_pairs={{0,4},{1,5},{2,6},{3,7},{4,0},{5,1},{6,2},{7,3},{8,12},{9,13},{10,... | collective-permute-start | bytes 98312 | tf_op jit(solution)/shard_map/ppermute | solution.py:25
  9.0 0.7 %copy-done.4 = s32[2,16]{1,0:T(2,128)S(1)} copy-done((s32[2,16]{1,0:T(2,128)S(1)}, s32[2,16]{1,0:T(2,128)}, u32[]{:S(2)}) %copy-start.4) | copy-done | bytes 152
  9.7 0.1 copy.16
  9.8 0.1 broadcast_in_dim.20
  9.9 0.1 reshape.56
  9.9 0.6 %gather_fusion = s32[128,128]{1,0:T(8,128)S(1)} fusion(s32[16,128]{1,0:T(8,128)S(1)} %bitcast.3, s32[1024]{0:T(1024)S(1)} %pad_clamp_fusion), kind=kCustom, calls=%fused_computation | custom fusion | bytes 131584 | tf_op jit(solution)/shard_map/jit(_take)/gather | solution.py:169
  10.6 0.4 %collective-permute-done.1 = bf16[16,1024]{1,0:T(8,128)(2,1)S(1)} collective-permute-done((bf16[16,1024]{1,0:T(8,128)(2,1)S(1)}, bf16[16,1024]{1,0:T(8,128)(2,1)S(1)}, u32[]{:S(2)}, u32[]{:S(2)}) %collective-permute-start.1) | collective-permute-done | bytes 32800 | tf_op jit(solution)/shard_map/ppermute | solution.py:25
  11.0 1.9 %collective-permute-start.2 = (bf16[32,1024]{1,0:T(8,128)(2,1)S(1)}, bf16[32,1024]{1,0:T(8,128)(2,1)S(1)}, u32[]{:S(2)}, u32[]{:S(2)}) collective-permute-start(bf16[32,1024]{1,0:T(8,128)(2,1)S(1)} %pad_maximum_fusion.1), channel_id=1, source_target_pairs={{0,2},{1,3},{2,0},{3,1},{4,6},{5,7},{6,4},{7,5},{8,10},{9,11},{10,... | collective-permute-start | bytes 196616 | tf_op jit(solution)/shard_map/ppermute | solution.py:25
  12.9 0.7 %fusion.3.vis_ref = f32[128,128]{1,0:T(8,128)} fusion(s32[128,128]{1,0:T(8,128)S(1)} %gather_fusion, pred[128]{0:T(512)(128)(4,1)S(1)} %get-tuple-element.15), kind=kLoop, calls=%fused_computation.9 | loop fusion | flops 49152 | bytes 131200 | tf_op jit(solution)/shard_map/convert_element_type | solution.py:169
  13.6 0.1 broadcast_in_dim.23
  13.7 0.1 reshape.57
  13.8 1.5 %collective-permute-done.2 = bf16[32,1024]{1,0:T(8,128)(2,1)S(1)} collective-permute-done((bf16[32,1024]{1,0:T(8,128)(2,1)S(1)}, bf16[32,1024]{1,0:T(8,128)(2,1)S(1)}, u32[]{:S(2)}, u32[]{:S(2)}) %collective-permute-start.2) | collective-permute-done | bytes 65568 | tf_op jit(solution)/shard_map/ppermute | solution.py:25
  15.3 0.1 collective-permute-start.3
  15.4 0.5 %compare_convert_fusion.live_ref = f32[1,128]{1,0:T(1,128)} fusion(s32[1,128]{1,0:T(1,128)S(1)} %reshape.57), kind=kLoop, calls=%fused_computation.23 | loop fusion | flops 1024 | bytes 1024 | tf_op jit(solution)/shard_map/convert_element_type | solution.py:149
  15.9 0.8 %collective-permute-done.3.kvb_ref = bf16[64,1024]{1,0:T(8,128)(2,1)S(1)} collective-permute-done((bf16[64,1024]{1,0:T(8,128)(2,1)S(1)}, bf16[64,1024]{1,0:T(8,128)(2,1)S(1)}, u32[]{:S(2)}, u32[]{:S(2)}) %collective-permute-start.3) | collective-permute-done | bytes 131104 | tf_op jit(solution)/shard_map/ppermute | solution.py:25
  16.7 0.7 %copy-done.2 = bf16[64,1024]{1,0:T(8,128)(2,1)} copy-done((bf16[64,1024]{1,0:T(8,128)(2,1)}, bf16[64,1024]{1,0:T(8,128)(2,1)S(1)}, u32[]{:S(2)}) %copy-start.2) | copy-done | bytes 131096
  17.4 5.5 %shard_map.146 = (bf16[128,2560]{1,0:T(8,128)(2,1)}, f32[64,1024]{1,0:T(8,128)}, f32[64,1024]{1,0:T(8,128)}, bf16[128,512]{1,0:T(8,128)(2,1)}, bf16[128,512]{1,0:T(8,128)(2,1)}) custom-call(bf16[128,2560]{1,0:T(8,128)(2,1)} %q_ref.1, bf16[128,2560]{1,0:T(8,128)(2,1)} %do_ref.1, bf16[64,1024]{1,0:T(8,128)(2,1)} %copy-done, bf16[64,1024]{1,0:T(8,128)(2,1)} %copy-done.2, ...), custom_call_target="tpu_custom_call" | custom-call | tf_op jit(solution)/shard_map/pallas_call | solution.py:172
  22.9 0.1 collective-permute-start.4
  23.0 1.6 %collective-permute-done.4 = f32[64,1024]{1,0:T(8,128)S(1)} collective-permute-done((f32[64,1024]{1,0:T(8,128)}, f32[64,1024]{1,0:T(8,128)S(1)}, u32[]{:S(2)}, u32[]{:S(2)}) %collective-permute-start.4) | collective-permute-done | bytes 262176 | tf_op jit(solution)/shard_map/ppermute | solution.py:25
  24.6 1.0 %fusion = bf16[32,1024]{1,0:T(8,128)(2,1)S(1)} fusion(f32[64,1024]{1,0:T(8,128)S(1)} %collective-permute-done.4, f32[64,1024]{1,0:T(8,128)} %get-tuple-element.11), kind=kLoop, calls=%fused_computation.2 | loop fusion | flops 65536 | bytes 327680 | tf_op jit(solution)/shard_map/convert_element_type | solution.py:55
  25.6 1.9 %collective-permute-start.5 = (bf16[32,1024]{1,0:T(8,128)(2,1)S(1)}, bf16[32,1024]{1,0:T(8,128)(2,1)S(1)}, u32[]{:S(2)}, u32[]{:S(2)}) collective-permute-start(bf16[32,1024]{1,0:T(8,128)(2,1)S(1)} %fusion), channel_id=1, source_target_pairs={{0,2},{1,3},{2,0},{3,1},{4,6},{5,7},{6,4},{7,5},{8,10},{9,11},{10,... | collective-permute-start | bytes 196616 | tf_op jit(solution)/shard_map/ppermute | solution.py:25
  27.6 2.4 %collective-permute-done.5 = bf16[32,1024]{1,0:T(8,128)(2,1)S(1)} collective-permute-done((bf16[32,1024]{1,0:T(8,128)(2,1)S(1)}, bf16[32,1024]{1,0:T(8,128)(2,1)S(1)}, u32[]{:S(2)}, u32[]{:S(2)}) %collective-permute-start.5) | collective-permute-done | bytes 65568 | tf_op jit(solution)/shard_map/ppermute | solution.py:25
  30.0 2.0 %collective-permute-start.6 = (bf16[16,1024]{1,0:T(8,128)(2,1)S(1)}, bf16[16,1024]{1,0:T(8,128)(2,1)S(1)}, u32[]{:S(2)}, u32[]{:S(2)}) collective-permute-start(bf16[16,1024]{1,0:T(8,128)(2,1)S(1)} %fusion.2), channel_id=1, source_target_pairs={{0,4},{1,5},{2,6},{3,7},{4,0},{5,1},{6,2},{7,3},{8,12},{9,13},{10,... | collective-permute-start | bytes 98312 | tf_op jit(solution)/shard_map/ppermute | solution.py:25
  32.0 2.0 %collective-permute-done.6 = bf16[16,1024]{1,0:T(8,128)(2,1)S(1)} collective-permute-done((bf16[16,1024]{1,0:T(8,128)(2,1)S(1)}, bf16[16,1024]{1,0:T(8,128)(2,1)S(1)}, u32[]{:S(2)}, u32[]{:S(2)}) %collective-permute-start.6) | collective-permute-done | bytes 32800 | tf_op jit(solution)/shard_map/ppermute | solution.py:25
  34.0 3.0 %collective-permute-start.7 = (f32[8,1024]{1,0:T(8,128)S(1)}, f32[8,1024]{1,0:T(8,128)S(1)}, u32[]{:S(2)}, u32[]{:S(2)}) collective-permute-start(f32[8,1024]{1,0:T(8,128)S(1)} %fusion.4), channel_id=1, source_target_pairs={{0,8},{1,9},{2,10},{3,11},{4,12},{5,13},{6,14},{7,15},{8,0},{9,1},... | collective-permute-start | bytes 98312 | tf_op jit(solution)/shard_map/ppermute | solution.py:25
  37.0 1.9 %collective-permute-done.7 = f32[8,1024]{1,0:T(8,128)S(1)} collective-permute-done((f32[8,1024]{1,0:T(8,128)S(1)}, f32[8,1024]{1,0:T(8,128)S(1)}, u32[]{:S(2)}, u32[]{:S(2)}) %collective-permute-start.7) | collective-permute-done | bytes 32800 | tf_op jit(solution)/shard_map/ppermute | solution.py:25
  38.9 0.6 %fusion.7 = (bf16[8,512]{1,0:T(8,128)(2,1)}, bf16[8,512]{1,0:T(8,128)(2,1)}) fusion(bf16[8,1024]{1,0:T(8,128)(2,1)S(1)} %fusion.6), kind=kLoop, calls=%fused_computation.30 | loop fusion | bytes 32768 | tf_op jit(solution)/shard_map/slice | solution.py:196
  (23 shorter events, 0.1 us)
Async XLA Ops:
  0.6 0.7 %copy-start.3 = (bf16[8,512]{1,0:T(8,128)(2,1)S(1)}, bf16[8,512]{1,0:T(8,128)(2,1)}, u32[]{:S(2)}) copy-start(bf16[8,512]{1,0:T(8,128)(2,1)} %param.15) | copy-start | bytes 24580
  1.4 5.8 %collective-permute-start = (bf16[8,1024]{1,0:T(8,128)(2,1)S(1)}, bf16[8,1024]{1,0:T(8,128)(2,1)S(1)}, u32[]{:S(2)}, u32[]{:S(2)}) collective-permute-start(bf16[8,1024]{1,0:T(8,128)(2,1)S(1)} %constant_dynamic-update-slice_fusion), channel_id=1, source_target_pairs={{0,8},{1,9},{2,10},{3,11},{4,12},{5,13},{6,14},{7,15},{8,0},{9,1},... | collective-permute-start | bytes 49160 | tf_op jit(solution)/shard_map/ppermute | solution.py:25
  5.4 0.7 %copy-start.5 = (s32[128]{0:T(128)S(1)}, s32[128]{0:T(128)}, u32[]{:S(2)}) copy-start(s32[128]{0:T(128)} %constant.61.clone) | copy-start | bytes 1540
  5.4 0.7 %copy-start.6 = (s32[128]{0:T(128)S(1)}, s32[128]{0:T(128)}, u32[]{:S(2)}) copy-start(s32[128]{0:T(128)} %constant.60.clone) | copy-start | bytes 1540
  7.1 3.9 %collective-permute-start.1 = (bf16[16,1024]{1,0:T(8,128)(2,1)S(1)}, bf16[16,1024]{1,0:T(8,128)(2,1)S(1)}, u32[]{:S(2)}, u32[]{:S(2)}) collective-permute-start(bf16[16,1024]{1,0:T(8,128)(2,1)S(1)} %pad_maximum_fusion.2), channel_id=1, source_target_pairs={{0,4},{1,5},{2,6},{3,7},{4,0},{5,1},{6,2},{7,3},{8,12},{9,13},{10,... | collective-permute-start | bytes 98312 | tf_op jit(solution)/shard_map/ppermute | solution.py:25
  9.0 0.7 %copy-start.4 = (s32[2,16]{1,0:T(2,128)S(1)}, s32[2,16]{1,0:T(2,128)}, u32[]{:S(2)}) copy-start(s32[2,16]{1,0:T(2,128)} %param.18) | copy-start | bytes 388
  11.0 4.3 %collective-permute-start.2 = (bf16[32,1024]{1,0:T(8,128)(2,1)S(1)}, bf16[32,1024]{1,0:T(8,128)(2,1)S(1)}, u32[]{:S(2)}, u32[]{:S(2)}) collective-permute-start(bf16[32,1024]{1,0:T(8,128)(2,1)S(1)} %pad_maximum_fusion.1), channel_id=1, source_target_pairs={{0,2},{1,3},{2,0},{3,1},{4,6},{5,7},{6,4},{7,5},{8,10},{9,11},{10,... | collective-permute-start | bytes 196616 | tf_op jit(solution)/shard_map/ppermute | solution.py:25
  12.9 0.7 %copy-start.7 = (s32[2]{0:T(128)S(1)}, s32[2]{0:T(128)}, u32[]{:S(2)}) copy-start(s32[2]{0:T(128)} %param.17) | copy-start | bytes 28
  15.3 1.4 %copy-start = (bf16[64,1024]{1,0:T(8,128)(2,1)}, bf16[64,1024]{1,0:T(8,128)(2,1)S(1)}, u32[]{:S(2)}) copy-start(bf16[64,1024]{1,0:T(8,128)(2,1)S(1)} %pad_maximum_fusion.kva_ref) | copy-start | bytes 393220
  15.3 1.4 %collective-permute-start.3 = (bf16[64,1024]{1,0:T(8,128)(2,1)S(1)}, bf16[64,1024]{1,0:T(8,128)(2,1)S(1)}, u32[]{:S(2)}, u32[]{:S(2)}) collective-permute-start(bf16[64,1024]{1,0:T(8,128)(2,1)S(1)} %pad_maximum_fusion.kva_ref), channel_id=1, source_target_pairs={{0,1},{1,0},{2,3},{3,2},{4,5},{5,4},{6,7},{7,6},{8,9},{9,8},{10,11... | collective-permute-start | bytes 393224 | tf_op jit(solution)/shard_map/ppermute | solution.py:25
  16.7 0.7 %copy-start.2 = (bf16[64,1024]{1,0:T(8,128)(2,1)}, bf16[64,1024]{1,0:T(8,128)(2,1)S(1)}, u32[]{:S(2)}) copy-start(bf16[64,1024]{1,0:T(8,128)(2,1)S(1)} %collective-permute-done.3.kvb_ref) | copy-start | bytes 393220
  22.9 1.7 %collective-permute-start.4 = (f32[64,1024]{1,0:T(8,128)}, f32[64,1024]{1,0:T(8,128)S(1)}, u32[]{:S(2)}, u32[]{:S(2)}) collective-permute-start(f32[64,1024]{1,0:T(8,128)} %get-tuple-element.12), channel_id=1, source_target_pairs={{0,1},{1,0},{2,3},{3,2},{4,5},{5,4},{6,7},{7,6},{8,9},{9,8},{10,11... | collective-permute-start | bytes 786440 | tf_op jit(solution)/shard_map/ppermute | solution.py:25
  24.6 5.4 %copy-start.1 = (f32[64,1024]{1,0:T(8,128)S(1)}, f32[64,1024]{1,0:T(8,128)}, u32[]{:S(2)}) copy-start(f32[64,1024]{1,0:T(8,128)} %get-tuple-element.11) | copy-start | bytes 786436
  25.6 4.3 %collective-permute-start.5 = (bf16[32,1024]{1,0:T(8,128)(2,1)S(1)}, bf16[32,1024]{1,0:T(8,128)(2,1)S(1)}, u32[]{:S(2)}, u32[]{:S(2)}) collective-permute-start(bf16[32,1024]{1,0:T(8,128)(2,1)S(1)} %fusion), channel_id=1, source_target_pairs={{0,2},{1,3},{2,0},{3,1},{4,6},{5,7},{6,4},{7,5},{8,10},{9,11},{10,... | collective-permute-start | bytes 196616 | tf_op jit(solution)/shard_map/ppermute | solution.py:25
  30.0 4.0 %collective-permute-start.6 = (bf16[16,1024]{1,0:T(8,128)(2,1)S(1)}, bf16[16,1024]{1,0:T(8,128)(2,1)S(1)}, u32[]{:S(2)}, u32[]{:S(2)}) collective-permute-start(bf16[16,1024]{1,0:T(8,128)(2,1)S(1)} %fusion.2), channel_id=1, source_target_pairs={{0,4},{1,5},{2,6},{3,7},{4,0},{5,1},{6,2},{7,3},{8,12},{9,13},{10,... | collective-permute-start | bytes 98312 | tf_op jit(solution)/shard_map/ppermute | solution.py:25
  34.0 4.9 %collective-permute-start.7 = (f32[8,1024]{1,0:T(8,128)S(1)}, f32[8,1024]{1,0:T(8,128)S(1)}, u32[]{:S(2)}, u32[]{:S(2)}) collective-permute-start(f32[8,1024]{1,0:T(8,128)S(1)} %fusion.4), channel_id=1, source_target_pairs={{0,8},{1,9},{2,10},{3,11},{4,12},{5,13},{6,14},{7,15},{8,0},{9,1},... | collective-permute-start | bytes 98312 | tf_op jit(solution)/shard_map/ppermute | solution.py:25

commit v13 on v8

--- a/solution.py
+++ b/solution.py
@@ -77,52 +77,91 @@
     )
 
 
-def attention_kernel(
-    q_ref, do_ref, kva_ref, kvb_ref, ks_ref, vs_ref, vis_ref, self_ref, live_ref,
-    dq_ref, keep_ref, send_ref, sk_ref, sv_ref,
+def own_stats_kernel(q_ref, do_ref, ks_ref, vs_ref, self_ref, stats_ref):
+    score_scale = HEAD_SIZE ** (-0.5)
+    self_seen = jnp.concatenate([self_ref[...]] * GROUP_HEADS, axis=1) > 0.5
+    for c in range(KEY_HEADS):
+        columns = slice(c * HEAD_SIZE, (c + 1) * HEAD_SIZE)
+        q = stacked_heads(q_ref, c)
+        do = stacked_heads(do_ref, c)
+        ss = jnp.where(self_seen, contract_cols(ks_ref[:, columns], q) * score_scale, masked_score)
+        top = jnp.max(ss, axis=0, keepdims=True)
+        es = jnp.exp(ss - top)
+        gs = contract_cols(vs_ref[:, columns], do)
+        stats_ref[c:c + 1, :] = top
+        stats_ref[KEY_HEADS + c:KEY_HEADS + c + 1, :] = jnp.sum(es, axis=0, keepdims=True)
+        stats_ref[2 * KEY_HEADS + c:2 * KEY_HEADS + c + 1, :] = jnp.sum(
+            es * gs, axis=0, keepdims=True
+        )
+
+
+def document_kernel(
+    q_ref, do_ref, kva_ref, kvb_ref, vis_ref, own_ref, live_ref,
+    keep_ref, send_ref, stats_ref, dsd_ref,
 ):
-    token_rows = q_ref.shape[0]
     width = KEY_HEADS * HEAD_SIZE
     half = kva_ref.shape[0]
     score_scale = HEAD_SIZE ** (-0.5)
     doc_seen = jnp.concatenate([vis_ref[...]] * GROUP_HEADS, axis=1) > 0.5
-    self_seen = jnp.concatenate([self_ref[...]] * GROUP_HEADS, axis=1) > 0.5
     live = jnp.concatenate([live_ref[...]] * GROUP_HEADS, axis=1)
     for c in range(KEY_HEADS):
         columns = slice(c * HEAD_SIZE, (c + 1) * HEAD_SIZE)
         value_columns = slice(width + c * HEAD_SIZE, width + (c + 1) * HEAD_SIZE)
         kd = jnp.concatenate([kva_ref[:, columns], kvb_ref[:, columns]], axis=0)
         vd = jnp.concatenate([kva_ref[:, value_columns], kvb_ref[:, value_columns]], axis=0)
-        ks = ks_ref[:, columns]
-        vs = vs_ref[:, columns]
         q = stacked_heads(q_ref, c)
         do = stacked_heads(do_ref, c)
+        own_top = own_ref[c:c + 1, :]
+        own_total = own_ref[KEY_HEADS + c:KEY_HEADS + c + 1, :]
+        own_weighted = own_ref[2 * KEY_HEADS + c:2 * KEY_HEADS + c + 1, :]
         sd = jnp.where(doc_seen, contract_cols(kd, q) * score_scale, masked_score)
-        ss = jnp.where(self_seen, contract_cols(ks, q) * score_scale, masked_score)
-        top = jnp.maximum(jnp.max(sd, axis=0, keepdims=True), jnp.max(ss, axis=0, keepdims=True))
+        top = jnp.maximum(jnp.max(sd, axis=0, keepdims=True), own_top)
         ed = jnp.exp(sd - top)
-        es = jnp.exp(ss - top)
-        total = jnp.sum(ed, axis=0, keepdims=True) + jnp.sum(es, axis=0, keepdims=True)
+        factor = jnp.exp(own_top - top)
+        gd = contract_cols(vd, do)
+        total = jnp.sum(ed, axis=0, keepdims=True) + own_total * factor
         weight = live / total
+        drift = (jnp.sum(ed * gd, axis=0, keepdims=True) + own_weighted * factor) * weight
         pd = ed * weight
-        ps = es * weight
-        gd = contract_cols(vd, do)
-        gs = contract_cols(vs, do)
-        drift = jnp.sum(pd * gd, axis=0, keepdims=True) + jnp.sum(ps * gs, axis=0, keepdims=True)
         dsd = (pd * (gd - drift)).astype(jnp.bfloat16)
-        dss = (ps * (gs - drift)).astype(jnp.bfloat16)
-        dq = (contract_rows(dsd, kd) + contract_rows(dss, ks)) * score_scale
-        for g in range(GROUP_HEADS):
-            h = c * GROUP_HEADS + g
-            dq_ref[:, h * HEAD_SIZE:(h + 1) * HEAD_SIZE] = dq[
-                g * token_rows:(g + 1) * token_rows
-            ].astype(dq_ref.dtype)
+        dsd_ref[c] = dsd
+        stats_ref[c:c + 1, :] = top
+        stats_ref[KEY_HEADS + c:KEY_HEADS + c + 1, :] = weight
+        stats_ref[2 * KEY_HEADS + c:2 * KEY_HEADS + c + 1, :] = drift
         doc_key = jnp.dot(dsd, q, preferred_element_type=jnp.float32) * score_scale
         doc_value = jnp.dot(pd.astype(jnp.bfloat16), do, preferred_element_type=jnp.float32)
         keep_ref[:, columns] = doc_key[:half]
         send_ref[:, columns] = doc_key[half:].astype(send_ref.dtype)
         keep_ref[:, value_columns] = doc_value[:half]
         send_ref[:, value_columns] = doc_value[half:].astype(send_ref.dtype)
+
+
+def response_kernel(
+    q_ref, do_ref, kva_ref, kvb_ref, ks_ref, vs_ref, self_ref, stats_ref, dsd_ref,
+    dq_ref, sk_ref, sv_ref,
+):
+    token_rows = q_ref.shape[0]
+    score_scale = HEAD_SIZE ** (-0.5)
+    self_seen = jnp.concatenate([self_ref[...]] * GROUP_HEADS, axis=1) > 0.5
+    for c in range(KEY_HEADS):
+        columns = slice(c * HEAD_SIZE, (c + 1) * HEAD_SIZE)
+        kd = jnp.concatenate([kva_ref[:, columns], kvb_ref[:, columns]], axis=0)
+        ks = ks_ref[:, columns]
+        q = stacked_heads(q_ref, c)
+        do = stacked_heads(do_ref, c)
+        top = stats_ref[c:c + 1, :]
+        weight = stats_ref[KEY_HEADS + c:KEY_HEADS + c + 1, :]
+        drift = stats_ref[2 * KEY_HEADS + c:2 * KEY_HEADS + c + 1, :]
+        ss = jnp.where(self_seen, contract_cols(ks, q) * score_scale, masked_score)
+        ps = jnp.exp(ss - top) * weight
+        gs = contract_cols(vs_ref[:, columns], do)
+        dss = (ps * (gs - drift)).astype(jnp.bfloat16)
+        dq = (contract_rows(dsd_ref[c], kd) + contract_rows(dss, ks)) * score_scale
+        for g in range(GROUP_HEADS):
+            h = c * GROUP_HEADS + g
+            dq_ref[:, h * HEAD_SIZE:(h + 1) * HEAD_SIZE] = dq[
+                g * token_rows:(g + 1) * token_rows
+            ].astype(dq_ref.dtype)
         sk_ref[:, columns] = (
             jnp.dot(dss, q, preferred_element_type=jnp.float32) * score_scale
         ).astype(sk_ref.dtype)
@@ -172,25 +211,30 @@
     doc_visible = (jnp.take(row_masks.T, global_rows // block_rows, axis=0) == 1).astype(
         jnp.float32
     )
-    query_gradient, doc_keep, doc_send, self_key, self_value = pl.pallas_call(
-        attention_kernel,
+    stacked_rows = GROUP_HEADS * token_rows
+    own_stats = pl.pallas_call(
+        own_stats_kernel,
+        out_shape=jax.ShapeDtypeStruct((3 * KEY_HEADS, stacked_rows), jnp.float32),
+    )(queries, grad_out, response_keys, response_values, self_visible)
+    doc_keep, doc_send, row_stats, doc_dscore = pl.pallas_call(
+        document_kernel,
+        out_shape=(
+            jax.ShapeDtypeStruct((half_rows, 2 * key_value_width), jnp.float32),
+            jax.ShapeDtypeStruct((half_rows, 2 * key_value_width), jnp.bfloat16),
+            jax.ShapeDtypeStruct((3 * KEY_HEADS, stacked_rows), jnp.float32),
+            jax.ShapeDtypeStruct((KEY_HEADS, doc_rows, stacked_rows), jnp.bfloat16),
+        ),
+    )(queries, grad_out, doc_mine, doc_other, doc_visible, own_stats, live)
+    query_gradient, self_key, self_value = pl.pallas_call(
+        response_kernel,
         out_shape=(
             jax.ShapeDtypeStruct(queries.shape, jnp.bfloat16),
-            jax.ShapeDtypeStruct((half_rows, 2 * key_value_width), jnp.float32),
-            jax.ShapeDtypeStruct((half_rows, 2 * key_value_width), jnp.bfloat16),
             jax.ShapeDtypeStruct(response_keys.shape, jnp.bfloat16),
             jax.ShapeDtypeStruct(response_values.shape, jnp.bfloat16),
         ),
     )(
-        queries,
-        grad_out,
-        doc_mine,
-        doc_other,
-        response_keys,
-        response_values,
-        doc_visible,
-        self_visible,
-        live,
+        queries, grad_out, doc_mine, doc_other, response_keys, response_values,
+        self_visible, row_stats, doc_dscore,
     )
     summed = scatter_sum_rows(doc_keep, doc_send, "resp")
     return (

time: 38.6 us -> 40.2 us (1.041)
  Pallas kernels: 5.57 us -> 10.8 us
  starting transfers between devices: 14.9 us -> 13 us
  waiting for transfers between devices: 11.3 us -> 9.62 us
    pallas_call x1 -> x3, Pallas kernels: 5.57 us -> 10.8 us  [the longest x1 4.41 us: per_device(): pl.pallas_call(response_kernel, out_shape=(jax.ShapeDtypeStruct(queries.s...]
    ppermute x8, starting transfers between devices: 14.9 us -> 13 us  [swap_with(): return lax.ppermute(block, axis_name, pairs)]
    ppermute x8, waiting for transfers between devices: 11.3 us -> 9.62 us  [swap_with(): return lax.ppermute(block, axis_name, pairs)]
  transfers between devices with their start and end apart: 8 -> 8, of which waited for: 8 -> 6; matrix products, arithmetic and copies ran while one was open for 6% -> 6% of each run, Pallas kernels for 0% -> 18%
where the time goes in v13:
time: 40.2 us; the launch traced here: 39.9 us
  starting transfers between devices  13 us (32%)
  Pallas kernels  10.8 us (27%)
  waiting for transfers between devices  9.62 us (24%)
  local copies, waits for them, and re-layouts  4.36 us (11%)
  other arithmetic  1.36 us (3%)
  between operations  0.72 us (2%)
    ppermute x8, starting transfers between devices, swap_with(): return lax.ppermute(block, axis_name, pairs)  13 us
    ppermute x8, waiting for transfers between devices, swap_with(): return lax.ppermute(block, axis_name, pairs)  9.62 us
    pallas_call x1, Pallas kernels, per_device(): pl.pallas_call(response_kernel, out_shape=(jax.ShapeDtypeStruct(queries.s...  4.41 us
    pallas_call x1, Pallas kernels, per_device(): pl.pallas_call(document_kernel, out_shape=(jax.ShapeDtypeStruct((half_row...  3.74 us
    unnamed x18, local copies, waits for them, and re-layouts  2.79 us
    pallas_call x1, Pallas kernels, per_device(): pl.pallas_call(own_stats_kernel, out_shape=jax.ShapeDtypeStruct((3 * KEY_...  2.66 us
  transfers between devices with their start and end apart: 8, of which 6 were waited for; matrix products, arithmetic and copies ran while one was open for 6% of the time, Pallas kernels for 18%

profile of v13, /device:TPU:0, one launch (start us, length us, event | category | flops | bytes accessed | tf_op | source)
XLA Modules:
  0.0 39.9 jit_solution(9350459235651040880)
XLA Ops:
  0.6 0.7 %constant_dynamic-update-slice_fusion.1 = bf16[8,1024]{1,0:T(8,128)(2,1)S(1)} fusion(bf16[8,512]{1,0:T(8,128)(2,1)} %param.14), kind=kLoop, calls=%fused_computation.22 | loop fusion | bytes 16384
  1.4 4.0 %collective-permute-start = (bf16[8,1024]{1,0:T(8,128)(2,1)S(1)}, bf16[8,1024]{1,0:T(8,128)(2,1)S(1)}, u32[]{:S(2)}, u32[]{:S(2)}) collective-permute-start(bf16[8,1024]{1,0:T(8,128)(2,1)S(1)} %constant_dynamic-update-slice_fusion), channel_id=1, source_target_pairs={{0,8},{1,9},{2,10},{3,11},{4,12},{5,13},{6,14},{7,15},{8,0},{9,1},... | collective-permute-start | bytes 49160 | tf_op jit(solution)/shard_map/ppermute | solution.py:25
  5.4 0.7 %copy-done.5 = s32[128]{0:T(128)S(1)} copy-done((s32[128]{0:T(128)S(1)}, s32[128]{0:T(128)}, u32[]{:S(2)}) %copy-start.5) | copy-done | bytes 536
  6.0 0.0 copy-done.6
  6.1 1.0 %collective-permute-done = bf16[8,1024]{1,0:T(8,128)(2,1)S(1)} collective-permute-done((bf16[8,1024]{1,0:T(8,128)(2,1)S(1)}, bf16[8,1024]{1,0:T(8,128)(2,1)S(1)}, u32[]{:S(2)}, u32[]{:S(2)}) %collective-permute-start) | collective-permute-done | bytes 16416 | tf_op jit(solution)/shard_map/ppermute | solution.py:25
  7.1 1.9 %collective-permute-start.1 = (bf16[16,1024]{1,0:T(8,128)(2,1)S(1)}, bf16[16,1024]{1,0:T(8,128)(2,1)S(1)}, u32[]{:S(2)}, u32[]{:S(2)}) collective-permute-start(bf16[16,1024]{1,0:T(8,128)(2,1)S(1)} %pad_maximum_fusion.2), channel_id=1, source_target_pairs={{0,4},{1,5},{2,6},{3,7},{4,0},{5,1},{6,2},{7,3},{8,12},{9,13},{10,... | collective-permute-start | bytes 98312 | tf_op jit(solution)/shard_map/ppermute | solution.py:25
  9.0 0.7 %copy-done.4 = s32[2,16]{1,0:T(2,128)S(1)} copy-done((s32[2,16]{1,0:T(2,128)S(1)}, s32[2,16]{1,0:T(2,128)}, u32[]{:S(2)}) %copy-start.4) | copy-done | bytes 152
  9.7 0.1 copy.16
  9.8 0.1 broadcast_in_dim.20
  9.9 0.1 reshape.56
  9.9 0.6 %gather_fusion = s32[128,128]{1,0:T(8,128)S(1)} fusion(s32[16,128]{1,0:T(8,128)S(1)} %bitcast.3, s32[1024]{0:T(1024)S(1)} %pad_clamp_fusion), kind=kCustom, calls=%fused_computation | custom fusion | bytes 131584 | tf_op jit(solution)/shard_map/jit(_take)/gather | solution.py:211
  10.6 0.4 %collective-permute-done.1 = bf16[16,1024]{1,0:T(8,128)(2,1)S(1)} collective-permute-done((bf16[16,1024]{1,0:T(8,128)(2,1)S(1)}, bf16[16,1024]{1,0:T(8,128)(2,1)S(1)}, u32[]{:S(2)}, u32[]{:S(2)}) %collective-permute-start.1) | collective-permute-done | bytes 32800 | tf_op jit(solution)/shard_map/ppermute | solution.py:25
  11.0 1.9 %collective-permute-start.2 = (bf16[32,1024]{1,0:T(8,128)(2,1)S(1)}, bf16[32,1024]{1,0:T(8,128)(2,1)S(1)}, u32[]{:S(2)}, u32[]{:S(2)}) collective-permute-start(bf16[32,1024]{1,0:T(8,128)(2,1)S(1)} %pad_maximum_fusion.1), channel_id=1, source_target_pairs={{0,2},{1,3},{2,0},{3,1},{4,6},{5,7},{6,4},{7,5},{8,10},{9,11},{10,... | collective-permute-start | bytes 196616 | tf_op jit(solution)/shard_map/ppermute | solution.py:25
  12.9 0.7 %fusion.3.vis_ref = f32[128,128]{1,0:T(8,128)} fusion(s32[128,128]{1,0:T(8,128)S(1)} %gather_fusion, pred[128]{0:T(512)(128)(4,1)S(1)} %get-tuple-element.19), kind=kLoop, calls=%fused_computation.9 | loop fusion | flops 49152 | bytes 131200 | tf_op jit(solution)/shard_map/convert_element_type | solution.py:211
  13.6 0.1 broadcast_in_dim.23
  13.7 0.1 reshape.57
  13.8 2.7 %shard_map.146.own_ref = f32[12,640]{1,0:T(8,128)} custom-call(bf16[128,2560]{1,0:T(8,128)(2,1)} %q_ref.5, bf16[128,2560]{1,0:T(8,128)(2,1)} %do_ref.5, bf16[128,512]{1,0:T(8,128)(2,1)} %ks_ref.3, bf16[128,512]{1,0:T(8,128)(2,1)} %vs_ref.3, f32[128,128]{1,0:T(8,128)} %constant.59.clone.self_ref), custom_call_target="tpu_custom_call" | custom-call | tf_op jit(solution)/shard_map/pallas_call | solution.py:215
  16.5 0.1 collective-permute-start.3
  16.6 0.5 %compare_convert_fusion.live_ref = f32[1,128]{1,0:T(1,128)} fusion(s32[1,128]{1,0:T(1,128)S(1)} %reshape.57), kind=kLoop, calls=%fused_computation.24 | loop fusion | flops 1024 | bytes 1024 | tf_op jit(solution)/shard_map/convert_element_type | solution.py:191
  17.1 0.8 %collective-permute-done.3.kvb_ref = bf16[64,1024]{1,0:T(8,128)(2,1)S(1)} collective-permute-done((bf16[64,1024]{1,0:T(8,128)(2,1)S(1)}, bf16[64,1024]{1,0:T(8,128)(2,1)S(1)}, u32[]{:S(2)}, u32[]{:S(2)}) %collective-permute-start.3) | collective-permute-done | bytes 131104 | tf_op jit(solution)/shard_map/ppermute | solution.py:25
  17.9 0.6 %copy-done.1 = bf16[64,1024]{1,0:T(8,128)(2,1)} copy-done((bf16[64,1024]{1,0:T(8,128)(2,1)}, bf16[64,1024]{1,0:T(8,128)(2,1)S(1)}, u32[]{:S(2)}) %copy-start.1) | copy-done | bytes 131096
  18.5 3.7 %shard_map.147 = (f32[64,1024]{1,0:T(8,128)}, bf16[64,1024]{1,0:T(8,128)(2,1)}, f32[12,640]{1,0:T(8,128)}, bf16[4,128,640]{2,1,0:T(8,128)(2,1)}) custom-call(bf16[128,2560]{1,0:T(8,128)(2,1)} %q_ref.5, bf16[128,2560]{1,0:T(8,128)(2,1)} %do_ref.5, bf16[64,1024]{1,0:T(8,128)(2,1)} %copy-done, bf16[64,1024]{1,0:T(8,128)(2,1)} %copy-done.1, ...), custom_call_target="tpu_custom_call" | custom-call | tf_op jit(solution)/shard_map/pallas_call | solution.py:219
  22.3 0.1 collective-permute-start.4
  22.4 1.4 %collective-permute-done.4 = bf16[64,1024]{1,0:T(8,128)(2,1)S(1)} collective-permute-done((bf16[64,1024]{1,0:T(8,128)(2,1)}, bf16[64,1024]{1,0:T(8,128)(2,1)S(1)}, u32[]{:S(2)}, u32[]{:S(2)}) %collective-permute-start.4) | collective-permute-done | bytes 131104 | tf_op jit(solution)/shard_map/ppermute | solution.py:25
  23.9 0.8 %collective-permute-start.5 = (bf16[32,1024]{1,0:T(8,128)(2,1)S(1)}, bf16[32,1024]{1,0:T(8,128)(2,1)S(1)}, u32[]{:S(2)}, u32[]{:S(2)}) collective-permute-start(bf16[32,1024]{1,0:T(8,128)(2,1)S(1)} %fusion), channel_id=1, source_target_pairs={{0,2},{1,3},{2,0},{3,1},{4,6},{5,7},{6,4},{7,5},{8,10},{9,11},{10,... | collective-permute-start | bytes 196616 | tf_op jit(solution)/shard_map/ppermute | solution.py:25
  24.7 3.5 %collective-permute-done.5 = bf16[32,1024]{1,0:T(8,128)(2,1)S(1)} collective-permute-done((bf16[32,1024]{1,0:T(8,128)(2,1)S(1)}, bf16[32,1024]{1,0:T(8,128)(2,1)S(1)}, u32[]{:S(2)}, u32[]{:S(2)}) %collective-permute-start.5) | collective-permute-done | bytes 65568 | tf_op jit(solution)/shard_map/ppermute | solution.py:25
  28.3 1.6 %collective-permute-start.6 = (bf16[16,1024]{1,0:T(8,128)(2,1)S(1)}, bf16[16,1024]{1,0:T(8,128)(2,1)S(1)}, u32[]{:S(2)}, u32[]{:S(2)}) collective-permute-start(bf16[16,1024]{1,0:T(8,128)(2,1)S(1)} %fusion.2), channel_id=1, source_target_pairs={{0,4},{1,5},{2,6},{3,7},{4,0},{5,1},{6,2},{7,3},{8,12},{9,13},{10,... | collective-permute-start | bytes 98312 | tf_op jit(solution)/shard_map/ppermute | solution.py:25
  29.9 2.4 %collective-permute-done.6 = bf16[16,1024]{1,0:T(8,128)(2,1)S(1)} collective-permute-done((bf16[16,1024]{1,0:T(8,128)(2,1)S(1)}, bf16[16,1024]{1,0:T(8,128)(2,1)S(1)}, u32[]{:S(2)}, u32[]{:S(2)}) %collective-permute-start.6) | collective-permute-done | bytes 32800 | tf_op jit(solution)/shard_map/ppermute | solution.py:25
  32.3 2.6 %collective-permute-start.7 = (bf16[8,1024]{1,0:T(8,128)(2,1)S(1)}, bf16[8,1024]{1,0:T(8,128)(2,1)S(1)}, u32[]{:S(2)}, u32[]{:S(2)}) collective-permute-start(bf16[8,1024]{1,0:T(8,128)(2,1)S(1)} %fusion.5), channel_id=1, source_target_pairs={{0,8},{1,9},{2,10},{3,11},{4,12},{5,13},{6,14},{7,15},{8,0},{9,1},... | collective-permute-start | bytes 49160 | tf_op jit(solution)/shard_map/ppermute | solution.py:25
  34.9 4.4 %shard_map.148 = (bf16[128,2560]{1,0:T(8,128)(2,1)}, bf16[128,512]{1,0:T(8,128)(2,1)}, bf16[128,512]{1,0:T(8,128)(2,1)}) custom-call(bf16[128,2560]{1,0:T(8,128)(2,1)} %q_ref.5, bf16[128,2560]{1,0:T(8,128)(2,1)} %do_ref.5, bf16[64,1024]{1,0:T(8,128)(2,1)} %copy-done, bf16[64,1024]{1,0:T(8,128)(2,1)} %copy-done.1, bf16[128,512]{1,0:T(8,128)(2,1)} %ks_ref.3, ...), custom_call_target="tpu_custom_call" | custom-call | tf_op jit(solution)/shard_map/pallas_call | solution.py:228
  39.3 0.0 collective-permute-done.7
  39.3 0.6 %fusion.8 = (bf16[8,512]{1,0:T(8,128)(2,1)}, bf16[8,512]{1,0:T(8,128)(2,1)}) fusion(bf16[8,1024]{1,0:T(8,128)(2,1)S(1)} %fusion.7), kind=kLoop, calls=%fused_computation.31 | loop fusion | bytes 32768 | tf_op jit(solution)/shard_map/slice | solution.py:243
  (26 shorter events, 0.2 us)
Async XLA Ops:
  0.6 0.7 %copy-start.3 = (bf16[8,512]{1,0:T(8,128)(2,1)S(1)}, bf16[8,512]{1,0:T(8,128)(2,1)}, u32[]{:S(2)}) copy-start(bf16[8,512]{1,0:T(8,128)(2,1)} %param.15) | copy-start | bytes 24580
  1.4 5.8 %collective-permute-start = (bf16[8,1024]{1,0:T(8,128)(2,1)S(1)}, bf16[8,1024]{1,0:T(8,128)(2,1)S(1)}, u32[]{:S(2)}, u32[]{:S(2)}) collective-permute-start(bf16[8,1024]{1,0:T(8,128)(2,1)S(1)} %constant_dynamic-update-slice_fusion), channel_id=1, source_target_pairs={{0,8},{1,9},{2,10},{3,11},{4,12},{5,13},{6,14},{7,15},{8,0},{9,1},... | collective-permute-start | bytes 49160 | tf_op jit(solution)/shard_map/ppermute | solution.py:25
  5.4 0.7 %copy-start.5 = (s32[128]{0:T(128)S(1)}, s32[128]{0:T(128)}, u32[]{:S(2)}) copy-start(s32[128]{0:T(128)} %constant.60.clone) | copy-start | bytes 1540
  5.4 0.7 %copy-start.6 = (s32[128]{0:T(128)S(1)}, s32[128]{0:T(128)}, u32[]{:S(2)}) copy-start(s32[128]{0:T(128)} %constant.61.clone) | copy-start | bytes 1540
  7.1 3.9 %collective-permute-start.1 = (bf16[16,1024]{1,0:T(8,128)(2,1)S(1)}, bf16[16,1024]{1,0:T(8,128)(2,1)S(1)}, u32[]{:S(2)}, u32[]{:S(2)}) collective-permute-start(bf16[16,1024]{1,0:T(8,128)(2,1)S(1)} %pad_maximum_fusion.2), channel_id=1, source_target_pairs={{0,4},{1,5},{2,6},{3,7},{4,0},{5,1},{6,2},{7,3},{8,12},{9,13},{10,... | collective-permute-start | bytes 98312 | tf_op jit(solution)/shard_map/ppermute | solution.py:25
  9.0 0.7 %copy-start.4 = (s32[2,16]{1,0:T(2,128)S(1)}, s32[2,16]{1,0:T(2,128)}, u32[]{:S(2)}) copy-start(s32[2,16]{1,0:T(2,128)} %param.18) | copy-start | bytes 388
  11.0 5.4 %collective-permute-start.2 = (bf16[32,1024]{1,0:T(8,128)(2,1)S(1)}, bf16[32,1024]{1,0:T(8,128)(2,1)S(1)}, u32[]{:S(2)}, u32[]{:S(2)}) collective-permute-start(bf16[32,1024]{1,0:T(8,128)(2,1)S(1)} %pad_maximum_fusion.1), channel_id=1, source_target_pairs={{0,2},{1,3},{2,0},{3,1},{4,6},{5,7},{6,4},{7,5},{8,10},{9,11},{10,... | collective-permute-start | bytes 196616 | tf_op jit(solution)/shard_map/ppermute | solution.py:25
  12.9 0.7 %copy-start.7 = (s32[2]{0:T(128)S(1)}, s32[2]{0:T(128)}, u32[]{:S(2)}) copy-start(s32[2]{0:T(128)} %param.17) | copy-start | bytes 28
  16.5 1.4 %copy-start = (bf16[64,1024]{1,0:T(8,128)(2,1)}, bf16[64,1024]{1,0:T(8,128)(2,1)S(1)}, u32[]{:S(2)}) copy-start(bf16[64,1024]{1,0:T(8,128)(2,1)S(1)} %pad_maximum_fusion.kva_ref) | copy-start | bytes 393220
  16.5 1.4 %collective-permute-start.3 = (bf16[64,1024]{1,0:T(8,128)(2,1)S(1)}, bf16[64,1024]{1,0:T(8,128)(2,1)S(1)}, u32[]{:S(2)}, u32[]{:S(2)}) collective-permute-start(bf16[64,1024]{1,0:T(8,128)(2,1)S(1)} %pad_maximum_fusion.kva_ref), channel_id=1, source_target_pairs={{0,1},{1,0},{2,3},{3,2},{4,5},{5,4},{6,7},{7,6},{8,9},{9,8},{10,11... | collective-permute-start | bytes 393224 | tf_op jit(solution)/shard_map/ppermute | solution.py:25
  17.9 0.6 %copy-start.1 = (bf16[64,1024]{1,0:T(8,128)(2,1)}, bf16[64,1024]{1,0:T(8,128)(2,1)S(1)}, u32[]{:S(2)}) copy-start(bf16[64,1024]{1,0:T(8,128)(2,1)S(1)} %collective-permute-done.3.kvb_ref) | copy-start | bytes 393220
  22.3 1.6 %copy-start.2 = (f32[64,1024]{1,0:T(8,128)S(1)}, f32[64,1024]{1,0:T(8,128)}, u32[]{:S(2)}) copy-start(f32[64,1024]{1,0:T(8,128)} %get-tuple-element.15) | copy-start | bytes 786436
  22.3 1.6 %collective-permute-start.4 = (bf16[64,1024]{1,0:T(8,128)(2,1)}, bf16[64,1024]{1,0:T(8,128)(2,1)S(1)}, u32[]{:S(2)}, u32[]{:S(2)}) collective-permute-start(bf16[64,1024]{1,0:T(8,128)(2,1)} %get-tuple-element.16), channel_id=1, source_target_pairs={{0,1},{1,0},{2,3},{3,2},{4,5},{5,4},{6,7},{7,6},{8,9},{9,8},{10,11... | collective-permute-start | bytes 393224 | tf_op jit(solution)/shard_map/ppermute | solution.py:25
  23.9 4.3 %collective-permute-start.5 = (bf16[32,1024]{1,0:T(8,128)(2,1)S(1)}, bf16[32,1024]{1,0:T(8,128)(2,1)S(1)}, u32[]{:S(2)}, u32[]{:S(2)}) collective-permute-start(bf16[32,1024]{1,0:T(8,128)(2,1)S(1)} %fusion), channel_id=1, source_target_pairs={{0,2},{1,3},{2,0},{3,1},{4,6},{5,7},{6,4},{7,5},{8,10},{9,11},{10,... | collective-permute-start | bytes 196616 | tf_op jit(solution)/shard_map/ppermute | solution.py:25
  28.3 4.0 %collective-permute-start.6 = (bf16[16,1024]{1,0:T(8,128)(2,1)S(1)}, bf16[16,1024]{1,0:T(8,128)(2,1)S(1)}, u32[]{:S(2)}, u32[]{:S(2)}) collective-permute-start(bf16[16,1024]{1,0:T(8,128)(2,1)S(1)} %fusion.2), channel_id=1, source_target_pairs={{0,4},{1,5},{2,6},{3,7},{4,0},{5,1},{6,2},{7,3},{8,12},{9,13},{10,... | collective-permute-start | bytes 98312 | tf_op jit(solution)/shard_map/ppermute | solution.py:25
  32.3 7.0 %collective-permute-start.7 = (bf16[8,1024]{1,0:T(8,128)(2,1)S(1)}, bf16[8,1024]{1,0:T(8,128)(2,1)S(1)}, u32[]{:S(2)}, u32[]{:S(2)}) collective-permute-start(bf16[8,1024]{1,0:T(8,128)(2,1)S(1)} %fusion.5), channel_id=1, source_target_pairs={{0,8},{1,9},{2,10},{3,11},{4,12},{5,13},{6,14},{7,15},{8,0},{9,1},... | collective-permute-start | bytes 49160 | tf_op jit(solution)/shard_map/ppermute | solution.py:25

commit v14 on v11

--- a/solution.py
+++ b/solution.py
@@ -3,6 +3,7 @@
 import jax.numpy as jnp
 from jax import lax
 from jax.experimental import pallas as pl
+from jax.experimental.pallas import tpu as pltpu
 from jax.sharding import PartitionSpec as P
 
 KEY_HEADS = 4
@@ -49,9 +50,9 @@
         if bit > 0:
             split = pending[0].shape[0] // 2
             send = sum(part[split:] for part in pending[1:])
-            send = pending[0][split:] + send
+            send = (pending[0][split:] + send).astype(jnp.bfloat16)
             pending = [part[:split] for part in pending]
-        pending.append(swap_with(send, axis_name, size, bit))
+        pending.append(swap_with(send, axis_name, size, bit).astype(jnp.float32))
     return sum(pending[1:], pending[0])
 
 
@@ -78,10 +79,22 @@
 
 
 def attention_kernel(
-    q_ref, do_ref, kva_ref, kvb_ref, ks_ref, vs_ref, vis_ref, self_ref, live_ref,
-    dq_ref, keep_ref, send_ref, sk_ref, sv_ref,
+    q_hbm, do_hbm, kva_ref, kvb_ref, ks_ref, vs_ref, vis_ref, self_ref, live_ref,
+    dq_ref, keep_ref, send_ref, sk_ref, sv_ref, q_buf, do_buf, arrivals,
 ):
-    token_rows = q_ref.shape[0]
+    token_rows = q_buf.shape[1]
+    head_block = GROUP_HEADS * HEAD_SIZE
+
+    def fetch(c, slot):
+        block = slice(c * head_block, (c + 1) * head_block)
+        return (
+            pltpu.make_async_copy(q_hbm.at[:, block], q_buf.at[slot], arrivals.at[0, slot]),
+            pltpu.make_async_copy(do_hbm.at[:, block], do_buf.at[slot], arrivals.at[1, slot]),
+        )
+
+    pending = fetch(0, 0)
+    for copy in pending:
+        copy.start()
     width = KEY_HEADS * HEAD_SIZE
     half = kva_ref.shape[0]
     doc_rows = 2 * half
@@ -91,6 +104,14 @@
     ) > 0.5
     live = jnp.concatenate([live_ref[...]] * GROUP_HEADS, axis=1)
     for c in range(KEY_HEADS):
+        slot = c % 2
+        current = pending
+        if c + 1 < KEY_HEADS:
+            pending = fetch(c + 1, 1 - slot)
+            for copy in pending:
+                copy.start()
+        for copy in current:
+            copy.wait()
         columns = slice(c * HEAD_SIZE, (c + 1) * HEAD_SIZE)
         value_columns = slice(width + c * HEAD_SIZE, width + (c + 1) * HEAD_SIZE)
         keys = jnp.concatenate(
@@ -99,8 +120,8 @@
         values = jnp.concatenate(
             [kva_ref[:, value_columns], kvb_ref[:, value_columns], vs_ref[:, columns]], axis=0
         )
-        q = stacked_heads(q_ref, c)
-        do = stacked_heads(do_ref, c)
+        q = stacked_heads(q_buf.at[slot], 0)
+        do = stacked_heads(do_buf.at[slot], 0)
         score = jnp.where(seen, contract_cols(keys, q) * score_scale, masked_score)
         top = jnp.max(score, axis=0, keepdims=True)
         grown = jnp.exp(score - top)
@@ -117,9 +138,9 @@
         key_total = jnp.dot(dscore, q, preferred_element_type=jnp.float32) * score_scale
         value_total = jnp.dot(prob.astype(jnp.bfloat16), do, preferred_element_type=jnp.float32)
         keep_ref[:, columns] = key_total[:half]
-        send_ref[:, columns] = key_total[half:doc_rows]
+        send_ref[:, columns] = key_total[half:doc_rows].astype(send_ref.dtype)
         keep_ref[:, value_columns] = value_total[:half]
-        send_ref[:, value_columns] = value_total[half:doc_rows]
+        send_ref[:, value_columns] = value_total[half:doc_rows].astype(send_ref.dtype)
         sk_ref[:, columns] = key_total[doc_rows:].astype(sk_ref.dtype)
         sv_ref[:, columns] = value_total[doc_rows:].astype(sv_ref.dtype)
 
@@ -170,10 +191,17 @@
         out_shape=(
             jax.ShapeDtypeStruct(queries.shape, jnp.bfloat16),
             jax.ShapeDtypeStruct((half_rows, 2 * key_value_width), jnp.float32),
-            jax.ShapeDtypeStruct((half_rows, 2 * key_value_width), jnp.float32),
+            jax.ShapeDtypeStruct((half_rows, 2 * key_value_width), jnp.bfloat16),
             jax.ShapeDtypeStruct(response_keys.shape, jnp.bfloat16),
             jax.ShapeDtypeStruct(response_values.shape, jnp.bfloat16),
         ),
+        in_specs=[pl.BlockSpec(memory_space=pl.ANY)] * 2
+        + [pl.BlockSpec(memory_space=pltpu.VMEM)] * 7,
+        scratch_shapes=[
+            pltpu.VMEM((2, token_rows, GROUP_HEADS * HEAD_SIZE), jnp.bfloat16),
+            pltpu.VMEM((2, token_rows, GROUP_HEADS * HEAD_SIZE), jnp.bfloat16),
+            pltpu.SemaphoreType.DMA((2, 2)),
+        ],
     )(
         queries,
         grad_out,

time: 41.5 us -> 39.9 us (0.961)
  waiting for transfers between devices: 13.7 us -> 11.4 us
  Pallas kernels: 5.48 us -> 6.76 us
  other arithmetic: 2.22 us -> 1.37 us
    ppermute x8, waiting for transfers between devices: 13.7 us -> 11.4 us  [swap_with(): return lax.ppermute(block, axis_name, pairs)]
    pallas_call x1, Pallas kernels: 5.48 us -> 6.76 us  [per_device(): pl.pallas_call(attention_kernel, out_shape=(jax.ShapeDtypeStruct(queries....]
    add x3 -> x0, other arithmetic: 0.95 us -> none  [scatter_sum_rows(): send = pending[0][split:] + send]
where the time goes in v14:
time: 39.9 us; the launch traced here: 39.5 us
  starting transfers between devices  15 us (38%)
  waiting for transfers between devices  11.4 us (29%)
  Pallas kernels  6.76 us (17%)
  local copies, waits for them, and re-layouts  4.36 us (11%)
  other arithmetic  1.37 us (3%)
  between operations  0.73 us (2%)
    ppermute x8, starting transfers between devices, swap_with(): return lax.ppermute(block, axis_name, pairs)  15 us
    ppermute x8, waiting for transfers between devices, swap_with(): return lax.ppermute(block, axis_name, pairs)  11.4 us
    pallas_call x1, Pallas kernels, per_device(): pl.pallas_call(attention_kernel, out_shape=(jax.ShapeDtypeStruct(queries....  6.76 us
    unnamed x18, local copies, waits for them, and re-layouts  2.79 us
  transfers between devices with their start and end apart: 8, of which 8 were waited for; matrix products, arithmetic and copies ran while one was open for 6% of the time, Pallas kernels for 0%

profile of v14, /device:TPU:0, one launch (start us, length us, event | category | flops | bytes accessed | tf_op | source)
XLA Modules:
  0.0 39.5 jit_solution(3257185914117734466)
XLA Ops:
  0.6 0.7 %constant_dynamic-update-slice_fusion.1 = bf16[8,1024]{1,0:T(8,128)(2,1)S(1)} fusion(bf16[8,512]{1,0:T(8,128)(2,1)} %param.14), kind=kLoop, calls=%fused_computation.22 | loop fusion | bytes 16384
  1.3 0.0 copy-done.3
  1.4 4.0 %collective-permute-start = (bf16[8,1024]{1,0:T(8,128)(2,1)S(1)}, bf16[8,1024]{1,0:T(8,128)(2,1)S(1)}, u32[]{:S(2)}, u32[]{:S(2)}) collective-permute-start(bf16[8,1024]{1,0:T(8,128)(2,1)S(1)} %constant_dynamic-update-slice_fusion), channel_id=1, source_target_pairs={{0,8},{1,9},{2,10},{3,11},{4,12},{5,13},{6,14},{7,15},{8,0},{9,1},... | collective-permute-start | bytes 49160 | tf_op jit(solution)/shard_map/ppermute | solution.py:26
  5.4 0.7 %copy-done.5 = s32[128]{0:T(128)S(1)} copy-done((s32[128]{0:T(128)S(1)}, s32[128]{0:T(128)}, u32[]{:S(2)}) %copy-start.5) | copy-done | bytes 536
  6.0 0.0 copy-done.6
  6.1 1.0 %collective-permute-done = bf16[8,1024]{1,0:T(8,128)(2,1)S(1)} collective-permute-done((bf16[8,1024]{1,0:T(8,128)(2,1)S(1)}, bf16[8,1024]{1,0:T(8,128)(2,1)S(1)}, u32[]{:S(2)}, u32[]{:S(2)}) %collective-permute-start) | collective-permute-done | bytes 16416 | tf_op jit(solution)/shard_map/ppermute | solution.py:26
  7.1 1.9 %collective-permute-start.1 = (bf16[16,1024]{1,0:T(8,128)(2,1)S(1)}, bf16[16,1024]{1,0:T(8,128)(2,1)S(1)}, u32[]{:S(2)}, u32[]{:S(2)}) collective-permute-start(bf16[16,1024]{1,0:T(8,128)(2,1)S(1)} %pad_maximum_fusion.2), channel_id=1, source_target_pairs={{0,4},{1,5},{2,6},{3,7},{4,0},{5,1},{6,2},{7,3},{8,12},{9,13},{10,... | collective-permute-start | bytes 98312 | tf_op jit(solution)/shard_map/ppermute | solution.py:26
  9.0 0.7 %copy-done.4 = s32[2,16]{1,0:T(2,128)S(1)} copy-done((s32[2,16]{1,0:T(2,128)S(1)}, s32[2,16]{1,0:T(2,128)}, u32[]{:S(2)}) %copy-start.4) | copy-done | bytes 152
  9.7 0.1 copy.16
  9.8 0.1 broadcast_in_dim.20
  9.9 0.1 reshape.56
  9.9 0.6 %gather_fusion = s32[128,128]{1,0:T(8,128)S(1)} fusion(s32[16,128]{1,0:T(8,128)S(1)} %bitcast.3, s32[1024]{0:T(1024)S(1)} %pad_clamp_fusion), kind=kCustom, calls=%fused_computation | custom fusion | bytes 131584 | tf_op jit(solution)/shard_map/jit(_take)/gather | solution.py:186
  10.6 0.4 %collective-permute-done.1 = bf16[16,1024]{1,0:T(8,128)(2,1)S(1)} collective-permute-done((bf16[16,1024]{1,0:T(8,128)(2,1)S(1)}, bf16[16,1024]{1,0:T(8,128)(2,1)S(1)}, u32[]{:S(2)}, u32[]{:S(2)}) %collective-permute-start.1) | collective-permute-done | bytes 32800 | tf_op jit(solution)/shard_map/ppermute | solution.py:26
  11.0 1.9 %collective-permute-start.2 = (bf16[32,1024]{1,0:T(8,128)(2,1)S(1)}, bf16[32,1024]{1,0:T(8,128)(2,1)S(1)}, u32[]{:S(2)}, u32[]{:S(2)}) collective-permute-start(bf16[32,1024]{1,0:T(8,128)(2,1)S(1)} %pad_maximum_fusion.1), channel_id=1, source_target_pairs={{0,2},{1,3},{2,0},{3,1},{4,6},{5,7},{6,4},{7,5},{8,10},{9,11},{10,... | collective-permute-start | bytes 196616 | tf_op jit(solution)/shard_map/ppermute | solution.py:26
  12.9 0.7 %fusion.3.vis_ref = f32[128,128]{1,0:T(8,128)} fusion(s32[128,128]{1,0:T(8,128)S(1)} %gather_fusion, pred[128]{0:T(512)(128)(4,1)S(1)} %get-tuple-element.15), kind=kLoop, calls=%fused_computation.9 | loop fusion | flops 49152 | bytes 131200 | tf_op jit(solution)/shard_map/convert_element_type | solution.py:186
  13.6 0.1 broadcast_in_dim.23
  13.7 0.1 reshape.57
  13.8 1.5 %collective-permute-done.2 = bf16[32,1024]{1,0:T(8,128)(2,1)S(1)} collective-permute-done((bf16[32,1024]{1,0:T(8,128)(2,1)S(1)}, bf16[32,1024]{1,0:T(8,128)(2,1)S(1)}, u32[]{:S(2)}, u32[]{:S(2)}) %collective-permute-start.2) | collective-permute-done | bytes 65568 | tf_op jit(solution)/shard_map/ppermute | solution.py:26
  15.3 0.1 collective-permute-start.3
  15.4 0.5 %compare_convert_fusion.live_ref = f32[1,128]{1,0:T(1,128)} fusion(s32[1,128]{1,0:T(1,128)S(1)} %reshape.57), kind=kLoop, calls=%fused_computation.24 | loop fusion | flops 1024 | bytes 1024 | tf_op jit(solution)/shard_map/convert_element_type | solution.py:166
  15.9 0.8 %collective-permute-done.3.kvb_ref = bf16[64,1024]{1,0:T(8,128)(2,1)S(1)} collective-permute-done((bf16[64,1024]{1,0:T(8,128)(2,1)S(1)}, bf16[64,1024]{1,0:T(8,128)(2,1)S(1)}, u32[]{:S(2)}, u32[]{:S(2)}) %collective-permute-start.3) | collective-permute-done | bytes 131104 | tf_op jit(solution)/shard_map/ppermute | solution.py:26
  16.7 0.6 %copy-done.2 = bf16[64,1024]{1,0:T(8,128)(2,1)} copy-done((bf16[64,1024]{1,0:T(8,128)(2,1)}, bf16[64,1024]{1,0:T(8,128)(2,1)S(1)}, u32[]{:S(2)}) %copy-start.2) | copy-done | bytes 131096
  17.4 6.8 %shard_map.146 = (bf16[128,2560]{1,0:T(8,128)(2,1)}, f32[64,1024]{1,0:T(8,128)}, bf16[64,1024]{1,0:T(8,128)(2,1)}, bf16[128,512]{1,0:T(8,128)(2,1)}, bf16[128,512]{1,0:T(8,128)(2,1)}) custom-call(bf16[128,2560]{1,0:T(8,128)(2,1)} %q_hbm.1, bf16[128,2560]{1,0:T(8,128)(2,1)} %do_hbm.1, bf16[64,1024]{1,0:T(8,128)(2,1)} %copy-done, bf16[64,1024]{1,0:T(8,128)(2,1)} %copy-done.2, ...), custom_call_target="tpu_custom_call" | custom-call | tf_op jit(solution)/shard_map/pallas_call | solution.py:189
  24.2 0.2 collective-permute-start.4
  24.4 1.4 %collective-permute-done.4 = bf16[64,1024]{1,0:T(8,128)(2,1)S(1)} collective-permute-done((bf16[64,1024]{1,0:T(8,128)(2,1)}, bf16[64,1024]{1,0:T(8,128)(2,1)S(1)}, u32[]{:S(2)}, u32[]{:S(2)}) %collective-permute-start.4) | collective-permute-done | bytes 131104 | tf_op jit(solution)/shard_map/ppermute | solution.py:26
  25.8 1.9 %collective-permute-start.5 = (bf16[32,1024]{1,0:T(8,128)(2,1)S(1)}, bf16[32,1024]{1,0:T(8,128)(2,1)S(1)}, u32[]{:S(2)}, u32[]{:S(2)}) collective-permute-start(bf16[32,1024]{1,0:T(8,128)(2,1)S(1)} %fusion), channel_id=1, source_target_pairs={{0,2},{1,3},{2,0},{3,1},{4,6},{5,7},{6,4},{7,5},{8,10},{9,11},{10,... | collective-permute-start | bytes 196616 | tf_op jit(solution)/shard_map/ppermute | solution.py:26
  27.8 2.4 %collective-permute-done.5 = bf16[32,1024]{1,0:T(8,128)(2,1)S(1)} collective-permute-done((bf16[32,1024]{1,0:T(8,128)(2,1)S(1)}, bf16[32,1024]{1,0:T(8,128)(2,1)S(1)}, u32[]{:S(2)}, u32[]{:S(2)}) %collective-permute-start.5) | collective-permute-done | bytes 65568 | tf_op jit(solution)/shard_map/ppermute | solution.py:26
  30.2 2.0 %collective-permute-start.6 = (bf16[16,1024]{1,0:T(8,128)(2,1)S(1)}, bf16[16,1024]{1,0:T(8,128)(2,1)S(1)}, u32[]{:S(2)}, u32[]{:S(2)}) collective-permute-start(bf16[16,1024]{1,0:T(8,128)(2,1)S(1)} %fusion.2), channel_id=1, source_target_pairs={{0,4},{1,5},{2,6},{3,7},{4,0},{5,1},{6,2},{7,3},{8,12},{9,13},{10,... | collective-permute-start | bytes 98312 | tf_op jit(solution)/shard_map/ppermute | solution.py:26
  32.2 2.0 %collective-permute-done.6 = bf16[16,1024]{1,0:T(8,128)(2,1)S(1)} collective-permute-done((bf16[16,1024]{1,0:T(8,128)(2,1)S(1)}, bf16[16,1024]{1,0:T(8,128)(2,1)S(1)}, u32[]{:S(2)}, u32[]{:S(2)}) %collective-permute-start.6) | collective-permute-done | bytes 32800 | tf_op jit(solution)/shard_map/ppermute | solution.py:26
  34.2 3.0 %collective-permute-start.7 = (bf16[8,1024]{1,0:T(8,128)(2,1)S(1)}, bf16[8,1024]{1,0:T(8,128)(2,1)S(1)}, u32[]{:S(2)}, u32[]{:S(2)}) collective-permute-start(bf16[8,1024]{1,0:T(8,128)(2,1)S(1)} %fusion.5), channel_id=1, source_target_pairs={{0,8},{1,9},{2,10},{3,11},{4,12},{5,13},{6,14},{7,15},{8,0},{9,1},... | collective-permute-start | bytes 49160 | tf_op jit(solution)/shard_map/ppermute | solution.py:26
  37.2 1.7 %collective-permute-done.7 = bf16[8,1024]{1,0:T(8,128)(2,1)S(1)} collective-permute-done((bf16[8,1024]{1,0:T(8,128)(2,1)S(1)}, bf16[8,1024]{1,0:T(8,128)(2,1)S(1)}, u32[]{:S(2)}, u32[]{:S(2)}) %collective-permute-start.7) | collective-permute-done | bytes 16416 | tf_op jit(solution)/shard_map/ppermute | solution.py:26
  38.9 0.6 %fusion.8 = (bf16[8,512]{1,0:T(8,128)(2,1)}, bf16[8,512]{1,0:T(8,128)(2,1)}) fusion(bf16[8,1024]{1,0:T(8,128)(2,1)S(1)} %fusion.7), kind=kLoop, calls=%fused_computation.31 | loop fusion | bytes 32768 | tf_op jit(solution)/shard_map/slice | solution.py:220
  (24 shorter events, 0.2 us)
Async XLA Ops:
  0.6 0.7 %copy-start.3 = (bf16[8,512]{1,0:T(8,128)(2,1)S(1)}, bf16[8,512]{1,0:T(8,128)(2,1)}, u32[]{:S(2)}) copy-start(bf16[8,512]{1,0:T(8,128)(2,1)} %param.15) | copy-start | bytes 24580
  1.4 5.8 %collective-permute-start = (bf16[8,1024]{1,0:T(8,128)(2,1)S(1)}, bf16[8,1024]{1,0:T(8,128)(2,1)S(1)}, u32[]{:S(2)}, u32[]{:S(2)}) collective-permute-start(bf16[8,1024]{1,0:T(8,128)(2,1)S(1)} %constant_dynamic-update-slice_fusion), channel_id=1, source_target_pairs={{0,8},{1,9},{2,10},{3,11},{4,12},{5,13},{6,14},{7,15},{8,0},{9,1},... | collective-permute-start | bytes 49160 | tf_op jit(solution)/shard_map/ppermute | solution.py:26
  5.4 0.7 %copy-start.5 = (s32[128]{0:T(128)S(1)}, s32[128]{0:T(128)}, u32[]{:S(2)}) copy-start(s32[128]{0:T(128)} %constant.61.clone) | copy-start | bytes 1540
  5.4 0.7 %copy-start.6 = (s32[128]{0:T(128)S(1)}, s32[128]{0:T(128)}, u32[]{:S(2)}) copy-start(s32[128]{0:T(128)} %constant.60.clone) | copy-start | bytes 1540
  7.1 3.9 %collective-permute-start.1 = (bf16[16,1024]{1,0:T(8,128)(2,1)S(1)}, bf16[16,1024]{1,0:T(8,128)(2,1)S(1)}, u32[]{:S(2)}, u32[]{:S(2)}) collective-permute-start(bf16[16,1024]{1,0:T(8,128)(2,1)S(1)} %pad_maximum_fusion.2), channel_id=1, source_target_pairs={{0,4},{1,5},{2,6},{3,7},{4,0},{5,1},{6,2},{7,3},{8,12},{9,13},{10,... | collective-permute-start | bytes 98312 | tf_op jit(solution)/shard_map/ppermute | solution.py:26
  9.0 0.7 %copy-start.4 = (s32[2,16]{1,0:T(2,128)S(1)}, s32[2,16]{1,0:T(2,128)}, u32[]{:S(2)}) copy-start(s32[2,16]{1,0:T(2,128)} %param.18) | copy-start | bytes 388
  11.0 4.3 %collective-permute-start.2 = (bf16[32,1024]{1,0:T(8,128)(2,1)S(1)}, bf16[32,1024]{1,0:T(8,128)(2,1)S(1)}, u32[]{:S(2)}, u32[]{:S(2)}) collective-permute-start(bf16[32,1024]{1,0:T(8,128)(2,1)S(1)} %pad_maximum_fusion.1), channel_id=1, source_target_pairs={{0,2},{1,3},{2,0},{3,1},{4,6},{5,7},{6,4},{7,5},{8,10},{9,11},{10,... | collective-permute-start | bytes 196616 | tf_op jit(solution)/shard_map/ppermute | solution.py:26
  12.9 0.7 %copy-start.7 = (s32[2]{0:T(128)S(1)}, s32[2]{0:T(128)}, u32[]{:S(2)}) copy-start(s32[2]{0:T(128)} %param.17) | copy-start | bytes 28
  15.3 1.4 %copy-start = (bf16[64,1024]{1,0:T(8,128)(2,1)}, bf16[64,1024]{1,0:T(8,128)(2,1)S(1)}, u32[]{:S(2)}) copy-start(bf16[64,1024]{1,0:T(8,128)(2,1)S(1)} %pad_maximum_fusion.kva_ref) | copy-start | bytes 393220
  15.3 1.4 %collective-permute-start.3 = (bf16[64,1024]{1,0:T(8,128)(2,1)S(1)}, bf16[64,1024]{1,0:T(8,128)(2,1)S(1)}, u32[]{:S(2)}, u32[]{:S(2)}) collective-permute-start(bf16[64,1024]{1,0:T(8,128)(2,1)S(1)} %pad_maximum_fusion.kva_ref), channel_id=1, source_target_pairs={{0,1},{1,0},{2,3},{3,2},{4,5},{5,4},{6,7},{7,6},{8,9},{9,8},{10,11... | collective-permute-start | bytes 393224 | tf_op jit(solution)/shard_map/ppermute | solution.py:26
  16.7 0.6 %copy-start.2 = (bf16[64,1024]{1,0:T(8,128)(2,1)}, bf16[64,1024]{1,0:T(8,128)(2,1)S(1)}, u32[]{:S(2)}) copy-start(bf16[64,1024]{1,0:T(8,128)(2,1)S(1)} %collective-permute-done.3.kvb_ref) | copy-start | bytes 393220
  24.1 1.7 %copy-start.1 = (f32[64,1024]{1,0:T(8,128)S(1)}, f32[64,1024]{1,0:T(8,128)}, u32[]{:S(2)}) copy-start(f32[64,1024]{1,0:T(8,128)} %get-tuple-element.11) | copy-start | bytes 786436
  24.2 1.6 %collective-permute-start.4 = (bf16[64,1024]{1,0:T(8,128)(2,1)}, bf16[64,1024]{1,0:T(8,128)(2,1)S(1)}, u32[]{:S(2)}, u32[]{:S(2)}) collective-permute-start(bf16[64,1024]{1,0:T(8,128)(2,1)} %get-tuple-element.12), channel_id=1, source_target_pairs={{0,1},{1,0},{2,3},{3,2},{4,5},{5,4},{6,7},{7,6},{8,9},{9,8},{10,11... | collective-permute-start | bytes 393224 | tf_op jit(solution)/shard_map/ppermute | solution.py:26
  25.8 4.3 %collective-permute-start.5 = (bf16[32,1024]{1,0:T(8,128)(2,1)S(1)}, bf16[32,1024]{1,0:T(8,128)(2,1)S(1)}, u32[]{:S(2)}, u32[]{:S(2)}) collective-permute-start(bf16[32,1024]{1,0:T(8,128)(2,1)S(1)} %fusion), channel_id=1, source_target_pairs={{0,2},{1,3},{2,0},{3,1},{4,6},{5,7},{6,4},{7,5},{8,10},{9,11},{10,... | collective-permute-start | bytes 196616 | tf_op jit(solution)/shard_map/ppermute | solution.py:26
  30.2 4.0 %collective-permute-start.6 = (bf16[16,1024]{1,0:T(8,128)(2,1)S(1)}, bf16[16,1024]{1,0:T(8,128)(2,1)S(1)}, u32[]{:S(2)}, u32[]{:S(2)}) collective-permute-start(bf16[16,1024]{1,0:T(8,128)(2,1)S(1)} %fusion.2), channel_id=1, source_target_pairs={{0,4},{1,5},{2,6},{3,7},{4,0},{5,1},{6,2},{7,3},{8,12},{9,13},{10,... | collective-permute-start | bytes 98312 | tf_op jit(solution)/shard_map/ppermute | solution.py:26
  34.2 4.7 %collective-permute-start.7 = (bf16[8,1024]{1,0:T(8,128)(2,1)S(1)}, bf16[8,1024]{1,0:T(8,128)(2,1)S(1)}, u32[]{:S(2)}, u32[]{:S(2)}) collective-permute-start(bf16[8,1024]{1,0:T(8,128)(2,1)S(1)} %fusion.5), channel_id=1, source_target_pairs={{0,8},{1,9},{2,10},{3,11},{4,12},{5,13},{6,14},{7,15},{8,0},{9,1},... | collective-permute-start | bytes 49160 | tf_op jit(solution)/shard_map/ppermute | solution.py:26

commit v15 on v11

--- a/solution.py
+++ b/solution.py
@@ -25,16 +25,25 @@
     return lax.ppermute(block, axis_name, pairs)
 
 
+def exchange_sequence(bits):
+    order = list(reversed(range(bits)))
+    if bits >= 3:
+        order[-3], order[-2] = order[-2], order[-3]
+    return order
+
+
 def exchange_pattern(size):
-    bits = exchange_bits(size)
-    return [int(format(spot, "0%db" % bits)[::-1], 2) for spot in range(size)]
+    order = exchange_sequence(exchange_bits(size))
+    return [
+        sum(((spot >> step) & 1) << bit for step, bit in enumerate(order)) for spot in range(size)
+    ]
 
 
 def gather_rows(blocks, axis_name):
     size = lax.axis_size(axis_name)
     bits = exchange_bits(size)
     halves = None
-    for bit in reversed(range(bits)):
+    for bit in exchange_sequence(bits):
         if halves is not None:
             blocks = jnp.concatenate(halves)
         halves = (blocks, swap_with(blocks, axis_name, size, bit))
@@ -45,13 +54,13 @@
     size = lax.axis_size(axis_name)
     bits = exchange_bits(size)
     pending = [keep]
-    for bit in range(bits):
-        if bit > 0:
+    for step, bit in enumerate(reversed(exchange_sequence(bits))):
+        if step > 0:
             split = pending[0].shape[0] // 2
             send = sum(part[split:] for part in pending[1:])
-            send = pending[0][split:] + send
+            send = (pending[0][split:] + send).astype(jnp.bfloat16)
             pending = [part[:split] for part in pending]
-        pending.append(swap_with(send, axis_name, size, bit))
+        pending.append(swap_with(send, axis_name, size, bit).astype(jnp.float32))
     return sum(pending[1:], pending[0])
 
 
@@ -117,9 +126,9 @@
         key_total = jnp.dot(dscore, q, preferred_element_type=jnp.float32) * score_scale
         value_total = jnp.dot(prob.astype(jnp.bfloat16), do, preferred_element_type=jnp.float32)
         keep_ref[:, columns] = key_total[:half]
-        send_ref[:, columns] = key_total[half:doc_rows]
+        send_ref[:, columns] = key_total[half:doc_rows].astype(send_ref.dtype)
         keep_ref[:, value_columns] = value_total[:half]
-        send_ref[:, value_columns] = value_total[half:doc_rows]
+        send_ref[:, value_columns] = value_total[half:doc_rows].astype(send_ref.dtype)
         sk_ref[:, columns] = key_total[doc_rows:].astype(sk_ref.dtype)
         sv_ref[:, columns] = value_total[doc_rows:].astype(sv_ref.dtype)
 
@@ -170,7 +179,7 @@
         out_shape=(
             jax.ShapeDtypeStruct(queries.shape, jnp.bfloat16),
             jax.ShapeDtypeStruct((half_rows, 2 * key_value_width), jnp.float32),
-            jax.ShapeDtypeStruct((half_rows, 2 * key_value_width), jnp.float32),
+            jax.ShapeDtypeStruct((half_rows, 2 * key_value_width), jnp.bfloat16),
             jax.ShapeDtypeStruct(response_keys.shape, jnp.bfloat16),
             jax.ShapeDtypeStruct(response_values.shape, jnp.bfloat16),
         ),

time: 41.5 us -> 38.5 us (0.928)
  waiting for transfers between devices: 13.7 us -> 11.4 us
  other arithmetic: 2.22 us -> 1.37 us
    ppermute x8, waiting for transfers between devices: 13.7 us -> 11.4 us  [swap_with(): return lax.ppermute(block, axis_name, pairs)]
    add x3 -> x0, other arithmetic: 0.95 us -> none  [scatter_sum_rows(): send = pending[0][split:] + send]
where the time goes in v15:
time: 38.5 us; the launch traced here: 38.2 us
  starting transfers between devices  14.9 us (39%)
  waiting for transfers between devices  11.4 us (30%)
  Pallas kernels  5.44 us (14%)
  local copies, waits for them, and re-layouts  4.36 us (11%)
  other arithmetic  1.37 us (4%)
  between operations  0.72 us (2%)
    ppermute x8, starting transfers between devices, swap_with(): return lax.ppermute(block, axis_name, pairs)  14.9 us
    ppermute x8, waiting for transfers between devices, swap_with(): return lax.ppermute(block, axis_name, pairs)  11.4 us
    pallas_call x1, Pallas kernels, per_device(): pl.pallas_call(attention_kernel, out_shape=(jax.ShapeDtypeStruct(queries....  5.44 us
    unnamed x18, local copies, waits for them, and re-layouts  2.79 us
  transfers between devices with their start and end apart: 8, of which 8 were waited for; matrix products, arithmetic and copies ran while one was open for 6% of the time, Pallas kernels for 0%

profile of v15, /device:TPU:0, one launch (start us, length us, event | category | flops | bytes accessed | tf_op | source)
XLA Modules:
  0.0 38.2 jit_solution(11605414993458365645)
XLA Ops:
  0.6 0.7 %constant_dynamic-update-slice_fusion.1 = bf16[8,1024]{1,0:T(8,128)(2,1)S(1)} fusion(bf16[8,512]{1,0:T(8,128)(2,1)} %param.14), kind=kLoop, calls=%fused_computation.22 | loop fusion | bytes 16384
  1.4 4.0 %collective-permute-start = (bf16[8,1024]{1,0:T(8,128)(2,1)S(1)}, bf16[8,1024]{1,0:T(8,128)(2,1)S(1)}, u32[]{:S(2)}, u32[]{:S(2)}) collective-permute-start(bf16[8,1024]{1,0:T(8,128)(2,1)S(1)} %constant_dynamic-update-slice_fusion), channel_id=1, source_target_pairs={{0,8},{1,9},{2,10},{3,11},{4,12},{5,13},{6,14},{7,15},{8,0},{9,1},... | collective-permute-start | bytes 49160 | tf_op jit(solution)/shard_map/ppermute | solution.py:25
  5.4 0.7 %copy-done.5 = s32[128]{0:T(128)S(1)} copy-done((s32[128]{0:T(128)S(1)}, s32[128]{0:T(128)}, u32[]{:S(2)}) %copy-start.5) | copy-done | bytes 536
  6.0 0.0 copy-done.6
  6.1 1.0 %collective-permute-done = bf16[8,1024]{1,0:T(8,128)(2,1)S(1)} collective-permute-done((bf16[8,1024]{1,0:T(8,128)(2,1)S(1)}, bf16[8,1024]{1,0:T(8,128)(2,1)S(1)}, u32[]{:S(2)}, u32[]{:S(2)}) %collective-permute-start) | collective-permute-done | bytes 16416 | tf_op jit(solution)/shard_map/ppermute | solution.py:25
  7.1 1.9 %collective-permute-start.1 = (bf16[16,1024]{1,0:T(8,128)(2,1)S(1)}, bf16[16,1024]{1,0:T(8,128)(2,1)S(1)}, u32[]{:S(2)}, u32[]{:S(2)}) collective-permute-start(bf16[16,1024]{1,0:T(8,128)(2,1)S(1)} %pad_maximum_fusion.2), channel_id=1, source_target_pairs={{0,2},{1,3},{2,0},{3,1},{4,6},{5,7},{6,4},{7,5},{8,10},{9,11},{10,... | collective-permute-start | bytes 98312 | tf_op jit(solution)/shard_map/ppermute | solution.py:25
  9.0 0.7 %copy-done.4 = s32[2,16]{1,0:T(2,128)S(1)} copy-done((s32[2,16]{1,0:T(2,128)S(1)}, s32[2,16]{1,0:T(2,128)}, u32[]{:S(2)}) %copy-start.4) | copy-done | bytes 152
  9.7 0.1 copy.16
  9.7 0.1 broadcast_in_dim.20
  9.8 0.1 reshape.56
  9.9 0.6 %gather_fusion = s32[128,128]{1,0:T(8,128)S(1)} fusion(s32[16,128]{1,0:T(8,128)S(1)} %bitcast.3, s32[1024]{0:T(1024)S(1)} %pad_clamp_fusion), kind=kCustom, calls=%fused_computation | custom fusion | bytes 131584 | tf_op jit(solution)/shard_map/jit(_take)/gather | solution.py:174
  10.6 0.5 %collective-permute-done.1 = bf16[16,1024]{1,0:T(8,128)(2,1)S(1)} collective-permute-done((bf16[16,1024]{1,0:T(8,128)(2,1)S(1)}, bf16[16,1024]{1,0:T(8,128)(2,1)S(1)}, u32[]{:S(2)}, u32[]{:S(2)}) %collective-permute-start.1) | collective-permute-done | bytes 32800 | tf_op jit(solution)/shard_map/ppermute | solution.py:25
  11.0 1.9 %collective-permute-start.2 = (bf16[32,1024]{1,0:T(8,128)(2,1)S(1)}, bf16[32,1024]{1,0:T(8,128)(2,1)S(1)}, u32[]{:S(2)}, u32[]{:S(2)}) collective-permute-start(bf16[32,1024]{1,0:T(8,128)(2,1)S(1)} %pad_maximum_fusion.1), channel_id=1, source_target_pairs={{0,4},{1,5},{2,6},{3,7},{4,0},{5,1},{6,2},{7,3},{8,12},{9,13},{10,... | collective-permute-start | bytes 196616 | tf_op jit(solution)/shard_map/ppermute | solution.py:25
  12.9 0.7 %fusion.3.vis_ref = f32[128,128]{1,0:T(8,128)} fusion(s32[128,128]{1,0:T(8,128)S(1)} %gather_fusion, pred[128]{0:T(512)(128)(4,1)S(1)} %get-tuple-element.15), kind=kLoop, calls=%fused_computation.9 | loop fusion | flops 49152 | bytes 131200 | tf_op jit(solution)/shard_map/convert_element_type | solution.py:174
  13.7 0.1 broadcast_in_dim.23
  13.7 0.1 reshape.57
  13.8 1.5 %collective-permute-done.2 = bf16[32,1024]{1,0:T(8,128)(2,1)S(1)} collective-permute-done((bf16[32,1024]{1,0:T(8,128)(2,1)S(1)}, bf16[32,1024]{1,0:T(8,128)(2,1)S(1)}, u32[]{:S(2)}, u32[]{:S(2)}) %collective-permute-start.2) | collective-permute-done | bytes 65568 | tf_op jit(solution)/shard_map/ppermute | solution.py:25
  15.3 0.1 collective-permute-start.3
  15.4 0.5 %compare_convert_fusion.live_ref = f32[1,128]{1,0:T(1,128)} fusion(s32[1,128]{1,0:T(1,128)S(1)} %reshape.57), kind=kLoop, calls=%fused_computation.24 | loop fusion | flops 1024 | bytes 1024 | tf_op jit(solution)/shard_map/convert_element_type | solution.py:154
  15.9 0.8 %collective-permute-done.3.kvb_ref = bf16[64,1024]{1,0:T(8,128)(2,1)S(1)} collective-permute-done((bf16[64,1024]{1,0:T(8,128)(2,1)S(1)}, bf16[64,1024]{1,0:T(8,128)(2,1)S(1)}, u32[]{:S(2)}, u32[]{:S(2)}) %collective-permute-start.3) | collective-permute-done | bytes 131104 | tf_op jit(solution)/shard_map/ppermute | solution.py:25
  16.7 0.0 copy-done
  16.7 0.6 %copy-done.2 = bf16[64,1024]{1,0:T(8,128)(2,1)} copy-done((bf16[64,1024]{1,0:T(8,128)(2,1)}, bf16[64,1024]{1,0:T(8,128)(2,1)S(1)}, u32[]{:S(2)}) %copy-start.2) | copy-done | bytes 131096
  17.4 5.4 %shard_map.146 = (bf16[128,2560]{1,0:T(8,128)(2,1)}, f32[64,1024]{1,0:T(8,128)}, bf16[64,1024]{1,0:T(8,128)(2,1)}, bf16[128,512]{1,0:T(8,128)(2,1)}, bf16[128,512]{1,0:T(8,128)(2,1)}) custom-call(bf16[128,2560]{1,0:T(8,128)(2,1)} %q_ref.1, bf16[128,2560]{1,0:T(8,128)(2,1)} %do_ref.1, bf16[64,1024]{1,0:T(8,128)(2,1)} %copy-done, bf16[64,1024]{1,0:T(8,128)(2,1)} %copy-done.2, ...), custom_call_target="tpu_custom_call" | custom-call | tf_op jit(solution)/shard_map/pallas_call | solution.py:177
  22.8 0.1 collective-permute-start.4
  23.0 1.4 %collective-permute-done.4 = bf16[64,1024]{1,0:T(8,128)(2,1)S(1)} collective-permute-done((bf16[64,1024]{1,0:T(8,128)(2,1)}, bf16[64,1024]{1,0:T(8,128)(2,1)S(1)}, u32[]{:S(2)}, u32[]{:S(2)}) %collective-permute-start.4) | collective-permute-done | bytes 131104 | tf_op jit(solution)/shard_map/ppermute | solution.py:25
  24.4 2.0 %collective-permute-start.5 = (bf16[32,1024]{1,0:T(8,128)(2,1)S(1)}, bf16[32,1024]{1,0:T(8,128)(2,1)S(1)}, u32[]{:S(2)}, u32[]{:S(2)}) collective-permute-start(bf16[32,1024]{1,0:T(8,128)(2,1)S(1)} %fusion), channel_id=1, source_target_pairs={{0,4},{1,5},{2,6},{3,7},{4,0},{5,1},{6,2},{7,3},{8,12},{9,13},{10,... | collective-permute-start | bytes 196616 | tf_op jit(solution)/shard_map/ppermute | solution.py:25
  26.4 2.4 %collective-permute-done.5 = bf16[32,1024]{1,0:T(8,128)(2,1)S(1)} collective-permute-done((bf16[32,1024]{1,0:T(8,128)(2,1)S(1)}, bf16[32,1024]{1,0:T(8,128)(2,1)S(1)}, u32[]{:S(2)}, u32[]{:S(2)}) %collective-permute-start.5) | collective-permute-done | bytes 65568 | tf_op jit(solution)/shard_map/ppermute | solution.py:25
  28.8 1.9 %collective-permute-start.6 = (bf16[16,1024]{1,0:T(8,128)(2,1)S(1)}, bf16[16,1024]{1,0:T(8,128)(2,1)S(1)}, u32[]{:S(2)}, u32[]{:S(2)}) collective-permute-start(bf16[16,1024]{1,0:T(8,128)(2,1)S(1)} %fusion.2), channel_id=1, source_target_pairs={{0,2},{1,3},{2,0},{3,1},{4,6},{5,7},{6,4},{7,5},{8,10},{9,11},{10,... | collective-permute-start | bytes 98312 | tf_op jit(solution)/shard_map/ppermute | solution.py:25
  30.7 2.1 %collective-permute-done.6 = bf16[16,1024]{1,0:T(8,128)(2,1)S(1)} collective-permute-done((bf16[16,1024]{1,0:T(8,128)(2,1)S(1)}, bf16[16,1024]{1,0:T(8,128)(2,1)S(1)}, u32[]{:S(2)}, u32[]{:S(2)}) %collective-permute-start.6) | collective-permute-done | bytes 32800 | tf_op jit(solution)/shard_map/ppermute | solution.py:25
  32.8 3.0 %collective-permute-start.7 = (bf16[8,1024]{1,0:T(8,128)(2,1)S(1)}, bf16[8,1024]{1,0:T(8,128)(2,1)S(1)}, u32[]{:S(2)}, u32[]{:S(2)}) collective-permute-start(bf16[8,1024]{1,0:T(8,128)(2,1)S(1)} %fusion.5), channel_id=1, source_target_pairs={{0,8},{1,9},{2,10},{3,11},{4,12},{5,13},{6,14},{7,15},{8,0},{9,1},... | collective-permute-start | bytes 49160 | tf_op jit(solution)/shard_map/ppermute | solution.py:25
  35.8 1.7 %collective-permute-done.7 = bf16[8,1024]{1,0:T(8,128)(2,1)S(1)} collective-permute-done((bf16[8,1024]{1,0:T(8,128)(2,1)S(1)}, bf16[8,1024]{1,0:T(8,128)(2,1)S(1)}, u32[]{:S(2)}, u32[]{:S(2)}) %collective-permute-start.7) | collective-permute-done | bytes 16416 | tf_op jit(solution)/shard_map/ppermute | solution.py:25
  37.6 0.6 %fusion.8 = (bf16[8,512]{1,0:T(8,128)(2,1)}, bf16[8,512]{1,0:T(8,128)(2,1)}) fusion(bf16[8,1024]{1,0:T(8,128)(2,1)S(1)} %fusion.7), kind=kLoop, calls=%fused_computation.31 | loop fusion | bytes 32768 | tf_op jit(solution)/shard_map/slice | solution.py:201
  (24 shorter events, 0.2 us)
Async XLA Ops:
  0.6 0.7 %copy-start.3 = (bf16[8,512]{1,0:T(8,128)(2,1)S(1)}, bf16[8,512]{1,0:T(8,128)(2,1)}, u32[]{:S(2)}) copy-start(bf16[8,512]{1,0:T(8,128)(2,1)} %param.15) | copy-start | bytes 24580
  1.4 5.8 %collective-permute-start = (bf16[8,1024]{1,0:T(8,128)(2,1)S(1)}, bf16[8,1024]{1,0:T(8,128)(2,1)S(1)}, u32[]{:S(2)}, u32[]{:S(2)}) collective-permute-start(bf16[8,1024]{1,0:T(8,128)(2,1)S(1)} %constant_dynamic-update-slice_fusion), channel_id=1, source_target_pairs={{0,8},{1,9},{2,10},{3,11},{4,12},{5,13},{6,14},{7,15},{8,0},{9,1},... | collective-permute-start | bytes 49160 | tf_op jit(solution)/shard_map/ppermute | solution.py:25
  5.4 0.7 %copy-start.5 = (s32[128]{0:T(128)S(1)}, s32[128]{0:T(128)}, u32[]{:S(2)}) copy-start(s32[128]{0:T(128)} %constant.61.clone) | copy-start | bytes 1540
  5.4 0.7 %copy-start.6 = (s32[128]{0:T(128)S(1)}, s32[128]{0:T(128)}, u32[]{:S(2)}) copy-start(s32[128]{0:T(128)} %constant.60.clone) | copy-start | bytes 1540
  7.1 3.9 %collective-permute-start.1 = (bf16[16,1024]{1,0:T(8,128)(2,1)S(1)}, bf16[16,1024]{1,0:T(8,128)(2,1)S(1)}, u32[]{:S(2)}, u32[]{:S(2)}) collective-permute-start(bf16[16,1024]{1,0:T(8,128)(2,1)S(1)} %pad_maximum_fusion.2), channel_id=1, source_target_pairs={{0,2},{1,3},{2,0},{3,1},{4,6},{5,7},{6,4},{7,5},{8,10},{9,11},{10,... | collective-permute-start | bytes 98312 | tf_op jit(solution)/shard_map/ppermute | solution.py:25
  9.0 0.7 %copy-start.4 = (s32[2,16]{1,0:T(2,128)S(1)}, s32[2,16]{1,0:T(2,128)}, u32[]{:S(2)}) copy-start(s32[2,16]{1,0:T(2,128)} %param.18) | copy-start | bytes 388
  11.0 4.3 %collective-permute-start.2 = (bf16[32,1024]{1,0:T(8,128)(2,1)S(1)}, bf16[32,1024]{1,0:T(8,128)(2,1)S(1)}, u32[]{:S(2)}, u32[]{:S(2)}) collective-permute-start(bf16[32,1024]{1,0:T(8,128)(2,1)S(1)} %pad_maximum_fusion.1), channel_id=1, source_target_pairs={{0,4},{1,5},{2,6},{3,7},{4,0},{5,1},{6,2},{7,3},{8,12},{9,13},{10,... | collective-permute-start | bytes 196616 | tf_op jit(solution)/shard_map/ppermute | solution.py:25
  12.9 0.7 %copy-start.7 = (s32[2]{0:T(128)S(1)}, s32[2]{0:T(128)}, u32[]{:S(2)}) copy-start(s32[2]{0:T(128)} %param.17) | copy-start | bytes 28
  15.3 1.4 %copy-start = (bf16[64,1024]{1,0:T(8,128)(2,1)}, bf16[64,1024]{1,0:T(8,128)(2,1)S(1)}, u32[]{:S(2)}) copy-start(bf16[64,1024]{1,0:T(8,128)(2,1)S(1)} %pad_maximum_fusion.kva_ref) | copy-start | bytes 393220
  15.3 1.4 %collective-permute-start.3 = (bf16[64,1024]{1,0:T(8,128)(2,1)S(1)}, bf16[64,1024]{1,0:T(8,128)(2,1)S(1)}, u32[]{:S(2)}, u32[]{:S(2)}) collective-permute-start(bf16[64,1024]{1,0:T(8,128)(2,1)S(1)} %pad_maximum_fusion.kva_ref), channel_id=1, source_target_pairs={{0,1},{1,0},{2,3},{3,2},{4,5},{5,4},{6,7},{7,6},{8,9},{9,8},{10,11... | collective-permute-start | bytes 393224 | tf_op jit(solution)/shard_map/ppermute | solution.py:25
  16.7 0.6 %copy-start.2 = (bf16[64,1024]{1,0:T(8,128)(2,1)}, bf16[64,1024]{1,0:T(8,128)(2,1)S(1)}, u32[]{:S(2)}) copy-start(bf16[64,1024]{1,0:T(8,128)(2,1)S(1)} %collective-permute-done.3.kvb_ref) | copy-start | bytes 393220
  22.8 1.6 %copy-start.1 = (f32[64,1024]{1,0:T(8,128)S(1)}, f32[64,1024]{1,0:T(8,128)}, u32[]{:S(2)}) copy-start(f32[64,1024]{1,0:T(8,128)} %get-tuple-element.11) | copy-start | bytes 786436
  22.8 1.6 %collective-permute-start.4 = (bf16[64,1024]{1,0:T(8,128)(2,1)}, bf16[64,1024]{1,0:T(8,128)(2,1)S(1)}, u32[]{:S(2)}, u32[]{:S(2)}) collective-permute-start(bf16[64,1024]{1,0:T(8,128)(2,1)} %get-tuple-element.12), channel_id=1, source_target_pairs={{0,1},{1,0},{2,3},{3,2},{4,5},{5,4},{6,7},{7,6},{8,9},{9,8},{10,11... | collective-permute-start | bytes 393224 | tf_op jit(solution)/shard_map/ppermute | solution.py:25
  24.4 4.4 %collective-permute-start.5 = (bf16[32,1024]{1,0:T(8,128)(2,1)S(1)}, bf16[32,1024]{1,0:T(8,128)(2,1)S(1)}, u32[]{:S(2)}, u32[]{:S(2)}) collective-permute-start(bf16[32,1024]{1,0:T(8,128)(2,1)S(1)} %fusion), channel_id=1, source_target_pairs={{0,4},{1,5},{2,6},{3,7},{4,0},{5,1},{6,2},{7,3},{8,12},{9,13},{10,... | collective-permute-start | bytes 196616 | tf_op jit(solution)/shard_map/ppermute | solution.py:25
  28.8 4.0 %collective-permute-start.6 = (bf16[16,1024]{1,0:T(8,128)(2,1)S(1)}, bf16[16,1024]{1,0:T(8,128)(2,1)S(1)}, u32[]{:S(2)}, u32[]{:S(2)}) collective-permute-start(bf16[16,1024]{1,0:T(8,128)(2,1)S(1)} %fusion.2), channel_id=1, source_target_pairs={{0,2},{1,3},{2,0},{3,1},{4,6},{5,7},{6,4},{7,5},{8,10},{9,11},{10,... | collective-permute-start | bytes 98312 | tf_op jit(solution)/shard_map/ppermute | solution.py:25
  32.8 4.7 %collective-permute-start.7 = (bf16[8,1024]{1,0:T(8,128)(2,1)S(1)}, bf16[8,1024]{1,0:T(8,128)(2,1)S(1)}, u32[]{:S(2)}, u32[]{:S(2)}) collective-permute-start(bf16[8,1024]{1,0:T(8,128)(2,1)S(1)} %fusion.5), channel_id=1, source_target_pairs={{0,8},{1,9},{2,10},{3,11},{4,12},{5,13},{6,14},{7,15},{8,0},{9,1},... | collective-permute-start | bytes 49160 | tf_op jit(solution)/shard_map/ppermute | solution.py:25

commit v16 on v15

--- a/solution.py
+++ b/solution.py
@@ -45,7 +45,9 @@
     halves = None
     for bit in exchange_sequence(bits):
         if halves is not None:
-            blocks = jnp.concatenate(halves)
+            blocks = jnp.concatenate(
+                [jnp.concatenate(part, axis=1) if isinstance(part, tuple) else part for part in halves]
+            )
         halves = (blocks, swap_with(blocks, axis_name, size, bit))
     return halves
 
@@ -159,9 +161,7 @@
         jnp.float32,
     )
     size = lax.axis_size("resp")
-    doc_mine, doc_other = gather_rows(
-        jnp.concatenate([document_keys, document_values], axis=1), "resp"
-    )
+    doc_mine, doc_other = gather_rows((document_keys, document_values), "resp")
     slab_rows = document_keys.shape[0]
     doc_rows = size * slab_rows
     half_rows = doc_rows // 2

time: 38.5 us -> 40.8 us (1.060)
  waiting for transfers between devices: 11.4 us -> 17.8 us
  starting transfers between devices: 14.9 us -> 10.8 us
    ppermute x8 -> x9, waiting for transfers between devices: 11.4 us -> 17.8 us  [swap_with(): return lax.ppermute(block, axis_name, pairs)]
    ppermute x8 -> x9, starting transfers between devices: 14.9 us -> 10.8 us  [swap_with(): return lax.ppermute(block, axis_name, pairs)]
    unnamed x18 -> x19, local copies, waits for them, and re-layouts: 2.79 us -> 2.8 us
  transfers between devices with their start and end apart: 8 -> 9, of which waited for: 8 -> 9; matrix products, arithmetic and copies ran while one was open for 6% -> 7% of each run, Pallas kernels for 0% -> 0%
where the time goes in v16:
time: 40.8 us; the launch traced here: 40.5 us
  waiting for transfers between devices  17.8 us (44%)
  starting transfers between devices  10.8 us (26%)
  Pallas kernels  5.44 us (13%)
  local copies, waits for them, and re-layouts  4.37 us (11%)
  other arithmetic  1.37 us (3%)
  between operations  0.72 us (2%)
    ppermute x9, waiting for transfers between devices, swap_with(): return lax.ppermute(block, axis_name, pairs)  17.8 us
    ppermute x9, starting transfers between devices, swap_with(): return lax.ppermute(block, axis_name, pairs)  10.8 us
    pallas_call x1, Pallas kernels, per_device(): pl.pallas_call(attention_kernel, out_shape=(jax.ShapeDtypeStruct(queries....  5.44 us
    unnamed x19, local copies, waits for them, and re-layouts  2.8 us
  transfers between devices with their start and end apart: 9, of which 9 were waited for; matrix products, arithmetic and copies ran while one was open for 7% of the time, Pallas kernels for 0%

profile of v16, /device:TPU:0, one launch (start us, length us, event | category | flops | bytes accessed | tf_op | source)
XLA Modules:
  0.0 40.5 jit_solution(3259258007771463116)
XLA Ops:
  0.6 4.1 %collective-permute-start = (bf16[8,512]{1,0:T(8,128)(2,1)}, bf16[8,512]{1,0:T(8,128)(2,1)S(1)}, u32[]{:S(2)}, u32[]{:S(2)}) collective-permute-start(bf16[8,512]{1,0:T(8,128)(2,1)} %param.14), channel_id=1, source_target_pairs={{0,8},{1,9},{2,10},{3,11},{4,12},{5,13},{6,14},{7,15},{8,0},{9,1},... | collective-permute-start | bytes 24584 | tf_op jit(solution)/shard_map/ppermute | solution.py:25
  4.7 0.1 collective-permute-start.1
  4.8 0.7 %constant_dynamic-update-slice_fusion.1 = bf16[8,1024]{1,0:T(8,128)(2,1)S(1)} fusion(bf16[8,512]{1,0:T(8,128)(2,1)} %param.14), kind=kLoop, calls=%fused_computation.21 | loop fusion | bytes 16384
  5.5 0.7 %copy-done.5 = s32[128]{0:T(128)S(1)} copy-done((s32[128]{0:T(128)S(1)}, s32[128]{0:T(128)}, u32[]{:S(2)}) %copy-start.5) | copy-done | bytes 536
  6.2 0.3 collective-permute-done
  6.6 2.9 %collective-permute-done.1 = bf16[8,512]{1,0:T(8,128)(2,1)S(1)} collective-permute-done((bf16[8,512]{1,0:T(8,128)(2,1)}, bf16[8,512]{1,0:T(8,128)(2,1)S(1)}, u32[]{:S(2)}, u32[]{:S(2)}) %collective-permute-start.1) | collective-permute-done | bytes 8224 | tf_op jit(solution)/shard_map/ppermute | solution.py:25
  9.5 1.5 %collective-permute-start.2 = (bf16[16,1024]{1,0:T(8,128)(2,1)S(1)}, bf16[16,1024]{1,0:T(8,128)(2,1)S(1)}, u32[]{:S(2)}, u32[]{:S(2)}) collective-permute-start(bf16[16,1024]{1,0:T(8,128)(2,1)S(1)} %pad_maximum_fusion.2), channel_id=1, source_target_pairs={{0,2},{1,3},{2,0},{3,1},{4,6},{5,7},{6,4},{7,5},{8,10},{9,11},{10,... | collective-permute-start | bytes 98312 | tf_op jit(solution)/shard_map/ppermute | solution.py:25
  11.0 0.7 %copy-done.4 = s32[2,16]{1,0:T(2,128)S(1)} copy-done((s32[2,16]{1,0:T(2,128)S(1)}, s32[2,16]{1,0:T(2,128)}, u32[]{:S(2)}) %copy-start.4) | copy-done | bytes 152
  11.7 0.1 copy.16
  11.8 0.1 broadcast_in_dim.20
  11.8 0.1 reshape.56
  11.9 0.6 %gather_fusion = s32[128,128]{1,0:T(8,128)S(1)} fusion(s32[16,128]{1,0:T(8,128)S(1)} %bitcast.3, s32[1024]{0:T(1024)S(1)} %pad_clamp_fusion), kind=kCustom, calls=%fused_computation | custom fusion | bytes 131584 | tf_op jit(solution)/shard_map/jit(_take)/gather | solution.py:174
  12.6 0.8 %collective-permute-done.2 = bf16[16,1024]{1,0:T(8,128)(2,1)S(1)} collective-permute-done((bf16[16,1024]{1,0:T(8,128)(2,1)S(1)}, bf16[16,1024]{1,0:T(8,128)(2,1)S(1)}, u32[]{:S(2)}, u32[]{:S(2)}) %collective-permute-start.2) | collective-permute-done | bytes 32800 | tf_op jit(solution)/shard_map/ppermute | solution.py:25
  13.4 1.6 %collective-permute-start.3 = (bf16[32,1024]{1,0:T(8,128)(2,1)S(1)}, bf16[32,1024]{1,0:T(8,128)(2,1)S(1)}, u32[]{:S(2)}, u32[]{:S(2)}) collective-permute-start(bf16[32,1024]{1,0:T(8,128)(2,1)S(1)} %pad_maximum_fusion.1), channel_id=1, source_target_pairs={{0,4},{1,5},{2,6},{3,7},{4,0},{5,1},{6,2},{7,3},{8,12},{9,13},{10,... | collective-permute-start | bytes 196616 | tf_op jit(solution)/shard_map/ppermute | solution.py:25
  15.0 0.7 %fusion.3.vis_ref = f32[128,128]{1,0:T(8,128)} fusion(s32[128,128]{1,0:T(8,128)S(1)} %gather_fusion, pred[128]{0:T(512)(128)(4,1)S(1)} %get-tuple-element.15), kind=kLoop, calls=%fused_computation.9 | loop fusion | flops 49152 | bytes 131200 | tf_op jit(solution)/shard_map/convert_element_type | solution.py:174
  15.7 0.1 broadcast_in_dim.23
  15.8 0.1 reshape.57
  15.9 1.8 %collective-permute-done.3 = bf16[32,1024]{1,0:T(8,128)(2,1)S(1)} collective-permute-done((bf16[32,1024]{1,0:T(8,128)(2,1)S(1)}, bf16[32,1024]{1,0:T(8,128)(2,1)S(1)}, u32[]{:S(2)}, u32[]{:S(2)}) %collective-permute-start.3) | collective-permute-done | bytes 65568 | tf_op jit(solution)/shard_map/ppermute | solution.py:25
  17.7 0.1 collective-permute-start.4
  17.8 0.5 %compare_convert_fusion.live_ref = f32[1,128]{1,0:T(1,128)} fusion(s32[1,128]{1,0:T(1,128)S(1)} %reshape.57), kind=kLoop, calls=%fused_computation.26 | loop fusion | flops 1024 | bytes 1024 | tf_op jit(solution)/shard_map/convert_element_type | solution.py:156
  18.3 0.8 %collective-permute-done.4.kvb_ref = bf16[64,1024]{1,0:T(8,128)(2,1)S(1)} collective-permute-done((bf16[64,1024]{1,0:T(8,128)(2,1)S(1)}, bf16[64,1024]{1,0:T(8,128)(2,1)S(1)}, u32[]{:S(2)}, u32[]{:S(2)}) %collective-permute-start.4) | collective-permute-done | bytes 131104 | tf_op jit(solution)/shard_map/ppermute | solution.py:25
  19.1 0.6 %copy-done.2 = bf16[64,1024]{1,0:T(8,128)(2,1)} copy-done((bf16[64,1024]{1,0:T(8,128)(2,1)}, bf16[64,1024]{1,0:T(8,128)(2,1)S(1)}, u32[]{:S(2)}) %copy-start.2) | copy-done | bytes 131096
  19.8 5.4 %shard_map.146 = (bf16[128,2560]{1,0:T(8,128)(2,1)}, f32[64,1024]{1,0:T(8,128)}, bf16[64,1024]{1,0:T(8,128)(2,1)}, bf16[128,512]{1,0:T(8,128)(2,1)}, bf16[128,512]{1,0:T(8,128)(2,1)}) custom-call(bf16[128,2560]{1,0:T(8,128)(2,1)} %q_ref.1, bf16[128,2560]{1,0:T(8,128)(2,1)} %do_ref.1, bf16[64,1024]{1,0:T(8,128)(2,1)} %copy-done, bf16[64,1024]{1,0:T(8,128)(2,1)} %copy-done.2, ...), custom_call_target="tpu_custom_call" | custom-call | tf_op jit(solution)/shard_map/pallas_call | solution.py:177
  25.2 0.1 collective-permute-start.5
  25.4 1.4 %collective-permute-done.5 = bf16[64,1024]{1,0:T(8,128)(2,1)S(1)} collective-permute-done((bf16[64,1024]{1,0:T(8,128)(2,1)}, bf16[64,1024]{1,0:T(8,128)(2,1)S(1)}, u32[]{:S(2)}, u32[]{:S(2)}) %collective-permute-start.5) | collective-permute-done | bytes 131104 | tf_op jit(solution)/shard_map/ppermute | solution.py:25
  26.8 1.6 %collective-permute-start.6 = (bf16[32,1024]{1,0:T(8,128)(2,1)S(1)}, bf16[32,1024]{1,0:T(8,128)(2,1)S(1)}, u32[]{:S(2)}, u32[]{:S(2)}) collective-permute-start(bf16[32,1024]{1,0:T(8,128)(2,1)S(1)} %fusion), channel_id=1, source_target_pairs={{0,4},{1,5},{2,6},{3,7},{4,0},{5,1},{6,2},{7,3},{8,12},{9,13},{10,... | collective-permute-start | bytes 196616 | tf_op jit(solution)/shard_map/ppermute | solution.py:25
  28.5 2.7 %collective-permute-done.6 = bf16[32,1024]{1,0:T(8,128)(2,1)S(1)} collective-permute-done((bf16[32,1024]{1,0:T(8,128)(2,1)S(1)}, bf16[32,1024]{1,0:T(8,128)(2,1)S(1)}, u32[]{:S(2)}, u32[]{:S(2)}) %collective-permute-start.6) | collective-permute-done | bytes 65568 | tf_op jit(solution)/shard_map/ppermute | solution.py:25
  31.2 1.6 %collective-permute-start.7 = (bf16[16,1024]{1,0:T(8,128)(2,1)S(1)}, bf16[16,1024]{1,0:T(8,128)(2,1)S(1)}, u32[]{:S(2)}, u32[]{:S(2)}) collective-permute-start(bf16[16,1024]{1,0:T(8,128)(2,1)S(1)} %fusion.2), channel_id=1, source_target_pairs={{0,2},{1,3},{2,0},{3,1},{4,6},{5,7},{6,4},{7,5},{8,10},{9,11},{10,... | collective-permute-start | bytes 98312 | tf_op jit(solution)/shard_map/ppermute | solution.py:25
  32.8 2.4 %collective-permute-done.7 = bf16[16,1024]{1,0:T(8,128)(2,1)S(1)} collective-permute-done((bf16[16,1024]{1,0:T(8,128)(2,1)S(1)}, bf16[16,1024]{1,0:T(8,128)(2,1)S(1)}, u32[]{:S(2)}, u32[]{:S(2)}) %collective-permute-start.7) | collective-permute-done | bytes 32800 | tf_op jit(solution)/shard_map/ppermute | solution.py:25
  35.2 0.2 collective-permute-start.8
  35.4 4.5 %collective-permute-done.8 = bf16[8,1024]{1,0:T(8,128)(2,1)S(1)} collective-permute-done((bf16[8,1024]{1,0:T(8,128)(2,1)S(1)}, bf16[8,1024]{1,0:T(8,128)(2,1)S(1)}, u32[]{:S(2)}, u32[]{:S(2)}) %collective-permute-start.8) | collective-permute-done | bytes 16416 | tf_op jit(solution)/shard_map/ppermute | solution.py:25
  39.9 0.6 %fusion.8 = (bf16[8,512]{1,0:T(8,128)(2,1)}, bf16[8,512]{1,0:T(8,128)(2,1)}) fusion(bf16[8,1024]{1,0:T(8,128)(2,1)S(1)} %fusion.7), kind=kLoop, calls=%fused_computation.33 | loop fusion | bytes 32768 | tf_op jit(solution)/shard_map/slice | solution.py:201
  (28 shorter events, 0.2 us)
Async XLA Ops:
  0.6 5.9 %collective-permute-start = (bf16[8,512]{1,0:T(8,128)(2,1)}, bf16[8,512]{1,0:T(8,128)(2,1)S(1)}, u32[]{:S(2)}, u32[]{:S(2)}) collective-permute-start(bf16[8,512]{1,0:T(8,128)(2,1)} %param.14), channel_id=1, source_target_pairs={{0,8},{1,9},{2,10},{3,11},{4,12},{5,13},{6,14},{7,15},{8,0},{9,1},... | collective-permute-start | bytes 24584 | tf_op jit(solution)/shard_map/ppermute | solution.py:25
  4.7 4.8 %collective-permute-start.1 = (bf16[8,512]{1,0:T(8,128)(2,1)}, bf16[8,512]{1,0:T(8,128)(2,1)S(1)}, u32[]{:S(2)}, u32[]{:S(2)}) collective-permute-start(bf16[8,512]{1,0:T(8,128)(2,1)} %param.15), channel_id=1, source_target_pairs={{0,8},{1,9},{2,10},{3,11},{4,12},{5,13},{6,14},{7,15},{8,0},{9,1},... | collective-permute-start | bytes 24584 | tf_op jit(solution)/shard_map/ppermute | solution.py:25
  4.8 1.4 %copy-start.3 = (bf16[8,512]{1,0:T(8,128)(2,1)S(1)}, bf16[8,512]{1,0:T(8,128)(2,1)}, u32[]{:S(2)}) copy-start(bf16[8,512]{1,0:T(8,128)(2,1)} %param.15) | copy-start | bytes 24580
  5.5 0.7 %copy-start.5 = (s32[128]{0:T(128)S(1)}, s32[128]{0:T(128)}, u32[]{:S(2)}) copy-start(s32[128]{0:T(128)} %constant.61.clone) | copy-start | bytes 1540
  5.5 0.7 %copy-start.6 = (s32[128]{0:T(128)S(1)}, s32[128]{0:T(128)}, u32[]{:S(2)}) copy-start(s32[128]{0:T(128)} %constant.60.clone) | copy-start | bytes 1540
  9.5 3.9 %collective-permute-start.2 = (bf16[16,1024]{1,0:T(8,128)(2,1)S(1)}, bf16[16,1024]{1,0:T(8,128)(2,1)S(1)}, u32[]{:S(2)}, u32[]{:S(2)}) collective-permute-start(bf16[16,1024]{1,0:T(8,128)(2,1)S(1)} %pad_maximum_fusion.2), channel_id=1, source_target_pairs={{0,2},{1,3},{2,0},{3,1},{4,6},{5,7},{6,4},{7,5},{8,10},{9,11},{10,... | collective-permute-start | bytes 98312 | tf_op jit(solution)/shard_map/ppermute | solution.py:25
  11.0 0.7 %copy-start.4 = (s32[2,16]{1,0:T(2,128)S(1)}, s32[2,16]{1,0:T(2,128)}, u32[]{:S(2)}) copy-start(s32[2,16]{1,0:T(2,128)} %param.18) | copy-start | bytes 388
  13.4 4.3 %collective-permute-start.3 = (bf16[32,1024]{1,0:T(8,128)(2,1)S(1)}, bf16[32,1024]{1,0:T(8,128)(2,1)S(1)}, u32[]{:S(2)}, u32[]{:S(2)}) collective-permute-start(bf16[32,1024]{1,0:T(8,128)(2,1)S(1)} %pad_maximum_fusion.1), channel_id=1, source_target_pairs={{0,4},{1,5},{2,6},{3,7},{4,0},{5,1},{6,2},{7,3},{8,12},{9,13},{10,... | collective-permute-start | bytes 196616 | tf_op jit(solution)/shard_map/ppermute | solution.py:25
  15.0 0.7 %copy-start.7 = (s32[2]{0:T(128)S(1)}, s32[2]{0:T(128)}, u32[]{:S(2)}) copy-start(s32[2]{0:T(128)} %param.17) | copy-start | bytes 28
  17.7 1.4 %copy-start = (bf16[64,1024]{1,0:T(8,128)(2,1)}, bf16[64,1024]{1,0:T(8,128)(2,1)S(1)}, u32[]{:S(2)}) copy-start(bf16[64,1024]{1,0:T(8,128)(2,1)S(1)} %pad_maximum_fusion.kva_ref) | copy-start | bytes 393220
  17.7 1.4 %collective-permute-start.4 = (bf16[64,1024]{1,0:T(8,128)(2,1)S(1)}, bf16[64,1024]{1,0:T(8,128)(2,1)S(1)}, u32[]{:S(2)}, u32[]{:S(2)}) collective-permute-start(bf16[64,1024]{1,0:T(8,128)(2,1)S(1)} %pad_maximum_fusion.kva_ref), channel_id=1, source_target_pairs={{0,1},{1,0},{2,3},{3,2},{4,5},{5,4},{6,7},{7,6},{8,9},{9,8},{10,11... | collective-permute-start | bytes 393224 | tf_op jit(solution)/shard_map/ppermute | solution.py:25
  19.1 0.6 %copy-start.2 = (bf16[64,1024]{1,0:T(8,128)(2,1)}, bf16[64,1024]{1,0:T(8,128)(2,1)S(1)}, u32[]{:S(2)}) copy-start(bf16[64,1024]{1,0:T(8,128)(2,1)S(1)} %collective-permute-done.4.kvb_ref) | copy-start | bytes 393220
  25.2 1.6 %copy-start.1 = (f32[64,1024]{1,0:T(8,128)S(1)}, f32[64,1024]{1,0:T(8,128)}, u32[]{:S(2)}) copy-start(f32[64,1024]{1,0:T(8,128)} %get-tuple-element.11) | copy-start | bytes 786436
  25.2 1.6 %collective-permute-start.5 = (bf16[64,1024]{1,0:T(8,128)(2,1)}, bf16[64,1024]{1,0:T(8,128)(2,1)S(1)}, u32[]{:S(2)}, u32[]{:S(2)}) collective-permute-start(bf16[64,1024]{1,0:T(8,128)(2,1)} %get-tuple-element.12), channel_id=1, source_target_pairs={{0,1},{1,0},{2,3},{3,2},{4,5},{5,4},{6,7},{7,6},{8,9},{9,8},{10,11... | collective-permute-start | bytes 393224 | tf_op jit(solution)/shard_map/ppermute | solution.py:25
  26.8 4.3 %collective-permute-start.6 = (bf16[32,1024]{1,0:T(8,128)(2,1)S(1)}, bf16[32,1024]{1,0:T(8,128)(2,1)S(1)}, u32[]{:S(2)}, u32[]{:S(2)}) collective-permute-start(bf16[32,1024]{1,0:T(8,128)(2,1)S(1)} %fusion), channel_id=1, source_target_pairs={{0,4},{1,5},{2,6},{3,7},{4,0},{5,1},{6,2},{7,3},{8,12},{9,13},{10,... | collective-permute-start | bytes 196616 | tf_op jit(solution)/shard_map/ppermute | solution.py:25
  31.2 4.0 %collective-permute-start.7 = (bf16[16,1024]{1,0:T(8,128)(2,1)S(1)}, bf16[16,1024]{1,0:T(8,128)(2,1)S(1)}, u32[]{:S(2)}, u32[]{:S(2)}) collective-permute-start(bf16[16,1024]{1,0:T(8,128)(2,1)S(1)} %fusion.2), channel_id=1, source_target_pairs={{0,2},{1,3},{2,0},{3,1},{4,6},{5,7},{6,4},{7,5},{8,10},{9,11},{10,... | collective-permute-start | bytes 98312 | tf_op jit(solution)/shard_map/ppermute | solution.py:25
  35.2 4.7 %collective-permute-start.8 = (bf16[8,1024]{1,0:T(8,128)(2,1)S(1)}, bf16[8,1024]{1,0:T(8,128)(2,1)S(1)}, u32[]{:S(2)}, u32[]{:S(2)}) collective-permute-start(bf16[8,1024]{1,0:T(8,128)(2,1)S(1)} %fusion.5), channel_id=1, source_target_pairs={{0,8},{1,9},{2,10},{3,11},{4,12},{5,13},{6,14},{7,15},{8,0},{9,1},... | collective-permute-start | bytes 49160 | tf_op jit(solution)/shard_map/ppermute | solution.py:25

commit v17 on v11

--- a/solution.py
+++ b/solution.py
@@ -45,14 +45,29 @@
     size = lax.axis_size(axis_name)
     bits = exchange_bits(size)
     pending = [keep]
-    for bit in range(bits):
+    ring_bits = bits - 2 if bits >= 3 else bits
+    for bit in range(ring_bits):
         if bit > 0:
             split = pending[0].shape[0] // 2
             send = sum(part[split:] for part in pending[1:])
-            send = pending[0][split:] + send
+            send = (pending[0][split:] + send).astype(jnp.bfloat16)
             pending = [part[:split] for part in pending]
-        pending.append(swap_with(send, axis_name, size, bit))
-    return sum(pending[1:], pending[0])
+        pending.append(swap_with(send, axis_name, size, bit).astype(jnp.float32))
+    if ring_bits == bits:
+        return sum(pending[1:], pending[0])
+    if ring_bits == 0:
+        pending = [keep, send]
+    quarter = pending[0].shape[0] // 4
+    received = []
+    for spot in range(1, 4):
+        rows = slice(spot * quarter, (spot + 1) * quarter)
+        piece = sum(part[rows] for part in pending[1:])
+        piece = (pending[0][rows] + piece).astype(jnp.bfloat16)
+        flip = ((spot >> 1) & 1) << (bits - 2) | (spot & 1) << (bits - 1)
+        pairs = [(index, index ^ flip) for index in range(size)]
+        received.append(lax.ppermute(piece, axis_name, pairs).astype(jnp.float32))
+    total = sum(part[:quarter] for part in pending[1:])
+    return pending[0][:quarter] + total + sum(received[1:], received[0])
 
 
 def contract_rows(left, right):
@@ -117,9 +132,9 @@
         key_total = jnp.dot(dscore, q, preferred_element_type=jnp.float32) * score_scale
         value_total = jnp.dot(prob.astype(jnp.bfloat16), do, preferred_element_type=jnp.float32)
         keep_ref[:, columns] = key_total[:half]
-        send_ref[:, columns] = key_total[half:doc_rows]
+        send_ref[:, columns] = key_total[half:doc_rows].astype(send_ref.dtype)
         keep_ref[:, value_columns] = value_total[:half]
-        send_ref[:, value_columns] = value_total[half:doc_rows]
+        send_ref[:, value_columns] = value_total[half:doc_rows].astype(send_ref.dtype)
         sk_ref[:, columns] = key_total[doc_rows:].astype(sk_ref.dtype)
         sv_ref[:, columns] = value_total[doc_rows:].astype(sv_ref.dtype)
 
@@ -170,7 +185,7 @@
         out_shape=(
             jax.ShapeDtypeStruct(queries.shape, jnp.bfloat16),
             jax.ShapeDtypeStruct((half_rows, 2 * key_value_width), jnp.float32),
-            jax.ShapeDtypeStruct((half_rows, 2 * key_value_width), jnp.float32),
+            jax.ShapeDtypeStruct((half_rows, 2 * key_value_width), jnp.bfloat16),
             jax.ShapeDtypeStruct(response_keys.shape, jnp.bfloat16),
             jax.ShapeDtypeStruct(response_values.shape, jnp.bfloat16),
         ),

time: 41.5 us -> 38.3 us (0.923)
  waiting for transfers between devices: 13.7 us -> 11.5 us
  other arithmetic: 2.22 us -> 1.36 us
    ppermute x8 -> x6, waiting for transfers between devices: 13.7 us -> 7.6 us  [swap_with(): return lax.ppermute(block, axis_name, pairs)]
    ppermute x8 -> x6, starting transfers between devices: 14.7 us -> 9.98 us  [swap_with(): return lax.ppermute(block, axis_name, pairs)]
    ppermute x0 -> x3, starting transfers between devices: none -> 4.62 us  [scatter_sum_rows(): received.append(lax.ppermute(piece, axis_name, pairs).astype(jnp.float32))]
    ppermute x0 -> x3, waiting for transfers between devices: none -> 3.9 us  [scatter_sum_rows(): received.append(lax.ppermute(piece, axis_name, pairs).astype(jnp.float32))]
    add x3 -> x0, other arithmetic: 0.95 us -> none  [scatter_sum_rows(): send = pending[0][split:] + send]
  transfers between devices with their start and end apart: 8 -> 9, of which waited for: 8 -> 8; matrix products, arithmetic and copies ran while one was open for 6% -> 6% of each run, Pallas kernels for 0% -> 0%
where the time goes in v17:
time: 38.3 us; the launch traced here: 38 us
  starting transfers between devices  14.6 us (38%)
  waiting for transfers between devices  11.5 us (30%)
  Pallas kernels  5.43 us (14%)
  local copies, waits for them, and re-layouts  4.37 us (11%)
  other arithmetic  1.36 us (4%)
  between operations  0.72 us (2%)
    ppermute x6, starting transfers between devices, swap_with(): return lax.ppermute(block, axis_name, pairs)  9.98 us
    ppermute x6, waiting for transfers between devices, swap_with(): return lax.ppermute(block, axis_name, pairs)  7.6 us
    pallas_call x1, Pallas kernels, per_device(): pl.pallas_call(attention_kernel, out_shape=(jax.ShapeDtypeStruct(queries....  5.43 us
    ppermute x3, starting transfers between devices, scatter_sum_rows(): received.append(lax.ppermute(piece, axis_name, pairs).astype(jnp.float32))  4.62 us
    ppermute x3, waiting for transfers between devices, scatter_sum_rows(): received.append(lax.ppermute(piece, axis_name, pairs).astype(jnp.float32))  3.9 us
    unnamed x18, local copies, waits for them, and re-layouts  2.8 us
  transfers between devices with their start and end apart: 9, of which 8 were waited for; matrix products, arithmetic and copies ran while one was open for 6% of the time, Pallas kernels for 0%

profile of v17, /device:TPU:0, one launch (start us, length us, event | category | flops | bytes accessed | tf_op | source)
XLA Modules:
  0.0 38.0 jit_solution(2231605680291282627)
XLA Ops:
  0.6 0.7 %constant_dynamic-update-slice_fusion.1 = bf16[8,1024]{1,0:T(8,128)(2,1)S(1)} fusion(bf16[8,512]{1,0:T(8,128)(2,1)} %param.14), kind=kLoop, calls=%fused_computation.23 | loop fusion | bytes 16384
  1.4 4.0 %collective-permute-start = (bf16[8,1024]{1,0:T(8,128)(2,1)S(1)}, bf16[8,1024]{1,0:T(8,128)(2,1)S(1)}, u32[]{:S(2)}, u32[]{:S(2)}) collective-permute-start(bf16[8,1024]{1,0:T(8,128)(2,1)S(1)} %constant_dynamic-update-slice_fusion), channel_id=1, source_target_pairs={{0,8},{1,9},{2,10},{3,11},{4,12},{5,13},{6,14},{7,15},{8,0},{9,1},... | collective-permute-start | bytes 49160 | tf_op jit(solution)/shard_map/ppermute | solution.py:25
  5.4 0.7 %copy-done.5 = s32[128]{0:T(128)S(1)} copy-done((s32[128]{0:T(128)S(1)}, s32[128]{0:T(128)}, u32[]{:S(2)}) %copy-start.5) | copy-done | bytes 536
  6.0 0.0 copy-done.6
  6.1 1.0 %collective-permute-done = bf16[8,1024]{1,0:T(8,128)(2,1)S(1)} collective-permute-done((bf16[8,1024]{1,0:T(8,128)(2,1)S(1)}, bf16[8,1024]{1,0:T(8,128)(2,1)S(1)}, u32[]{:S(2)}, u32[]{:S(2)}) %collective-permute-start) | collective-permute-done | bytes 16416 | tf_op jit(solution)/shard_map/ppermute | solution.py:25
  7.1 1.9 %collective-permute-start.1 = (bf16[16,1024]{1,0:T(8,128)(2,1)S(1)}, bf16[16,1024]{1,0:T(8,128)(2,1)S(1)}, u32[]{:S(2)}, u32[]{:S(2)}) collective-permute-start(bf16[16,1024]{1,0:T(8,128)(2,1)S(1)} %pad_maximum_fusion.2), channel_id=1, source_target_pairs={{0,4},{1,5},{2,6},{3,7},{4,0},{5,1},{6,2},{7,3},{8,12},{9,13},{10,... | collective-permute-start | bytes 98312 | tf_op jit(solution)/shard_map/ppermute | solution.py:25
  9.0 0.7 %copy-done.4 = s32[2,16]{1,0:T(2,128)S(1)} copy-done((s32[2,16]{1,0:T(2,128)S(1)}, s32[2,16]{1,0:T(2,128)}, u32[]{:S(2)}) %copy-start.4) | copy-done | bytes 152
  9.7 0.1 copy.16
  9.8 0.1 broadcast_in_dim.20
  9.9 0.1 reshape.56
  9.9 0.6 %gather_fusion = s32[128,128]{1,0:T(8,128)S(1)} fusion(s32[16,128]{1,0:T(8,128)S(1)} %bitcast.3, s32[1024]{0:T(1024)S(1)} %pad_clamp_fusion), kind=kCustom, calls=%fused_computation | custom fusion | bytes 131584 | tf_op jit(solution)/shard_map/jit(_take)/gather | solution.py:180
  10.6 0.4 %collective-permute-done.1 = bf16[16,1024]{1,0:T(8,128)(2,1)S(1)} collective-permute-done((bf16[16,1024]{1,0:T(8,128)(2,1)S(1)}, bf16[16,1024]{1,0:T(8,128)(2,1)S(1)}, u32[]{:S(2)}, u32[]{:S(2)}) %collective-permute-start.1) | collective-permute-done | bytes 32800 | tf_op jit(solution)/shard_map/ppermute | solution.py:25
  11.0 1.9 %collective-permute-start.2 = (bf16[32,1024]{1,0:T(8,128)(2,1)S(1)}, bf16[32,1024]{1,0:T(8,128)(2,1)S(1)}, u32[]{:S(2)}, u32[]{:S(2)}) collective-permute-start(bf16[32,1024]{1,0:T(8,128)(2,1)S(1)} %pad_maximum_fusion.1), channel_id=1, source_target_pairs={{0,2},{1,3},{2,0},{3,1},{4,6},{5,7},{6,4},{7,5},{8,10},{9,11},{10,... | collective-permute-start | bytes 196616 | tf_op jit(solution)/shard_map/ppermute | solution.py:25
  12.9 0.7 %fusion.1.vis_ref = f32[128,128]{1,0:T(8,128)} fusion(s32[128,128]{1,0:T(8,128)S(1)} %gather_fusion, pred[128]{0:T(512)(128)(4,1)S(1)} %get-tuple-element.15), kind=kLoop, calls=%fused_computation.6 | loop fusion | flops 49152 | bytes 131200 | tf_op jit(solution)/shard_map/convert_element_type | solution.py:180
  13.6 0.1 broadcast_in_dim.23
  13.7 0.1 reshape.57
  13.8 1.5 %collective-permute-done.2 = bf16[32,1024]{1,0:T(8,128)(2,1)S(1)} collective-permute-done((bf16[32,1024]{1,0:T(8,128)(2,1)S(1)}, bf16[32,1024]{1,0:T(8,128)(2,1)S(1)}, u32[]{:S(2)}, u32[]{:S(2)}) %collective-permute-start.2) | collective-permute-done | bytes 65568 | tf_op jit(solution)/shard_map/ppermute | solution.py:25
  15.3 0.1 collective-permute-start.3
  15.4 0.5 %compare_convert_fusion.live_ref = f32[1,128]{1,0:T(1,128)} fusion(s32[1,128]{1,0:T(1,128)S(1)} %reshape.57), kind=kLoop, calls=%fused_computation.25 | loop fusion | flops 1024 | bytes 1024 | tf_op jit(solution)/shard_map/convert_element_type | solution.py:160
  15.9 0.8 %collective-permute-done.3.kvb_ref = bf16[64,1024]{1,0:T(8,128)(2,1)S(1)} collective-permute-done((bf16[64,1024]{1,0:T(8,128)(2,1)S(1)}, bf16[64,1024]{1,0:T(8,128)(2,1)S(1)}, u32[]{:S(2)}, u32[]{:S(2)}) %collective-permute-start.3) | collective-permute-done | bytes 131104 | tf_op jit(solution)/shard_map/ppermute | solution.py:25
  16.7 0.7 %copy-done.2 = bf16[64,1024]{1,0:T(8,128)(2,1)} copy-done((bf16[64,1024]{1,0:T(8,128)(2,1)}, bf16[64,1024]{1,0:T(8,128)(2,1)S(1)}, u32[]{:S(2)}) %copy-start.2) | copy-done | bytes 131096
  17.4 5.4 %shard_map.146 = (bf16[128,2560]{1,0:T(8,128)(2,1)}, f32[64,1024]{1,0:T(8,128)}, bf16[64,1024]{1,0:T(8,128)(2,1)}, bf16[128,512]{1,0:T(8,128)(2,1)}, bf16[128,512]{1,0:T(8,128)(2,1)}) custom-call(bf16[128,2560]{1,0:T(8,128)(2,1)} %q_ref.1, bf16[128,2560]{1,0:T(8,128)(2,1)} %do_ref.1, bf16[64,1024]{1,0:T(8,128)(2,1)} %copy-done, bf16[64,1024]{1,0:T(8,128)(2,1)} %copy-done.2, ...), custom_call_target="tpu_custom_call" | custom-call | tf_op jit(solution)/shard_map/pallas_call | solution.py:183
  22.8 0.1 collective-permute-start.4
  23.0 1.4 %collective-permute-done.4 = bf16[64,1024]{1,0:T(8,128)(2,1)S(1)} collective-permute-done((bf16[64,1024]{1,0:T(8,128)(2,1)}, bf16[64,1024]{1,0:T(8,128)(2,1)S(1)}, u32[]{:S(2)}, u32[]{:S(2)}) %collective-permute-start.4) | collective-permute-done | bytes 131104 | tf_op jit(solution)/shard_map/ppermute | solution.py:25
  24.4 1.9 %collective-permute-start.5 = (bf16[32,1024]{1,0:T(8,128)(2,1)S(1)}, bf16[32,1024]{1,0:T(8,128)(2,1)S(1)}, u32[]{:S(2)}, u32[]{:S(2)}) collective-permute-start(bf16[32,1024]{1,0:T(8,128)(2,1)S(1)} %fusion), channel_id=1, source_target_pairs={{0,2},{1,3},{2,0},{3,1},{4,6},{5,7},{6,4},{7,5},{8,10},{9,11},{10,... | collective-permute-start | bytes 196616 | tf_op jit(solution)/shard_map/ppermute | solution.py:25
  26.4 2.4 %collective-permute-done.5 = bf16[32,1024]{1,0:T(8,128)(2,1)S(1)} collective-permute-done((bf16[32,1024]{1,0:T(8,128)(2,1)S(1)}, bf16[32,1024]{1,0:T(8,128)(2,1)S(1)}, u32[]{:S(2)}, u32[]{:S(2)}) %collective-permute-start.5) | collective-permute-done | bytes 65568 | tf_op jit(solution)/shard_map/ppermute | solution.py:25
  28.8 3.0 %collective-permute-start.6 = (bf16[8,1024]{1,0:T(8,128)(2,1)S(1)}, bf16[8,1024]{1,0:T(8,128)(2,1)S(1)}, u32[]{:S(2)}, u32[]{:S(2)}) collective-permute-start(bf16[8,1024]{1,0:T(8,128)(2,1)S(1)} %get-tuple-element.17), channel_id=1, source_target_pairs={{0,8},{1,9},{2,10},{3,11},{4,12},{5,13},{6,14},{7,15},{8,0},{9,1},... | collective-permute-start | bytes 49160 | tf_op jit(solution)/shard_map/ppermute | solution.py:68
  31.8 1.3 %collective-permute-start.8 = (bf16[8,1024]{1,0:T(8,128)(2,1)S(1)}, bf16[8,1024]{1,0:T(8,128)(2,1)S(1)}, u32[]{:S(2)}, u32[]{:S(2)}) collective-permute-start(bf16[8,1024]{1,0:T(8,128)(2,1)S(1)} %get-tuple-element.18), channel_id=1, source_target_pairs={{0,12},{1,13},{2,14},{3,15},{4,8},{5,9},{6,10},{7,11},{8,4},{9,5},... | collective-permute-start | bytes 49160 | tf_op jit(solution)/shard_map/ppermute | solution.py:68
  33.2 0.3 collective-permute-start.7
  33.5 0.1 collective-permute-done.6
  33.5 3.8 %collective-permute-done.8 = bf16[8,1024]{1,0:T(8,128)(2,1)S(1)} collective-permute-done((bf16[8,1024]{1,0:T(8,128)(2,1)S(1)}, bf16[8,1024]{1,0:T(8,128)(2,1)S(1)}, u32[]{:S(2)}, u32[]{:S(2)}) %collective-permute-start.8) | collective-permute-done | bytes 16416 | tf_op jit(solution)/shard_map/ppermute | solution.py:68
  37.4 0.6 %fusion.11 = (bf16[8,512]{1,0:T(8,128)(2,1)}, bf16[8,512]{1,0:T(8,128)(2,1)}) fusion(bf16[8,1024]{1,0:T(8,128)(2,1)S(1)} %fusion.10), kind=kLoop, calls=%fused_computation.32 | loop fusion | bytes 32768 | tf_op jit(solution)/shard_map/slice | solution.py:207
  (24 shorter events, 0.1 us)
Async XLA Ops:
  0.6 0.7 %copy-start.3 = (bf16[8,512]{1,0:T(8,128)(2,1)S(1)}, bf16[8,512]{1,0:T(8,128)(2,1)}, u32[]{:S(2)}) copy-start(bf16[8,512]{1,0:T(8,128)(2,1)} %param.15) | copy-start | bytes 24580
  1.4 5.8 %collective-permute-start = (bf16[8,1024]{1,0:T(8,128)(2,1)S(1)}, bf16[8,1024]{1,0:T(8,128)(2,1)S(1)}, u32[]{:S(2)}, u32[]{:S(2)}) collective-permute-start(bf16[8,1024]{1,0:T(8,128)(2,1)S(1)} %constant_dynamic-update-slice_fusion), channel_id=1, source_target_pairs={{0,8},{1,9},{2,10},{3,11},{4,12},{5,13},{6,14},{7,15},{8,0},{9,1},... | collective-permute-start | bytes 49160 | tf_op jit(solution)/shard_map/ppermute | solution.py:25
  5.4 0.7 %copy-start.5 = (s32[128]{0:T(128)S(1)}, s32[128]{0:T(128)}, u32[]{:S(2)}) copy-start(s32[128]{0:T(128)} %constant.61.clone) | copy-start | bytes 1540
  5.4 0.7 %copy-start.6 = (s32[128]{0:T(128)S(1)}, s32[128]{0:T(128)}, u32[]{:S(2)}) copy-start(s32[128]{0:T(128)} %constant.60.clone) | copy-start | bytes 1540
  7.1 3.9 %collective-permute-start.1 = (bf16[16,1024]{1,0:T(8,128)(2,1)S(1)}, bf16[16,1024]{1,0:T(8,128)(2,1)S(1)}, u32[]{:S(2)}, u32[]{:S(2)}) collective-permute-start(bf16[16,1024]{1,0:T(8,128)(2,1)S(1)} %pad_maximum_fusion.2), channel_id=1, source_target_pairs={{0,4},{1,5},{2,6},{3,7},{4,0},{5,1},{6,2},{7,3},{8,12},{9,13},{10,... | collective-permute-start | bytes 98312 | tf_op jit(solution)/shard_map/ppermute | solution.py:25
  9.0 0.7 %copy-start.4 = (s32[2,16]{1,0:T(2,128)S(1)}, s32[2,16]{1,0:T(2,128)}, u32[]{:S(2)}) copy-start(s32[2,16]{1,0:T(2,128)} %param.18) | copy-start | bytes 388
  11.0 4.3 %collective-permute-start.2 = (bf16[32,1024]{1,0:T(8,128)(2,1)S(1)}, bf16[32,1024]{1,0:T(8,128)(2,1)S(1)}, u32[]{:S(2)}, u32[]{:S(2)}) collective-permute-start(bf16[32,1024]{1,0:T(8,128)(2,1)S(1)} %pad_maximum_fusion.1), channel_id=1, source_target_pairs={{0,2},{1,3},{2,0},{3,1},{4,6},{5,7},{6,4},{7,5},{8,10},{9,11},{10,... | collective-permute-start | bytes 196616 | tf_op jit(solution)/shard_map/ppermute | solution.py:25
  12.9 0.7 %copy-start.7 = (s32[2]{0:T(128)S(1)}, s32[2]{0:T(128)}, u32[]{:S(2)}) copy-start(s32[2]{0:T(128)} %param.17) | copy-start | bytes 28
  15.3 1.4 %copy-start = (bf16[64,1024]{1,0:T(8,128)(2,1)}, bf16[64,1024]{1,0:T(8,128)(2,1)S(1)}, u32[]{:S(2)}) copy-start(bf16[64,1024]{1,0:T(8,128)(2,1)S(1)} %pad_maximum_fusion.kva_ref) | copy-start | bytes 393220
  15.3 1.4 %collective-permute-start.3 = (bf16[64,1024]{1,0:T(8,128)(2,1)S(1)}, bf16[64,1024]{1,0:T(8,128)(2,1)S(1)}, u32[]{:S(2)}, u32[]{:S(2)}) collective-permute-start(bf16[64,1024]{1,0:T(8,128)(2,1)S(1)} %pad_maximum_fusion.kva_ref), channel_id=1, source_target_pairs={{0,1},{1,0},{2,3},{3,2},{4,5},{5,4},{6,7},{7,6},{8,9},{9,8},{10,11... | collective-permute-start | bytes 393224 | tf_op jit(solution)/shard_map/ppermute | solution.py:25
  16.7 0.7 %copy-start.2 = (bf16[64,1024]{1,0:T(8,128)(2,1)}, bf16[64,1024]{1,0:T(8,128)(2,1)S(1)}, u32[]{:S(2)}) copy-start(bf16[64,1024]{1,0:T(8,128)(2,1)S(1)} %collective-permute-done.3.kvb_ref) | copy-start | bytes 393220
  22.8 1.6 %copy-start.1 = (f32[64,1024]{1,0:T(8,128)S(1)}, f32[64,1024]{1,0:T(8,128)}, u32[]{:S(2)}) copy-start(f32[64,1024]{1,0:T(8,128)} %get-tuple-element.11) | copy-start | bytes 786436
  22.8 1.6 %collective-permute-start.4 = (bf16[64,1024]{1,0:T(8,128)(2,1)}, bf16[64,1024]{1,0:T(8,128)(2,1)S(1)}, u32[]{:S(2)}, u32[]{:S(2)}) collective-permute-start(bf16[64,1024]{1,0:T(8,128)(2,1)} %get-tuple-element.12), channel_id=1, source_target_pairs={{0,1},{1,0},{2,3},{3,2},{4,5},{5,4},{6,7},{7,6},{8,9},{9,8},{10,11... | collective-permute-start | bytes 393224 | tf_op jit(solution)/shard_map/ppermute | solution.py:25
  24.4 4.3 %collective-permute-start.5 = (bf16[32,1024]{1,0:T(8,128)(2,1)S(1)}, bf16[32,1024]{1,0:T(8,128)(2,1)S(1)}, u32[]{:S(2)}, u32[]{:S(2)}) collective-permute-start(bf16[32,1024]{1,0:T(8,128)(2,1)S(1)} %fusion), channel_id=1, source_target_pairs={{0,2},{1,3},{2,0},{3,1},{4,6},{5,7},{6,4},{7,5},{8,10},{9,11},{10,... | collective-permute-start | bytes 196616 | tf_op jit(solution)/shard_map/ppermute | solution.py:25
  28.8 4.7 %collective-permute-start.6 = (bf16[8,1024]{1,0:T(8,128)(2,1)S(1)}, bf16[8,1024]{1,0:T(8,128)(2,1)S(1)}, u32[]{:S(2)}, u32[]{:S(2)}) collective-permute-start(bf16[8,1024]{1,0:T(8,128)(2,1)S(1)} %get-tuple-element.17), channel_id=1, source_target_pairs={{0,8},{1,9},{2,10},{3,11},{4,12},{5,13},{6,14},{7,15},{8,0},{9,1},... | collective-permute-start | bytes 49160 | tf_op jit(solution)/shard_map/ppermute | solution.py:68
  31.8 5.5 %collective-permute-start.8 = (bf16[8,1024]{1,0:T(8,128)(2,1)S(1)}, bf16[8,1024]{1,0:T(8,128)(2,1)S(1)}, u32[]{:S(2)}, u32[]{:S(2)}) collective-permute-start(bf16[8,1024]{1,0:T(8,128)(2,1)S(1)} %get-tuple-element.18), channel_id=1, source_target_pairs={{0,12},{1,13},{2,14},{3,15},{4,8},{5,9},{6,10},{7,11},{8,4},{9,5},... | collective-permute-start | bytes 49160 | tf_op jit(solution)/shard_map/ppermute | solution.py:68
  33.2 4.2 %collective-permute-start.7 = (bf16[8,1024]{1,0:T(8,128)(2,1)S(1)}, bf16[8,1024]{1,0:T(8,128)(2,1)S(1)}, u32[]{:S(2)}, u32[]{:S(2)}) collective-permute-start(bf16[8,1024]{1,0:T(8,128)(2,1)S(1)} %get-tuple-element.19), channel_id=1, source_target_pairs={{0,4},{1,5},{2,6},{3,7},{4,0},{5,1},{6,2},{7,3},{8,12},{9,13},{10,... | collective-permute-start | bytes 49160 | tf_op jit(solution)/shard_map/ppermute | solution.py:68

commit v18 on v15

--- a/solution.py
+++ b/solution.py
@@ -87,7 +87,7 @@
 
 
 def attention_kernel(
-    q_ref, do_ref, kva_ref, kvb_ref, ks_ref, vs_ref, vis_ref, self_ref, live_ref,
+    q_ref, do_ref, kva_ref, kvb_ref, ks_ref, vs_ref, bias_ref, live_ref,
     dq_ref, keep_ref, send_ref, sk_ref, sv_ref,
 ):
     token_rows = q_ref.shape[0]
@@ -95,9 +95,6 @@
     half = kva_ref.shape[0]
     doc_rows = 2 * half
     score_scale = HEAD_SIZE ** (-0.5)
-    seen = jnp.concatenate(
-        [jnp.concatenate([vis_ref[...], self_ref[...]], axis=0)] * GROUP_HEADS, axis=1
-    ) > 0.5
     live = jnp.concatenate([live_ref[...]] * GROUP_HEADS, axis=1)
     for c in range(KEY_HEADS):
         columns = slice(c * HEAD_SIZE, (c + 1) * HEAD_SIZE)
@@ -110,7 +107,7 @@
         )
         q = stacked_heads(q_ref, c)
         do = stacked_heads(do_ref, c)
-        score = jnp.where(seen, contract_cols(keys, q) * score_scale, masked_score)
+        score = contract_cols(keys, q) * score_scale + bias_ref[...]
         top = jnp.max(score, axis=0, keepdims=True)
         grown = jnp.exp(score - top)
         prob = grown * (live / jnp.sum(grown, axis=0, keepdims=True))
@@ -190,8 +187,11 @@
         doc_other,
         response_keys,
         response_values,
-        doc_visible,
-        self_visible,
+        jnp.concatenate(
+            [jnp.where(jnp.concatenate([doc_visible, self_visible]) > 0.5, 0.0, masked_score)]
+            * GROUP_HEADS,
+            axis=1,
+        ),
         live,
     )
     summed = scatter_sum_rows(doc_keep, doc_send, "resp")

time: 38.5 us -> 40.2 us (1.044)
  waiting for transfers between devices: 11.4 us -> 15.5 us
  starting transfers between devices: 14.9 us -> 12.1 us
  local copies, waits for them, and re-layouts: 4.36 us -> 5.1 us
  other arithmetic: 1.37 us -> 0.82 us
    ppermute x8, waiting for transfers between devices: 11.4 us -> 15.5 us  [swap_with(): return lax.ppermute(block, axis_name, pairs)]
    ppermute x8, starting transfers between devices: 14.9 us -> 12.1 us  [swap_with(): return lax.ppermute(block, axis_name, pairs)]
    unnamed x18 -> x22, local copies, waits for them, and re-layouts: 2.79 us -> 3.53 us
    convert_element_type x1, other arithmetic: 0.72 us -> 0.08 us  [per_device(): (jnp.take(row_masks.T, global_rows // block_rows, axis=0) == 1).astype(jn...]
  transfers between devices with their start and end apart: 8 -> 8, of which waited for: 8 -> 7; matrix products, arithmetic and copies ran while one was open for 6% -> 4% of each run, Pallas kernels for 0% -> 0%
where the time goes in v18:
time: 40.2 us; the launch traced here: 39.9 us
  waiting for transfers between devices  15.5 us (39%)
  starting transfers between devices  12.1 us (30%)
  Pallas kernels  5.62 us (14%)
  local copies, waits for them, and re-layouts  5.1 us (13%)
  other arithmetic  0.82 us (2%)
  between operations  0.8 us (2%)
    ppermute x8, waiting for transfers between devices, swap_with(): return lax.ppermute(block, axis_name, pairs)  15.5 us
    ppermute x8, starting transfers between devices, swap_with(): return lax.ppermute(block, axis_name, pairs)  12.1 us
    pallas_call x1, Pallas kernels, per_device(): pl.pallas_call(attention_kernel, out_shape=(jax.ShapeDtypeStruct(queries....  5.62 us
    unnamed x22, local copies, waits for them, and re-layouts  3.53 us
  transfers between devices with their start and end apart: 8, of which 7 were waited for; matrix products, arithmetic and copies ran while one was open for 4% of the time, Pallas kernels for 0%

profile of v18, /device:TPU:0, one launch (start us, length us, event | category | flops | bytes accessed | tf_op | source)
XLA Modules:
  0.0 39.9 jit_solution(3873726441182291391)
XLA Ops:
  0.6 0.7 %constant_dynamic-update-slice_fusion.1 = bf16[8,1024]{1,0:T(8,128)(2,1)S(1)} fusion(bf16[8,512]{1,0:T(8,128)(2,1)} %param.14), kind=kLoop, calls=%fused_computation.27 | loop fusion | bytes 16384
  1.4 4.0 %collective-permute-start = (bf16[8,1024]{1,0:T(8,128)(2,1)S(1)}, bf16[8,1024]{1,0:T(8,128)(2,1)S(1)}, u32[]{:S(2)}, u32[]{:S(2)}) collective-permute-start(bf16[8,1024]{1,0:T(8,128)(2,1)S(1)} %constant_dynamic-update-slice_fusion), channel_id=1, source_target_pairs={{0,8},{1,9},{2,10},{3,11},{4,12},{5,13},{6,14},{7,15},{8,0},{9,1},... | collective-permute-start | bytes 49160 | tf_op jit(solution)/shard_map/ppermute | solution.py:25
  5.4 0.7 %copy-done.7 = s32[128]{0:T(128)S(1)} copy-done((s32[128]{0:T(128)S(1)}, s32[128]{0:T(128)}, u32[]{:S(2)}) %copy-start.7) | copy-done | bytes 536
  6.0 0.0 copy-done.8
  6.1 0.0 copy-start.6
  6.1 0.7 %copy-done.6 = s32[2,16]{1,0:T(2,128)S(1)} copy-done((s32[2,16]{1,0:T(2,128)S(1)}, s32[2,16]{1,0:T(2,128)}, u32[]{:S(2)}) %copy-start.6) | copy-done | bytes 152
  6.8 0.1 copy.16
  6.8 0.1 broadcast_in_dim.28
  6.9 0.1 reshape.56
  7.0 0.6 %gather_fusion = s32[128,128]{1,0:T(8,128)S(1)} fusion(s32[16,128]{1,0:T(8,128)S(1)} %bitcast.3, s32[1024]{0:T(1024)S(1)} %pad_clamp_fusion), kind=kCustom, calls=%fused_computation | custom fusion | bytes 131584 | tf_op jit(solution)/shard_map/jit(_take)/gather | solution.py:171
  7.7 0.1 fusion.3
  7.8 0.7 %copy-done.4 = f32[128,128]{1,0:T(8,128)S(1)} copy-done((f32[128,128]{1,0:T(8,128)S(1)}, f32[128,128]{1,0:T(8,128)}, u32[]{:S(2)}) %copy-start.4) | copy-done | bytes 65560
  8.6 1.6 %collective-permute-start.1 = (bf16[16,1024]{1,0:T(8,128)(2,1)S(1)}, bf16[16,1024]{1,0:T(8,128)(2,1)S(1)}, u32[]{:S(2)}, u32[]{:S(2)}) collective-permute-start(bf16[16,1024]{1,0:T(8,128)(2,1)S(1)} %pad_maximum_fusion.2), channel_id=1, source_target_pairs={{0,2},{1,3},{2,0},{3,1},{4,6},{5,7},{6,4},{7,5},{8,10},{9,11},{10,... | collective-permute-start | bytes 98312 | tf_op jit(solution)/shard_map/ppermute | solution.py:25
  10.2 2.4 %collective-permute-done.1 = bf16[16,1024]{1,0:T(8,128)(2,1)S(1)} collective-permute-done((bf16[16,1024]{1,0:T(8,128)(2,1)S(1)}, bf16[16,1024]{1,0:T(8,128)(2,1)S(1)}, u32[]{:S(2)}, u32[]{:S(2)}) %collective-permute-start.1) | collective-permute-done | bytes 32800 | tf_op jit(solution)/shard_map/ppermute | solution.py:25
  12.6 1.6 %collective-permute-start.2 = (bf16[32,1024]{1,0:T(8,128)(2,1)S(1)}, bf16[32,1024]{1,0:T(8,128)(2,1)S(1)}, u32[]{:S(2)}, u32[]{:S(2)}) collective-permute-start(bf16[32,1024]{1,0:T(8,128)(2,1)S(1)} %pad_maximum_fusion.1), channel_id=1, source_target_pairs={{0,4},{1,5},{2,6},{3,7},{4,0},{5,1},{6,2},{7,3},{8,12},{9,13},{10,... | collective-permute-start | bytes 196616 | tf_op jit(solution)/shard_map/ppermute | solution.py:25
  14.3 0.1 broadcast_in_dim.33
  14.3 0.1 reshape.57
  14.4 2.5 %collective-permute-done.2 = bf16[32,1024]{1,0:T(8,128)(2,1)S(1)} collective-permute-done((bf16[32,1024]{1,0:T(8,128)(2,1)S(1)}, bf16[32,1024]{1,0:T(8,128)(2,1)S(1)}, u32[]{:S(2)}, u32[]{:S(2)}) %collective-permute-start.2) | collective-permute-done | bytes 65568 | tf_op jit(solution)/shard_map/ppermute | solution.py:25
  16.9 0.1 collective-permute-start.3
  17.0 0.5 %compare_convert_fusion.live_ref = f32[1,128]{1,0:T(1,128)} fusion(s32[1,128]{1,0:T(1,128)S(1)} %reshape.57), kind=kLoop, calls=%fused_computation.30 | loop fusion | flops 1024 | bytes 1024 | tf_op jit(solution)/shard_map/convert_element_type | solution.py:151
  17.5 0.8 %collective-permute-done.3.kvb_ref = bf16[64,1024]{1,0:T(8,128)(2,1)S(1)} collective-permute-done((bf16[64,1024]{1,0:T(8,128)(2,1)S(1)}, bf16[64,1024]{1,0:T(8,128)(2,1)S(1)}, u32[]{:S(2)}, u32[]{:S(2)}) %collective-permute-start.3) | collective-permute-done | bytes 131104 | tf_op jit(solution)/shard_map/ppermute | solution.py:25
  18.4 0.7 %copy-done.3 = bf16[64,1024]{1,0:T(8,128)(2,1)} copy-done((bf16[64,1024]{1,0:T(8,128)(2,1)}, bf16[64,1024]{1,0:T(8,128)(2,1)S(1)}, u32[]{:S(2)}) %copy-start.3) | copy-done | bytes 131096
  19.0 5.6 %shard_map.146 = (bf16[128,2560]{1,0:T(8,128)(2,1)}, f32[64,1024]{1,0:T(8,128)}, bf16[64,1024]{1,0:T(8,128)(2,1)}, bf16[128,512]{1,0:T(8,128)(2,1)}, bf16[128,512]{1,0:T(8,128)(2,1)}) custom-call(bf16[128,2560]{1,0:T(8,128)(2,1)} %q_ref.1, bf16[128,2560]{1,0:T(8,128)(2,1)} %do_ref.1, bf16[64,1024]{1,0:T(8,128)(2,1)} %copy-done.1, ...), custom_call_target="tpu_custom_call" | custom-call | tf_op jit(solution)/shard_map/pallas_call | solution.py:174
  24.6 0.1 collective-permute-start.4
  24.8 1.4 %collective-permute-done.4 = bf16[64,1024]{1,0:T(8,128)(2,1)S(1)} collective-permute-done((bf16[64,1024]{1,0:T(8,128)(2,1)}, bf16[64,1024]{1,0:T(8,128)(2,1)S(1)}, u32[]{:S(2)}, u32[]{:S(2)}) %collective-permute-start.4) | collective-permute-done | bytes 131104 | tf_op jit(solution)/shard_map/ppermute | solution.py:25
  26.3 1.6 %collective-permute-start.5 = (bf16[32,1024]{1,0:T(8,128)(2,1)S(1)}, bf16[32,1024]{1,0:T(8,128)(2,1)S(1)}, u32[]{:S(2)}, u32[]{:S(2)}) collective-permute-start(bf16[32,1024]{1,0:T(8,128)(2,1)S(1)} %fusion), channel_id=1, source_target_pairs={{0,4},{1,5},{2,6},{3,7},{4,0},{5,1},{6,2},{7,3},{8,12},{9,13},{10,... | collective-permute-start | bytes 196616 | tf_op jit(solution)/shard_map/ppermute | solution.py:25
  27.9 2.7 %collective-permute-done.5 = bf16[32,1024]{1,0:T(8,128)(2,1)S(1)} collective-permute-done((bf16[32,1024]{1,0:T(8,128)(2,1)S(1)}, bf16[32,1024]{1,0:T(8,128)(2,1)S(1)}, u32[]{:S(2)}, u32[]{:S(2)}) %collective-permute-start.5) | collective-permute-done | bytes 65568 | tf_op jit(solution)/shard_map/ppermute | solution.py:25
  30.6 1.5 %collective-permute-start.6 = (bf16[16,1024]{1,0:T(8,128)(2,1)S(1)}, bf16[16,1024]{1,0:T(8,128)(2,1)S(1)}, u32[]{:S(2)}, u32[]{:S(2)}) collective-permute-start(bf16[16,1024]{1,0:T(8,128)(2,1)S(1)} %fusion.2), channel_id=1, source_target_pairs={{0,2},{1,3},{2,0},{3,1},{4,6},{5,7},{6,4},{7,5},{8,10},{9,11},{10,... | collective-permute-start | bytes 98312 | tf_op jit(solution)/shard_map/ppermute | solution.py:25
  32.2 2.4 %collective-permute-done.6 = bf16[16,1024]{1,0:T(8,128)(2,1)S(1)} collective-permute-done((bf16[16,1024]{1,0:T(8,128)(2,1)S(1)}, bf16[16,1024]{1,0:T(8,128)(2,1)S(1)}, u32[]{:S(2)}, u32[]{:S(2)}) %collective-permute-start.6) | collective-permute-done | bytes 32800 | tf_op jit(solution)/shard_map/ppermute | solution.py:25
  34.6 1.4 %collective-permute-start.7 = (bf16[8,1024]{1,0:T(8,128)(2,1)S(1)}, bf16[8,1024]{1,0:T(8,128)(2,1)S(1)}, u32[]{:S(2)}, u32[]{:S(2)}) collective-permute-start(bf16[8,1024]{1,0:T(8,128)(2,1)S(1)} %fusion.5), channel_id=1, source_target_pairs={{0,8},{1,9},{2,10},{3,11},{4,12},{5,13},{6,14},{7,15},{8,0},{9,1},... | collective-permute-start | bytes 49160 | tf_op jit(solution)/shard_map/ppermute | solution.py:25
  36.1 3.3 %collective-permute-done.7 = bf16[8,1024]{1,0:T(8,128)(2,1)S(1)} collective-permute-done((bf16[8,1024]{1,0:T(8,128)(2,1)S(1)}, bf16[8,1024]{1,0:T(8,128)(2,1)S(1)}, u32[]{:S(2)}, u32[]{:S(2)}) %collective-permute-start.7) | collective-permute-done | bytes 16416 | tf_op jit(solution)/shard_map/ppermute | solution.py:25
  39.3 0.6 %fusion.8 = (bf16[8,512]{1,0:T(8,128)(2,1)}, bf16[8,512]{1,0:T(8,128)(2,1)}) fusion(bf16[8,1024]{1,0:T(8,128)(2,1)S(1)} %fusion.7), kind=kLoop, calls=%fused_computation.37 | loop fusion | bytes 32768 | tf_op jit(solution)/shard_map/slice | solution.py:201
  (33 shorter events, 0.3 us)
Async XLA Ops:
  0.6 0.7 %copy-start.5 = (bf16[8,512]{1,0:T(8,128)(2,1)S(1)}, bf16[8,512]{1,0:T(8,128)(2,1)}, u32[]{:S(2)}) copy-start(bf16[8,512]{1,0:T(8,128)(2,1)} %param.15) | copy-start | bytes 24580
  1.4 7.2 %collective-permute-start = (bf16[8,1024]{1,0:T(8,128)(2,1)S(1)}, bf16[8,1024]{1,0:T(8,128)(2,1)S(1)}, u32[]{:S(2)}, u32[]{:S(2)}) collective-permute-start(bf16[8,1024]{1,0:T(8,128)(2,1)S(1)} %constant_dynamic-update-slice_fusion), channel_id=1, source_target_pairs={{0,8},{1,9},{2,10},{3,11},{4,12},{5,13},{6,14},{7,15},{8,0},{9,1},... | collective-permute-start | bytes 49160 | tf_op jit(solution)/shard_map/ppermute | solution.py:25
  5.4 0.7 %copy-start.7 = (s32[128]{0:T(128)S(1)}, s32[128]{0:T(128)}, u32[]{:S(2)}) copy-start(s32[128]{0:T(128)} %constant.67.clone) | copy-start | bytes 1540
  5.4 0.7 %copy-start.8 = (s32[128]{0:T(128)S(1)}, s32[128]{0:T(128)}, u32[]{:S(2)}) copy-start(s32[128]{0:T(128)} %constant.66.clone) | copy-start | bytes 1540
  6.1 0.7 %copy-start.6 = (s32[2,16]{1,0:T(2,128)S(1)}, s32[2,16]{1,0:T(2,128)}, u32[]{:S(2)}) copy-start(s32[2,16]{1,0:T(2,128)} %param.18) | copy-start | bytes 388
  7.7 0.8 %copy-start.4 = (f32[128,128]{1,0:T(8,128)S(1)}, f32[128,128]{1,0:T(8,128)}, u32[]{:S(2)}) copy-start(f32[128,128]{1,0:T(8,128)} %constant.65.clone) | copy-start | bytes 196612
  8.6 4.0 %collective-permute-start.1 = (bf16[16,1024]{1,0:T(8,128)(2,1)S(1)}, bf16[16,1024]{1,0:T(8,128)(2,1)S(1)}, u32[]{:S(2)}, u32[]{:S(2)}) collective-permute-start(bf16[16,1024]{1,0:T(8,128)(2,1)S(1)} %pad_maximum_fusion.2), channel_id=1, source_target_pairs={{0,2},{1,3},{2,0},{3,1},{4,6},{5,7},{6,4},{7,5},{8,10},{9,11},{10,... | collective-permute-start | bytes 98312 | tf_op jit(solution)/shard_map/ppermute | solution.py:25
  12.6 1.7 %copy-start.9 = (s32[2]{0:T(128)S(1)}, s32[2]{0:T(128)}, u32[]{:S(2)}) copy-start(s32[2]{0:T(128)} %param.17) | copy-start | bytes 28
  12.6 4.3 %collective-permute-start.2 = (bf16[32,1024]{1,0:T(8,128)(2,1)S(1)}, bf16[32,1024]{1,0:T(8,128)(2,1)S(1)}, u32[]{:S(2)}, u32[]{:S(2)}) collective-permute-start(bf16[32,1024]{1,0:T(8,128)(2,1)S(1)} %pad_maximum_fusion.1), channel_id=1, source_target_pairs={{0,4},{1,5},{2,6},{3,7},{4,0},{5,1},{6,2},{7,3},{8,12},{9,13},{10,... | collective-permute-start | bytes 196616 | tf_op jit(solution)/shard_map/ppermute | solution.py:25
  14.3 4.1 %copy-start = (f32[256,640]{1,0:T(8,128)}, f32[256,640]{1,0:T(8,128)S(1)}, u32[]{:S(2)}) copy-start(f32[256,640]{1,0:T(8,128)S(1)} %select_dynamic-update-slice_fusion.4.bias_ref) | copy-start | bytes 1966084
  16.9 1.4 %copy-start.1 = (bf16[64,1024]{1,0:T(8,128)(2,1)}, bf16[64,1024]{1,0:T(8,128)(2,1)S(1)}, u32[]{:S(2)}) copy-start(bf16[64,1024]{1,0:T(8,128)(2,1)S(1)} %pad_maximum_fusion.kva_ref) | copy-start | bytes 393220
  16.9 1.4 %collective-permute-start.3 = (bf16[64,1024]{1,0:T(8,128)(2,1)S(1)}, bf16[64,1024]{1,0:T(8,128)(2,1)S(1)}, u32[]{:S(2)}, u32[]{:S(2)}) collective-permute-start(bf16[64,1024]{1,0:T(8,128)(2,1)S(1)} %pad_maximum_fusion.kva_ref), channel_id=1, source_target_pairs={{0,1},{1,0},{2,3},{3,2},{4,5},{5,4},{6,7},{7,6},{8,9},{9,8},{10,11... | collective-permute-start | bytes 393224 | tf_op jit(solution)/shard_map/ppermute | solution.py:25
  18.4 0.7 %copy-start.3 = (bf16[64,1024]{1,0:T(8,128)(2,1)}, bf16[64,1024]{1,0:T(8,128)(2,1)S(1)}, u32[]{:S(2)}) copy-start(bf16[64,1024]{1,0:T(8,128)(2,1)S(1)} %collective-permute-done.3.kvb_ref) | copy-start | bytes 393220
  24.6 1.6 %copy-start.2 = (f32[64,1024]{1,0:T(8,128)S(1)}, f32[64,1024]{1,0:T(8,128)}, u32[]{:S(2)}) copy-start(f32[64,1024]{1,0:T(8,128)} %get-tuple-element.11) | copy-start | bytes 786436
  24.6 1.6 %collective-permute-start.4 = (bf16[64,1024]{1,0:T(8,128)(2,1)}, bf16[64,1024]{1,0:T(8,128)(2,1)S(1)}, u32[]{:S(2)}, u32[]{:S(2)}) collective-permute-start(bf16[64,1024]{1,0:T(8,128)(2,1)} %get-tuple-element.12), channel_id=1, source_target_pairs={{0,1},{1,0},{2,3},{3,2},{4,5},{5,4},{6,7},{7,6},{8,9},{9,8},{10,11... | collective-permute-start | bytes 393224 | tf_op jit(solution)/shard_map/ppermute | solution.py:25
  26.3 4.3 %collective-permute-start.5 = (bf16[32,1024]{1,0:T(8,128)(2,1)S(1)}, bf16[32,1024]{1,0:T(8,128)(2,1)S(1)}, u32[]{:S(2)}, u32[]{:S(2)}) collective-permute-start(bf16[32,1024]{1,0:T(8,128)(2,1)S(1)} %fusion), channel_id=1, source_target_pairs={{0,4},{1,5},{2,6},{3,7},{4,0},{5,1},{6,2},{7,3},{8,12},{9,13},{10,... | collective-permute-start | bytes 196616 | tf_op jit(solution)/shard_map/ppermute | solution.py:25
  30.6 4.0 %collective-permute-start.6 = (bf16[16,1024]{1,0:T(8,128)(2,1)S(1)}, bf16[16,1024]{1,0:T(8,128)(2,1)S(1)}, u32[]{:S(2)}, u32[]{:S(2)}) collective-permute-start(bf16[16,1024]{1,0:T(8,128)(2,1)S(1)} %fusion.2), channel_id=1, source_target_pairs={{0,2},{1,3},{2,0},{3,1},{4,6},{5,7},{6,4},{7,5},{8,10},{9,11},{10,... | collective-permute-start | bytes 98312 | tf_op jit(solution)/shard_map/ppermute | solution.py:25
  34.6 4.7 %collective-permute-start.7 = (bf16[8,1024]{1,0:T(8,128)(2,1)S(1)}, bf16[8,1024]{1,0:T(8,128)(2,1)S(1)}, u32[]{:S(2)}, u32[]{:S(2)}) collective-permute-start(bf16[8,1024]{1,0:T(8,128)(2,1)S(1)} %fusion.5), channel_id=1, source_target_pairs={{0,8},{1,9},{2,10},{3,11},{4,12},{5,13},{6,14},{7,15},{8,0},{9,1},... | collective-permute-start | bytes 49160 | tf_op jit(solution)/shard_map/ppermute | solution.py:25

commit v19 on v15

--- a/solution.py
+++ b/solution.py
@@ -90,7 +90,7 @@
     q_ref, do_ref, kva_ref, kvb_ref, ks_ref, vs_ref, vis_ref, self_ref, live_ref,
     dq_ref, keep_ref, send_ref, sk_ref, sv_ref,
 ):
-    token_rows = q_ref.shape[0]
+    token_rows = q_ref.shape[1] // GROUP_HEADS
     width = KEY_HEADS * HEAD_SIZE
     half = kva_ref.shape[0]
     doc_rows = 2 * half
@@ -108,8 +108,8 @@
         values = jnp.concatenate(
             [kva_ref[:, value_columns], kvb_ref[:, value_columns], vs_ref[:, columns]], axis=0
         )
-        q = stacked_heads(q_ref, c)
-        do = stacked_heads(do_ref, c)
+        q = q_ref[c]
+        do = do_ref[c]
         score = jnp.where(seen, contract_cols(keys, q) * score_scale, masked_score)
         top = jnp.max(score, axis=0, keepdims=True)
         grown = jnp.exp(score - top)
@@ -184,8 +184,12 @@
             jax.ShapeDtypeStruct(response_values.shape, jnp.bfloat16),
         ),
     )(
-        queries,
-        grad_out,
+        jnp.transpose(
+            queries.reshape(token_rows, KEY_HEADS, GROUP_HEADS, HEAD_SIZE), (1, 2, 0, 3)
+        ).reshape(KEY_HEADS, GROUP_HEADS * token_rows, HEAD_SIZE),
+        jnp.transpose(
+            grad_out.reshape(token_rows, KEY_HEADS, GROUP_HEADS, HEAD_SIZE), (1, 2, 0, 3)
+        ).reshape(KEY_HEADS, GROUP_HEADS * token_rows, HEAD_SIZE),
         doc_mine,
         doc_other,
         response_keys,

time: 38.5 us -> 40 us (1.039)
  local copies, waits for them, and re-layouts: 4.36 us -> 6.62 us
  starting transfers between devices: 14.9 us -> 12.9 us
  waiting for transfers between devices: 11.4 us -> 12.7 us
    transpose x0 -> x2, local copies, waits for them, and re-layouts: none -> 2.2 us  [the longest x1 1.1 us: per_device(): jnp.transpose(grad_out.reshape(token_rows, KEY_HEADS, GROUP_HEADS, HEAD_S...]
    ppermute x8, starting transfers between devices: 14.9 us -> 12.9 us  [swap_with(): return lax.ppermute(block, axis_name, pairs)]
    ppermute x8, waiting for transfers between devices: 11.4 us -> 12.7 us  [swap_with(): return lax.ppermute(block, axis_name, pairs)]
    unnamed x18 -> x22, local copies, waits for them, and re-layouts: 2.79 us -> 2.85 us
  transfers between devices with their start and end apart: 8 -> 8, of which waited for: 8 -> 7; matrix products, arithmetic and copies ran while one was open for 6% -> 15% of each run, Pallas kernels for 0% -> 0%
where the time goes in v19:
time: 40 us; the launch traced here: 39.7 us
  starting transfers between devices  12.9 us (32%)
  waiting for transfers between devices  12.7 us (32%)
  local copies, waits for them, and re-layouts  6.62 us (17%)
  Pallas kernels  5.42 us (14%)
  other arithmetic  1.35 us (3%)
  between operations  0.76 us (2%)
    ppermute x8, starting transfers between devices, swap_with(): return lax.ppermute(block, axis_name, pairs)  12.9 us
    ppermute x8, waiting for transfers between devices, swap_with(): return lax.ppermute(block, axis_name, pairs)  12.7 us
    pallas_call x1, Pallas kernels, per_device(): pl.pallas_call(attention_kernel, out_shape=(jax.ShapeDtypeStruct(queries....  5.42 us
    unnamed x22, local copies, waits for them, and re-layouts  2.85 us
    transpose x1, local copies, waits for them, and re-layouts, per_device(): jnp.transpose(grad_out.reshape(token_rows, KEY_HEADS, GROUP_HEADS, HEAD_S...  1.1 us
    transpose x1, local copies, waits for them, and re-layouts, per_device(): jnp.transpose(queries.reshape(token_rows, KEY_HEADS, GROUP_HEADS, HEAD_SI...  1.1 us
  transfers between devices with their start and end apart: 8, of which 7 were waited for; matrix products, arithmetic and copies ran while one was open for 15% of the time, Pallas kernels for 0%

profile of v19, /device:TPU:0, one launch (start us, length us, event | category | flops | bytes accessed | tf_op | source)
XLA Modules:
  0.0 39.7 jit_solution(17774650155564038754)
XLA Ops:
  0.6 0.0 copy-start.6
  0.7 0.8 %constant_dynamic-update-slice_fusion.1 = bf16[8,1024]{1,0:T(8,128)(2,1)S(1)} fusion(bf16[8,512]{1,0:T(8,128)(2,1)} %param.14), kind=kLoop, calls=%fused_computation.22 | loop fusion | bytes 16384
  1.4 4.0 %collective-permute-start = (bf16[8,1024]{1,0:T(8,128)(2,1)S(1)}, bf16[8,1024]{1,0:T(8,128)(2,1)S(1)}, u32[]{:S(2)}, u32[]{:S(2)}) collective-permute-start(bf16[8,1024]{1,0:T(8,128)(2,1)S(1)} %constant_dynamic-update-slice_fusion), channel_id=1, source_target_pairs={{0,8},{1,9},{2,10},{3,11},{4,12},{5,13},{6,14},{7,15},{8,0},{9,1},... | collective-permute-start | bytes 49160 | tf_op jit(solution)/shard_map/ppermute | solution.py:25
  5.5 1.7 %collective-permute-done = bf16[8,1024]{1,0:T(8,128)(2,1)S(1)} collective-permute-done((bf16[8,1024]{1,0:T(8,128)(2,1)S(1)}, bf16[8,1024]{1,0:T(8,128)(2,1)S(1)}, u32[]{:S(2)}, u32[]{:S(2)}) %collective-permute-start) | collective-permute-done | bytes 16416 | tf_op jit(solution)/shard_map/ppermute | solution.py:25
  7.2 1.9 %collective-permute-start.1 = (bf16[16,1024]{1,0:T(8,128)(2,1)S(1)}, bf16[16,1024]{1,0:T(8,128)(2,1)S(1)}, u32[]{:S(2)}, u32[]{:S(2)}) collective-permute-start(bf16[16,1024]{1,0:T(8,128)(2,1)S(1)} %pad_maximum_fusion.2), channel_id=1, source_target_pairs={{0,2},{1,3},{2,0},{3,1},{4,6},{5,7},{6,4},{7,5},{8,10},{9,11},{10,... | collective-permute-start | bytes 98312 | tf_op jit(solution)/shard_map/ppermute | solution.py:25
  9.1 0.8 %copy.23 = s32[2,16]{0,1:T(8,128)S(1)} copy(s32[2,16]{1,0:T(2,128)} %param.18) | data formatting | bytes 256 | tf_op args[7]
  9.8 0.1 broadcast_in_dim.20
  9.9 0.1 reshape.72
  10.0 0.6 %gather_fusion = s32[128,128]{1,0:T(8,128)S(1)} fusion(s32[16,128]{1,0:T(8,128)S(1)} %bitcast.11, s32[1024]{0:T(1024)S(1)} %pad_clamp_fusion), kind=kCustom, calls=%fused_computation | custom fusion | bytes 131584 | tf_op jit(solution)/shard_map/jit(_take)/gather | solution.py:174
  10.7 0.5 %collective-permute-done.1 = bf16[16,1024]{1,0:T(8,128)(2,1)S(1)} collective-permute-done((bf16[16,1024]{1,0:T(8,128)(2,1)S(1)}, bf16[16,1024]{1,0:T(8,128)(2,1)S(1)}, u32[]{:S(2)}, u32[]{:S(2)}) %collective-permute-start.1) | collective-permute-done | bytes 32800 | tf_op jit(solution)/shard_map/ppermute | solution.py:25
  11.1 1.9 %collective-permute-start.2 = (bf16[32,1024]{1,0:T(8,128)(2,1)S(1)}, bf16[32,1024]{1,0:T(8,128)(2,1)S(1)}, u32[]{:S(2)}, u32[]{:S(2)}) collective-permute-start(bf16[32,1024]{1,0:T(8,128)(2,1)S(1)} %pad_maximum_fusion.1), channel_id=1, source_target_pairs={{0,4},{1,5},{2,6},{3,7},{4,0},{5,1},{6,2},{7,3},{8,12},{9,13},{10,... | collective-permute-start | bytes 196616 | tf_op jit(solution)/shard_map/ppermute | solution.py:25
  13.0 0.7 %fusion.3.vis_ref = f32[128,128]{1,0:T(8,128)} fusion(s32[128,128]{1,0:T(8,128)S(1)} %gather_fusion, pred[128]{0:T(512)(128)(4,1)S(1)} %get-tuple-element.15), kind=kLoop, calls=%fused_computation.9 | loop fusion | flops 49152 | bytes 131200 | tf_op jit(solution)/shard_map/convert_element_type | solution.py:174
  13.7 0.1 broadcast_in_dim.23
  13.8 0.1 reshape.73
  13.9 0.3 copy.19
  14.2 1.1 %copy.20 = bf16[4,5,128,128]{3,2,1,0:T(8,128)(2,1)} copy(bf16[4,5,128,128]{2,3,1,0:T(8,128)(2,1)S(1)} %bitcast.14) | data formatting | bytes 1310720 | tf_op jit(solution)/shard_map/transpose | solution.py:187
  15.3 0.3 copy.21
  15.7 1.1 %copy.22 = bf16[4,5,128,128]{3,2,1,0:T(8,128)(2,1)} copy(bf16[4,5,128,128]{2,3,1,0:T(8,128)(2,1)S(1)} %bitcast.15) | data formatting | bytes 1310720 | tf_op jit(solution)/shard_map/transpose | solution.py:190
  16.8 0.1 collective-permute-start.3
  16.9 0.5 %compare_convert_fusion.live_ref = f32[1,128]{1,0:T(1,128)} fusion(s32[1,128]{1,0:T(1,128)S(1)} %reshape.73), kind=kLoop, calls=%fused_computation.24 | loop fusion | flops 1024 | bytes 1024 | tf_op jit(solution)/shard_map/convert_element_type | solution.py:154
  17.4 0.8 %collective-permute-done.3.kvb_ref = bf16[64,1024]{1,0:T(8,128)(2,1)S(1)} collective-permute-done((bf16[64,1024]{1,0:T(8,128)(2,1)S(1)}, bf16[64,1024]{1,0:T(8,128)(2,1)S(1)}, u32[]{:S(2)}, u32[]{:S(2)}) %collective-permute-start.3) | collective-permute-done | bytes 131104 | tf_op jit(solution)/shard_map/ppermute | solution.py:25
  18.2 0.6 %copy-done.4 = bf16[64,1024]{1,0:T(8,128)(2,1)} copy-done((bf16[64,1024]{1,0:T(8,128)(2,1)}, bf16[64,1024]{1,0:T(8,128)(2,1)S(1)}, u32[]{:S(2)}) %copy-start.4) | copy-done | bytes 131096
  18.9 5.4 %shard_map.146 = (bf16[128,2560]{1,0:T(8,128)(2,1)}, f32[64,1024]{1,0:T(8,128)}, bf16[64,1024]{1,0:T(8,128)(2,1)}, bf16[128,512]{1,0:T(8,128)(2,1)}, bf16[128,512]{1,0:T(8,128)(2,1)}) custom-call(bf16[4,640,128]{2,1,0:T(8,128)(2,1)} %bitcast.12, bf16[4,640,128]{2,1,0:T(8,128)(2,1)} %bitcast.13, bf16[64,1024]{1,0:T(8,128)(2,1)} %copy-done.2, ...), custom_call_target="tpu_custom_call" | custom-call | tf_op jit(solution)/shard_map/pallas_call | solution.py:177
  24.3 0.1 collective-permute-start.4
  24.4 1.4 %collective-permute-done.4 = bf16[64,1024]{1,0:T(8,128)(2,1)S(1)} collective-permute-done((bf16[64,1024]{1,0:T(8,128)(2,1)}, bf16[64,1024]{1,0:T(8,128)(2,1)S(1)}, u32[]{:S(2)}, u32[]{:S(2)}) %collective-permute-start.4) | collective-permute-done | bytes 131104 | tf_op jit(solution)/shard_map/ppermute | solution.py:25
  25.9 0.6 %collective-permute-start.5 = (bf16[32,1024]{1,0:T(8,128)(2,1)S(1)}, bf16[32,1024]{1,0:T(8,128)(2,1)S(1)}, u32[]{:S(2)}, u32[]{:S(2)}) collective-permute-start(bf16[32,1024]{1,0:T(8,128)(2,1)S(1)} %fusion), channel_id=1, source_target_pairs={{0,4},{1,5},{2,6},{3,7},{4,0},{5,1},{6,2},{7,3},{8,12},{9,13},{10,... | collective-permute-start | bytes 196616 | tf_op jit(solution)/shard_map/ppermute | solution.py:25
  26.5 3.7 %collective-permute-done.5 = bf16[32,1024]{1,0:T(8,128)(2,1)S(1)} collective-permute-done((bf16[32,1024]{1,0:T(8,128)(2,1)S(1)}, bf16[32,1024]{1,0:T(8,128)(2,1)S(1)}, u32[]{:S(2)}, u32[]{:S(2)}) %collective-permute-start.5) | collective-permute-done | bytes 65568 | tf_op jit(solution)/shard_map/ppermute | solution.py:25
  30.3 1.6 %collective-permute-start.6 = (bf16[16,1024]{1,0:T(8,128)(2,1)S(1)}, bf16[16,1024]{1,0:T(8,128)(2,1)S(1)}, u32[]{:S(2)}, u32[]{:S(2)}) collective-permute-start(bf16[16,1024]{1,0:T(8,128)(2,1)S(1)} %fusion.2), channel_id=1, source_target_pairs={{0,2},{1,3},{2,0},{3,1},{4,6},{5,7},{6,4},{7,5},{8,10},{9,11},{10,... | collective-permute-start | bytes 98312 | tf_op jit(solution)/shard_map/ppermute | solution.py:25
  31.8 2.4 %collective-permute-done.6 = bf16[16,1024]{1,0:T(8,128)(2,1)S(1)} collective-permute-done((bf16[16,1024]{1,0:T(8,128)(2,1)S(1)}, bf16[16,1024]{1,0:T(8,128)(2,1)S(1)}, u32[]{:S(2)}, u32[]{:S(2)}) %collective-permute-start.6) | collective-permute-done | bytes 32800 | tf_op jit(solution)/shard_map/ppermute | solution.py:25
  34.3 2.7 %collective-permute-start.7 = (bf16[8,1024]{1,0:T(8,128)(2,1)S(1)}, bf16[8,1024]{1,0:T(8,128)(2,1)S(1)}, u32[]{:S(2)}, u32[]{:S(2)}) collective-permute-start(bf16[8,1024]{1,0:T(8,128)(2,1)S(1)} %fusion.5), channel_id=1, source_target_pairs={{0,8},{1,9},{2,10},{3,11},{4,12},{5,13},{6,14},{7,15},{8,0},{9,1},... | collective-permute-start | bytes 49160 | tf_op jit(solution)/shard_map/ppermute | solution.py:25
  37.0 2.1 %collective-permute-done.7 = bf16[8,1024]{1,0:T(8,128)(2,1)S(1)} collective-permute-done((bf16[8,1024]{1,0:T(8,128)(2,1)S(1)}, bf16[8,1024]{1,0:T(8,128)(2,1)S(1)}, u32[]{:S(2)}, u32[]{:S(2)}) %collective-permute-start.7) | collective-permute-done | bytes 16416 | tf_op jit(solution)/shard_map/ppermute | solution.py:25
  39.1 0.6 %fusion.8 = (bf16[8,512]{1,0:T(8,128)(2,1)}, bf16[8,512]{1,0:T(8,128)(2,1)}) fusion(bf16[8,1024]{1,0:T(8,128)(2,1)S(1)} %fusion.7), kind=kLoop, calls=%fused_computation.31 | loop fusion | bytes 32768 | tf_op jit(solution)/shard_map/slice | solution.py:205
  (30 shorter events, 0.2 us)
Async XLA Ops:
  0.6 4.9 %copy-start.6 = (s32[128]{0:T(128)S(1)}, s32[128]{0:T(128)}, u32[]{:S(2)}) copy-start(s32[128]{0:T(128)} %constant.61.clone) | copy-start | bytes 1540
  0.6 4.8 %copy-start.7 = (s32[128]{0:T(128)S(1)}, s32[128]{0:T(128)}, u32[]{:S(2)}) copy-start(s32[128]{0:T(128)} %constant.60.clone) | copy-start | bytes 1540
  0.7 0.8 %copy-start.5 = (bf16[8,512]{1,0:T(8,128)(2,1)S(1)}, bf16[8,512]{1,0:T(8,128)(2,1)}, u32[]{:S(2)}) copy-start(bf16[8,512]{1,0:T(8,128)(2,1)} %param.15) | copy-start | bytes 24580
  0.7 13.2 %copy-start = (bf16[128,2560]{1,0:T(8,128)(2,1)S(1)}, bf16[128,2560]{1,0:T(8,128)(2,1)}, u32[]{:S(2)}) copy-start(bf16[128,2560]{1,0:T(8,128)(2,1)} %param.11) | copy-start | bytes 1966084
  1.4 5.8 %collective-permute-start = (bf16[8,1024]{1,0:T(8,128)(2,1)S(1)}, bf16[8,1024]{1,0:T(8,128)(2,1)S(1)}, u32[]{:S(2)}, u32[]{:S(2)}) collective-permute-start(bf16[8,1024]{1,0:T(8,128)(2,1)S(1)} %constant_dynamic-update-slice_fusion), channel_id=1, source_target_pairs={{0,8},{1,9},{2,10},{3,11},{4,12},{5,13},{6,14},{7,15},{8,0},{9,1},... | collective-permute-start | bytes 49160 | tf_op jit(solution)/shard_map/ppermute | solution.py:25
  7.2 3.9 %collective-permute-start.1 = (bf16[16,1024]{1,0:T(8,128)(2,1)S(1)}, bf16[16,1024]{1,0:T(8,128)(2,1)S(1)}, u32[]{:S(2)}, u32[]{:S(2)}) collective-permute-start(bf16[16,1024]{1,0:T(8,128)(2,1)S(1)} %pad_maximum_fusion.2), channel_id=1, source_target_pairs={{0,2},{1,3},{2,0},{3,1},{4,6},{5,7},{6,4},{7,5},{8,10},{9,11},{10,... | collective-permute-start | bytes 98312 | tf_op jit(solution)/shard_map/ppermute | solution.py:25
  11.1 5.7 %collective-permute-start.2 = (bf16[32,1024]{1,0:T(8,128)(2,1)S(1)}, bf16[32,1024]{1,0:T(8,128)(2,1)S(1)}, u32[]{:S(2)}, u32[]{:S(2)}) collective-permute-start(bf16[32,1024]{1,0:T(8,128)(2,1)S(1)} %pad_maximum_fusion.1), channel_id=1, source_target_pairs={{0,4},{1,5},{2,6},{3,7},{4,0},{5,1},{6,2},{7,3},{8,12},{9,13},{10,... | collective-permute-start | bytes 196616 | tf_op jit(solution)/shard_map/ppermute | solution.py:25
  13.0 0.7 %copy-start.8 = (s32[2]{0:T(128)S(1)}, s32[2]{0:T(128)}, u32[]{:S(2)}) copy-start(s32[2]{0:T(128)} %param.17) | copy-start | bytes 28
  14.2 1.1 %copy-start.1 = (bf16[128,2560]{1,0:T(8,128)(2,1)S(1)}, bf16[128,2560]{1,0:T(8,128)(2,1)}, u32[]{:S(2)}) copy-start(bf16[128,2560]{1,0:T(8,128)(2,1)} %param.16) | copy-start | bytes 1966084
  16.8 1.4 %copy-start.2 = (bf16[64,1024]{1,0:T(8,128)(2,1)}, bf16[64,1024]{1,0:T(8,128)(2,1)S(1)}, u32[]{:S(2)}) copy-start(bf16[64,1024]{1,0:T(8,128)(2,1)S(1)} %pad_maximum_fusion.kva_ref) | copy-start | bytes 393220
  16.8 1.4 %collective-permute-start.3 = (bf16[64,1024]{1,0:T(8,128)(2,1)S(1)}, bf16[64,1024]{1,0:T(8,128)(2,1)S(1)}, u32[]{:S(2)}, u32[]{:S(2)}) collective-permute-start(bf16[64,1024]{1,0:T(8,128)(2,1)S(1)} %pad_maximum_fusion.kva_ref), channel_id=1, source_target_pairs={{0,1},{1,0},{2,3},{3,2},{4,5},{5,4},{6,7},{7,6},{8,9},{9,8},{10,11... | collective-permute-start | bytes 393224 | tf_op jit(solution)/shard_map/ppermute | solution.py:25
  18.2 0.7 %copy-start.4 = (bf16[64,1024]{1,0:T(8,128)(2,1)}, bf16[64,1024]{1,0:T(8,128)(2,1)S(1)}, u32[]{:S(2)}) copy-start(bf16[64,1024]{1,0:T(8,128)(2,1)S(1)} %collective-permute-done.3.kvb_ref) | copy-start | bytes 393220
  24.3 1.6 %copy-start.3 = (f32[64,1024]{1,0:T(8,128)S(1)}, f32[64,1024]{1,0:T(8,128)}, u32[]{:S(2)}) copy-start(f32[64,1024]{1,0:T(8,128)} %get-tuple-element.11) | copy-start | bytes 786436
  24.3 1.6 %collective-permute-start.4 = (bf16[64,1024]{1,0:T(8,128)(2,1)}, bf16[64,1024]{1,0:T(8,128)(2,1)S(1)}, u32[]{:S(2)}, u32[]{:S(2)}) collective-permute-start(bf16[64,1024]{1,0:T(8,128)(2,1)} %get-tuple-element.12), channel_id=1, source_target_pairs={{0,1},{1,0},{2,3},{3,2},{4,5},{5,4},{6,7},{7,6},{8,9},{9,8},{10,11... | collective-permute-start | bytes 393224 | tf_op jit(solution)/shard_map/ppermute | solution.py:25
  25.9 4.3 %collective-permute-start.5 = (bf16[32,1024]{1,0:T(8,128)(2,1)S(1)}, bf16[32,1024]{1,0:T(8,128)(2,1)S(1)}, u32[]{:S(2)}, u32[]{:S(2)}) collective-permute-start(bf16[32,1024]{1,0:T(8,128)(2,1)S(1)} %fusion), channel_id=1, source_target_pairs={{0,4},{1,5},{2,6},{3,7},{4,0},{5,1},{6,2},{7,3},{8,12},{9,13},{10,... | collective-permute-start | bytes 196616 | tf_op jit(solution)/shard_map/ppermute | solution.py:25
  30.3 4.0 %collective-permute-start.6 = (bf16[16,1024]{1,0:T(8,128)(2,1)S(1)}, bf16[16,1024]{1,0:T(8,128)(2,1)S(1)}, u32[]{:S(2)}, u32[]{:S(2)}) collective-permute-start(bf16[16,1024]{1,0:T(8,128)(2,1)S(1)} %fusion.2), channel_id=1, source_target_pairs={{0,2},{1,3},{2,0},{3,1},{4,6},{5,7},{6,4},{7,5},{8,10},{9,11},{10,... | collective-permute-start | bytes 98312 | tf_op jit(solution)/shard_map/ppermute | solution.py:25
  34.3 4.8 %collective-permute-start.7 = (bf16[8,1024]{1,0:T(8,128)(2,1)S(1)}, bf16[8,1024]{1,0:T(8,128)(2,1)S(1)}, u32[]{:S(2)}, u32[]{:S(2)}) collective-permute-start(bf16[8,1024]{1,0:T(8,128)(2,1)S(1)} %fusion.5), channel_id=1, source_target_pairs={{0,8},{1,9},{2,10},{3,11},{4,12},{5,13},{6,14},{7,15},{8,0},{9,1},... | collective-permute-start | bytes 49160 | tf_op jit(solution)/shard_map/ppermute | solution.py:25

commit v20 on v15

--- a/solution.py
+++ b/solution.py
@@ -87,7 +87,7 @@
 
 
 def attention_kernel(
-    q_ref, do_ref, kva_ref, kvb_ref, ks_ref, vs_ref, vis_ref, self_ref, live_ref,
+    q_ref, do_ref, kva_ref, kvb_ref, ks_ref, vs_ref, seen_ref, live_ref,
     dq_ref, keep_ref, send_ref, sk_ref, sv_ref,
 ):
     token_rows = q_ref.shape[0]
@@ -95,9 +95,7 @@
     half = kva_ref.shape[0]
     doc_rows = 2 * half
     score_scale = HEAD_SIZE ** (-0.5)
-    seen = jnp.concatenate(
-        [jnp.concatenate([vis_ref[...], self_ref[...]], axis=0)] * GROUP_HEADS, axis=1
-    ) > 0.5
+    seen = jnp.concatenate([seen_ref[...]] * GROUP_HEADS, axis=1) > 0.5
     live = jnp.concatenate([live_ref[...]] * GROUP_HEADS, axis=1)
     for c in range(KEY_HEADS):
         columns = slice(c * HEAD_SIZE, (c + 1) * HEAD_SIZE)
@@ -190,8 +188,7 @@
         doc_other,
         response_keys,
         response_values,
-        doc_visible,
-        self_visible,
+        jnp.concatenate([doc_visible, self_visible]),
         live,
     )
     summed = scatter_sum_rows(doc_keep, doc_send, "resp")

time: 38.5 us -> 38.7 us (level)
  local copies, waits for them, and re-layouts: 4.36 us -> 4.92 us
    concatenate x0 -> x1, other arithmetic: none -> 0.65 us  [per_device(): jnp.concatenate([doc_visible, self_visible])]
    convert_element_type x1, other arithmetic: 0.72 us -> 0.08 us  [per_device(): (jnp.take(row_masks.T, global_rows // block_rows, axis=0) == 1).astype(jn...]
    unnamed x18 -> x20, local copies, waits for them, and re-layouts: 2.79 us -> 3.35 us
where the time goes in v20:
time: 38.7 us; the launch traced here: 38.4 us
  starting transfers between devices  14.8 us (38%)
  waiting for transfers between devices  11.1 us (29%)
  Pallas kernels  5.46 us (14%)
  local copies, waits for them, and re-layouts  4.92 us (13%)
  other arithmetic  1.38 us (4%)
  between operations  0.73 us (2%)
    ppermute x8, starting transfers between devices, swap_with(): return lax.ppermute(block, axis_name, pairs)  14.8 us
    ppermute x8, waiting for transfers between devices, swap_with(): return lax.ppermute(block, axis_name, pairs)  11.1 us
    pallas_call x1, Pallas kernels, per_device(): pl.pallas_call(attention_kernel, out_shape=(jax.ShapeDtypeStruct(queries....  5.46 us
    unnamed x20, local copies, waits for them, and re-layouts  3.35 us
  transfers between devices with their start and end apart: 8, of which 8 were waited for; matrix products, arithmetic and copies ran while one was open for 6% of the time, Pallas kernels for 0%

profile of v20, /device:TPU:0, one launch (start us, length us, event | category | flops | bytes accessed | tf_op | source)
XLA Modules:
  0.0 38.4 jit_solution(5935418675854907431)
XLA Ops:
  0.6 0.7 %constant_dynamic-update-slice_fusion.1 = bf16[8,1024]{1,0:T(8,128)(2,1)S(1)} fusion(bf16[8,512]{1,0:T(8,128)(2,1)} %param.14), kind=kLoop, calls=%fused_computation.23 | loop fusion | bytes 16384
  1.4 4.0 %collective-permute-start = (bf16[8,1024]{1,0:T(8,128)(2,1)S(1)}, bf16[8,1024]{1,0:T(8,128)(2,1)S(1)}, u32[]{:S(2)}, u32[]{:S(2)}) collective-permute-start(bf16[8,1024]{1,0:T(8,128)(2,1)S(1)} %constant_dynamic-update-slice_fusion), channel_id=1, source_target_pairs={{0,8},{1,9},{2,10},{3,11},{4,12},{5,13},{6,14},{7,15},{8,0},{9,1},... | collective-permute-start | bytes 49160 | tf_op jit(solution)/shard_map/ppermute | solution.py:25
  5.4 0.7 %copy-done.6 = s32[128]{0:T(128)S(1)} copy-done((s32[128]{0:T(128)S(1)}, s32[128]{0:T(128)}, u32[]{:S(2)}) %copy-start.6) | copy-done | bytes 536
  6.1 1.0 %collective-permute-done = bf16[8,1024]{1,0:T(8,128)(2,1)S(1)} collective-permute-done((bf16[8,1024]{1,0:T(8,128)(2,1)S(1)}, bf16[8,1024]{1,0:T(8,128)(2,1)S(1)}, u32[]{:S(2)}, u32[]{:S(2)}) %collective-permute-start) | collective-permute-done | bytes 16416 | tf_op jit(solution)/shard_map/ppermute | solution.py:25
  7.1 1.9 %collective-permute-start.1 = (bf16[16,1024]{1,0:T(8,128)(2,1)S(1)}, bf16[16,1024]{1,0:T(8,128)(2,1)S(1)}, u32[]{:S(2)}, u32[]{:S(2)}) collective-permute-start(bf16[16,1024]{1,0:T(8,128)(2,1)S(1)} %pad_maximum_fusion.3), channel_id=1, source_target_pairs={{0,2},{1,3},{2,0},{3,1},{4,6},{5,7},{6,4},{7,5},{8,10},{9,11},{10,... | collective-permute-start | bytes 98312 | tf_op jit(solution)/shard_map/ppermute | solution.py:25
  9.0 0.7 %copy-done.5 = s32[2,16]{1,0:T(2,128)S(1)} copy-done((s32[2,16]{1,0:T(2,128)S(1)}, s32[2,16]{1,0:T(2,128)}, u32[]{:S(2)}) %copy-start.5) | copy-done | bytes 152
  9.7 0.1 copy.16
  9.7 0.1 broadcast_in_dim.20
  9.8 0.1 reshape.56
  9.9 0.6 %gather_fusion = s32[128,128]{1,0:T(8,128)S(1)} fusion(s32[16,128]{1,0:T(8,128)S(1)} %bitcast.3, s32[1024]{0:T(1024)S(1)} %pad_clamp_fusion), kind=kCustom, calls=%fused_computation | custom fusion | bytes 131584 | tf_op jit(solution)/shard_map/jit(_take)/gather | solution.py:172
  10.6 0.5 %collective-permute-done.1 = bf16[16,1024]{1,0:T(8,128)(2,1)S(1)} collective-permute-done((bf16[16,1024]{1,0:T(8,128)(2,1)S(1)}, bf16[16,1024]{1,0:T(8,128)(2,1)S(1)}, u32[]{:S(2)}, u32[]{:S(2)}) %collective-permute-start.1) | collective-permute-done | bytes 32800 | tf_op jit(solution)/shard_map/ppermute | solution.py:25
  11.0 1.9 %collective-permute-start.2 = (bf16[32,1024]{1,0:T(8,128)(2,1)S(1)}, bf16[32,1024]{1,0:T(8,128)(2,1)S(1)}, u32[]{:S(2)}, u32[]{:S(2)}) collective-permute-start(bf16[32,1024]{1,0:T(8,128)(2,1)S(1)} %pad_maximum_fusion.2), channel_id=1, source_target_pairs={{0,4},{1,5},{2,6},{3,7},{4,0},{5,1},{6,2},{7,3},{8,12},{9,13},{10,... | collective-permute-start | bytes 196616 | tf_op jit(solution)/shard_map/ppermute | solution.py:25
  12.9 0.1 fusion.3
  13.0 0.6 %copy-done.8 = s32[2]{0:T(128)S(1)} copy-done((s32[2]{0:T(128)S(1)}, s32[2]{0:T(128)}, u32[]{:S(2)}) %copy-start.8) | copy-done | bytes 32
  13.6 0.1 broadcast_in_dim.23
  13.7 0.1 reshape.57
  13.8 1.5 %collective-permute-done.2 = bf16[32,1024]{1,0:T(8,128)(2,1)S(1)} collective-permute-done((bf16[32,1024]{1,0:T(8,128)(2,1)S(1)}, bf16[32,1024]{1,0:T(8,128)(2,1)S(1)}, u32[]{:S(2)}, u32[]{:S(2)}) %collective-permute-start.2) | collective-permute-done | bytes 65568 | tf_op jit(solution)/shard_map/ppermute | solution.py:25
  15.3 0.1 collective-permute-start.3
  15.4 0.5 %compare_convert_fusion.live_ref = f32[1,128]{1,0:T(1,128)} fusion(s32[1,128]{1,0:T(1,128)S(1)} %reshape.57), kind=kLoop, calls=%fused_computation.25 | loop fusion | flops 1024 | bytes 1024 | tf_op jit(solution)/shard_map/convert_element_type | solution.py:152
  15.9 0.7 %pad_maximum_fusion.1.seen_ref = f32[256,128]{1,0:T(8,128)} fusion(f32[128,128]{1,0:T(8,128)S(1)} %copy-done.3, f32[128,128]{1,0:T(8,128)S(1)} %fusion.3), kind=kLoop, calls=%fused_computation.4 | loop fusion | flops 32768 | bytes 262144 | tf_op jit(solution)/shard_map/concatenate | solution.py:191
  16.6 0.2 collective-permute-done.3.kvb_ref
  16.7 0.6 %copy-done.2 = bf16[64,1024]{1,0:T(8,128)(2,1)} copy-done((bf16[64,1024]{1,0:T(8,128)(2,1)}, bf16[64,1024]{1,0:T(8,128)(2,1)S(1)}, u32[]{:S(2)}) %copy-start.2) | copy-done | bytes 131096
  17.4 5.5 %shard_map.146 = (bf16[128,2560]{1,0:T(8,128)(2,1)}, f32[64,1024]{1,0:T(8,128)}, bf16[64,1024]{1,0:T(8,128)(2,1)}, bf16[128,512]{1,0:T(8,128)(2,1)}, bf16[128,512]{1,0:T(8,128)(2,1)}) custom-call(bf16[128,2560]{1,0:T(8,128)(2,1)} %q_ref.1, bf16[128,2560]{1,0:T(8,128)(2,1)} %do_ref.1, bf16[64,1024]{1,0:T(8,128)(2,1)} %copy-done, bf16[64,1024]{1,0:T(8,128)(2,1)} %copy-done.2, ...), custom_call_target="tpu_custom_call" | custom-call | tf_op jit(solution)/shard_map/pallas_call | solution.py:175
  22.8 0.3 collective-permute-start.4
  23.2 1.2 %collective-permute-done.4 = bf16[64,1024]{1,0:T(8,128)(2,1)S(1)} collective-permute-done((bf16[64,1024]{1,0:T(8,128)(2,1)}, bf16[64,1024]{1,0:T(8,128)(2,1)S(1)}, u32[]{:S(2)}, u32[]{:S(2)}) %collective-permute-start.4) | collective-permute-done | bytes 131104 | tf_op jit(solution)/shard_map/ppermute | solution.py:25
  24.5 2.0 %collective-permute-start.5 = (bf16[32,1024]{1,0:T(8,128)(2,1)S(1)}, bf16[32,1024]{1,0:T(8,128)(2,1)S(1)}, u32[]{:S(2)}, u32[]{:S(2)}) collective-permute-start(bf16[32,1024]{1,0:T(8,128)(2,1)S(1)} %fusion), channel_id=1, source_target_pairs={{0,4},{1,5},{2,6},{3,7},{4,0},{5,1},{6,2},{7,3},{8,12},{9,13},{10,... | collective-permute-start | bytes 196616 | tf_op jit(solution)/shard_map/ppermute | solution.py:25
  26.4 2.6 %collective-permute-done.5 = bf16[32,1024]{1,0:T(8,128)(2,1)S(1)} collective-permute-done((bf16[32,1024]{1,0:T(8,128)(2,1)S(1)}, bf16[32,1024]{1,0:T(8,128)(2,1)S(1)}, u32[]{:S(2)}, u32[]{:S(2)}) %collective-permute-start.5) | collective-permute-done | bytes 65568 | tf_op jit(solution)/shard_map/ppermute | solution.py:25
  29.1 1.8 %collective-permute-start.6 = (bf16[16,1024]{1,0:T(8,128)(2,1)S(1)}, bf16[16,1024]{1,0:T(8,128)(2,1)S(1)}, u32[]{:S(2)}, u32[]{:S(2)}) collective-permute-start(bf16[16,1024]{1,0:T(8,128)(2,1)S(1)} %fusion.2), channel_id=1, source_target_pairs={{0,2},{1,3},{2,0},{3,1},{4,6},{5,7},{6,4},{7,5},{8,10},{9,11},{10,... | collective-permute-start | bytes 98312 | tf_op jit(solution)/shard_map/ppermute | solution.py:25
  30.8 2.2 %collective-permute-done.6 = bf16[16,1024]{1,0:T(8,128)(2,1)S(1)} collective-permute-done((bf16[16,1024]{1,0:T(8,128)(2,1)S(1)}, bf16[16,1024]{1,0:T(8,128)(2,1)S(1)}, u32[]{:S(2)}, u32[]{:S(2)}) %collective-permute-start.6) | collective-permute-done | bytes 32800 | tf_op jit(solution)/shard_map/ppermute | solution.py:25
  33.1 2.8 %collective-permute-start.7 = (bf16[8,1024]{1,0:T(8,128)(2,1)S(1)}, bf16[8,1024]{1,0:T(8,128)(2,1)S(1)}, u32[]{:S(2)}, u32[]{:S(2)}) collective-permute-start(bf16[8,1024]{1,0:T(8,128)(2,1)S(1)} %fusion.5), channel_id=1, source_target_pairs={{0,8},{1,9},{2,10},{3,11},{4,12},{5,13},{6,14},{7,15},{8,0},{9,1},... | collective-permute-start | bytes 49160 | tf_op jit(solution)/shard_map/ppermute | solution.py:25
  35.9 1.9 %collective-permute-done.7 = bf16[8,1024]{1,0:T(8,128)(2,1)S(1)} collective-permute-done((bf16[8,1024]{1,0:T(8,128)(2,1)S(1)}, bf16[8,1024]{1,0:T(8,128)(2,1)S(1)}, u32[]{:S(2)}, u32[]{:S(2)}) %collective-permute-start.7) | collective-permute-done | bytes 16416 | tf_op jit(solution)/shard_map/ppermute | solution.py:25
  37.8 0.6 %fusion.8 = (bf16[8,512]{1,0:T(8,128)(2,1)}, bf16[8,512]{1,0:T(8,128)(2,1)}) fusion(bf16[8,1024]{1,0:T(8,128)(2,1)S(1)} %fusion.7), kind=kLoop, calls=%fused_computation.32 | loop fusion | bytes 32768 | tf_op jit(solution)/shard_map/slice | solution.py:198
  (27 shorter events, 0.2 us)
Async XLA Ops:
  0.6 0.7 %copy-start.4 = (bf16[8,512]{1,0:T(8,128)(2,1)S(1)}, bf16[8,512]{1,0:T(8,128)(2,1)}, u32[]{:S(2)}) copy-start(bf16[8,512]{1,0:T(8,128)(2,1)} %param.15) | copy-start | bytes 24580
  1.4 5.8 %collective-permute-start = (bf16[8,1024]{1,0:T(8,128)(2,1)S(1)}, bf16[8,1024]{1,0:T(8,128)(2,1)S(1)}, u32[]{:S(2)}, u32[]{:S(2)}) collective-permute-start(bf16[8,1024]{1,0:T(8,128)(2,1)S(1)} %constant_dynamic-update-slice_fusion), channel_id=1, source_target_pairs={{0,8},{1,9},{2,10},{3,11},{4,12},{5,13},{6,14},{7,15},{8,0},{9,1},... | collective-permute-start | bytes 49160 | tf_op jit(solution)/shard_map/ppermute | solution.py:25
  5.4 0.7 %copy-start.6 = (s32[128]{0:T(128)S(1)}, s32[128]{0:T(128)}, u32[]{:S(2)}) copy-start(s32[128]{0:T(128)} %constant.61.clone) | copy-start | bytes 1540
  5.4 0.7 %copy-start.7 = (s32[128]{0:T(128)S(1)}, s32[128]{0:T(128)}, u32[]{:S(2)}) copy-start(s32[128]{0:T(128)} %constant.60.clone) | copy-start | bytes 1540
  7.1 3.9 %collective-permute-start.1 = (bf16[16,1024]{1,0:T(8,128)(2,1)S(1)}, bf16[16,1024]{1,0:T(8,128)(2,1)S(1)}, u32[]{:S(2)}, u32[]{:S(2)}) collective-permute-start(bf16[16,1024]{1,0:T(8,128)(2,1)S(1)} %pad_maximum_fusion.3), channel_id=1, source_target_pairs={{0,2},{1,3},{2,0},{3,1},{4,6},{5,7},{6,4},{7,5},{8,10},{9,11},{10,... | collective-permute-start | bytes 98312 | tf_op jit(solution)/shard_map/ppermute | solution.py:25
  9.0 0.7 %copy-start.5 = (s32[2,16]{1,0:T(2,128)S(1)}, s32[2,16]{1,0:T(2,128)}, u32[]{:S(2)}) copy-start(s32[2,16]{1,0:T(2,128)} %param.18) | copy-start | bytes 388
  11.0 4.3 %collective-permute-start.2 = (bf16[32,1024]{1,0:T(8,128)(2,1)S(1)}, bf16[32,1024]{1,0:T(8,128)(2,1)S(1)}, u32[]{:S(2)}, u32[]{:S(2)}) collective-permute-start(bf16[32,1024]{1,0:T(8,128)(2,1)S(1)} %pad_maximum_fusion.2), channel_id=1, source_target_pairs={{0,4},{1,5},{2,6},{3,7},{4,0},{5,1},{6,2},{7,3},{8,12},{9,13},{10,... | collective-permute-start | bytes 196616 | tf_op jit(solution)/shard_map/ppermute | solution.py:25
  12.9 0.7 %copy-start.8 = (s32[2]{0:T(128)S(1)}, s32[2]{0:T(128)}, u32[]{:S(2)}) copy-start(s32[2]{0:T(128)} %param.17) | copy-start | bytes 28
  13.7 2.2 %copy-start.3 = (f32[128,128]{1,0:T(8,128)S(1)}, f32[128,128]{1,0:T(8,128)}, u32[]{:S(2)}) copy-start(f32[128,128]{1,0:T(8,128)} %constant.59.clone) | copy-start | bytes 196612
  15.3 1.3 %copy-start = (bf16[64,1024]{1,0:T(8,128)(2,1)}, bf16[64,1024]{1,0:T(8,128)(2,1)S(1)}, u32[]{:S(2)}) copy-start(bf16[64,1024]{1,0:T(8,128)(2,1)S(1)} %pad_maximum_fusion.kva_ref) | copy-start | bytes 393220
  15.3 1.4 %collective-permute-start.3 = (bf16[64,1024]{1,0:T(8,128)(2,1)S(1)}, bf16[64,1024]{1,0:T(8,128)(2,1)S(1)}, u32[]{:S(2)}, u32[]{:S(2)}) collective-permute-start(bf16[64,1024]{1,0:T(8,128)(2,1)S(1)} %pad_maximum_fusion.kva_ref), channel_id=1, source_target_pairs={{0,1},{1,0},{2,3},{3,2},{4,5},{5,4},{6,7},{7,6},{8,9},{9,8},{10,11... | collective-permute-start | bytes 393224 | tf_op jit(solution)/shard_map/ppermute | solution.py:25
  16.7 0.6 %copy-start.2 = (bf16[64,1024]{1,0:T(8,128)(2,1)}, bf16[64,1024]{1,0:T(8,128)(2,1)S(1)}, u32[]{:S(2)}) copy-start(bf16[64,1024]{1,0:T(8,128)(2,1)S(1)} %collective-permute-done.3.kvb_ref) | copy-start | bytes 393220
  22.8 1.6 %copy-start.1 = (f32[64,1024]{1,0:T(8,128)S(1)}, f32[64,1024]{1,0:T(8,128)}, u32[]{:S(2)}) copy-start(f32[64,1024]{1,0:T(8,128)} %get-tuple-element.11) | copy-start | bytes 786436
  22.8 1.6 %collective-permute-start.4 = (bf16[64,1024]{1,0:T(8,128)(2,1)}, bf16[64,1024]{1,0:T(8,128)(2,1)S(1)}, u32[]{:S(2)}, u32[]{:S(2)}) collective-permute-start(bf16[64,1024]{1,0:T(8,128)(2,1)} %get-tuple-element.12), channel_id=1, source_target_pairs={{0,1},{1,0},{2,3},{3,2},{4,5},{5,4},{6,7},{7,6},{8,9},{9,8},{10,11... | collective-permute-start | bytes 393224 | tf_op jit(solution)/shard_map/ppermute | solution.py:25
  24.5 4.6 %collective-permute-start.5 = (bf16[32,1024]{1,0:T(8,128)(2,1)S(1)}, bf16[32,1024]{1,0:T(8,128)(2,1)S(1)}, u32[]{:S(2)}, u32[]{:S(2)}) collective-permute-start(bf16[32,1024]{1,0:T(8,128)(2,1)S(1)} %fusion), channel_id=1, source_target_pairs={{0,4},{1,5},{2,6},{3,7},{4,0},{5,1},{6,2},{7,3},{8,12},{9,13},{10,... | collective-permute-start | bytes 196616 | tf_op jit(solution)/shard_map/ppermute | solution.py:25
  29.1 4.0 %collective-permute-start.6 = (bf16[16,1024]{1,0:T(8,128)(2,1)S(1)}, bf16[16,1024]{1,0:T(8,128)(2,1)S(1)}, u32[]{:S(2)}, u32[]{:S(2)}) collective-permute-start(bf16[16,1024]{1,0:T(8,128)(2,1)S(1)} %fusion.2), channel_id=1, source_target_pairs={{0,2},{1,3},{2,0},{3,1},{4,6},{5,7},{6,4},{7,5},{8,10},{9,11},{10,... | collective-permute-start | bytes 98312 | tf_op jit(solution)/shard_map/ppermute | solution.py:25
  33.1 4.7 %collective-permute-start.7 = (bf16[8,1024]{1,0:T(8,128)(2,1)S(1)}, bf16[8,1024]{1,0:T(8,128)(2,1)S(1)}, u32[]{:S(2)}, u32[]{:S(2)}) collective-permute-start(bf16[8,1024]{1,0:T(8,128)(2,1)S(1)} %fusion.5), channel_id=1, source_target_pairs={{0,8},{1,9},{2,10},{3,11},{4,12},{5,13},{6,14},{7,15},{8,0},{9,1},... | collective-permute-start | bytes 49160 | tf_op jit(solution)/shard_map/ppermute | solution.py:25
